TPU v7x, 32 devices: a whole 2x2x4 slice. The times are simulated.
32 devices in a mesh: sub: 8 (over y, x, core), grp: 4 (over z).
Axes of the slice: x: 2, y: 2, z: 4, core: 2. Of those that a mesh axis runs over, the one named last changes fastest.
Arguments:
- gaps: float32 [4, 16, 96, 1024], P('grp', 'sub'), may hold values from -6 to 6
- dual_op: bfloat16 [4, 16, 1024, 1024], P('grp', 'sub'), may hold values from -1 to 2.5, as said below
- dirichlet: bfloat16 [4, 16, 1024, 1024], P('grp', 'sub'), may hold values from -1 to 2.5, as said below
- modes: float32 [4, 16, 6, 1024], P('grp', 'sub'), may hold values from -6 to 6
- coarse_op: float32 [4, 16, 6, 384], P('grp', 'sub'), may hold values from -0.0009765625 to 0.0009765625, as said below
- slot_map: int32 [4, 16, 1024], P('grp', 'sub'), may hold values from 0 to 1023, as said below
Outputs:
- multipliers: float32 [4, 16, 96, 1024], P('grp', 'sub')
- residual: float32 [4, 16, 96, 1024], P('grp', 'sub')
Inputs may be any that keep to these rules, and one draw needn't show every extreme that they name: `dual_op`: each subdomain's block is symmetric positive definite. `dirichlet`: each subdomain's block is symmetric positive definite. The 384 x 384 matrix whose row (16 y + x) * 6 + k is coarse_op[y, x, k] is symmetric. `slot_map`: for every subdomain and face f, the entries f * 256 to (f + 1) * 256 - 1 are a permutation of those same slot numbers.
All inputs are finite; a program needn't handle non-finite values.
Results may differ from a plain program's by a relative error of at most 0.012.
The roundings to bfloat16 on the way count: a program that leaves them out, or rounds other values in their place, can miss the bound.
Values sent between devices are 32-bit elements; how exact they have to be, the bound alone decides.
No kernel may reach another device: no remote copies, remote signals or barrier semaphores. Data moves between devices by JAX's collectives and lax.ppermute only.
A program may use at most 128 MiB of HBM per device.

v0:
```python
import jax
import jax.numpy as jnp
from jax import lax
from jax.sharding import PartitionSpec as P

MODES = 6
ITERS = 2


HIGHEST = lax.Precision.HIGHEST


def extended(block, sides, width):
    for axis, dim in sides:
        count = lax.axis_size(axis)
        forward = [(i, i + 1) for i in range(count - 1)]
        backward = [(target, source) for source, target in forward]
        low = lax.ppermute(
            lax.slice_in_dim(block, block.shape[dim] - width, None, axis=dim), axis, forward
        )
        high = lax.ppermute(lax.slice_in_dim(block, 0, width, axis=dim), axis, backward)
        block = jnp.concatenate([low, block, high], axis=dim)
    return block


def inverse_map(maps):
    width = maps.shape[-1]

    def invert(perm_row):
        return jnp.zeros_like(perm_row).at[perm_row].set(jnp.arange(width, dtype=jnp.int32))

    return jax.vmap(invert)(maps)


def reorder_block(matrix, order):
    rows_first = jnp.take(matrix, order, axis=0)
    swapped = jnp.swapaxes(rows_first, 0, 1)
    both = jnp.take(swapped, order, axis=0)
    return jnp.swapaxes(both, 0, 1)


def jump_local(values):
    subdomains, columns, width = values.shape
    faces = values.reshape(subdomains, columns, 4, width // 4)
    edges = jnp.stack([faces[0, :, 0], faces[-1, :, 1]])
    beside = extended(edges, (("sub", 0),), 1)
    rims = jnp.stack([faces[:, :, 2], faces[:, :, 3]])
    across = extended(rims, (("grp", 0),), 1)
    from_left = jnp.concatenate([beside[0][None], faces[:-1, :, 1]], axis=0)
    from_right = jnp.concatenate([faces[1:, :, 0], beside[3][None]], axis=0)
    partner = jnp.stack([from_left, from_right, across[0], across[3]], axis=2)
    return (faces - partner).reshape(subdomains, columns, width)


def apply_blocks(values, matrices):
    return jnp.einsum(
        "snm,smk->snk", values.astype(jnp.bfloat16), matrices, preferred_element_type=jnp.float32
    )


def shards(gaps, dual_op, dirichlet, modes, coarse_op, slot_map):
    maps = slot_map[0]
    back_map = inverse_map(maps)
    vectors = jnp.take_along_axis(gaps[0], maps[:, None, :], axis=2)
    subdomains, columns, width = vectors.shape
    quarter = width // 4
    sub_total = lax.axis_size("sub")
    grp_total = lax.axis_size("grp")
    x_position = lax.axis_index("sub") * subdomains + jnp.arange(subdomains, dtype=jnp.int32)
    grp_here = lax.axis_index("grp")
    filler = jnp.ones((subdomains,), jnp.float32)
    face_weight = jnp.stack(
        [
            jnp.where(x_position == 0, 1.0, 2.0) * filler,
            jnp.where(x_position == sub_total * subdomains - 1, 1.0, 2.0) * filler,
            jnp.where(grp_here == 0, 1.0, 2.0) * filler,
            jnp.where(grp_here == grp_total - 1, 1.0, 2.0) * filler,
        ],
        axis=1,
    )
    slot_weight = jnp.repeat(face_weight, quarter, axis=1)
    ordered_modes = jnp.take_along_axis(modes[0], maps[:, None, :], axis=2)
    weighted_modes = ordered_modes * slot_weight[:, None, :]
    stiffness = jax.vmap(reorder_block)(dual_op[0], maps)
    schur_blocks = jax.vmap(reorder_block)(dirichlet[0], maps)
    rows_here = coarse_op[0].reshape(subdomains * MODES, -1)
    rows_count = rows_here.shape[0]
    rows_sub_major = rows_here.reshape(rows_count, grp_total, sub_total, rows_count)
    rows_sub_major = rows_sub_major.transpose(0, 2, 1, 3).reshape(rows_count, -1)
    coarse_total = rows_here.shape[1]
    face_modes = ordered_modes.reshape(subdomains, MODES, 4, quarter).transpose(0, 2, 1, 3)
    own_rows = rows_here.reshape(subdomains, 1, MODES, coarse_total)
    packed = jnp.concatenate(
        [face_modes, jnp.broadcast_to(own_rows, (subdomains, 4, MODES, coarse_total))], axis=3
    )
    edge_pack = jnp.stack([packed[0, 0], packed[-1, 1]])
    beside_pack = extended(edge_pack, (("sub", 0),), 1)
    rim_pack = jnp.stack([packed[:, 2], packed[:, 3]])
    across_pack = extended(rim_pack, (("grp", 0),), 1)
    left_pack = jnp.concatenate([beside_pack[0][None], packed[:-1, 1]], axis=0)
    right_pack = jnp.concatenate([packed[1:, 0], beside_pack[3][None]], axis=0)
    partner_pack = jnp.stack([left_pack, right_pack, across_pack[0], across_pack[3]], axis=1)
    partner_modes = partner_pack[:, :, :, :quarter]
    partner_rows = partner_pack[:, :, :, quarter:]

    def coefficients(values):
        return jnp.einsum("skm,snm->skn", weighted_modes, values, precision=HIGHEST)

    def gathered(coeffs):
        grouped = lax.all_gather(coeffs[None], "grp", axis=0, tiled=True)
        everything = lax.all_gather(grouped, "sub", axis=1, tiled=True)
        return everything.reshape(-1, columns)

    def amounts_of(flat):
        return jnp.dot(rows_here, flat, precision=HIGHEST, preferred_element_type=jnp.float32)

    def lift(amounts, flat):
        shaped = amounts.reshape(subdomains, MODES, columns)
        own_face = jnp.einsum("sfkm,skn->snfm", face_modes, shaped, precision=HIGHEST)
        far_amounts = jnp.einsum("sfkc,cn->sfkn", partner_rows, flat, precision=HIGHEST)
        far_face = jnp.einsum("sfkm,sfkn->snfm", partner_modes, far_amounts, precision=HIGHEST)
        return (own_face - far_face).reshape(subdomains, columns, width)

    def project(values):
        flat = gathered(coefficients(values))
        return values - lift(amounts_of(flat), flat)

    dual = jump_local(vectors)
    multipliers = jnp.zeros_like(dual)
    residual = project(dual)
    direction = jnp.zeros_like(dual)
    rho_prev = jnp.ones((columns,), jnp.float32)
    for step_index in range(ITERS):
        projected = project(residual)
        precond = jump_local(apply_blocks(projected, schur_blocks))
        rho_now = lax.psum(jnp.sum(projected * precond, axis=(0, 2)), ("sub", "grp"))
        search = project(precond)
        if step_index > 0:
            search = search + (rho_now / rho_prev)[None, :, None] * direction
        direction = search
        image = jump_local(apply_blocks(direction, stiffness))
        partial_dot = jnp.sum(direction * image, axis=(0, 2))
        curvature = lax.psum(partial_dot, ("sub", "grp"))
        step_len = rho_now / curvature
        multipliers = multipliers + step_len[None, :, None] * direction
        residual = residual - step_len[None, :, None] * image
        rho_prev = rho_now
    multipliers = jnp.take_along_axis(multipliers, back_map[:, None, :], axis=2)
    residual = jnp.take_along_axis(residual, back_map[:, None, :], axis=2)
    return (multipliers[None], residual[None])


def solution(mesh):
    placed = (
        P("grp", "sub", None, None),
        P("grp", "sub", None, None),
        P("grp", "sub", None, None),
        P("grp", "sub", None, None),
        P("grp", "sub", None, None),
        P("grp", "sub", None),
    )
    return jax.shard_map(
        shards,
        mesh=mesh,
        in_specs=placed,
        out_specs=(P("grp", "sub", None, None), P("grp", "sub", None, None)),
        check_vma=False,
    )
```

profile of v0, /device:TPU:0, one launch (start us, length us, event | category | flops | bytes accessed | tf_op | source)
XLA Modules:
  0.0 632.4 jit_solution(5257530324860456469)
XLA Ops:
  2.6 13.0 %gather_fusion = f32[2048,6]{1,0:T(8,128)S(1)} fusion(f32[2,6,1024]{1,2,0:T(8,128)S(1)} %bitcast.393, s32[2048]{0:T(1024)S(1)} %get-tuple-element.61), kind=kCustom, calls=%fused_computation.7 | custom fusion | bytes 114688 | tf_op jit(solution)/shard_map/jit(take_along_axis)/gather | solution.py:82
  21.3 4.3 collective-permute-start.6
  27.3 13.0 %gather_fusion.1 = f32[2048,96]{1,0:T(8,128)S(1)} fusion(f32[2,96,1024]{1,2,0:T(8,128)S(1)} %bitcast.378, s32[2048]{0:T(1024)S(1)} %bitcast.377), kind=kCustom, calls=%fused_computation.clone | custom fusion | bytes 1589248 | tf_op jit(solution)/shard_map/jit(take_along_axis)/gather | solution.py:64
  46.2 42.2 %gather_fusion.2 = bf16[2048,1024]{1,0:T(8,128)(2,1)} fusion(bf16[2,1024,1024]{2,1,0:T(8,128)(2,1)} %bitcast.375, s32[2048]{0:T(1024)S(1)} %get-tuple-element.60), kind=kCustom, calls=%fused_computation.1.clone | custom fusion | bytes 8404992 | tf_op jit(solution)/shard_map/vmap(jit(_take))/gather | solution.py:36
  88.4 6.2 copy.139
  94.6 42.0 %gather_fusion.4 = bf16[2048,1024]{1,0:T(8,128)(2,1)} fusion(bf16[2,1024,1024]{2,1,0:T(8,128)(2,1)} %bitcast.376, s32[2048]{0:T(1024)S(1)} %get-tuple-element.60), kind=kCustom, calls=%fused_computation.5.clone | custom fusion | bytes 8404992 | tf_op jit(solution)/shard_map/vmap(jit(_take))/gather | solution.py:36
  136.6 6.3 copy.148
  143.1 8.0 %scatter_custom_fusion = s32[2048]{0:T(1024)S(1)} fusion(s32[2048]{0:T(1024)S(1)} %get-tuple-element.65, s32[2048]{0:T(1024)S(1)} %get-tuple-element.64, s32[]{:T(128)} %constant.29.clone.1), kind=kCustom, calls=%fused_computation.184 | custom fusion | bytes 8196
  151.3 7.5 %select_bitcast_fusion = (bf16[2,1024,1024]{2,1,0:T(8,128)(2,1)}, bf16[2,1024,1024]{2,1,0:T(8,128)(2,1)}) fusion(bf16[2,1024,1024]{1,2,0:T(8,128)(2,1)} %copy.148, pred[2,1024]{1,0:T(4,128)(4,1)S(1)} %compare_and_fusion.1, bf16[2,1024,1024]{1,2,0:T(8,128)(2,1)} %copy.139), kind=kLoop, calls=%fused_computation.9 | loop fusion | flops 4194304 | bytes 16779264 | tf_op jit(solution)/shard_map/vmap()/transpose | solution.py:37
  159.4 40.6 %gather_fusion.3 = bf16[2048,1024]{1,0:T(8,128)(2,1)} fusion(bf16[2,1024,1024]{2,1,0:T(8,128)(2,1)} %get-tuple-element.57, s32[2048]{0:T(1024)S(1)} %get-tuple-element.60), kind=kCustom, calls=%fused_computation.4.clone | custom fusion | bytes 8404992 | tf_op jit(solution)/shard_map/vmap(jit(_take))/gather | solution.py:38
  200.0 40.6 %gather_fusion.5 = bf16[2048,1024]{1,0:T(8,128)(2,1)} fusion(bf16[2,1024,1024]{2,1,0:T(8,128)(2,1)} %get-tuple-element.56, s32[2048]{0:T(1024)S(1)} %get-tuple-element.60), kind=kCustom, calls=%fused_computation.6.clone | custom fusion | bytes 8404992 | tf_op jit(solution)/shard_map/vmap(jit(_take))/gather | solution.py:38
  241.9 4.4 collective-permute-start.2
  249.4 4.7 collective-permute-done.3
  256.2 13.7 %all-gather = f32[8,6,96]{2,1,0:T(8,128)S(1)} all-gather(f32[2,6,96]{2,1,0:T(8,128)S(1)} %fusion.40), channel_id=2, replica_groups=mesh['sub'=8,'grp'=4] {'grp'}, dimensions={0}, use_global_device_ids=true | all-gather | bytes 23040 | tf_op jit(solution)/shard_map/all_gather | solution.py:110
  269.9 13.6 %all_gather.31 = f32[4,16,6,96]{3,2,1,0:T(8,128)S(1)} all-gather(f32[4,2,6,96]{3,2,1,0:T(8,128)S(1)} %bitcast.410), channel_id=1, replica_groups=mesh['sub'=8,'grp'=4] {'sub'}, dimensions={1}, use_global_device_ids=true | all-gather | bytes 165888 | tf_op jit(solution)/shard_map/all_gather | solution.py:111
  286.7 13.1 %all-gather.1 = f32[8,6,96]{2,1,0:T(8,128)S(1)} all-gather(f32[2,6,96]{2,1,0:T(8,128)S(1)} %fusion.38), channel_id=3, replica_groups=mesh['sub'=8,'grp'=4] {'grp'}, dimensions={0}, use_global_device_ids=true | all-gather | bytes 23040 | tf_op jit(solution)/shard_map/all_gather | solution.py:110
  299.8 7.9 %all_gather.33 = f32[4,16,6,96]{3,2,1,0:T(8,128)S(1)} all-gather(f32[4,2,6,96]{3,2,1,0:T(8,128)S(1)} %bitcast.411), channel_id=1, replica_groups=mesh['sub'=8,'grp'=4] {'sub'}, dimensions={1}, use_global_device_ids=true | all-gather | bytes 165888 | tf_op jit(solution)/shard_map/all_gather | solution.py:111
  322.0 4.7 collective-permute-done.11
  330.0 13.3 %all-gather.2 = f32[8,6,96]{2,1,0:T(8,128)S(1)} all-gather(f32[2,6,96]{2,1,0:T(8,128)S(1)} %fusion.36), channel_id=4, replica_groups=mesh['sub'=8,'grp'=4] {'grp'}, dimensions={0}, use_global_device_ids=true | all-gather | bytes 23040 | tf_op jit(solution)/shard_map/all_gather | solution.py:110
  343.3 11.7 %all_gather.35 = f32[4,16,6,96]{3,2,1,0:T(8,128)S(1)} all-gather(f32[4,2,6,96]{3,2,1,0:T(8,128)S(1)} %bitcast.412), channel_id=1, replica_groups=mesh['sub'=8,'grp'=4] {'sub'}, dimensions={1}, use_global_device_ids=true | all-gather | bytes 165888 | tf_op jit(solution)/shard_map/all_gather | solution.py:111
  370.9 4.4 collective-permute-done.15
  379.0 39.3 %all-reduce = (f32[96]{0:T(128)S(1)}, f32[96]{0:T(128)S(1)}) all-reduce(f32[96]{0:T(128)S(1)} %get-tuple-element.12, f32[96]{0:T(128)S(1)} %get-tuple-element.10), channel_id=1, replica_groups=mesh['sub'=8,'grp'=4] {'sub','grp'}, use_global_device_ids=true, to_apply=%region_1.4 | all-reduce | flops 192 | bytes 1536 | tf_op jit(solution)/shard_map/psum | solution.py:136
  419.3 13.1 %all-gather.3 = f32[8,6,96]{2,1,0:T(8,128)S(1)} all-gather(f32[2,6,96]{2,1,0:T(8,128)S(1)} %fusion.34), channel_id=5, replica_groups=mesh['sub'=8,'grp'=4] {'grp'}, dimensions={0}, use_global_device_ids=true | all-gather | bytes 23040 | tf_op jit(solution)/shard_map/all_gather | solution.py:110
  432.4 10.3 %all_gather.37 = f32[4,16,6,96]{3,2,1,0:T(8,128)S(1)} all-gather(f32[4,2,6,96]{3,2,1,0:T(8,128)S(1)} %bitcast.413), channel_id=1, replica_groups=mesh['sub'=8,'grp'=4] {'sub'}, dimensions={1}, use_global_device_ids=true | all-gather | bytes 165888 | tf_op jit(solution)/shard_map/all_gather | solution.py:111
  453.7 4.6 collective-permute-start.18
  467.9 13.2 %all-gather.4 = f32[8,6,96]{2,1,0:T(8,128)S(1)} all-gather(f32[2,6,96]{2,1,0:T(8,128)S(1)} %fusion.32), channel_id=6, replica_groups=mesh['sub'=8,'grp'=4] {'grp'}, dimensions={0}, use_global_device_ids=true | all-gather | bytes 23040 | tf_op jit(solution)/shard_map/all_gather | solution.py:110
  481.1 10.2 %all_gather.39 = f32[4,16,6,96]{3,2,1,0:T(8,128)S(1)} all-gather(f32[4,2,6,96]{3,2,1,0:T(8,128)S(1)} %bitcast.414), channel_id=1, replica_groups=mesh['sub'=8,'grp'=4] {'sub'}, dimensions={1}, use_global_device_ids=true | all-gather | bytes 165888 | tf_op jit(solution)/shard_map/all_gather | solution.py:111
  491.8 38.7 %psum.30 = f32[96]{0:T(128)S(1)} all-reduce(f32[96]{0:T(128)S(1)} %get-tuple-element.8), channel_id=1, replica_groups=mesh['sub'=8,'grp'=4] {'sub','grp'}, use_global_device_ids=true, to_apply=%region_5.8 | all-reduce | flops 96 | bytes 768 | tf_op jit(solution)/shard_map/psum | solution.py:136
  546.6 4.4 collective-permute-done.23
  555.6 43.3 %psum.31 = f32[96]{0:T(128)S(1)} all-reduce(f32[96]{0:T(128)S(1)} %get-tuple-element.6), channel_id=1, replica_groups=mesh['sub'=8,'grp'=4] {'sub','grp'}, use_global_device_ids=true, to_apply=%region_7.10 | all-reduce | flops 96 | bytes 768 | tf_op jit(solution)/shard_map/psum | solution.py:143
  602.7 13.0 %gather_fusion.6 = f32[2048,96]{1,0:T(8,128)S(1)} fusion(f32[2,96,1024]{1,2,0:T(8,128)S(1)} %copy.169, s32[2048]{0:T(1024)S(1)} %bitcast.373), kind=kCustom, calls=%fused_computation.2.clone | custom fusion | bytes 1589248 | tf_op jit(solution)/shard_map/jit(take_along_axis)/gather | solution.py:148
  617.3 13.0 %gather_fusion.7 = f32[2048,96]{1,0:T(8,128)S(1)} fusion(f32[2,96,1024]{1,2,0:T(8,128)S(1)} %copy.171, s32[2048]{0:T(1024)S(1)} %bitcast.374), kind=kCustom, calls=%fused_computation.3.clone | custom fusion | bytes 1589248 | tf_op jit(solution)/shard_map/jit(take_along_axis)/gather | solution.py:149
  (224 shorter events, 111.6 us)
Async XLA Ops:
  0.6 26.3 %copy-start.10 = (s32[1,2,1024]{2,1,0:T(2,128)S(1)}, s32[1,2,1024]{2,1,0:T(2,128)}, u32[]{:S(2)}) copy-start(s32[1,2,1024]{2,1,0:T(2,128)} %param.15) | copy-start | bytes 24580
  0.6 26.3 %copy-start.9 = (f32[1,2,96,1024]{3,2,1,0:T(8,128)S(1)}, f32[1,2,96,1024]{3,2,1,0:T(8,128)}, u32[]{:S(2)}) copy-start(f32[1,2,96,1024]{3,2,1,0:T(8,128)} %param.10) | copy-start | bytes 2359300
  17.6 223.0 %collective-permute-start.4 = (f32[1,6,640]{2,1,0:T(8,128)S(1)}, f32[1,6,640]{2,1,0:T(8,128)S(1)}, u32[]{:S(2)}, u32[]{:S(2)}) collective-permute-start(f32[1,6,640]{2,1,0:T(8,128)S(1)} %get-tuple-element.44), channel_id=1, source_target_pairs={{0,4},{4,8},{8,12},{12,16},{16,20},{20,24},{24,28},{1,5},{5,9},{9,... | collective-permute-start | bytes 46088 | tf_op jit(solution)/shard_map/ppermute | solution.py:18
  19.9 221.9 %collective-permute-start.5 = (f32[1,6,640]{2,1,0:T(8,128)S(1)}, f32[1,6,640]{2,1,0:T(8,128)S(1)}, u32[]{:S(2)}, u32[]{:S(2)}) collective-permute-start(f32[1,6,640]{2,1,0:T(8,128)S(1)} %get-tuple-element.45), channel_id=1, source_target_pairs={{4,0},{8,4},{12,8},{16,12},{20,16},{24,20},{28,24},{5,1},{9,5},{13... | collective-permute-start | bytes 46088 | tf_op jit(solution)/shard_map/ppermute | solution.py:21
  21.3 225.0 %collective-permute-start.6 = (f32[1,2,6,640]{3,2,1,0:T(8,128)S(1)}, f32[1,2,6,640]{3,2,1,0:T(8,128)S(1)}, u32[]{:S(2)}, u32[]{:S(2)}) collective-permute-start(f32[1,2,6,640]{3,2,1,0:T(8,128)S(1)} %get-tuple-element.48), channel_id=1, source_target_pairs={{0,1},{1,2},{2,3},{4,5},{5,6},{6,7},{8,9},{9,10},{10,11},{12,13},{... | collective-permute-start | bytes 92168 | tf_op jit(solution)/shard_map/ppermute | solution.py:18
  25.6 222.5 %collective-permute-start.7 = (f32[1,2,6,640]{3,2,1,0:T(8,128)S(1)}, f32[1,2,6,640]{3,2,1,0:T(8,128)S(1)}, u32[]{:S(2)}, u32[]{:S(2)}) collective-permute-start(f32[1,2,6,640]{3,2,1,0:T(8,128)S(1)} %get-tuple-element.49), channel_id=1, source_target_pairs={{1,0},{2,1},{3,2},{5,4},{6,5},{7,6},{9,8},{10,9},{11,10},{13,12},{... | collective-permute-start | bytes 92168 | tf_op jit(solution)/shard_map/ppermute | solution.py:21
  41.5 206.6 %collective-permute-start = (f32[1,96,256]{2,0,1:T(1,128)S(1)}, f32[1,96,256]{2,0,1:T(1,128)S(1)}, u32[]{:S(2)}, u32[]{:S(2)}) collective-permute-start(f32[1,96,256]{2,0,1:T(1,128)S(1)} %get-tuple-element.38), channel_id=1, source_target_pairs={{0,4},{4,8},{8,12},{12,16},{16,20},{20,24},{24,28},{1,5},{5,9},{9,... | collective-permute-start | bytes 294920 | tf_op jit(solution)/shard_map/ppermute | solution.py:18
  45.9 105.4 %copy-start.12 = (pred[2,1024]{1,0:T(4,128)(4,1)}, pred[2,1024]{1,0:T(4,128)(4,1)S(1)}, u32[]{:S(2)}) copy-start(pred[2,1024]{1,0:T(4,128)(4,1)S(1)} %compare_and_fusion.1) | copy-start | bytes 6148
  240.5 8.0 %collective-permute-start.1 = (f32[1,96,256]{2,0,1:T(1,128)S(1)}, f32[1,96,256]{2,0,1:T(1,128)S(1)}, u32[]{:S(2)}, u32[]{:S(2)}) collective-permute-start(f32[1,96,256]{2,0,1:T(1,128)S(1)} %get-tuple-element.39), channel_id=1, source_target_pairs={{4,0},{8,4},{12,8},{16,12},{20,16},{24,20},{28,24},{5,1},{9,5},{13... | collective-permute-start | bytes 294920 | tf_op jit(solution)/shard_map/ppermute | solution.py:21
  241.9 7.5 %collective-permute-start.2 = (f32[1,2,96,256]{3,0,2,1:T(1,128)S(1)}, f32[1,2,96,256]{3,0,2,1:T(1,128)S(1)}, u32[]{:S(2)}, u32[]{:S(2)}) collective-permute-start(f32[1,2,96,256]{3,0,2,1:T(1,128)S(1)} %get-tuple-element.42), channel_id=1, source_target_pairs={{0,1},{1,2},{2,3},{4,5},{5,6},{6,7},{8,9},{9,10},{10,11},{12,13},{... | collective-permute-start | bytes 589832 | tf_op jit(solution)/shard_map/ppermute | solution.py:18
  246.3 7.8 %collective-permute-start.3 = (f32[1,2,96,256]{3,0,2,1:T(1,128)S(1)}, f32[1,2,96,256]{3,0,2,1:T(1,128)S(1)}, u32[]{:S(2)}, u32[]{:S(2)}) collective-permute-start(f32[1,2,96,256]{3,0,2,1:T(1,128)S(1)} %get-tuple-element.43), channel_id=1, source_target_pairs={{1,0},{2,1},{3,2},{5,4},{6,5},{7,6},{9,8},{10,9},{11,10},{13,12},{... | collective-permute-start | bytes 589832 | tf_op jit(solution)/shard_map/ppermute | solution.py:21
  286.0 24.2 %copy-start.13 = (pred[2,1024]{1,0:T(4,128)(4,1)S(1)}, pred[2,1024]{1,0:T(4,128)(4,1)}, u32[]{:S(2)}) copy-start(pred[2,1024]{1,0:T(4,128)(4,1)} %copy-done.12) | copy-start | bytes 6148
  312.9 6.9 %collective-permute-start.8 = (f32[1,96,256]{2,0,1:T(1,128)S(1)}, f32[1,96,256]{2,0,1:T(1,128)S(1)}, u32[]{:S(2)}, u32[]{:S(2)}) collective-permute-start(f32[1,96,256]{2,0,1:T(1,128)S(1)} %get-tuple-element.32), channel_id=1, source_target_pairs={{0,4},{4,8},{8,12},{12,16},{16,20},{20,24},{24,28},{1,5},{5,9},{9,... | collective-permute-start | bytes 294920 | tf_op jit(solution)/shard_map/ppermute | solution.py:18
  315.5 4.7 collective-permute-start.9
  316.8 5.2 collective-permute-start.10
  318.3 8.4 %collective-permute-start.11 = (f32[1,2,96,256]{3,0,2,1:T(1,128)S(1)}, f32[1,2,96,256]{3,0,2,1:T(1,128)S(1)}, u32[]{:S(2)}, u32[]{:S(2)}) collective-permute-start(f32[1,2,96,256]{3,0,2,1:T(1,128)S(1)} %get-tuple-element.37), channel_id=1, source_target_pairs={{1,0},{2,1},{3,2},{5,4},{6,5},{7,6},{9,8},{10,9},{11,10},{13,12},{... | collective-permute-start | bytes 589832 | tf_op jit(solution)/shard_map/ppermute | solution.py:21
  359.5 16.6 %copy-start.6 = (f32[2,96,1024]{2,1,0:T(8,128)}, f32[2,96,1024]{2,1,0:T(8,128)S(1)}, u32[]{:S(2)}) copy-start(f32[2,96,1024]{2,1,0:T(8,128)S(1)} %fusion.3) | copy-start | bytes 2359300
  360.2 6.9 %collective-permute-start.12 = (f32[1,96,256]{2,0,1:T(1,128)S(1)}, f32[1,96,256]{2,0,1:T(1,128)S(1)}, u32[]{:S(2)}, u32[]{:S(2)}) collective-permute-start(f32[1,96,256]{2,0,1:T(1,128)S(1)} %get-tuple-element.26), channel_id=1, source_target_pairs={{0,4},{4,8},{8,12},{12,16},{16,20},{20,24},{24,28},{1,5},{5,9},{9,... | collective-permute-start | bytes 294920 | tf_op jit(solution)/shard_map/ppermute | solution.py:18
  362.8 4.7 collective-permute-start.13
  364.1 6.8 %collective-permute-start.14 = (f32[1,2,96,256]{3,0,2,1:T(1,128)S(1)}, f32[1,2,96,256]{3,0,2,1:T(1,128)S(1)}, u32[]{:S(2)}, u32[]{:S(2)}) collective-permute-start(f32[1,2,96,256]{3,0,2,1:T(1,128)S(1)} %get-tuple-element.30), channel_id=1, source_target_pairs={{0,1},{1,2},{2,3},{4,5},{5,6},{6,7},{8,9},{9,10},{10,11},{12,13},{... | collective-permute-start | bytes 589832 | tf_op jit(solution)/shard_map/ppermute | solution.py:18
  365.8 9.5 %collective-permute-start.15 = (f32[1,2,96,256]{3,0,2,1:T(1,128)S(1)}, f32[1,2,96,256]{3,0,2,1:T(1,128)S(1)}, u32[]{:S(2)}, u32[]{:S(2)}) collective-permute-start(f32[1,2,96,256]{3,0,2,1:T(1,128)S(1)} %get-tuple-element.31), channel_id=1, source_target_pairs={{1,0},{2,1},{3,2},{5,4},{6,5},{7,6},{9,8},{10,9},{11,10},{13,12},{... | collective-permute-start | bytes 589832 | tf_op jit(solution)/shard_map/ppermute | solution.py:21
  447.8 16.1 %copy-start.5 = (f32[2,96,1024]{2,1,0:T(8,128)}, f32[2,96,1024]{2,1,0:T(8,128)S(1)}, u32[]{:S(2)}) copy-start(f32[2,96,1024]{2,1,0:T(8,128)S(1)} %fusion) | copy-start | bytes 2359300
  448.5 9.8 %collective-permute-start.16 = (f32[1,96,256]{2,0,1:T(1,128)S(1)}, f32[1,96,256]{2,0,1:T(1,128)S(1)}, u32[]{:S(2)}, u32[]{:S(2)}) collective-permute-start(f32[1,96,256]{2,0,1:T(1,128)S(1)} %get-tuple-element.20), channel_id=1, source_target_pairs={{0,4},{4,8},{8,12},{12,16},{16,20},{20,24},{24,28},{1,5},{5,9},{9,... | collective-permute-start | bytes 294920 | tf_op jit(solution)/shard_map/ppermute | solution.py:18
  451.1 7.6 %collective-permute-start.17 = (f32[1,96,256]{2,0,1:T(1,128)S(1)}, f32[1,96,256]{2,0,1:T(1,128)S(1)}, u32[]{:S(2)}, u32[]{:S(2)}) collective-permute-start(f32[1,96,256]{2,0,1:T(1,128)S(1)} %get-tuple-element.21), channel_id=1, source_target_pairs={{4,0},{8,4},{12,8},{16,12},{20,16},{24,20},{28,24},{5,1},{9,5},{13... | collective-permute-start | bytes 294920 | tf_op jit(solution)/shard_map/ppermute | solution.py:21
  452.4 9.0 %collective-permute-start.19 = (f32[1,2,96,256]{3,0,2,1:T(1,128)S(1)}, f32[1,2,96,256]{3,0,2,1:T(1,128)S(1)}, u32[]{:S(2)}, u32[]{:S(2)}) collective-permute-start(f32[1,2,96,256]{3,0,2,1:T(1,128)S(1)} %get-tuple-element.25), channel_id=1, source_target_pairs={{1,0},{2,1},{3,2},{5,4},{6,5},{7,6},{9,8},{10,9},{11,10},{13,12},{... | collective-permute-start | bytes 589832 | tf_op jit(solution)/shard_map/ppermute | solution.py:21
  453.7 9.5 %collective-permute-start.18 = (f32[1,2,96,256]{3,0,2,1:T(1,128)S(1)}, f32[1,2,96,256]{3,0,2,1:T(1,128)S(1)}, u32[]{:S(2)}, u32[]{:S(2)}) collective-permute-start(f32[1,2,96,256]{3,0,2,1:T(1,128)S(1)} %get-tuple-element.24), channel_id=1, source_target_pairs={{0,1},{1,2},{2,3},{4,5},{5,6},{6,7},{8,9},{9,10},{10,11},{12,13},{... | collective-permute-start | bytes 589832 | tf_op jit(solution)/shard_map/ppermute | solution.py:18
  537.1 7.7 %collective-permute-start.20 = (f32[1,96,256]{2,0,1:T(1,128)S(1)}, f32[1,96,256]{2,0,1:T(1,128)S(1)}, u32[]{:S(2)}, u32[]{:S(2)}) collective-permute-start(f32[1,96,256]{2,0,1:T(1,128)S(1)} %get-tuple-element.14), channel_id=1, source_target_pairs={{0,4},{4,8},{8,12},{12,16},{16,20},{20,24},{24,28},{1,5},{5,9},{9,... | collective-permute-start | bytes 294920 | tf_op jit(solution)/shard_map/ppermute | solution.py:18
  538.7 6.5 %collective-permute-start.21 = (f32[1,96,256]{2,0,1:T(1,128)S(1)}, f32[1,96,256]{2,0,1:T(1,128)S(1)}, u32[]{:S(2)}, u32[]{:S(2)}) collective-permute-start(f32[1,96,256]{2,0,1:T(1,128)S(1)} %get-tuple-element.15), channel_id=1, source_target_pairs={{4,0},{8,4},{12,8},{16,12},{20,16},{24,20},{28,24},{5,1},{9,5},{13... | collective-permute-start | bytes 294920 | tf_op jit(solution)/shard_map/ppermute | solution.py:21
  540.0 6.6 %collective-permute-start.22 = (f32[1,2,96,256]{3,0,2,1:T(1,128)S(1)}, f32[1,2,96,256]{3,0,2,1:T(1,128)S(1)}, u32[]{:S(2)}, u32[]{:S(2)}) collective-permute-start(f32[1,2,96,256]{3,0,2,1:T(1,128)S(1)} %get-tuple-element.18), channel_id=1, source_target_pairs={{0,1},{1,2},{2,3},{4,5},{5,6},{6,7},{8,9},{9,10},{10,11},{12,13},{... | collective-permute-start | bytes 589832 | tf_op jit(solution)/shard_map/ppermute | solution.py:18
  543.5 7.6 %collective-permute-start.23 = (f32[1,2,96,256]{3,0,2,1:T(1,128)S(1)}, f32[1,2,96,256]{3,0,2,1:T(1,128)S(1)}, u32[]{:S(2)}, u32[]{:S(2)}) collective-permute-start(f32[1,2,96,256]{3,0,2,1:T(1,128)S(1)} %get-tuple-element.19), channel_id=1, source_target_pairs={{1,0},{2,1},{3,2},{5,4},{6,5},{7,6},{9,8},{10,9},{11,10},{13,12},{... | collective-permute-start | bytes 589832 | tf_op jit(solution)/shard_map/ppermute | solution.py:21
  617.3 13.4 %copy-start.4 = (f32[2,1024,96]{1,2,0:T(8,128)S(1)}, f32[2,1024,96]{1,2,0:T(8,128)}, u32[]{:S(2)}) copy-start(f32[2,1024,96]{1,2,0:T(8,128)} %copy.170) | copy-start | bytes 2359300
  617.3 13.4 %copy-start.14 = (pred[2,1024]{1,0:T(4,128)(4,1)S(1)}, pred[2,1024]{1,0:T(4,128)(4,1)}, u32[]{:S(2)}) copy-start(pred[2,1024]{1,0:T(4,128)(4,1)} %and_bitcast_fusion) | copy-start | bytes 6148
  (9 other events, 33.4 us)
where the time goes:
time: 645 us; the launch traced here: 632 us
  local copies, waits for them, and re-layouts  260 us (40%)
  blocking collectives  241 us (37%)
  starting transfers between devices  50.5 us (8%)
  waiting for transfers between devices  28.3 us (4%)
  other arithmetic  27.6 us (4%)
  matrix products  22.5 us (3%)
    gather x5, local copies, waits for them, and re-layouts, reorder_block(): rows_first = jnp.take(matrix, order, axis=0)  96.7 us
    gather x2, local copies, waits for them, and re-layouts, reorder_block(): both = jnp.take(swapped, order, axis=0)  81.1 us
    psum x2, blocking collectives, shards(): lax.psum(jnp.sum(projected * precond, axis=(0, 2)), ('sub', 'grp'))  78.1 us
    all_gather x5, blocking collectives, gathered(): grouped = lax.all_gather(coeffs[None], 'grp', axis=0, tiled=True)  66.4 us
    all_gather x5, blocking collectives, gathered(): everything = lax.all_gather(grouped, 'sub', axis=1, tiled=True)  53.6 us
    psum x1, blocking collectives, shards(): curvature = lax.psum(partial_dot, ('sub', 'grp'))  43.3 us
    ppermute x12, starting transfers between devices, extended(): lax.ppermute(lax.slice_in_dim(block, block.shape[dim] - width, None, axis...  34.3 us
    ppermute x12, waiting for transfers between devices, extended(): lax.ppermute(lax.slice_in_dim(block, 0, width, axis=dim), axis, backward)  20.6 us
  transfers between devices with their start and end apart: 24, of which 10 were waited for; matrix products, arithmetic and copies ran while one was open for 34% of the time, Pallas kernels for 0%

commit v1 on v0

v1 whole, which is shorter than its diff:
```python
import jax
import jax.numpy as jnp
from jax import lax
from jax.sharding import PartitionSpec as P

MODES = 6
ITERS = 2


HIGHEST = lax.Precision.HIGHEST


def neighbors(d0, d1, d2, d3):
    sub_count = lax.axis_size("sub")
    grp_count = lax.axis_size("grp")
    up_sub = [(i, i + 1) for i in range(sub_count - 1)]
    down_sub = [(i + 1, i) for i in range(sub_count - 1)]
    up_grp = [(i, i + 1) for i in range(grp_count - 1)]
    down_grp = [(i + 1, i) for i in range(grp_count - 1)]
    left_dev = lax.ppermute(d1[-1:], "sub", up_sub)
    right_dev = lax.ppermute(d0[:1], "sub", down_sub)
    from_left = jnp.concatenate([left_dev, d1[:-1]], axis=0)
    from_right = jnp.concatenate([d0[1:], right_dev], axis=0)
    from_below = lax.ppermute(d3, "grp", up_grp)
    from_above = lax.ppermute(d2, "grp", down_grp)
    return jnp.stack([from_left, from_right, from_below, from_above], axis=1)


def face_split(values):
    quarter = values.shape[-1] // 4
    return [values[..., g * quarter:(g + 1) * quarter] for g in range(4)]


def inverse_map(maps):
    width = maps.shape[-1]

    def invert(perm_row):
        return jnp.zeros_like(perm_row).at[perm_row].set(jnp.arange(width, dtype=jnp.int32))

    return jax.vmap(invert)(maps)


def apply_blocks(values, matrices):
    return jnp.einsum(
        "snm,smk->snk", values.astype(jnp.bfloat16), matrices, preferred_element_type=jnp.float32
    )


def shards(gaps, dual_op, dirichlet, modes, coarse_op, slot_map):
    maps = slot_map[0]
    back_map = inverse_map(maps)
    vectors = gaps[0]
    stiffness = dual_op[0]
    schur_blocks = dirichlet[0]
    own_modes = modes[0]
    subdomains, columns, width = vectors.shape
    quarter = width // 4
    sub_total = lax.axis_size("sub")
    grp_total = lax.axis_size("grp")
    x_position = lax.axis_index("sub") * subdomains + jnp.arange(subdomains, dtype=jnp.int32)
    grp_here = lax.axis_index("grp")
    filler = jnp.ones((subdomains,), jnp.float32)
    face_weight = jnp.stack(
        [
            jnp.where(x_position == 0, 1.0, 2.0) * filler,
            jnp.where(x_position == sub_total * subdomains - 1, 1.0, 2.0) * filler,
            jnp.where(grp_here == 0, 1.0, 2.0) * filler,
            jnp.where(grp_here == grp_total - 1, 1.0, 2.0) * filler,
        ],
        axis=1,
    )
    slot_weight = jnp.repeat(face_weight, quarter, axis=1)
    weighted_modes = own_modes * slot_weight[:, None, :]
    rows_here = coarse_op[0].reshape(subdomains * MODES, -1)
    coarse_total = rows_here.shape[1]

    mode_faces = face_split(own_modes)
    map_faces = face_split(maps.astype(jnp.float32)[:, None, :])
    own_rows = coarse_op[0]
    packs = [
        jnp.concatenate(
            [
                mode_faces[g].reshape(subdomains, -1),
                map_faces[g].reshape(subdomains, -1),
                own_rows.reshape(subdomains, -1),
            ],
            axis=1,
        )
        for g in range(4)
    ]
    partner_pack = neighbors(*packs)
    partner_raw_modes = partner_pack[:, :, : MODES * quarter].reshape(subdomains, 4, MODES, quarter)
    partner_map = partner_pack[:, :, MODES * quarter:(MODES + 1) * quarter]
    partner_rows = partner_pack[:, :, (MODES + 1) * quarter:].reshape(
        subdomains, 4, MODES, coarse_total
    )

    opposite = jnp.array([1, 0, 3, 2], jnp.int32)
    local_multiplier = back_map.reshape(subdomains, 4, quarter) - (
        jnp.arange(4, dtype=jnp.int32) * quarter
    )[None, :, None]
    partner_slot = jnp.take_along_axis(
        partner_map.astype(jnp.int32), local_multiplier, axis=2
    ) - (opposite * quarter)[None, :, None]
    permutes = (
        jnp.arange(quarter, dtype=jnp.int32)[None, None, :, None] == partner_slot[:, :, None, :]
    ).astype(jnp.float32)

    def to_mine(raw):
        return jnp.einsum("sfcq,sfqr->sfcr", raw, permutes, precision=HIGHEST)

    partner_modes = to_mine(partner_raw_modes)

    def jump(values):
        raw = neighbors(*face_split(values))
        partner = to_mine(raw)
        partner = jnp.moveaxis(partner, 1, 2).reshape(values.shape)
        return values - partner

    def coefficients(values):
        return jnp.einsum("skm,snm->skn", weighted_modes, values, precision=HIGHEST)

    def gathered(coeffs, extra):
        payload = jnp.concatenate([coeffs.reshape(-1), extra.reshape(-1)])
        everything = lax.all_gather(payload, ("grp", "sub"), axis=0)
        count = coeffs.size
        extras = jnp.sum(everything[:, count:], axis=0)
        if count == 0:
            return None, extras
        flat = everything[:, :count].reshape(-1, columns)
        return flat, extras

    def lift(flat):
        amounts = jnp.dot(rows_here, flat, precision=HIGHEST, preferred_element_type=jnp.float32)
        shaped = amounts.reshape(subdomains, MODES, columns)
        own_part = jnp.einsum("skm,skn->snm", own_modes, shaped, precision=HIGHEST)
        far_amounts = jnp.einsum("sfkc,cn->sfkn", partner_rows, flat, precision=HIGHEST)
        far_part = jnp.einsum("sfkm,sfkn->snfm", partner_modes, far_amounts, precision=HIGHEST)
        return own_part - far_part.reshape(subdomains, columns, width)

    def project_with(values, flat):
        return values - lift(flat)

    nothing = jnp.zeros((1,), jnp.float32)
    dual = jump(vectors)
    flat_dual, _ = gathered(coefficients(dual), nothing)
    residual = project_with(dual, flat_dual)
    flat_residual, _ = gathered(coefficients(residual), nothing)
    multipliers = jnp.zeros_like(dual)
    direction = jnp.zeros_like(dual)
    rho_prev = jnp.ones((columns,), jnp.float32)
    for step_index in range(ITERS):
        projected = project_with(residual, flat_residual)
        precond = jump(apply_blocks(projected, schur_blocks))
        flat_precond, rho_now = gathered(
            coefficients(precond), jnp.sum(projected * precond, axis=(0, 2))
        )
        search = project_with(precond, flat_precond)
        if step_index > 0:
            search = search + (rho_now / rho_prev)[None, :, None] * direction
        direction = search
        image = jump(apply_blocks(direction, stiffness))
        partial_dot = jnp.sum(direction * image, axis=(0, 2))
        if step_index + 1 < ITERS:
            flat_image, curvature = gathered(coefficients(image), partial_dot)
        else:
            _, curvature = gathered(jnp.zeros((0,), jnp.float32), partial_dot)
        step_len = rho_now / curvature
        multipliers = multipliers + step_len[None, :, None] * direction
        residual = residual - step_len[None, :, None] * image
        if step_index + 1 < ITERS:
            flat_residual = flat_residual - step_len[None, :] * flat_image
        rho_prev = rho_now
    return (multipliers[None], residual[None])


def solution(mesh):
    placed = (
        P("grp", "sub", None, None),
        P("grp", "sub", None, None),
        P("grp", "sub", None, None),
        P("grp", "sub", None, None),
        P("grp", "sub", None, None),
        P("grp", "sub", None),
    )
    return jax.shard_map(
        shards,
        mesh=mesh,
        in_specs=placed,
        out_specs=(P("grp", "sub", None, None), P("grp", "sub", None, None)),
        check_vma=False,
    )
```

time: 645 us -> 861 us (1.33); the launches traced: 632 us -> 860 us
  waiting for transfers between devices: 28.3 us -> 644 us
  local copies, waits for them, and re-layouts: 260 us -> 48.8 us
  blocking collectives: 241 us -> 41.4 us
  other arithmetic: 27.6 us -> 11.4 us
  between operations: 2.45 us -> 16.7 us
  matrix products: 22.5 us -> 35.2 us
  starting transfers between devices: 50.5 us -> 61.9 us
    unnamed x0 -> x10, waiting for transfers between devices: none -> 618 us
    gather x17 -> x2, local copies, waits for them, and re-layouts: 232 us -> 20.4 us  [shards(): jnp.take_along_axis(partner_map.astype(jnp.int32), local_multiplier, axis=2)]
    psum x3 -> x0, blocking collectives: 121 us -> none  [the longest x2 78.1 us: shards(): lax.psum(jnp.sum(projected * precond, axis=(0, 2)), ('sub', 'grp'))]
    all_gather x10 -> x0, blocking collectives: 120 us -> none  [the longest x5 66.4 us: gathered(): grouped = lax.all_gather(coeffs[None], 'grp', axis=0, tiled=True)]
    unnamed x0 -> x1, blocking collectives: none -> 41.4 us
    ppermute x24, starting transfers between devices: 50.5 us -> 61.6 us  [the longest x6 28.4 us: neighbors(): from_below = lax.ppermute(d3, 'grp', up_grp)]
    another operation x25 -> x4, local copies, waits for them, and re-layouts: 9.94 us -> 0.1 us  [neighbors(): return jnp.stack([from_left, from_right, from_below, from_above], axis=1)]
  transfers between devices with their start and end apart: 24 -> 29, of which waited for: 10 -> 13; matrix products, arithmetic and copies ran while one was open for 34% -> 5% of each run, Pallas kernels for 0% -> 0%
where the time goes in v1:
time: 861 us; the launch traced here: 860 us
  waiting for transfers between devices  644 us (75%)
  starting transfers between devices  61.9 us (7%)
  local copies, waits for them, and re-layouts  48.8 us (6%)
  blocking collectives  41.4 us (5%)
  matrix products  35.2 us (4%)
  between operations  16.7 us (2%)
  other arithmetic  11.4 us (1%)
    unnamed x10, waiting for transfers between devices  618 us
    unnamed x1, blocking collectives  41.4 us
    ppermute x6, starting transfers between devices, neighbors(): from_below = lax.ppermute(d3, 'grp', up_grp)  28.4 us
    gather x2, local copies, waits for them, and re-layouts, shards(): jnp.take_along_axis(partner_map.astype(jnp.int32), local_multiplier, axis=2)  20.4 us
    ppermute x6, waiting for transfers between devices, neighbors(): from_above = lax.ppermute(d2, 'grp', down_grp)  18.7 us
    ppermute x6, starting transfers between devices, neighbors(): left_dev = lax.ppermute(d1[-1:], 'sub', up_sub)  17.4 us
  transfers between devices with their start and end apart: 29, of which 13 were waited for; matrix products, arithmetic and copies ran while one was open for 5% of the time, Pallas kernels for 0%

profile of v1, /device:TPU:0, one launch (start us, length us, event | category | flops | bytes accessed | tf_op | source)
XLA Modules:
  0.0 859.8 jit_solution(18326962557442521355)
XLA Ops:
  9.5 2.4 collective-permute-start.4
  13.2 4.3 collective-permute-start.6
  19.9 4.0 collective-permute-start
  27.2 8.0 scatter_custom_fusion
  41.0 4.3 collective-permute-start.2
  47.0 20.4 %gather_fusion = s32[2048]{0:T(1024)S(1)} fusion(s32[2,4,256]{2,1,0:T(4,128)S(1)} %maximum_convert_fusion, s32[2048]{0:T(1024)S(1)} %bitcast.194), kind=kCustom, calls=%fused_computation | custom fusion | bytes 40960 | tf_op jit(solution)/shard_map/jit(take_along_axis)/gather | solution.py:102
  71.3 126.6 %all-reduce.12.cloned.1.call-done = f32[36896]{0:T(1024)} async-done(((f32[36896]{0:T(1024)}), f32[36896]{0:T(1024)}) %all-reduce.12.cloned.1.call-update) | async-done | bytes 147600
  204.6 122.6 %all-reduce.14.cloned.1.call-done = f32[36896]{0:T(1024)} async-done(((f32[36896]{0:T(1024)}), f32[36896]{0:T(1024)}) %all-reduce.14.cloned.1.call-update) | async-done | bytes 147600
  332.2 3.0 fusion.6
  335.2 3.1 collective-permute-start.8
  339.8 4.7 collective-permute-start.10
  345.9 2.0 collective-permute-done.10
  347.9 4.7 collective-permute-done.11
  355.6 123.2 %all-reduce.16.cloned.1.call-done = f32[39936]{0:T(1024)} async-done(((f32[39936]{0:T(1024)}), f32[39936]{0:T(1024)}) %all-reduce.16.cloned.1.call-update) | async-done | bytes 159760
  483.1 3.0 fusion.2
  486.1 2.6 collective-permute-start.12
  490.1 5.0 collective-permute-start.14
  496.5 2.0 collective-permute-done.14
  498.5 4.7 collective-permute-done.15
  506.9 122.6 %all-reduce.18.cloned.1.call-done = f32[39936]{0:T(1024)} async-done(((f32[39936]{0:T(1024)}), f32[39936]{0:T(1024)}) %all-reduce.18.cloned.1.call-update) | async-done | bytes 159760
  633.3 3.0 fusion.4
  636.3 2.6 collective-permute-start.16
  640.3 5.0 collective-permute-start.18
  648.6 4.7 collective-permute-done.19
  657.7 122.9 %all-reduce.20.cloned.1.call-done = f32[39936]{0:T(1024)} async-done(((f32[39936]{0:T(1024)}), f32[39936]{0:T(1024)}) %all-reduce.20.cloned.1.call-update) | async-done | bytes 159760
  784.1 2.3 fusion.24
  786.4 3.0 fusion
  789.4 2.6 collective-permute-start.20
  793.4 5.0 collective-permute-start.22
  801.8 4.7 collective-permute-done.23
  809.0 41.4 %all-reduce.5 = f32[3072]{0:T(1024)S(1)} all-reduce(f32[3072]{0:T(1024)S(1)} %dynamic-update-slice.5), channel_id=7, replica_groups=mesh['sub'=8,'grp'=4] {'grp','sub'}, use_global_device_ids=true, to_apply=%add.5 | all-reduce | flops 3072 | bytes 24576
  850.5 2.8 subtract_bitcast_fusion
  (223 shorter events, 69.8 us)
Async XLA Ops:
  7.2 190.7 %all-reduce.12.cloned.1.call-start = ((), (), s32[]{:S(2)}) async-start(), calls=%async_computation | async-start | bytes 303104
  9.5 30.2 %collective-permute-start.4 = (f32[1,4096]{1,0:T(1,128)S(1)}, f32[1,4096]{1,0:T(1,128)S(1)}, u32[]{:S(2)}, u32[]{:S(2)}) collective-permute-start(f32[1,4096]{1,0:T(1,128)S(1)} %get-tuple-element.44), channel_id=1, source_target_pairs={{0,4},{4,8},{8,12},{12,16},{16,20},{20,24},{24,28},{1,5},{5,9},{9,... | collective-permute-start | bytes 49160 | tf_op jit(solution)/shard_map/ppermute | solution.py:20
  11.9 29.1 %collective-permute-start.5 = (f32[1,4096]{1,0:T(1,128)S(1)}, f32[1,4096]{1,0:T(1,128)S(1)}, u32[]{:S(2)}, u32[]{:S(2)}) collective-permute-start(f32[1,4096]{1,0:T(1,128)S(1)} %get-tuple-element.47), channel_id=1, source_target_pairs={{4,0},{8,4},{12,8},{16,12},{20,16},{24,20},{28,24},{5,1},{9,5},{13... | collective-permute-start | bytes 49160 | tf_op jit(solution)/shard_map/ppermute | solution.py:21
  13.2 32.2 %collective-permute-start.6 = (f32[2,4096]{1,0:T(2,128)S(1)}, f32[2,4096]{1,0:T(2,128)S(1)}, u32[]{:S(2)}, u32[]{:S(2)}) collective-permute-start(f32[2,4096]{1,0:T(2,128)S(1)} %get-tuple-element.50), channel_id=1, source_target_pairs={{0,1},{1,2},{2,3},{4,5},{5,6},{6,7},{8,9},{9,10},{10,11},{12,13},{... | collective-permute-start | bytes 98312 | tf_op jit(solution)/shard_map/ppermute | solution.py:24
  17.5 29.3 %collective-permute-start.7 = (f32[2,4096]{1,0:T(2,128)S(1)}, f32[2,4096]{1,0:T(2,128)S(1)}, u32[]{:S(2)}, u32[]{:S(2)}) collective-permute-start(f32[2,4096]{1,0:T(2,128)S(1)} %get-tuple-element.51), channel_id=1, source_target_pairs={{1,0},{2,1},{3,2},{5,4},{6,5},{7,6},{9,8},{10,9},{11,10},{13,12},{... | collective-permute-start | bytes 98312 | tf_op jit(solution)/shard_map/ppermute | solution.py:25
  19.9 47.7 %collective-permute-start = (f32[1,96,256]{2,1,0:T(8,128)S(1)}, f32[1,96,256]{2,1,0:T(8,128)S(1)}, u32[]{:S(2)}, u32[]{:S(2)}) collective-permute-start(f32[1,96,256]{2,1,0:T(8,128)S(1)} %get-tuple-element.34), channel_id=1, source_target_pairs={{0,4},{4,8},{8,12},{12,16},{16,20},{20,24},{24,28},{1,5},{5,9},{9,... | collective-permute-start | bytes 294920 | tf_op jit(solution)/shard_map/ppermute | solution.py:20
  39.7 28.0 %collective-permute-start.1 = (f32[1,96,256]{2,1,0:T(8,128)S(1)}, f32[1,96,256]{2,1,0:T(8,128)S(1)}, u32[]{:S(2)}, u32[]{:S(2)}) collective-permute-start(f32[1,96,256]{2,1,0:T(8,128)S(1)} %get-tuple-element.35), channel_id=1, source_target_pairs={{4,0},{8,4},{12,8},{16,12},{20,16},{24,20},{28,24},{5,1},{9,5},{13... | collective-permute-start | bytes 294920 | tf_op jit(solution)/shard_map/ppermute | solution.py:21
  41.0 26.6 %collective-permute-start.2 = (f32[2,96,256]{2,1,0:T(8,128)S(1)}, f32[2,96,256]{2,1,0:T(8,128)S(1)}, u32[]{:S(2)}, u32[]{:S(2)}) collective-permute-start(f32[2,96,256]{2,1,0:T(8,128)S(1)} %get-tuple-element.38), channel_id=1, source_target_pairs={{0,1},{1,2},{2,3},{4,5},{5,6},{6,7},{8,9},{9,10},{10,11},{12,13},{... | collective-permute-start | bytes 589832 | tf_op jit(solution)/shard_map/ppermute | solution.py:24
  45.4 22.3 %collective-permute-start.3 = (f32[2,96,256]{2,1,0:T(8,128)S(1)}, f32[2,96,256]{2,1,0:T(8,128)S(1)}, u32[]{:S(2)}, u32[]{:S(2)}) collective-permute-start(f32[2,96,256]{2,1,0:T(8,128)S(1)} %get-tuple-element.39), channel_id=1, source_target_pairs={{1,0},{2,1},{3,2},{5,4},{6,5},{7,6},{9,8},{10,9},{11,10},{13,12},{... | collective-permute-start | bytes 589832 | tf_op jit(solution)/shard_map/ppermute | solution.py:25
  68.6 132.8 %copy-start.2 = (f32[1,2,6,1024]{3,1,2,0:T(2,128)S(1)}, f32[1,2,6,1024]{3,1,2,0:T(2,128)}, u32[]{:S(2)}) copy-start(f32[1,2,6,1024]{3,1,2,0:T(2,128)} %param.10) | copy-start | bytes 147460
  70.4 256.8 %all-reduce.14.cloned.1.call-start = ((), (), s32[]{:S(2)}) async-start(), calls=%async_computation.1 | async-start | bytes 303104
  71.2 128.2 %copy-start.3 = (f32[2,4,6,256]{3,2,1,0:T(8,128)}, f32[2,4,6,256]{3,2,1,0:T(8,128)S(1)}, u32[]{:S(2)}) copy-start(f32[2,4,6,256]{3,2,1,0:T(8,128)S(1)} %fusion.12) | copy-start | bytes 147460
  201.4 129.1 %copy-start.4 = (f32[2,4,6,256]{3,2,1,0:T(8,128)S(1)}, f32[2,4,6,256]{3,2,1,0:T(8,128)}, u32[]{:S(2)}) copy-start(f32[2,4,6,256]{3,2,1,0:T(8,128)} %copy-done.3) | copy-start | bytes 147460
  204.0 274.9 %all-reduce.16.cloned.1.call-start = ((), (), s32[]{:S(2)}) async-start(), calls=%async_computation.2 | async-start | bytes 319488
  335.2 10.6 %collective-permute-start.8 = (f32[1,96,256]{2,1,0:T(8,128)S(1)}, f32[1,96,256]{2,1,0:T(8,128)S(1)}, u32[]{:S(2)}, u32[]{:S(2)}) collective-permute-start(f32[1,96,256]{2,1,0:T(8,128)S(1)} %get-tuple-element.28), channel_id=1, source_target_pairs={{0,4},{4,8},{8,12},{12,16},{16,20},{20,24},{24,28},{1,5},{5,9},{9,... | collective-permute-start | bytes 294920 | tf_op jit(solution)/shard_map/ppermute | solution.py:20
  338.4 7.5 collective-permute-start.9
  339.8 8.0 collective-permute-start.10
  344.5 8.1 collective-permute-start.11
  355.6 273.9 %all-reduce.18.cloned.1.call-start = ((), (), s32[]{:S(2)}) async-start(), calls=%async_computation.3 | async-start | bytes 319488
  486.1 10.3 %collective-permute-start.12 = (f32[1,96,256]{2,1,0:T(8,128)S(1)}, f32[1,96,256]{2,1,0:T(8,128)S(1)}, u32[]{:S(2)}, u32[]{:S(2)}) collective-permute-start(f32[1,96,256]{2,1,0:T(8,128)S(1)} %get-tuple-element.22), channel_id=1, source_target_pairs={{0,4},{4,8},{8,12},{12,16},{16,20},{20,24},{24,28},{1,5},{5,9},{9,... | collective-permute-start | bytes 294920 | tf_op jit(solution)/shard_map/ppermute | solution.py:20
  488.8 7.7 collective-permute-start.13
  490.1 8.4 collective-permute-start.14
  495.1 8.0 collective-permute-start.15
  506.1 274.4 %all-reduce.20.cloned.1.call-start = ((), (), s32[]{:S(2)}) async-start(), calls=%async_computation.4 | async-start | bytes 319488
  636.3 10.5 %collective-permute-start.16 = (f32[1,96,256]{2,1,0:T(8,128)S(1)}, f32[1,96,256]{2,1,0:T(8,128)S(1)}, u32[]{:S(2)}, u32[]{:S(2)}) collective-permute-start(f32[1,96,256]{2,1,0:T(8,128)S(1)} %get-tuple-element.16), channel_id=1, source_target_pairs={{0,4},{4,8},{8,12},{12,16},{16,20},{20,24},{24,28},{1,5},{5,9},{9,... | collective-permute-start | bytes 294920 | tf_op jit(solution)/shard_map/ppermute | solution.py:20
  639.0 7.9 collective-permute-start.17
  640.3 8.4 collective-permute-start.18
  645.3 8.0 collective-permute-start.19
  789.4 10.3 %collective-permute-start.20 = (f32[1,96,256]{2,1,0:T(8,128)S(1)}, f32[1,96,256]{2,1,0:T(8,128)S(1)}, u32[]{:S(2)}, u32[]{:S(2)}) collective-permute-start(f32[1,96,256]{2,1,0:T(8,128)S(1)} %get-tuple-element.10), channel_id=1, source_target_pairs={{0,4},{4,8},{8,12},{12,16},{16,20},{20,24},{24,28},{1,5},{5,9},{9,... | collective-permute-start | bytes 294920 | tf_op jit(solution)/shard_map/ppermute | solution.py:20
  792.1 7.7 collective-permute-start.21
  793.4 8.4 collective-permute-start.22
  798.4 8.0 collective-permute-start.23
  (12 other events, 282.4 us)
Sparse Core Ops, SparseCore 0:
  70.5 127.3 all-reduce.11
  204.1 123.0 all-reduce.13
  355.7 123.1 all-reduce.15
  506.3 123.1 all-reduce.17
  657.2 123.2 all-reduce.19

commit v2 on v1

--- a/solution.py
+++ b/solution.py
@@ -31,15 +31,6 @@
     return [values[..., g * quarter:(g + 1) * quarter] for g in range(4)]
 
 
-def inverse_map(maps):
-    width = maps.shape[-1]
-
-    def invert(perm_row):
-        return jnp.zeros_like(perm_row).at[perm_row].set(jnp.arange(width, dtype=jnp.int32))
-
-    return jax.vmap(invert)(maps)
-
-
 def apply_blocks(values, matrices):
     return jnp.einsum(
         "snm,smk->snk", values.astype(jnp.bfloat16), matrices, preferred_element_type=jnp.float32
@@ -48,7 +39,6 @@
 
 def shards(gaps, dual_op, dirichlet, modes, coarse_op, slot_map):
     maps = slot_map[0]
-    back_map = inverse_map(maps)
     vectors = gaps[0]
     stiffness = dual_op[0]
     schur_blocks = dirichlet[0]
@@ -96,15 +86,15 @@
     )
 
     opposite = jnp.array([1, 0, 3, 2], jnp.int32)
-    local_multiplier = back_map.reshape(subdomains, 4, quarter) - (
-        jnp.arange(4, dtype=jnp.int32) * quarter
-    )[None, :, None]
-    partner_slot = jnp.take_along_axis(
-        partner_map.astype(jnp.int32), local_multiplier, axis=2
-    ) - (opposite * quarter)[None, :, None]
-    permutes = (
-        jnp.arange(quarter, dtype=jnp.int32)[None, None, :, None] == partner_slot[:, :, None, :]
-    ).astype(jnp.float32)
+    offsets = (jnp.arange(4, dtype=jnp.int32) * quarter)[None, :, None]
+    my_slot = maps.reshape(subdomains, 4, quarter) - offsets
+    partner_slot = partner_map.astype(jnp.int32) - (opposite * quarter)[None, :, None]
+    local = jnp.arange(quarter, dtype=jnp.int32)[None, None, None, :]
+    mine_hot = (my_slot[..., None] == local).astype(jnp.bfloat16)
+    partner_hot = (partner_slot[..., None] == local).astype(jnp.bfloat16)
+    permutes = jnp.einsum(
+        "sfmt,sfmi->sfti", partner_hot, mine_hot, preferred_element_type=jnp.float32
+    )
 
     def to_mine(raw):
         return jnp.einsum("sfcq,sfqr->sfcr", raw, permutes, precision=HIGHEST)
@@ -122,7 +112,9 @@
 
     def gathered(coeffs, extra):
         payload = jnp.concatenate([coeffs.reshape(-1), extra.reshape(-1)])
-        everything = lax.all_gather(payload, ("grp", "sub"), axis=0)
+        devices = lax.axis_size("grp") * lax.axis_size("sub")
+        copies = jnp.broadcast_to(payload[None], (devices, payload.shape[0]))
+        everything = lax.all_to_all(copies, ("grp", "sub"), 0, 0, tiled=True)
         count = coeffs.size
         extras = jnp.sum(everything[:, count:], axis=0)
         if count == 0:

time: 861 us -> 222 us (0.26)
  waiting for transfers between devices: 644 us -> 51.9 us
  local copies, waits for them, and re-layouts: 48.8 us -> 18.7 us
  between operations: 16.7 us -> 1.83 us
    unnamed x10 -> x0, waiting for transfers between devices: 618 us -> none
    all_to_all x0 -> x4, blocking collectives: none -> 46 us  [gathered(): everything = lax.all_to_all(copies, ('grp', 'sub'), 0, 0, tiled=True)]
    unnamed x1 -> x0, blocking collectives: 41.4 us -> none
    gather x2 -> x0, local copies, waits for them, and re-layouts: 20.4 us -> none  [shards(): jnp.take_along_axis(partner_map.astype(jnp.int32), local_multiplier, axis=2)]
    all_to_all x0 -> x2, waiting for transfers between devices: none -> 15.2 us  [gathered(): everything = lax.all_to_all(copies, ('grp', 'sub'), 0, 0, tiled=True)]
    ppermute x6, starting transfers between devices: 28.4 us -> 15.3 us  [neighbors(): from_below = lax.ppermute(d3, 'grp', up_grp)]
    all_to_all x0 -> x2, starting transfers between devices: none -> 12.3 us  [gathered(): everything = lax.all_to_all(copies, ('grp', 'sub'), 0, 0, tiled=True)]
    unnamed x45 -> x46, local copies, waits for them, and re-layouts: 16 us -> 6.67 us
  transfers between devices with their start and end apart: 29 -> 26, of which waited for: 13 -> 11; matrix products, arithmetic and copies ran while one was open for 5% -> 3% of each run, Pallas kernels for 0% -> 0%
where the time goes in v2:
time: 222 us; the launch traced here: 221 us
  starting transfers between devices  59.1 us (27%)
  waiting for transfers between devices  51.9 us (23%)
  blocking collectives  46 us (21%)
  matrix products  34.2 us (15%)
  local copies, waits for them, and re-layouts  18.7 us (8%)
  other arithmetic  9.18 us (4%)
    all_to_all x4, blocking collectives, gathered(): everything = lax.all_to_all(copies, ('grp', 'sub'), 0, 0, tiled=True)  46 us
    ppermute x6, waiting for transfers between devices, neighbors(): from_above = lax.ppermute(d2, 'grp', down_grp)  23.1 us
    ppermute x6, starting transfers between devices, neighbors(): left_dev = lax.ppermute(d1[-1:], 'sub', up_sub)  15.6 us
    ppermute x6, starting transfers between devices, neighbors(): from_below = lax.ppermute(d3, 'grp', up_grp)  15.3 us
    all_to_all x2, waiting for transfers between devices, gathered(): everything = lax.all_to_all(copies, ('grp', 'sub'), 0, 0, tiled=True)  15.2 us
    ppermute x6, waiting for transfers between devices, neighbors(): from_below = lax.ppermute(d3, 'grp', up_grp)  13.7 us
    all_to_all x2, starting transfers between devices, gathered(): everything = lax.all_to_all(copies, ('grp', 'sub'), 0, 0, tiled=True)  12.3 us
    dot_general x5, matrix products, lift(): own_part = jnp.einsum('skm,skn->snm', own_modes, shaped, precision=HIGHEST)  8.37 us
  transfers between devices with their start and end apart: 26, of which 11 were waited for; matrix products, arithmetic and copies ran while one was open for 3% of the time, Pallas kernels for 0%

profile of v2, /device:TPU:0, one launch (start us, length us, event | category | flops | bytes accessed | tf_op | source)
XLA Modules:
  0.0 220.9 jit_solution(17358389923339529110)
XLA Ops:
  3.0 2.4 %collective-permute-start.4 = (f32[1,4096]{1,0:T(1,128)S(1)}, f32[1,4096]{1,0:T(1,128)S(1)}, u32[]{:S(2)}, u32[]{:S(2)}) collective-permute-start(f32[1,4096]{1,0:T(1,128)S(1)} %get-tuple-element.44), channel_id=1, source_target_pairs={{0,4},{4,8},{8,12},{12,16},{16,20},{20,24},{24,28},{1,5},{5,9},{9,... | collective-permute-start | bytes 49160 | tf_op jit(solution)/shard_map/ppermute | solution.py:20
  6.7 4.3 %collective-permute-start.6 = (f32[2,4096]{1,0:T(2,128)S(1)}, f32[2,4096]{1,0:T(2,128)S(1)}, u32[]{:S(2)}, u32[]{:S(2)}) collective-permute-start(f32[2,4096]{1,0:T(2,128)S(1)} %get-tuple-element.50), channel_id=1, source_target_pairs={{0,1},{1,2},{2,3},{4,5},{5,6},{6,7},{8,9},{9,10},{10,11},{12,13},{... | collective-permute-start | bytes 98312 | tf_op jit(solution)/shard_map/ppermute | solution.py:24
  13.4 4.0 %collective-permute-start = (f32[1,96,256]{2,1,0:T(8,128)S(1)}, f32[1,96,256]{2,1,0:T(8,128)S(1)}, u32[]{:S(2)}, u32[]{:S(2)}) collective-permute-start(f32[1,96,256]{2,1,0:T(8,128)S(1)} %get-tuple-element.34), channel_id=1, source_target_pairs={{0,4},{4,8},{8,12},{12,16},{16,20},{20,24},{24,28},{1,5},{5,9},{9,... | collective-permute-start | bytes 294920 | tf_op jit(solution)/shard_map/ppermute | solution.py:20
  21.0 4.3 %collective-permute-start.2 = (f32[2,96,256]{2,1,0:T(8,128)S(1)}, f32[2,96,256]{2,1,0:T(8,128)S(1)}, u32[]{:S(2)}, u32[]{:S(2)}) collective-permute-start(f32[2,96,256]{2,1,0:T(8,128)S(1)} %get-tuple-element.38), channel_id=1, source_target_pairs={{0,1},{1,2},{2,3},{4,5},{5,6},{6,7},{8,9},{9,10},{10,11},{12,13},{... | collective-permute-start | bytes 589832 | tf_op jit(solution)/shard_map/ppermute | solution.py:24
  28.7 4.6 %collective-permute-done.3 = f32[2,96,256]{2,1,0:T(8,128)S(1)} collective-permute-done((f32[2,96,256]{2,1,0:T(8,128)S(1)}, f32[2,96,256]{2,1,0:T(8,128)S(1)}, u32[]{:S(2)}, u32[]{:S(2)}) %collective-permute-start.3) | collective-permute-done | bytes 196640 | tf_op jit(solution)/shard_map/ppermute | solution.py:25
  37.3 8.4 %all-to-all-start = ((f32[32,1,1153]{2,1,0:T(1,128)}), f32[32,1,1153]{2,1,0:T(1,128)S(1)}, u32[]{:S(2)}, u32[]{:S(2)}) async-start(f32[32,1,1153]{2,1,0:T(1,128)} %broadcast_in_dim.31), calls=%async_computation | async-start | bytes 327680 | tf_op jit(solution)/shard_map/all_to_all | solution.py:117
  47.0 7.3 %all-to-all-done = f32[32,1,1153]{2,1,0:T(1,128)S(1)} async-done(((f32[32,1,1153]{2,1,0:T(1,128)}), f32[32,1,1153]{2,1,0:T(1,128)S(1)}, u32[]{:S(2)}, u32[]{:S(2)}) %all-to-all-start) | async-done | bytes 147616 | tf_op jit(solution)/shard_map/all_to_all | solution.py:117
  55.9 2.3 %fusion.13 = f32[2,96,1024]{2,1,0:T(8,128)S(1)} fusion(f32[2,96,1024]{2,1,0:T(8,128)S(1)} %bitcast.215, f32[2,6,96]{2,1,0:T(8,128)S(1)} %reshape.221, f32[2,6,1024]{2,0,1:T(2,128)S(1)} %bitcast.209, f32[2,96,1024]{2,1,0:T(8,128)} %bitcast.207, f32[1,2,96,1024]{3,2,1,0:T(8,128)} %param.7), kind=kOutput, calls=%fused_computation.25 | convolution fusion | flops 14745600 | bytes 3199488 | tf_op jit(solution)/shard_map/skm,skn->snm/dot_general | solution.py:128
  59.2 10.7 %all_to_all.51 = f32[32,1,1153]{2,1,0:T(1,128)S(1)} all-to-all(f32[32,1,1153]{2,1,0:T(1,128)S(1)} %broadcast_in_dim.32), channel_id=1, replica_groups=mesh['sub'=8,'grp'=4] {'grp','sub'}, dimensions={0} | all-to-all | bytes 295168 | tf_op jit(solution)/shard_map/all_to_all | solution.py:117
  72.8 1.7 convolution_bitcast_fusion.8
  76.4 2.3 %collective-permute-start.8 = (f32[1,96,256]{2,1,0:T(8,128)S(1)}, f32[1,96,256]{2,1,0:T(8,128)S(1)}, u32[]{:S(2)}, u32[]{:S(2)}) collective-permute-start(f32[1,96,256]{2,1,0:T(8,128)S(1)} %get-tuple-element.28), channel_id=1, source_target_pairs={{0,4},{4,8},{8,12},{12,16},{16,20},{20,24},{24,28},{1,5},{5,9},{9,... | collective-permute-start | bytes 294920 | tf_op jit(solution)/shard_map/ppermute | solution.py:20
  83.2 3.3 %collective-permute-done.10 = f32[2,96,256]{2,1,0:T(8,128)S(1)} collective-permute-done((f32[2,96,256]{2,1,0:T(8,128)S(1)}, f32[2,96,256]{2,1,0:T(8,128)S(1)}, u32[]{:S(2)}, u32[]{:S(2)}) %collective-permute-start.10) | collective-permute-done | bytes 196640 | tf_op jit(solution)/shard_map/ppermute | solution.py:24
  86.6 4.6 %collective-permute-done.11 = f32[2,96,256]{2,1,0:T(8,128)S(1)} collective-permute-done((f32[2,96,256]{2,1,0:T(8,128)S(1)}, f32[2,96,256]{2,1,0:T(8,128)S(1)}, u32[]{:S(2)}, u32[]{:S(2)}) %collective-permute-start.11) | collective-permute-done | bytes 196640 | tf_op jit(solution)/shard_map/ppermute | solution.py:25
  94.7 12.2 %all_to_all.52 = f32[32,1,1248]{2,1,0:T(1,128)S(1)} all-to-all(f32[32,1,1248]{2,1,0:T(1,128)S(1)} %broadcast_in_dim.33), channel_id=1, replica_groups=mesh['sub'=8,'grp'=4] {'grp','sub'}, dimensions={0} | all-to-all | bytes 319488 | tf_op jit(solution)/shard_map/all_to_all | solution.py:117
  110.5 1.7 convolution_bitcast_fusion.7
  112.3 2.0 fusion.11
  115.2 2.3 %collective-permute-start.12 = (f32[1,96,256]{2,1,0:T(8,128)S(1)}, f32[1,96,256]{2,1,0:T(8,128)S(1)}, u32[]{:S(2)}, u32[]{:S(2)}) collective-permute-start(f32[1,96,256]{2,1,0:T(8,128)S(1)} %get-tuple-element.22), channel_id=1, source_target_pairs={{0,4},{4,8},{8,12},{12,16},{16,20},{20,24},{24,28},{1,5},{5,9},{9,... | collective-permute-start | bytes 294920 | tf_op jit(solution)/shard_map/ppermute | solution.py:20
  121.9 3.5 %collective-permute-done.14 = f32[2,96,256]{2,1,0:T(8,128)S(1)} collective-permute-done((f32[2,96,256]{2,1,0:T(8,128)S(1)}, f32[2,96,256]{2,1,0:T(8,128)S(1)}, u32[]{:S(2)}, u32[]{:S(2)}) %collective-permute-start.14) | collective-permute-done | bytes 196640 | tf_op jit(solution)/shard_map/ppermute | solution.py:24
  125.4 4.6 %collective-permute-done.15 = f32[2,96,256]{2,1,0:T(8,128)S(1)} collective-permute-done((f32[2,96,256]{2,1,0:T(8,128)S(1)}, f32[2,96,256]{2,1,0:T(8,128)S(1)}, u32[]{:S(2)}, u32[]{:S(2)}) %collective-permute-start.15) | collective-permute-done | bytes 196640 | tf_op jit(solution)/shard_map/ppermute | solution.py:25
  134.2 4.0 %all-to-all-start.3 = ((f32[32,1,1248]{2,1,0:T(1,128)}), f32[32,1,1248]{2,1,0:T(1,128)}, u32[]{:S(2)}, u32[]{:S(2)}) async-start(f32[32,1,1248]{2,1,0:T(1,128)} %broadcast_in_dim.34), calls=%async_computation.3 | async-start | bytes 327680 | tf_op jit(solution)/shard_map/all_to_all | solution.py:117
  138.9 7.8 %all-to-all-done.3 = f32[32,1,1248]{2,1,0:T(1,128)} async-done(((f32[32,1,1248]{2,1,0:T(1,128)}), f32[32,1,1248]{2,1,0:T(1,128)}, u32[]{:S(2)}, u32[]{:S(2)}) %all-to-all-start.3) | async-done | bytes 159776 | tf_op jit(solution)/shard_map/all_to_all | solution.py:117
  154.0 2.3 %collective-permute-start.16 = (f32[1,96,256]{2,1,0:T(8,128)S(1)}, f32[1,96,256]{2,1,0:T(8,128)S(1)}, u32[]{:S(2)}, u32[]{:S(2)}) collective-permute-start(f32[1,96,256]{2,1,0:T(8,128)S(1)} %get-tuple-element.16), channel_id=1, source_target_pairs={{0,4},{4,8},{8,12},{12,16},{16,20},{20,24},{24,28},{1,5},{5,9},{9,... | collective-permute-start | bytes 294920 | tf_op jit(solution)/shard_map/ppermute | solution.py:20
  157.6 1.7 collective-permute-start.18
  160.9 3.3 %collective-permute-done.18 = f32[2,96,256]{2,1,0:T(8,128)S(1)} collective-permute-done((f32[2,96,256]{2,1,0:T(8,128)S(1)}, f32[2,96,256]{2,1,0:T(8,128)S(1)}, u32[]{:S(2)}, u32[]{:S(2)}) %collective-permute-start.18) | collective-permute-done | bytes 196640 | tf_op jit(solution)/shard_map/ppermute | solution.py:24
  164.2 4.6 %collective-permute-done.19 = f32[2,96,256]{2,1,0:T(8,128)S(1)} collective-permute-done((f32[2,96,256]{2,1,0:T(8,128)S(1)}, f32[2,96,256]{2,1,0:T(8,128)S(1)}, u32[]{:S(2)}, u32[]{:S(2)}) %collective-permute-start.19) | collective-permute-done | bytes 196640 | tf_op jit(solution)/shard_map/ppermute | solution.py:25
  172.3 12.2 %all_to_all.53 = f32[32,1,1248]{2,1,0:T(1,128)S(1)} all-to-all(f32[32,1,1248]{2,1,0:T(1,128)S(1)} %broadcast_in_dim.35), channel_id=1, replica_groups=mesh['sub'=8,'grp'=4] {'grp','sub'}, dimensions={0} | all-to-all | bytes 319488 | tf_op jit(solution)/shard_map/all_to_all | solution.py:117
  186.4 2.2 %fusion.14 = f32[2,96,1024]{2,1,0:T(8,128)S(1)} fusion(f32[2,96,1024]{2,1,0:T(8,128)} %copy-done.13, f32[2,96,1024]{2,1,0:T(8,128)S(1)} %bitcast.214, f32[2,6,96]{2,1,0:T(8,128)S(1)} %reshape.241, f32[2,96,1024]{2,1,0:T(8,128)S(1)} %copy-done.1, f32[96]{0:T(128)S(1)} %div.26, f32[2,6,1024]{2,0,1:T(2,128)S(1)} %bitcast.213), kind=kOutput, calls=%fused_computation.26 | convolution fusion | flops 14942208 | bytes 3199872 | tf_op jit(solution)/shard_map/skm,skn->snm/dot_general | solution.py:128
  189.5 2.3 %collective-permute-start.20 = (f32[1,96,256]{2,1,0:T(8,128)S(1)}, f32[1,96,256]{2,1,0:T(8,128)S(1)}, u32[]{:S(2)}, u32[]{:S(2)}) collective-permute-start(f32[1,96,256]{2,1,0:T(8,128)S(1)} %get-tuple-element.10), channel_id=1, source_target_pairs={{0,4},{4,8},{8,12},{12,16},{16,20},{20,24},{24,28},{1,5},{5,9},{9,... | collective-permute-start | bytes 294920 | tf_op jit(solution)/shard_map/ppermute | solution.py:20
  196.2 3.5 %collective-permute-done.22 = f32[2,96,256]{2,1,0:T(8,128)S(1)} collective-permute-done((f32[2,96,256]{2,1,0:T(8,128)S(1)}, f32[2,96,256]{2,1,0:T(8,128)S(1)}, u32[]{:S(2)}, u32[]{:S(2)}) %collective-permute-start.22) | collective-permute-done | bytes 196640 | tf_op jit(solution)/shard_map/ppermute | solution.py:24
  199.7 4.6 %collective-permute-done.23 = f32[2,96,256]{2,1,0:T(8,128)S(1)} collective-permute-done((f32[2,96,256]{2,1,0:T(8,128)S(1)}, f32[2,96,256]{2,1,0:T(8,128)S(1)}, u32[]{:S(2)}, u32[]{:S(2)}) %collective-permute-start.23) | collective-permute-done | bytes 196640 | tf_op jit(solution)/shard_map/ppermute | solution.py:25
  207.0 10.8 %all_to_all.54 = f32[32,1,96]{2,1,0:T(1,128)S(1)} all-to-all(f32[32,1,96]{2,1,0:T(1,128)S(1)} %broadcast_in_dim.36), channel_id=1, replica_groups=mesh['sub'=8,'grp'=4] {'grp','sub'}, dimensions={0} | all-to-all | bytes 24576 | tf_op jit(solution)/shard_map/all_to_all | solution.py:117
  217.9 3.0 %subtract_bitcast_fusion = (f32[1,2,96,1024]{3,2,1,0:T(8,128)}, f32[1,2,96,1024]{3,2,1,0:T(8,128)}) fusion(f32[2,96,1024]{2,1,0:T(8,128)} %get-tuple-element.3, f32[96]{0:T(128)S(1)} %div.27, f32[2,96,1024]{2,1,0:T(8,128)S(1)} %fusion.13, f32[2,96,1024]{2,1,0:T(8,128)S(1)} %copy-done.9, f32[96]{0:T(128)S(1)} %div.25, f32[2,96,1024]{2,1,0:T(8,128)} %copy-done.10, ...), kind=kLoop, calls=%fused_computation.54 | loop fusion | flops 1376256 | bytes 5505792 | tf_op jit(solution)/shard_map/broadcast_in_dim | solution.py:166
  (209 shorter events, 70.0 us)
Async XLA Ops:
  0.6 26.9 %copy-start.18 = (s32[4]{0:T(128)S(1)}, s32[4]{0:T(128)}, u32[]{:S(2)}) copy-start(s32[4]{0:T(128)} %constant.38) | copy-start | bytes 52
  0.6 18.9 %copy-start.15 = (f32[1,2,6,1024]{3,1,2,0:T(2,128)S(1)}, f32[1,2,6,1024]{3,1,2,0:T(2,128)}, u32[]{:S(2)}) copy-start(f32[1,2,6,1024]{3,1,2,0:T(2,128)} %param.10) | copy-start | bytes 147460
  0.7 19.0 %copy-start.17 = (f32[1,2,6,384]{3,1,2,0:T(2,128)S(1)}, f32[1,2,6,384]{3,1,2,0:T(2,128)}, u32[]{:S(2)}) copy-start(f32[1,2,6,384]{3,1,2,0:T(2,128)} %param.11) | copy-start | bytes 55300
  3.0 16.7 %collective-permute-start.4 = (f32[1,4096]{1,0:T(1,128)S(1)}, f32[1,4096]{1,0:T(1,128)S(1)}, u32[]{:S(2)}, u32[]{:S(2)}) collective-permute-start(f32[1,4096]{1,0:T(1,128)S(1)} %get-tuple-element.44), channel_id=1, source_target_pairs={{0,4},{4,8},{8,12},{12,16},{16,20},{20,24},{24,28},{1,5},{5,9},{9,... | collective-permute-start | bytes 49160 | tf_op jit(solution)/shard_map/ppermute | solution.py:20
  5.4 15.6 %collective-permute-start.5 = (f32[1,4096]{1,0:T(1,128)S(1)}, f32[1,4096]{1,0:T(1,128)S(1)}, u32[]{:S(2)}, u32[]{:S(2)}) collective-permute-start(f32[1,4096]{1,0:T(1,128)S(1)} %get-tuple-element.47), channel_id=1, source_target_pairs={{4,0},{8,4},{12,8},{16,12},{20,16},{24,20},{28,24},{5,1},{9,5},{13... | collective-permute-start | bytes 49160 | tf_op jit(solution)/shard_map/ppermute | solution.py:21
  6.7 18.7 %collective-permute-start.6 = (f32[2,4096]{1,0:T(2,128)S(1)}, f32[2,4096]{1,0:T(2,128)S(1)}, u32[]{:S(2)}, u32[]{:S(2)}) collective-permute-start(f32[2,4096]{1,0:T(2,128)S(1)} %get-tuple-element.50), channel_id=1, source_target_pairs={{0,1},{1,2},{2,3},{4,5},{5,6},{6,7},{8,9},{9,10},{10,11},{12,13},{... | collective-permute-start | bytes 98312 | tf_op jit(solution)/shard_map/ppermute | solution.py:24
  11.0 15.8 %collective-permute-start.7 = (f32[2,4096]{1,0:T(2,128)S(1)}, f32[2,4096]{1,0:T(2,128)S(1)}, u32[]{:S(2)}, u32[]{:S(2)}) collective-permute-start(f32[2,4096]{1,0:T(2,128)S(1)} %get-tuple-element.51), channel_id=1, source_target_pairs={{1,0},{2,1},{3,2},{5,4},{6,5},{7,6},{9,8},{10,9},{11,10},{13,12},{... | collective-permute-start | bytes 98312 | tf_op jit(solution)/shard_map/ppermute | solution.py:25
  13.4 15.3 %collective-permute-start = (f32[1,96,256]{2,1,0:T(8,128)S(1)}, f32[1,96,256]{2,1,0:T(8,128)S(1)}, u32[]{:S(2)}, u32[]{:S(2)}) collective-permute-start(f32[1,96,256]{2,1,0:T(8,128)S(1)} %get-tuple-element.34), channel_id=1, source_target_pairs={{0,4},{4,8},{8,12},{12,16},{16,20},{20,24},{24,28},{1,5},{5,9},{9,... | collective-permute-start | bytes 294920 | tf_op jit(solution)/shard_map/ppermute | solution.py:20
  19.6 9.0 %collective-permute-start.1 = (f32[1,96,256]{2,1,0:T(8,128)S(1)}, f32[1,96,256]{2,1,0:T(8,128)S(1)}, u32[]{:S(2)}, u32[]{:S(2)}) collective-permute-start(f32[1,96,256]{2,1,0:T(8,128)S(1)} %get-tuple-element.35), channel_id=1, source_target_pairs={{4,0},{8,4},{12,8},{16,12},{20,16},{24,20},{28,24},{5,1},{9,5},{13... | collective-permute-start | bytes 294920 | tf_op jit(solution)/shard_map/ppermute | solution.py:21
  21.0 7.7 %collective-permute-start.2 = (f32[2,96,256]{2,1,0:T(8,128)S(1)}, f32[2,96,256]{2,1,0:T(8,128)S(1)}, u32[]{:S(2)}, u32[]{:S(2)}) collective-permute-start(f32[2,96,256]{2,1,0:T(8,128)S(1)} %get-tuple-element.38), channel_id=1, source_target_pairs={{0,1},{1,2},{2,3},{4,5},{5,6},{6,7},{8,9},{9,10},{10,11},{12,13},{... | collective-permute-start | bytes 589832 | tf_op jit(solution)/shard_map/ppermute | solution.py:24
  25.4 7.9 %collective-permute-start.3 = (f32[2,96,256]{2,1,0:T(8,128)S(1)}, f32[2,96,256]{2,1,0:T(8,128)S(1)}, u32[]{:S(2)}, u32[]{:S(2)}) collective-permute-start(f32[2,96,256]{2,1,0:T(8,128)S(1)} %get-tuple-element.39), channel_id=1, source_target_pairs={{1,0},{2,1},{3,2},{5,4},{6,5},{7,6},{9,8},{10,9},{11,10},{13,12},{... | collective-permute-start | bytes 589832 | tf_op jit(solution)/shard_map/ppermute | solution.py:25
  37.3 17.0 %all-to-all-start = ((f32[32,1,1153]{2,1,0:T(1,128)}), f32[32,1,1153]{2,1,0:T(1,128)S(1)}, u32[]{:S(2)}, u32[]{:S(2)}) async-start(f32[32,1,1153]{2,1,0:T(1,128)} %broadcast_in_dim.31), calls=%async_computation | async-start | bytes 327680 | tf_op jit(solution)/shard_map/all_to_all | solution.py:117
  76.4 6.8 %collective-permute-start.8 = (f32[1,96,256]{2,1,0:T(8,128)S(1)}, f32[1,96,256]{2,1,0:T(8,128)S(1)}, u32[]{:S(2)}, u32[]{:S(2)}) collective-permute-start(f32[1,96,256]{2,1,0:T(8,128)S(1)} %get-tuple-element.28), channel_id=1, source_target_pairs={{0,4},{4,8},{8,12},{12,16},{16,20},{20,24},{24,28},{1,5},{5,9},{9,... | collective-permute-start | bytes 294920 | tf_op jit(solution)/shard_map/ppermute | solution.py:20
  78.7 4.5 %collective-permute-start.9 = (f32[1,96,256]{2,1,0:T(8,128)S(1)}, f32[1,96,256]{2,1,0:T(8,128)S(1)}, u32[]{:S(2)}, u32[]{:S(2)}) collective-permute-start(f32[1,96,256]{2,1,0:T(8,128)S(1)} %get-tuple-element.29), channel_id=1, source_target_pairs={{4,0},{8,4},{12,8},{16,12},{20,16},{24,20},{28,24},{5,1},{9,5},{13... | collective-permute-start | bytes 294920 | tf_op jit(solution)/shard_map/ppermute | solution.py:21
  80.0 6.6 %collective-permute-start.10 = (f32[2,96,256]{2,1,0:T(8,128)S(1)}, f32[2,96,256]{2,1,0:T(8,128)S(1)}, u32[]{:S(2)}, u32[]{:S(2)}) collective-permute-start(f32[2,96,256]{2,1,0:T(8,128)S(1)} %get-tuple-element.32), channel_id=1, source_target_pairs={{0,1},{1,2},{2,3},{4,5},{5,6},{6,7},{8,9},{9,10},{10,11},{12,13},{... | collective-permute-start | bytes 589832 | tf_op jit(solution)/shard_map/ppermute | solution.py:24
  81.7 9.5 %collective-permute-start.11 = (f32[2,96,256]{2,1,0:T(8,128)S(1)}, f32[2,96,256]{2,1,0:T(8,128)S(1)}, u32[]{:S(2)}, u32[]{:S(2)}) collective-permute-start(f32[2,96,256]{2,1,0:T(8,128)S(1)} %get-tuple-element.33), channel_id=1, source_target_pairs={{1,0},{2,1},{3,2},{5,4},{6,5},{7,6},{9,8},{10,9},{11,10},{13,12},{... | collective-permute-start | bytes 589832 | tf_op jit(solution)/shard_map/ppermute | solution.py:25
  114.3 17.2 %copy-start = (f32[2,96,1024]{2,1,0:T(8,128)}, f32[2,96,1024]{2,1,0:T(8,128)S(1)}, u32[]{:S(2)}) copy-start(f32[2,96,1024]{2,1,0:T(8,128)S(1)} %fusion.11) | copy-start | bytes 2359300
  115.2 6.6 %collective-permute-start.12 = (f32[1,96,256]{2,1,0:T(8,128)S(1)}, f32[1,96,256]{2,1,0:T(8,128)S(1)}, u32[]{:S(2)}, u32[]{:S(2)}) collective-permute-start(f32[1,96,256]{2,1,0:T(8,128)S(1)} %get-tuple-element.22), channel_id=1, source_target_pairs={{0,4},{4,8},{8,12},{12,16},{16,20},{20,24},{24,28},{1,5},{5,9},{9,... | collective-permute-start | bytes 294920 | tf_op jit(solution)/shard_map/ppermute | solution.py:20
  117.5 4.3 %collective-permute-start.13 = (f32[1,96,256]{2,1,0:T(8,128)S(1)}, f32[1,96,256]{2,1,0:T(8,128)S(1)}, u32[]{:S(2)}, u32[]{:S(2)}) collective-permute-start(f32[1,96,256]{2,1,0:T(8,128)S(1)} %get-tuple-element.23), channel_id=1, source_target_pairs={{4,0},{8,4},{12,8},{16,12},{20,16},{24,20},{28,24},{5,1},{9,5},{13... | collective-permute-start | bytes 294920 | tf_op jit(solution)/shard_map/ppermute | solution.py:21
  118.8 6.6 %collective-permute-start.14 = (f32[2,96,256]{2,1,0:T(8,128)S(1)}, f32[2,96,256]{2,1,0:T(8,128)S(1)}, u32[]{:S(2)}, u32[]{:S(2)}) collective-permute-start(f32[2,96,256]{2,1,0:T(8,128)S(1)} %get-tuple-element.26), channel_id=1, source_target_pairs={{0,1},{1,2},{2,3},{4,5},{5,6},{6,7},{8,9},{9,10},{10,11},{12,13},{... | collective-permute-start | bytes 589832 | tf_op jit(solution)/shard_map/ppermute | solution.py:24
  120.5 9.5 %collective-permute-start.15 = (f32[2,96,256]{2,1,0:T(8,128)S(1)}, f32[2,96,256]{2,1,0:T(8,128)S(1)}, u32[]{:S(2)}, u32[]{:S(2)}) collective-permute-start(f32[2,96,256]{2,1,0:T(8,128)S(1)} %get-tuple-element.27), channel_id=1, source_target_pairs={{1,0},{2,1},{3,2},{5,4},{6,5},{7,6},{9,8},{10,9},{11,10},{13,12},{... | collective-permute-start | bytes 589832 | tf_op jit(solution)/shard_map/ppermute | solution.py:25
  134.2 12.5 %all-to-all-start.3 = ((f32[32,1,1248]{2,1,0:T(1,128)}), f32[32,1,1248]{2,1,0:T(1,128)}, u32[]{:S(2)}, u32[]{:S(2)}) async-start(f32[32,1,1248]{2,1,0:T(1,128)} %broadcast_in_dim.34), calls=%async_computation.3 | async-start | bytes 327680 | tf_op jit(solution)/shard_map/all_to_all | solution.py:117
  154.0 6.8 %collective-permute-start.16 = (f32[1,96,256]{2,1,0:T(8,128)S(1)}, f32[1,96,256]{2,1,0:T(8,128)S(1)}, u32[]{:S(2)}, u32[]{:S(2)}) collective-permute-start(f32[1,96,256]{2,1,0:T(8,128)S(1)} %get-tuple-element.16), channel_id=1, source_target_pairs={{0,4},{4,8},{8,12},{12,16},{16,20},{20,24},{24,28},{1,5},{5,9},{9,... | collective-permute-start | bytes 294920 | tf_op jit(solution)/shard_map/ppermute | solution.py:20
  156.3 4.5 %collective-permute-start.17 = (f32[1,96,256]{2,1,0:T(8,128)S(1)}, f32[1,96,256]{2,1,0:T(8,128)S(1)}, u32[]{:S(2)}, u32[]{:S(2)}) collective-permute-start(f32[1,96,256]{2,1,0:T(8,128)S(1)} %get-tuple-element.17), channel_id=1, source_target_pairs={{4,0},{8,4},{12,8},{16,12},{20,16},{24,20},{28,24},{5,1},{9,5},{13... | collective-permute-start | bytes 294920 | tf_op jit(solution)/shard_map/ppermute | solution.py:21
  157.6 6.6 %collective-permute-start.18 = (f32[2,96,256]{2,1,0:T(8,128)S(1)}, f32[2,96,256]{2,1,0:T(8,128)S(1)}, u32[]{:S(2)}, u32[]{:S(2)}) collective-permute-start(f32[2,96,256]{2,1,0:T(8,128)S(1)} %get-tuple-element.20), channel_id=1, source_target_pairs={{0,1},{1,2},{2,3},{4,5},{5,6},{6,7},{8,9},{9,10},{10,11},{12,13},{... | collective-permute-start | bytes 589832 | tf_op jit(solution)/shard_map/ppermute | solution.py:24
  159.3 9.5 %collective-permute-start.19 = (f32[2,96,256]{2,1,0:T(8,128)S(1)}, f32[2,96,256]{2,1,0:T(8,128)S(1)}, u32[]{:S(2)}, u32[]{:S(2)}) collective-permute-start(f32[2,96,256]{2,1,0:T(8,128)S(1)} %get-tuple-element.21), channel_id=1, source_target_pairs={{1,0},{2,1},{3,2},{5,4},{6,5},{7,6},{9,8},{10,9},{11,10},{13,12},{... | collective-permute-start | bytes 589832 | tf_op jit(solution)/shard_map/ppermute | solution.py:25
  188.6 17.2 %copy-start.10 = (f32[2,96,1024]{2,1,0:T(8,128)}, f32[2,96,1024]{2,1,0:T(8,128)S(1)}, u32[]{:S(2)}) copy-start(f32[2,96,1024]{2,1,0:T(8,128)S(1)} %fusion.14) | copy-start | bytes 2359300
  189.5 6.6 %collective-permute-start.20 = (f32[1,96,256]{2,1,0:T(8,128)S(1)}, f32[1,96,256]{2,1,0:T(8,128)S(1)}, u32[]{:S(2)}, u32[]{:S(2)}) collective-permute-start(f32[1,96,256]{2,1,0:T(8,128)S(1)} %get-tuple-element.10), channel_id=1, source_target_pairs={{0,4},{4,8},{8,12},{12,16},{16,20},{20,24},{24,28},{1,5},{5,9},{9,... | collective-permute-start | bytes 294920 | tf_op jit(solution)/shard_map/ppermute | solution.py:20
  191.8 4.3 %collective-permute-start.21 = (f32[1,96,256]{2,1,0:T(8,128)S(1)}, f32[1,96,256]{2,1,0:T(8,128)S(1)}, u32[]{:S(2)}, u32[]{:S(2)}) collective-permute-start(f32[1,96,256]{2,1,0:T(8,128)S(1)} %get-tuple-element.11), channel_id=1, source_target_pairs={{4,0},{8,4},{12,8},{16,12},{20,16},{24,20},{28,24},{5,1},{9,5},{13... | collective-permute-start | bytes 294920 | tf_op jit(solution)/shard_map/ppermute | solution.py:21
  193.1 6.6 %collective-permute-start.22 = (f32[2,96,256]{2,1,0:T(8,128)S(1)}, f32[2,96,256]{2,1,0:T(8,128)S(1)}, u32[]{:S(2)}, u32[]{:S(2)}) collective-permute-start(f32[2,96,256]{2,1,0:T(8,128)S(1)} %get-tuple-element.14), channel_id=1, source_target_pairs={{0,1},{1,2},{2,3},{4,5},{5,6},{6,7},{8,9},{9,10},{10,11},{12,13},{... | collective-permute-start | bytes 589832 | tf_op jit(solution)/shard_map/ppermute | solution.py:24
  194.8 9.5 %collective-permute-start.23 = (f32[2,96,256]{2,1,0:T(8,128)S(1)}, f32[2,96,256]{2,1,0:T(8,128)S(1)}, u32[]{:S(2)}, u32[]{:S(2)}) collective-permute-start(f32[2,96,256]{2,1,0:T(8,128)S(1)} %get-tuple-element.15), channel_id=1, source_target_pairs={{1,0},{2,1},{3,2},{5,4},{6,5},{7,6},{9,8},{10,9},{11,10},{13,12},{... | collective-permute-start | bytes 589832 | tf_op jit(solution)/shard_map/ppermute | solution.py:25
  205.7 12.2 %copy-start.2 = (f32[2,96,1024]{2,1,0:T(8,128)S(1)}, f32[2,96,1024]{2,1,0:T(8,128)}, u32[]{:S(2)}) copy-start(f32[2,96,1024]{2,1,0:T(8,128)} %copy-done) | copy-start | bytes 2359300
  (14 other events, 43.4 us)

commit v3 on v2

--- a/solution.py
+++ b/solution.py
@@ -64,12 +64,15 @@
     rows_here = coarse_op[0].reshape(subdomains * MODES, -1)
     coarse_total = rows_here.shape[1]
 
+    gap_faces = face_split(vectors)
     mode_faces = face_split(own_modes)
     map_faces = face_split(maps.astype(jnp.float32)[:, None, :])
     own_rows = coarse_op[0]
+    gap_size = columns * quarter
     packs = [
         jnp.concatenate(
             [
+                gap_faces[g].reshape(subdomains, -1),
                 mode_faces[g].reshape(subdomains, -1),
                 map_faces[g].reshape(subdomains, -1),
                 own_rows.reshape(subdomains, -1),
@@ -79,6 +82,8 @@
         for g in range(4)
     ]
     partner_pack = neighbors(*packs)
+    partner_gaps = partner_pack[:, :, :gap_size].reshape(subdomains, 4, columns, quarter)
+    partner_pack = partner_pack[:, :, gap_size:]
     partner_raw_modes = partner_pack[:, :, : MODES * quarter].reshape(subdomains, 4, MODES, quarter)
     partner_map = partner_pack[:, :, MODES * quarter:(MODES + 1) * quarter]
     partner_rows = partner_pack[:, :, (MODES + 1) * quarter:].reshape(
@@ -101,11 +106,12 @@
 
     partner_modes = to_mine(partner_raw_modes)
 
+    def partner_values(raw, shape):
+        return jnp.moveaxis(to_mine(raw), 1, 2).reshape(shape)
+
     def jump(values):
         raw = neighbors(*face_split(values))
-        partner = to_mine(raw)
-        partner = jnp.moveaxis(partner, 1, 2).reshape(values.shape)
-        return values - partner
+        return values - partner_values(raw, values.shape)
 
     def coefficients(values):
         return jnp.einsum("skm,snm->skn", weighted_modes, values, precision=HIGHEST)
@@ -134,7 +140,7 @@
         return values - lift(flat)
 
     nothing = jnp.zeros((1,), jnp.float32)
-    dual = jump(vectors)
+    dual = vectors - partner_values(partner_gaps, vectors.shape)
     flat_dual, _ = gathered(coefficients(dual), nothing)
     residual = project_with(dual, flat_dual)
     flat_residual, _ = gathered(coefficients(residual), nothing)

time: 222 us -> 214 us (0.964)
  starting transfers between devices: 59.1 us -> 45.8 us
  local copies, waits for them, and re-layouts: 18.7 us -> 23.5 us
  matrix products: 34.2 us -> 31.5 us
    ppermute x6 -> x5, starting transfers between devices: 15.3 us -> 11 us  [neighbors(): from_below = lax.ppermute(d3, 'grp', up_grp)]
    ppermute x6 -> x5, starting transfers between devices: 15.6 us -> 11.5 us  [neighbors(): left_dev = lax.ppermute(d1[-1:], 'sub', up_sub)]
    unnamed x46 -> x65, local copies, waits for them, and re-layouts: 6.67 us -> 10.4 us
    ppermute x6 -> x5, waiting for transfers between devices: 13.7 us -> 16 us  [neighbors(): from_below = lax.ppermute(d3, 'grp', up_grp)]
    ppermute x6 -> x5, starting transfers between devices: 8.15 us -> 6.46 us  [neighbors(): from_above = lax.ppermute(d2, 'grp', down_grp)]
    ppermute x6 -> x5, starting transfers between devices: 7.75 us -> 6.46 us  [neighbors(): right_dev = lax.ppermute(d0[:1], 'sub', down_sub)]
    ppermute x6 -> x5, waiting for transfers between devices: 23.1 us -> 23 us  [neighbors(): from_above = lax.ppermute(d2, 'grp', down_grp)]
  transfers between devices with their start and end apart: 26 -> 22, of which waited for: 11 -> 12; matrix products, arithmetic and copies ran while one was open for 3% -> 2% of each run, Pallas kernels for 0% -> 0%
where the time goes in v3:
time: 214 us; the launch traced here: 213 us
  waiting for transfers between devices  53.2 us (25%)
  blocking collectives  46 us (21%)
  starting transfers between devices  45.8 us (21%)
  matrix products  31.5 us (15%)
  local copies, waits for them, and re-layouts  23.5 us (11%)
  other arithmetic  11.1 us (5%)
    all_to_all x4, blocking collectives, gathered(): everything = lax.all_to_all(copies, ('grp', 'sub'), 0, 0, tiled=True)  46 us
    ppermute x5, waiting for transfers between devices, neighbors(): from_above = lax.ppermute(d2, 'grp', down_grp)  23 us
    ppermute x5, waiting for transfers between devices, neighbors(): from_below = lax.ppermute(d3, 'grp', up_grp)  16 us
    all_to_all x2, waiting for transfers between devices, gathered(): everything = lax.all_to_all(copies, ('grp', 'sub'), 0, 0, tiled=True)  14.2 us
    ppermute x5, starting transfers between devices, neighbors(): left_dev = lax.ppermute(d1[-1:], 'sub', up_sub)  11.5 us
    ppermute x5, starting transfers between devices, neighbors(): from_below = lax.ppermute(d3, 'grp', up_grp)  11 us
    unnamed x65, local copies, waits for them, and re-layouts  10.4 us
    all_to_all x2, starting transfers between devices, gathered(): everything = lax.all_to_all(copies, ('grp', 'sub'), 0, 0, tiled=True)  10.4 us
  transfers between devices with their start and end apart: 22, of which 12 were waited for; matrix products, arithmetic and copies ran while one was open for 2% of the time, Pallas kernels for 0%

profile of v3, /device:TPU:0, one launch (start us, length us, event | category | flops | bytes accessed | tf_op | source)
XLA Modules:
  0.0 212.9 jit_solution(18290311867162140052)
XLA Ops:
  4.7 2.4 %collective-permute-start = (f32[1,28672]{1,0:T(1,128)S(1)}, f32[1,28672]{1,0:T(1,128)S(1)}, u32[]{:S(2)}, u32[]{:S(2)}) collective-permute-start(f32[1,28672]{1,0:T(1,128)S(1)} %get-tuple-element.38), channel_id=1, source_target_pairs={{0,4},{4,8},{8,12},{12,16},{16,20},{20,24},{24,28},{1,5},{5,9},{9,... | collective-permute-start | bytes 344072 | tf_op jit(solution)/shard_map/ppermute | solution.py:20
  8.6 4.3 %collective-permute-start.2 = (f32[2,28672]{1,0:T(2,128)S(1)}, f32[2,28672]{1,0:T(2,128)S(1)}, u32[]{:S(2)}, u32[]{:S(2)}) collective-permute-start(f32[2,28672]{1,0:T(2,128)S(1)} %get-tuple-element.48), channel_id=1, source_target_pairs={{0,1},{1,2},{2,3},{4,5},{5,6},{6,7},{8,9},{9,10},{10,11},{12,13},{... | collective-permute-start | bytes 688136 | tf_op jit(solution)/shard_map/ppermute | solution.py:24
  15.5 1.9 collective-permute-done.2
  17.6 4.6 %collective-permute-done.3 = f32[2,28672]{1,0:T(2,128)S(1)} collective-permute-done((f32[2,28672]{1,0:T(2,128)S(1)}, f32[2,28672]{1,0:T(2,128)S(1)}, u32[]{:S(2)}, u32[]{:S(2)}) %collective-permute-start.3) | collective-permute-done | bytes 229408 | tf_op jit(solution)/shard_map/ppermute | solution.py:25
  29.9 6.2 %all-to-all-start = ((f32[32,1,1153]{2,1,0:T(1,128)}), f32[32,1,1153]{2,1,0:T(1,128)S(1)}, u32[]{:S(2)}, u32[]{:S(2)}) async-start(f32[32,1,1153]{2,1,0:T(1,128)} %broadcast_in_dim.31), calls=%async_computation | async-start | bytes 327680 | tf_op jit(solution)/shard_map/all_to_all | solution.py:123
  38.1 6.6 %all-to-all-done = f32[32,1,1153]{2,1,0:T(1,128)S(1)} async-done(((f32[32,1,1153]{2,1,0:T(1,128)}), f32[32,1,1153]{2,1,0:T(1,128)S(1)}, u32[]{:S(2)}, u32[]{:S(2)}) %all-to-all-start) | async-done | bytes 147616 | tf_op jit(solution)/shard_map/all_to_all | solution.py:123
  46.4 2.3 %fusion.13 = f32[2,96,1024]{2,1,0:T(8,128)S(1)} fusion(f32[2,96,1024]{2,1,0:T(8,128)S(1)} %bitcast.210, f32[2,6,96]{2,1,0:T(8,128)S(1)} %reshape.241, f32[2,6,1024]{2,0,1:T(2,128)S(1)} %bitcast.204, f32[2,96,1024]{2,1,0:T(8,128)} %bitcast.202, f32[1,2,96,1024]{3,2,1,0:T(8,128)} %param.7), kind=kOutput, calls=%fused_computation.25 | convolution fusion | flops 14745600 | bytes 3199488 | tf_op jit(solution)/shard_map/skm,skn->snm/dot_general | solution.py:134
  49.6 10.7 %all_to_all.51 = f32[32,1,1153]{2,1,0:T(1,128)S(1)} all-to-all(f32[32,1,1153]{2,1,0:T(1,128)S(1)} %broadcast_in_dim.32), channel_id=1, replica_groups=mesh['sub'=8,'grp'=4] {'grp','sub'}, dimensions={0} | all-to-all | bytes 295168 | tf_op jit(solution)/shard_map/all_to_all | solution.py:123
  66.3 2.3 %collective-permute-start.4 = (f32[1,96,256]{2,1,0:T(8,128)S(1)}, f32[1,96,256]{2,1,0:T(8,128)S(1)}, u32[]{:S(2)}, u32[]{:S(2)}) collective-permute-start(f32[1,96,256]{2,1,0:T(8,128)S(1)} %get-tuple-element.28), channel_id=1, source_target_pairs={{0,4},{4,8},{8,12},{12,16},{16,20},{20,24},{24,28},{1,5},{5,9},{9,... | collective-permute-start | bytes 294920 | tf_op jit(solution)/shard_map/ppermute | solution.py:20
  69.9 1.7 collective-permute-start.6
  73.0 3.5 %collective-permute-done.6 = f32[2,96,256]{2,1,0:T(8,128)S(1)} collective-permute-done((f32[2,96,256]{2,1,0:T(8,128)S(1)}, f32[2,96,256]{2,1,0:T(8,128)S(1)}, u32[]{:S(2)}, u32[]{:S(2)}) %collective-permute-start.6) | collective-permute-done | bytes 196640 | tf_op jit(solution)/shard_map/ppermute | solution.py:24
  76.5 4.6 %collective-permute-done.7 = f32[2,96,256]{2,1,0:T(8,128)S(1)} collective-permute-done((f32[2,96,256]{2,1,0:T(8,128)S(1)}, f32[2,96,256]{2,1,0:T(8,128)S(1)}, u32[]{:S(2)}, u32[]{:S(2)}) %collective-permute-start.7) | collective-permute-done | bytes 196640 | tf_op jit(solution)/shard_map/ppermute | solution.py:25
  84.6 12.2 %all_to_all.52 = f32[32,1,1248]{2,1,0:T(1,128)S(1)} all-to-all(f32[32,1,1248]{2,1,0:T(1,128)S(1)} %broadcast_in_dim.33), channel_id=1, replica_groups=mesh['sub'=8,'grp'=4] {'grp','sub'}, dimensions={0} | all-to-all | bytes 319488 | tf_op jit(solution)/shard_map/all_to_all | solution.py:123
  100.7 2.3 %fusion.11 = f32[2,96,1024]{2,1,0:T(8,128)S(1)} fusion(f32[2,96,1024]{2,1,0:T(8,128)} %copy-done.14, f32[2,96,1024]{2,1,0:T(8,128)S(1)} %bitcast.211, f32[2,6,96]{2,1,0:T(8,128)S(1)} %reshape.252, f32[2,6,1024]{2,0,1:T(2,128)S(1)} %bitcast.206), kind=kOutput, calls=%fused_computation.21 | convolution fusion | flops 14548992 | bytes 2413056 | tf_op jit(solution)/shard_map/skm,skn->snm/dot_general | solution.py:134
  103.9 2.3 %collective-permute-start.8 = (f32[1,96,256]{2,1,0:T(8,128)S(1)}, f32[1,96,256]{2,1,0:T(8,128)S(1)}, u32[]{:S(2)}, u32[]{:S(2)}) collective-permute-start(f32[1,96,256]{2,1,0:T(8,128)S(1)} %get-tuple-element.22), channel_id=1, source_target_pairs={{0,4},{4,8},{8,12},{12,16},{16,20},{20,24},{24,28},{1,5},{5,9},{9,... | collective-permute-start | bytes 294920 | tf_op jit(solution)/shard_map/ppermute | solution.py:20
  107.6 1.7 collective-permute-start.10
  110.6 3.5 %collective-permute-done.10 = f32[2,96,256]{2,1,0:T(8,128)S(1)} collective-permute-done((f32[2,96,256]{2,1,0:T(8,128)S(1)}, f32[2,96,256]{2,1,0:T(8,128)S(1)}, u32[]{:S(2)}, u32[]{:S(2)}) %collective-permute-start.10) | collective-permute-done | bytes 196640 | tf_op jit(solution)/shard_map/ppermute | solution.py:24
  114.1 4.6 %collective-permute-done.11 = f32[2,96,256]{2,1,0:T(8,128)S(1)} collective-permute-done((f32[2,96,256]{2,1,0:T(8,128)S(1)}, f32[2,96,256]{2,1,0:T(8,128)S(1)}, u32[]{:S(2)}, u32[]{:S(2)}) %collective-permute-start.11) | collective-permute-done | bytes 196640 | tf_op jit(solution)/shard_map/ppermute | solution.py:25
  122.9 4.2 %all-to-all-start.3 = ((f32[32,1,1248]{2,1,0:T(1,128)}), f32[32,1,1248]{2,1,0:T(1,128)}, u32[]{:S(2)}, u32[]{:S(2)}) async-start(f32[32,1,1248]{2,1,0:T(1,128)} %broadcast_in_dim.34), calls=%async_computation.3 | async-start | bytes 327680 | tf_op jit(solution)/shard_map/all_to_all | solution.py:123
  127.9 7.6 %all-to-all-done.3 = f32[32,1,1248]{2,1,0:T(1,128)} async-done(((f32[32,1,1248]{2,1,0:T(1,128)}), f32[32,1,1248]{2,1,0:T(1,128)}, u32[]{:S(2)}, u32[]{:S(2)}) %all-to-all-start.3) | async-done | bytes 159776 | tf_op jit(solution)/shard_map/all_to_all | solution.py:123
  144.3 2.3 %collective-permute-start.12 = (f32[1,96,256]{2,1,0:T(8,128)S(1)}, f32[1,96,256]{2,1,0:T(8,128)S(1)}, u32[]{:S(2)}, u32[]{:S(2)}) collective-permute-start(f32[1,96,256]{2,1,0:T(8,128)S(1)} %get-tuple-element.16), channel_id=1, source_target_pairs={{0,4},{4,8},{8,12},{12,16},{16,20},{20,24},{24,28},{1,5},{5,9},{9,... | collective-permute-start | bytes 294920 | tf_op jit(solution)/shard_map/ppermute | solution.py:20
  147.9 1.7 collective-permute-start.14
  151.0 3.5 %collective-permute-done.14 = f32[2,96,256]{2,1,0:T(8,128)S(1)} collective-permute-done((f32[2,96,256]{2,1,0:T(8,128)S(1)}, f32[2,96,256]{2,1,0:T(8,128)S(1)}, u32[]{:S(2)}, u32[]{:S(2)}) %collective-permute-start.14) | collective-permute-done | bytes 196640 | tf_op jit(solution)/shard_map/ppermute | solution.py:24
  154.5 4.6 %collective-permute-done.15 = f32[2,96,256]{2,1,0:T(8,128)S(1)} collective-permute-done((f32[2,96,256]{2,1,0:T(8,128)S(1)}, f32[2,96,256]{2,1,0:T(8,128)S(1)}, u32[]{:S(2)}, u32[]{:S(2)}) %collective-permute-start.15) | collective-permute-done | bytes 196640 | tf_op jit(solution)/shard_map/ppermute | solution.py:25
  162.6 12.2 %all_to_all.53 = f32[32,1,1248]{2,1,0:T(1,128)S(1)} all-to-all(f32[32,1,1248]{2,1,0:T(1,128)S(1)} %broadcast_in_dim.35), channel_id=1, replica_groups=mesh['sub'=8,'grp'=4] {'grp','sub'}, dimensions={0} | all-to-all | bytes 319488 | tf_op jit(solution)/shard_map/all_to_all | solution.py:123
  178.3 2.2 %fusion.14 = f32[2,96,1024]{2,1,0:T(8,128)S(1)} fusion(f32[2,96,1024]{2,1,0:T(8,128)} %copy-done.13, f32[2,96,1024]{2,1,0:T(8,128)S(1)} %bitcast.209, f32[2,6,96]{2,1,0:T(8,128)S(1)} %reshape.261, f32[2,96,1024]{2,1,0:T(8,128)S(1)} %copy-done.1, f32[96]{0:T(128)S(1)} %div.26, f32[2,6,1024]{2,0,1:T(2,128)S(1)} %bitcast.208), kind=kOutput, calls=%fused_computation.26 | convolution fusion | flops 14942208 | bytes 3199872 | tf_op jit(solution)/shard_map/skm,skn->snm/dot_general | solution.py:134
  181.4 2.3 %collective-permute-start.16 = (f32[1,96,256]{2,1,0:T(8,128)S(1)}, f32[1,96,256]{2,1,0:T(8,128)S(1)}, u32[]{:S(2)}, u32[]{:S(2)}) collective-permute-start(f32[1,96,256]{2,1,0:T(8,128)S(1)} %get-tuple-element.10), channel_id=1, source_target_pairs={{0,4},{4,8},{8,12},{12,16},{16,20},{20,24},{24,28},{1,5},{5,9},{9,... | collective-permute-start | bytes 294920 | tf_op jit(solution)/shard_map/ppermute | solution.py:20
  185.0 1.7 collective-permute-start.18
  188.0 3.5 %collective-permute-done.18 = f32[2,96,256]{2,1,0:T(8,128)S(1)} collective-permute-done((f32[2,96,256]{2,1,0:T(8,128)S(1)}, f32[2,96,256]{2,1,0:T(8,128)S(1)}, u32[]{:S(2)}, u32[]{:S(2)}) %collective-permute-start.18) | collective-permute-done | bytes 196640 | tf_op jit(solution)/shard_map/ppermute | solution.py:24
  191.6 4.6 %collective-permute-done.19 = f32[2,96,256]{2,1,0:T(8,128)S(1)} collective-permute-done((f32[2,96,256]{2,1,0:T(8,128)S(1)}, f32[2,96,256]{2,1,0:T(8,128)S(1)}, u32[]{:S(2)}, u32[]{:S(2)}) %collective-permute-start.19) | collective-permute-done | bytes 196640 | tf_op jit(solution)/shard_map/ppermute | solution.py:25
  198.9 10.8 %all_to_all.54 = f32[32,1,96]{2,1,0:T(1,128)S(1)} all-to-all(f32[32,1,96]{2,1,0:T(1,128)S(1)} %broadcast_in_dim.36), channel_id=1, replica_groups=mesh['sub'=8,'grp'=4] {'grp','sub'}, dimensions={0} | all-to-all | bytes 24576 | tf_op jit(solution)/shard_map/all_to_all | solution.py:123
  209.7 3.2 %subtract_bitcast_fusion = (f32[1,2,96,1024]{3,2,1,0:T(8,128)}, f32[1,2,96,1024]{3,2,1,0:T(8,128)}) fusion(f32[2,96,1024]{2,1,0:T(8,128)} %get-tuple-element.3, f32[96]{0:T(128)S(1)} %div.27, f32[2,96,1024]{2,1,0:T(8,128)S(1)} %fusion.13, f32[2,96,1024]{2,1,0:T(8,128)S(1)} %copy-done.9, f32[96]{0:T(128)S(1)} %div.25, f32[2,96,1024]{2,1,0:T(8,128)} %copy-done.10, ...), kind=kLoop, calls=%fused_computation.48 | loop fusion | flops 1376256 | bytes 5505792 | tf_op jit(solution)/shard_map/broadcast_in_dim | solution.py:172
  (217 shorter events, 68.9 us)
Async XLA Ops:
  0.6 3.4 %copy-start.23 = (f32[1,2,6,384]{3,1,2,0:T(2,128)S(1)}, f32[1,2,6,384]{3,1,2,0:T(2,128)}, u32[]{:S(2)}) copy-start(f32[1,2,6,384]{3,1,2,0:T(2,128)} %param.11) | copy-start | bytes 55300
  3.4 10.8 %copy-start.24 = (s32[1,2,1024]{2,1,0:T(2,128)S(1)}, s32[1,2,1024]{2,1,0:T(2,128)}, u32[]{:S(2)}) copy-start(s32[1,2,1024]{2,1,0:T(2,128)} %param.12) | copy-start | bytes 24580
  3.6 11.0 %copy-start.17 = (f32[1,2,6,1024]{3,1,2,0:T(2,128)S(1)}, f32[1,2,6,1024]{3,1,2,0:T(2,128)}, u32[]{:S(2)}) copy-start(f32[1,2,6,1024]{3,1,2,0:T(2,128)} %param.10) | copy-start | bytes 147460
  4.7 10.0 %collective-permute-start = (f32[1,28672]{1,0:T(1,128)S(1)}, f32[1,28672]{1,0:T(1,128)S(1)}, u32[]{:S(2)}, u32[]{:S(2)}) collective-permute-start(f32[1,28672]{1,0:T(1,128)S(1)} %get-tuple-element.38), channel_id=1, source_target_pairs={{0,4},{4,8},{8,12},{12,16},{16,20},{20,24},{24,28},{1,5},{5,9},{9,... | collective-permute-start | bytes 344072 | tf_op jit(solution)/shard_map/ppermute | solution.py:20
  7.3 7.7 %collective-permute-start.1 = (f32[1,28672]{1,0:T(1,128)S(1)}, f32[1,28672]{1,0:T(1,128)S(1)}, u32[]{:S(2)}, u32[]{:S(2)}) collective-permute-start(f32[1,28672]{1,0:T(1,128)S(1)} %get-tuple-element.41), channel_id=1, source_target_pairs={{4,0},{8,4},{12,8},{16,12},{20,16},{24,20},{28,24},{5,1},{9,5},{13... | collective-permute-start | bytes 344072 | tf_op jit(solution)/shard_map/ppermute | solution.py:21
  8.6 8.8 %collective-permute-start.2 = (f32[2,28672]{1,0:T(2,128)S(1)}, f32[2,28672]{1,0:T(2,128)S(1)}, u32[]{:S(2)}, u32[]{:S(2)}) collective-permute-start(f32[2,28672]{1,0:T(2,128)S(1)} %get-tuple-element.48), channel_id=1, source_target_pairs={{0,1},{1,2},{2,3},{4,5},{5,6},{6,7},{8,9},{9,10},{10,11},{12,13},{... | collective-permute-start | bytes 688136 | tf_op jit(solution)/shard_map/ppermute | solution.py:24
  12.9 9.2 %collective-permute-start.3 = (f32[2,28672]{1,0:T(2,128)S(1)}, f32[2,28672]{1,0:T(2,128)S(1)}, u32[]{:S(2)}, u32[]{:S(2)}) collective-permute-start(f32[2,28672]{1,0:T(2,128)S(1)} %get-tuple-element.49), channel_id=1, source_target_pairs={{1,0},{2,1},{3,2},{5,4},{6,5},{7,6},{9,8},{10,9},{11,10},{13,12},{... | collective-permute-start | bytes 688136 | tf_op jit(solution)/shard_map/ppermute | solution.py:25
  15.3 7.9 %copy-start.25 = (s32[4]{0:T(128)S(1)}, s32[4]{0:T(128)}, u32[]{:S(2)}) copy-start(s32[4]{0:T(128)} %constant.38) | copy-start | bytes 52
  17.5 5.8 %copy-start.15 = (f32[2,1,28672]{2,1,0:T(1,128)}, f32[2,1,28672]{2,1,0:T(1,128)S(1)}, u32[]{:S(2)}) copy-start(f32[2,1,28672]{2,1,0:T(1,128)S(1)} %stack.91) | copy-start | bytes 688132
  29.9 14.8 %all-to-all-start = ((f32[32,1,1153]{2,1,0:T(1,128)}), f32[32,1,1153]{2,1,0:T(1,128)S(1)}, u32[]{:S(2)}, u32[]{:S(2)}) async-start(f32[32,1,1153]{2,1,0:T(1,128)} %broadcast_in_dim.31), calls=%async_computation | async-start | bytes 327680 | tf_op jit(solution)/shard_map/all_to_all | solution.py:123
  66.3 6.6 %collective-permute-start.4 = (f32[1,96,256]{2,1,0:T(8,128)S(1)}, f32[1,96,256]{2,1,0:T(8,128)S(1)}, u32[]{:S(2)}, u32[]{:S(2)}) collective-permute-start(f32[1,96,256]{2,1,0:T(8,128)S(1)} %get-tuple-element.28), channel_id=1, source_target_pairs={{0,4},{4,8},{8,12},{12,16},{16,20},{20,24},{24,28},{1,5},{5,9},{9,... | collective-permute-start | bytes 294920 | tf_op jit(solution)/shard_map/ppermute | solution.py:20
  68.6 4.3 %collective-permute-start.5 = (f32[1,96,256]{2,1,0:T(8,128)S(1)}, f32[1,96,256]{2,1,0:T(8,128)S(1)}, u32[]{:S(2)}, u32[]{:S(2)}) collective-permute-start(f32[1,96,256]{2,1,0:T(8,128)S(1)} %get-tuple-element.29), channel_id=1, source_target_pairs={{4,0},{8,4},{12,8},{16,12},{20,16},{24,20},{28,24},{5,1},{9,5},{13... | collective-permute-start | bytes 294920 | tf_op jit(solution)/shard_map/ppermute | solution.py:21
  69.9 6.6 %collective-permute-start.6 = (f32[2,96,256]{2,1,0:T(8,128)S(1)}, f32[2,96,256]{2,1,0:T(8,128)S(1)}, u32[]{:S(2)}, u32[]{:S(2)}) collective-permute-start(f32[2,96,256]{2,1,0:T(8,128)S(1)} %get-tuple-element.32), channel_id=1, source_target_pairs={{0,1},{1,2},{2,3},{4,5},{5,6},{6,7},{8,9},{9,10},{10,11},{12,13},{... | collective-permute-start | bytes 589832 | tf_op jit(solution)/shard_map/ppermute | solution.py:24
  71.6 9.5 %collective-permute-start.7 = (f32[2,96,256]{2,1,0:T(8,128)S(1)}, f32[2,96,256]{2,1,0:T(8,128)S(1)}, u32[]{:S(2)}, u32[]{:S(2)}) collective-permute-start(f32[2,96,256]{2,1,0:T(8,128)S(1)} %get-tuple-element.33), channel_id=1, source_target_pairs={{1,0},{2,1},{3,2},{5,4},{6,5},{7,6},{9,8},{10,9},{11,10},{13,12},{... | collective-permute-start | bytes 589832 | tf_op jit(solution)/shard_map/ppermute | solution.py:25
  103.1 17.2 %copy-start = (f32[2,96,1024]{2,1,0:T(8,128)}, f32[2,96,1024]{2,1,0:T(8,128)S(1)}, u32[]{:S(2)}) copy-start(f32[2,96,1024]{2,1,0:T(8,128)S(1)} %fusion.11) | copy-start | bytes 2359300
  103.9 6.6 %collective-permute-start.8 = (f32[1,96,256]{2,1,0:T(8,128)S(1)}, f32[1,96,256]{2,1,0:T(8,128)S(1)}, u32[]{:S(2)}, u32[]{:S(2)}) collective-permute-start(f32[1,96,256]{2,1,0:T(8,128)S(1)} %get-tuple-element.22), channel_id=1, source_target_pairs={{0,4},{4,8},{8,12},{12,16},{16,20},{20,24},{24,28},{1,5},{5,9},{9,... | collective-permute-start | bytes 294920 | tf_op jit(solution)/shard_map/ppermute | solution.py:20
  106.3 4.3 %collective-permute-start.9 = (f32[1,96,256]{2,1,0:T(8,128)S(1)}, f32[1,96,256]{2,1,0:T(8,128)S(1)}, u32[]{:S(2)}, u32[]{:S(2)}) collective-permute-start(f32[1,96,256]{2,1,0:T(8,128)S(1)} %get-tuple-element.23), channel_id=1, source_target_pairs={{4,0},{8,4},{12,8},{16,12},{20,16},{24,20},{28,24},{5,1},{9,5},{13... | collective-permute-start | bytes 294920 | tf_op jit(solution)/shard_map/ppermute | solution.py:21
  107.6 6.6 %collective-permute-start.10 = (f32[2,96,256]{2,1,0:T(8,128)S(1)}, f32[2,96,256]{2,1,0:T(8,128)S(1)}, u32[]{:S(2)}, u32[]{:S(2)}) collective-permute-start(f32[2,96,256]{2,1,0:T(8,128)S(1)} %get-tuple-element.26), channel_id=1, source_target_pairs={{0,1},{1,2},{2,3},{4,5},{5,6},{6,7},{8,9},{9,10},{10,11},{12,13},{... | collective-permute-start | bytes 589832 | tf_op jit(solution)/shard_map/ppermute | solution.py:24
  109.2 9.5 %collective-permute-start.11 = (f32[2,96,256]{2,1,0:T(8,128)S(1)}, f32[2,96,256]{2,1,0:T(8,128)S(1)}, u32[]{:S(2)}, u32[]{:S(2)}) collective-permute-start(f32[2,96,256]{2,1,0:T(8,128)S(1)} %get-tuple-element.27), channel_id=1, source_target_pairs={{1,0},{2,1},{3,2},{5,4},{6,5},{7,6},{9,8},{10,9},{11,10},{13,12},{... | collective-permute-start | bytes 589832 | tf_op jit(solution)/shard_map/ppermute | solution.py:25
  120.2 16.9 %copy-start.20 = (f32[32,1,1153]{2,0,1:T(8,128)S(1)}, f32[32,1,1153]{2,0,1:T(8,128)}, u32[]{:S(2)}) copy-start(f32[32,1,1153]{2,0,1:T(8,128)} %copy-done.19) | copy-start | bytes 442756
  122.9 12.5 %all-to-all-start.3 = ((f32[32,1,1248]{2,1,0:T(1,128)}), f32[32,1,1248]{2,1,0:T(1,128)}, u32[]{:S(2)}, u32[]{:S(2)}) async-start(f32[32,1,1248]{2,1,0:T(1,128)} %broadcast_in_dim.34), calls=%async_computation.3 | async-start | bytes 327680 | tf_op jit(solution)/shard_map/all_to_all | solution.py:123
  144.3 6.6 %collective-permute-start.12 = (f32[1,96,256]{2,1,0:T(8,128)S(1)}, f32[1,96,256]{2,1,0:T(8,128)S(1)}, u32[]{:S(2)}, u32[]{:S(2)}) collective-permute-start(f32[1,96,256]{2,1,0:T(8,128)S(1)} %get-tuple-element.16), channel_id=1, source_target_pairs={{0,4},{4,8},{8,12},{12,16},{16,20},{20,24},{24,28},{1,5},{5,9},{9,... | collective-permute-start | bytes 294920 | tf_op jit(solution)/shard_map/ppermute | solution.py:20
  146.6 4.3 %collective-permute-start.13 = (f32[1,96,256]{2,1,0:T(8,128)S(1)}, f32[1,96,256]{2,1,0:T(8,128)S(1)}, u32[]{:S(2)}, u32[]{:S(2)}) collective-permute-start(f32[1,96,256]{2,1,0:T(8,128)S(1)} %get-tuple-element.17), channel_id=1, source_target_pairs={{4,0},{8,4},{12,8},{16,12},{20,16},{24,20},{28,24},{5,1},{9,5},{13... | collective-permute-start | bytes 294920 | tf_op jit(solution)/shard_map/ppermute | solution.py:21
  147.9 6.6 %collective-permute-start.14 = (f32[2,96,256]{2,1,0:T(8,128)S(1)}, f32[2,96,256]{2,1,0:T(8,128)S(1)}, u32[]{:S(2)}, u32[]{:S(2)}) collective-permute-start(f32[2,96,256]{2,1,0:T(8,128)S(1)} %get-tuple-element.20), channel_id=1, source_target_pairs={{0,1},{1,2},{2,3},{4,5},{5,6},{6,7},{8,9},{9,10},{10,11},{12,13},{... | collective-permute-start | bytes 589832 | tf_op jit(solution)/shard_map/ppermute | solution.py:24
  149.6 9.5 %collective-permute-start.15 = (f32[2,96,256]{2,1,0:T(8,128)S(1)}, f32[2,96,256]{2,1,0:T(8,128)S(1)}, u32[]{:S(2)}, u32[]{:S(2)}) collective-permute-start(f32[2,96,256]{2,1,0:T(8,128)S(1)} %get-tuple-element.21), channel_id=1, source_target_pairs={{1,0},{2,1},{3,2},{5,4},{6,5},{7,6},{9,8},{10,9},{11,10},{13,12},{... | collective-permute-start | bytes 589832 | tf_op jit(solution)/shard_map/ppermute | solution.py:25
  180.5 17.2 %copy-start.10 = (f32[2,96,1024]{2,1,0:T(8,128)}, f32[2,96,1024]{2,1,0:T(8,128)S(1)}, u32[]{:S(2)}) copy-start(f32[2,96,1024]{2,1,0:T(8,128)S(1)} %fusion.14) | copy-start | bytes 2359300
  181.4 6.6 %collective-permute-start.16 = (f32[1,96,256]{2,1,0:T(8,128)S(1)}, f32[1,96,256]{2,1,0:T(8,128)S(1)}, u32[]{:S(2)}, u32[]{:S(2)}) collective-permute-start(f32[1,96,256]{2,1,0:T(8,128)S(1)} %get-tuple-element.10), channel_id=1, source_target_pairs={{0,4},{4,8},{8,12},{12,16},{16,20},{20,24},{24,28},{1,5},{5,9},{9,... | collective-permute-start | bytes 294920 | tf_op jit(solution)/shard_map/ppermute | solution.py:20
  183.7 4.3 %collective-permute-start.17 = (f32[1,96,256]{2,1,0:T(8,128)S(1)}, f32[1,96,256]{2,1,0:T(8,128)S(1)}, u32[]{:S(2)}, u32[]{:S(2)}) collective-permute-start(f32[1,96,256]{2,1,0:T(8,128)S(1)} %get-tuple-element.11), channel_id=1, source_target_pairs={{4,0},{8,4},{12,8},{16,12},{20,16},{24,20},{28,24},{5,1},{9,5},{13... | collective-permute-start | bytes 294920 | tf_op jit(solution)/shard_map/ppermute | solution.py:21
  185.0 6.6 %collective-permute-start.18 = (f32[2,96,256]{2,1,0:T(8,128)S(1)}, f32[2,96,256]{2,1,0:T(8,128)S(1)}, u32[]{:S(2)}, u32[]{:S(2)}) collective-permute-start(f32[2,96,256]{2,1,0:T(8,128)S(1)} %get-tuple-element.14), channel_id=1, source_target_pairs={{0,1},{1,2},{2,3},{4,5},{5,6},{6,7},{8,9},{9,10},{10,11},{12,13},{... | collective-permute-start | bytes 589832 | tf_op jit(solution)/shard_map/ppermute | solution.py:24
  186.7 9.5 %collective-permute-start.19 = (f32[2,96,256]{2,1,0:T(8,128)S(1)}, f32[2,96,256]{2,1,0:T(8,128)S(1)}, u32[]{:S(2)}, u32[]{:S(2)}) collective-permute-start(f32[2,96,256]{2,1,0:T(8,128)S(1)} %get-tuple-element.15), channel_id=1, source_target_pairs={{1,0},{2,1},{3,2},{5,4},{6,5},{7,6},{9,8},{10,9},{11,10},{13,12},{... | collective-permute-start | bytes 589832 | tf_op jit(solution)/shard_map/ppermute | solution.py:25
  197.6 12.2 %copy-start.2 = (f32[2,96,1024]{2,1,0:T(8,128)S(1)}, f32[2,96,1024]{2,1,0:T(8,128)}, u32[]{:S(2)}) copy-start(f32[2,96,1024]{2,1,0:T(8,128)} %copy-done) | copy-start | bytes 2359300
  197.6 12.2 %copy-start.9 = (f32[2,96,1024]{2,1,0:T(8,128)S(1)}, f32[2,96,1024]{2,1,0:T(8,128)}, u32[]{:S(2)}) copy-start(f32[2,96,1024]{2,1,0:T(8,128)} %copy-done.7) | copy-start | bytes 2359300
  (16 other events, 22.6 us)

commit v4 on v3

--- a/solution.py
+++ b/solution.py
@@ -147,28 +147,27 @@
     multipliers = jnp.zeros_like(dual)
     direction = jnp.zeros_like(dual)
     rho_prev = jnp.ones((columns,), jnp.float32)
-    for step_index in range(ITERS):
+
+    def iteration(_, state):
+        residual, flat_residual, multipliers, direction, rho_prev = state
         projected = project_with(residual, flat_residual)
         precond = jump(apply_blocks(projected, schur_blocks))
         flat_precond, rho_now = gathered(
             coefficients(precond), jnp.sum(projected * precond, axis=(0, 2))
         )
         search = project_with(precond, flat_precond)
-        if step_index > 0:
-            search = search + (rho_now / rho_prev)[None, :, None] * direction
-        direction = search
+        direction = search + (rho_now / rho_prev)[None, :, None] * direction
         image = jump(apply_blocks(direction, stiffness))
         partial_dot = jnp.sum(direction * image, axis=(0, 2))
-        if step_index + 1 < ITERS:
-            flat_image, curvature = gathered(coefficients(image), partial_dot)
-        else:
-            _, curvature = gathered(jnp.zeros((0,), jnp.float32), partial_dot)
+        flat_image, curvature = gathered(coefficients(image), partial_dot)
         step_len = rho_now / curvature
         multipliers = multipliers + step_len[None, :, None] * direction
         residual = residual - step_len[None, :, None] * image
-        if step_index + 1 < ITERS:
-            flat_residual = flat_residual - step_len[None, :] * flat_image
-        rho_prev = rho_now
+        flat_residual = flat_residual - step_len[None, :] * flat_image
+        return residual, flat_residual, multipliers, direction, rho_now
+
+    state = (residual, flat_residual, multipliers, direction, rho_prev)
+    residual, _, multipliers, _, _ = lax.fori_loop(0, ITERS, iteration, state)
     return (multipliers[None], residual[None])
 
 

time: 214 us -> 241 us (1.13)
  blocking collectives: 46 us -> 0 us
  starting transfers between devices: 45.8 us -> 72.8 us
  waiting for transfers between devices: 53.2 us -> 75.1 us
  matrix products: 31.5 us -> 47.3 us
  local copies, waits for them, and re-layouts: 23.5 us -> 30.6 us
    all_to_all x4 -> x0, blocking collectives: 46 us -> none  [gathered(): everything = lax.all_to_all(copies, ('grp', 'sub'), 0, 0, tiled=True)]
    all_to_all x2 -> x6, waiting for transfers between devices: 14.2 us -> 48.3 us  [gathered(): everything = lax.all_to_all(copies, ('grp', 'sub'), 0, 0, tiled=True)]
    all_to_all x2 -> x6, starting transfers between devices: 10.4 us -> 25.8 us  [gathered(): everything = lax.all_to_all(copies, ('grp', 'sub'), 0, 0, tiled=True)]
    ppermute x5, starting transfers between devices: 11 us -> 22.6 us  [neighbors(): from_below = lax.ppermute(d3, 'grp', up_grp)]
    dot_general x4, matrix products: 3.19 us -> 12 us  [apply_blocks(): jnp.einsum('snm,smk->snk', values.astype(jnp.bfloat16), matrices, preferr...]
    ppermute x5, waiting for transfers between devices: 16 us -> 7.9 us  [neighbors(): from_below = lax.ppermute(d3, 'grp', up_grp)]
    add x0 -> x2, other arithmetic: none -> 6.23 us  [iteration(): multipliers = multipliers + step_len[None, :, None] * direction]
    unnamed x65 -> x36, local copies, waits for them, and re-layouts: 10.4 us -> 5.72 us
  transfers between devices with their start and end apart: 22 -> 26, of which waited for: 12 -> 16; matrix products, arithmetic and copies ran while one was open for 2% -> 2% of each run, Pallas kernels for 0% -> 0%
where the time goes in v4:
time: 241 us; the launch traced here: 239 us
  waiting for transfers between devices  75.1 us (31%)
  starting transfers between devices  72.8 us (30%)
  matrix products  47.3 us (20%)
  local copies, waits for them, and re-layouts  30.6 us (13%)
  other arithmetic  11.1 us (5%)
    all_to_all x6, waiting for transfers between devices, gathered(): everything = lax.all_to_all(copies, ('grp', 'sub'), 0, 0, tiled=True)  48.3 us
    all_to_all x6, starting transfers between devices, gathered(): everything = lax.all_to_all(copies, ('grp', 'sub'), 0, 0, tiled=True)  25.8 us
    ppermute x5, starting transfers between devices, neighbors(): from_below = lax.ppermute(d3, 'grp', up_grp)  22.6 us
    ppermute x5, waiting for transfers between devices, neighbors(): from_above = lax.ppermute(d2, 'grp', down_grp)  18.9 us
    dot_general x4, matrix products, apply_blocks(): jnp.einsum('snm,smk->snk', values.astype(jnp.bfloat16), matrices, preferr...  12 us
    ppermute x5, starting transfers between devices, neighbors(): left_dev = lax.ppermute(d1[-1:], 'sub', up_sub)  11.5 us
    dot_general x5, matrix products, lift(): own_part = jnp.einsum('skm,skn->snm', own_modes, shaped, precision=HIGHEST)  11.5 us
    dot_general x6, matrix products, to_mine(): return jnp.einsum('sfcq,sfqr->sfcr', raw, permutes, precision=HIGHEST)  8.07 us
  transfers between devices with their start and end apart: 26, of which 16 were waited for; matrix products, arithmetic and copies ran while one was open for 2% of the time, Pallas kernels for 0%

profile of v4, /device:TPU:0, one launch (start us, length us, event | category | flops | bytes accessed | tf_op | source)
XLA Modules:
  0.0 239.1 jit_solution(12083911643072161608)
XLA Ops:
  4.2 2.4 collective-permute-start.8
  8.0 4.3 %collective-permute-start.10 = (f32[2,28672]{1,0:T(2,128)S(1)}, f32[2,28672]{1,0:T(2,128)S(1)}, u32[]{:S(2)}, u32[]{:S(2)}) collective-permute-start(f32[2,28672]{1,0:T(2,128)S(1)} %get-tuple-element.182), channel_id=1, source_target_pairs={{0,1},{1,2},{2,3},{4,5},{5,6},{6,7},{8,9},{9,10},{10,11},{12,13},{... | collective-permute-start | bytes 688136 | tf_op jit(solution)/shard_map/ppermute | solution.py:24
  17.0 4.6 %collective-permute-done.11 = f32[2,28672]{1,0:T(2,128)S(1)} collective-permute-done((f32[2,28672]{1,0:T(2,128)S(1)}, f32[2,28672]{1,0:T(2,128)S(1)}, u32[]{:S(2)}, u32[]{:S(2)}) %collective-permute-start.11) | collective-permute-done | bytes 229408 | tf_op jit(solution)/shard_map/ppermute | solution.py:25
  30.0 6.3 %all-to-all-start.2 = ((f32[32,1,1153]{2,1,0:T(1,128)}), f32[32,1,1153]{2,1,0:T(1,128)}, u32[]{:S(2)}, u32[]{:S(2)}) async-start(f32[32,1,1153]{2,1,0:T(1,128)} %broadcast_in_dim.29), calls=%async_computation.2 | async-start | bytes 327680 | tf_op jit(solution)/shard_map/all_to_all | solution.py:123
  39.2 5.7 %all-to-all-done.2 = f32[32,1,1153]{2,1,0:T(1,128)} async-done(((f32[32,1,1153]{2,1,0:T(1,128)}), f32[32,1,1153]{2,1,0:T(1,128)}, u32[]{:S(2)}, u32[]{:S(2)}) %all-to-all-start.2) | async-done | bytes 147616 | tf_op jit(solution)/shard_map/all_to_all | solution.py:123
  54.7 2.8 %all-to-all-start.3 = ((f32[32,1,1153]{2,1,0:T(1,128)}), f32[32,1,1153]{2,1,0:T(1,128)S(1)}, u32[]{:S(2)}, u32[]{:S(2)}) async-start(f32[32,1,1153]{2,1,0:T(1,128)} %broadcast_in_dim.30), calls=%async_computation.3 | async-start | bytes 327680 | tf_op jit(solution)/shard_map/all_to_all | solution.py:123
  57.5 8.3 %all-to-all-done.3 = f32[32,1,1153]{2,1,0:T(1,128)S(1)} async-done(((f32[32,1,1153]{2,1,0:T(1,128)}), f32[32,1,1153]{2,1,0:T(1,128)S(1)}, u32[]{:S(2)}, u32[]{:S(2)}) %all-to-all-start.3) | async-done | bytes 147616 | tf_op jit(solution)/shard_map/all_to_all | solution.py:123
  67.5 171.4 %while.19 = (s32[]{:T(128)}, f32[2,96,1024]{2,1,0:T(8,128)}, f32[384,96]{1,0:T(8,128)S(1)}, f32[2,96,1024]{2,1,0:T(8,128)}, f32[2,96,1024]{2,1,0:T(8,128)S(1)}, ...) while((s32[]{:T(128)}, f32[2,96,1024]{2,1,0:T(8,128)}, ...), condition=%wide.region_5.6_spmd.clone, body=%wide.region_0.5_spmd.clone.sunk | while | flops 2156675328 | bytes 66951832 | solution.py:170
  72.2 3.0 %fusion.131 = f32[2,96,1024]{2,1,0:T(8,128)S(1)} fusion(bf16[2,1024,1024]{2,1,0:T(8,128)(2,1)} %get-tuple-element.353, f32[2,96,1024]{2,1,0:T(8,128)S(1)} %fusion.130), kind=kOutput, calls=%fused_computation.24.clone.1 | convolution fusion | flops 402849792 | bytes 5767168 | tf_op jit(solution)/shard_map/while/body/eval_jaxpr/snm,smk->snk/dot_general | solution.py:35
  80.2 4.6 %collective-permute-start.1 = (f32[2,96,256]{2,1,0:T(8,128)S(1)}, f32[2,96,256]{2,1,0:T(8,128)S(1)}, u32[]{:S(2)}, u32[]{:S(2)}) collective-permute-start(f32[2,96,256]{2,1,0:T(8,128)S(1)} %get-tuple-element.294), channel_id=1, source_target_pairs={{0,1},{1,2},{2,3},{4,5},{5,6},{6,7},{8,9},{9,10},{10,11},{12,13},{... | collective-permute-start | bytes 589832 | tf_op jit(solution)/shard_map/while/body/eval_jaxpr/ppermute | solution.py:24
  84.8 3.6 %collective-permute-done = f32[2,96,256]{2,1,0:T(8,128)S(1)} collective-permute-done((f32[2,96,256]{2,1,0:T(8,128)S(1)}, f32[2,96,256]{2,1,0:T(8,128)S(1)}, u32[]{:S(2)}, u32[]{:S(2)}) %collective-permute-start) | collective-permute-done | bytes 196640 | tf_op jit(solution)/shard_map/while/body/eval_jaxpr/ppermute | solution.py:25
  94.1 4.2 %all-to-all-start = ((f32[32,1,1248]{2,1,0:T(1,128)}), f32[32,1,1248]{2,1,0:T(1,128)S(1)}, u32[]{:S(2)}, u32[]{:S(2)}) async-start(f32[32,1,1248]{2,1,0:T(1,128)} %broadcast_in_dim.73), calls=%async_computation | async-start | bytes 327680 | tf_op jit(solution)/shard_map/while/body/eval_jaxpr/all_to_all | solution.py:123
  98.3 8.6 %all-to-all-done = f32[32,1,1248]{2,1,0:T(1,128)S(1)} async-done(((f32[32,1,1248]{2,1,0:T(1,128)}), f32[32,1,1248]{2,1,0:T(1,128)S(1)}, u32[]{:S(2)}, u32[]{:S(2)}) %all-to-all-start) | async-done | bytes 159776 | tf_op jit(solution)/shard_map/while/body/eval_jaxpr/all_to_all | solution.py:123
  112.7 2.4 fusion.134
  115.1 3.0 %fusion.135 = f32[2,96,1024]{2,1,0:T(8,128)S(1)} fusion(bf16[2,1024,1024]{2,1,0:T(8,128)(2,1)} %get-tuple-element.356, f32[2,96,1024]{2,1,0:T(8,128)S(1)} %fusion.134), kind=kOutput, calls=%fused_computation.22.clone.1 | convolution fusion | flops 402849792 | bytes 5767168 | tf_op jit(solution)/shard_map/while/body/eval_jaxpr/snm,smk->snk/dot_general | solution.py:35
  123.1 4.6 %collective-permute-start.5 = (f32[2,96,256]{2,1,0:T(8,128)S(1)}, f32[2,96,256]{2,1,0:T(8,128)S(1)}, u32[]{:S(2)}, u32[]{:S(2)}) collective-permute-start(f32[2,96,256]{2,1,0:T(8,128)S(1)} %get-tuple-element.302), channel_id=1, source_target_pairs={{0,1},{1,2},{2,3},{4,5},{5,6},{6,7},{8,9},{9,10},{10,11},{12,13},{... | collective-permute-start | bytes 589832 | tf_op jit(solution)/shard_map/while/body/eval_jaxpr/ppermute | solution.py:24
  127.7 3.6 %collective-permute-done.4 = f32[2,96,256]{2,1,0:T(8,128)S(1)} collective-permute-done((f32[2,96,256]{2,1,0:T(8,128)S(1)}, f32[2,96,256]{2,1,0:T(8,128)S(1)}, u32[]{:S(2)}, u32[]{:S(2)}) %collective-permute-start.4) | collective-permute-done | bytes 196640 | tf_op jit(solution)/shard_map/while/body/eval_jaxpr/ppermute | solution.py:25
  137.1 4.2 %all-to-all-start.1 = ((f32[32,1,1248]{2,1,0:T(1,128)}), f32[32,1,1248]{2,1,0:T(1,128)S(1)}, u32[]{:S(2)}, u32[]{:S(2)}) async-start(f32[32,1,1248]{2,1,0:T(1,128)} %broadcast_in_dim.74), calls=%async_computation.1 | async-start | bytes 327680 | tf_op jit(solution)/shard_map/while/body/eval_jaxpr/all_to_all | solution.py:123
  141.3 8.6 %all-to-all-done.1 = f32[32,1,1248]{2,1,0:T(1,128)S(1)} async-done(((f32[32,1,1248]{2,1,0:T(1,128)}), f32[32,1,1248]{2,1,0:T(1,128)S(1)}, u32[]{:S(2)}, u32[]{:S(2)}) %all-to-all-start.1) | async-done | bytes 159776 | tf_op jit(solution)/shard_map/while/body/eval_jaxpr/all_to_all | solution.py:123
  150.1 3.0 %select_add_fusion.2 = (f32[2,96,1024]{2,1,0:T(8,128)}, f32[2,96,1024]{2,1,0:T(8,128)}) fusion(f32[2,96,1024]{2,1,0:T(8,128)} %get-tuple-element.330, f32[2,96,1024]{2,1,0:T(8,128)S(1)} %fusion.134, f32[96]{0:T(128)S(1)} %div.19, pred[]{:T(512)S(6)} %compare.3, f32[2,96,1024]{2,1,0:T(8,128)} %get-tuple-element.328, f32[2,96,1024]{2,1,0:T(8,128)} %copy-done), kind=kLoop, calls=%fused_computation.18.clone.1 | loop fusion | flops 983040 | bytes 4718977 | tf_op jit(solution)/shard_map/while/body/eval_jaxpr/add | solution.py:164
  157.8 3.0 %fusion.131 = f32[2,96,1024]{2,1,0:T(8,128)S(1)} fusion(bf16[2,1024,1024]{2,1,0:T(8,128)(2,1)} %get-tuple-element.353, f32[2,96,1024]{2,1,0:T(8,128)S(1)} %fusion.130), kind=kOutput, calls=%fused_computation.24.clone.1 | convolution fusion | flops 402849792 | bytes 5767168 | tf_op jit(solution)/shard_map/while/body/eval_jaxpr/snm,smk->snk/dot_general | solution.py:35
  165.8 4.6 %collective-permute-start.1 = (f32[2,96,256]{2,1,0:T(8,128)S(1)}, f32[2,96,256]{2,1,0:T(8,128)S(1)}, u32[]{:S(2)}, u32[]{:S(2)}) collective-permute-start(f32[2,96,256]{2,1,0:T(8,128)S(1)} %get-tuple-element.294), channel_id=1, source_target_pairs={{0,1},{1,2},{2,3},{4,5},{5,6},{6,7},{8,9},{9,10},{10,11},{12,13},{... | collective-permute-start | bytes 589832 | tf_op jit(solution)/shard_map/while/body/eval_jaxpr/ppermute | solution.py:24
  170.4 3.6 %collective-permute-done = f32[2,96,256]{2,1,0:T(8,128)S(1)} collective-permute-done((f32[2,96,256]{2,1,0:T(8,128)S(1)}, f32[2,96,256]{2,1,0:T(8,128)S(1)}, u32[]{:S(2)}, u32[]{:S(2)}) %collective-permute-start) | collective-permute-done | bytes 196640 | tf_op jit(solution)/shard_map/while/body/eval_jaxpr/ppermute | solution.py:25
  179.7 4.2 %all-to-all-start = ((f32[32,1,1248]{2,1,0:T(1,128)}), f32[32,1,1248]{2,1,0:T(1,128)S(1)}, u32[]{:S(2)}, u32[]{:S(2)}) async-start(f32[32,1,1248]{2,1,0:T(1,128)} %broadcast_in_dim.73), calls=%async_computation | async-start | bytes 327680 | tf_op jit(solution)/shard_map/while/body/eval_jaxpr/all_to_all | solution.py:123
  183.9 8.6 %all-to-all-done = f32[32,1,1248]{2,1,0:T(1,128)S(1)} async-done(((f32[32,1,1248]{2,1,0:T(1,128)}), f32[32,1,1248]{2,1,0:T(1,128)S(1)}, u32[]{:S(2)}, u32[]{:S(2)}) %all-to-all-start) | async-done | bytes 159776 | tf_op jit(solution)/shard_map/while/body/eval_jaxpr/all_to_all | solution.py:123
  198.3 2.4 fusion.134
  200.7 3.0 %fusion.135 = f32[2,96,1024]{2,1,0:T(8,128)S(1)} fusion(bf16[2,1024,1024]{2,1,0:T(8,128)(2,1)} %get-tuple-element.356, f32[2,96,1024]{2,1,0:T(8,128)S(1)} %fusion.134), kind=kOutput, calls=%fused_computation.22.clone.1 | convolution fusion | flops 402849792 | bytes 5767168 | tf_op jit(solution)/shard_map/while/body/eval_jaxpr/snm,smk->snk/dot_general | solution.py:35
  208.7 4.6 %collective-permute-start.5 = (f32[2,96,256]{2,1,0:T(8,128)S(1)}, f32[2,96,256]{2,1,0:T(8,128)S(1)}, u32[]{:S(2)}, u32[]{:S(2)}) collective-permute-start(f32[2,96,256]{2,1,0:T(8,128)S(1)} %get-tuple-element.302), channel_id=1, source_target_pairs={{0,1},{1,2},{2,3},{4,5},{5,6},{6,7},{8,9},{9,10},{10,11},{12,13},{... | collective-permute-start | bytes 589832 | tf_op jit(solution)/shard_map/while/body/eval_jaxpr/ppermute | solution.py:24
  213.3 3.6 %collective-permute-done.4 = f32[2,96,256]{2,1,0:T(8,128)S(1)} collective-permute-done((f32[2,96,256]{2,1,0:T(8,128)S(1)}, f32[2,96,256]{2,1,0:T(8,128)S(1)}, u32[]{:S(2)}, u32[]{:S(2)}) %collective-permute-start.4) | collective-permute-done | bytes 196640 | tf_op jit(solution)/shard_map/while/body/eval_jaxpr/ppermute | solution.py:25
  222.7 4.2 %all-to-all-start.1 = ((f32[32,1,1248]{2,1,0:T(1,128)}), f32[32,1,1248]{2,1,0:T(1,128)S(1)}, u32[]{:S(2)}, u32[]{:S(2)}) async-start(f32[32,1,1248]{2,1,0:T(1,128)} %broadcast_in_dim.74), calls=%async_computation.1 | async-start | bytes 327680 | tf_op jit(solution)/shard_map/while/body/eval_jaxpr/all_to_all | solution.py:123
  226.9 8.6 %all-to-all-done.1 = f32[32,1,1248]{2,1,0:T(1,128)S(1)} async-done(((f32[32,1,1248]{2,1,0:T(1,128)}), f32[32,1,1248]{2,1,0:T(1,128)S(1)}, u32[]{:S(2)}, u32[]{:S(2)}) %all-to-all-start.1) | async-done | bytes 159776 | tf_op jit(solution)/shard_map/while/body/eval_jaxpr/all_to_all | solution.py:123
  235.7 3.2 %select_add_fusion.2 = (f32[2,96,1024]{2,1,0:T(8,128)}, f32[2,96,1024]{2,1,0:T(8,128)}) fusion(f32[2,96,1024]{2,1,0:T(8,128)} %get-tuple-element.330, f32[2,96,1024]{2,1,0:T(8,128)S(1)} %fusion.134, f32[96]{0:T(128)S(1)} %div.19, pred[]{:T(512)S(6)} %compare.3, f32[2,96,1024]{2,1,0:T(8,128)} %get-tuple-element.328, f32[2,96,1024]{2,1,0:T(8,128)} %copy-done), kind=kLoop, calls=%fused_computation.18.clone.1 | loop fusion | flops 983040 | bytes 4718977 | tf_op jit(solution)/shard_map/while/body/eval_jaxpr/add | solution.py:164
  (244 shorter events, 96.1 us)
Async XLA Ops:
  4.2 10.0 %collective-permute-start.8 = (f32[1,28672]{1,0:T(1,128)S(1)}, f32[1,28672]{1,0:T(1,128)S(1)}, u32[]{:S(2)}, u32[]{:S(2)}) collective-permute-start(f32[1,28672]{1,0:T(1,128)S(1)} %get-tuple-element.172), channel_id=1, source_target_pairs={{0,4},{4,8},{8,12},{12,16},{16,20},{20,24},{24,28},{1,5},{5,9},{9,... | collective-permute-start | bytes 344072 | tf_op jit(solution)/shard_map/ppermute | solution.py:20
  6.7 7.6 %collective-permute-start.9 = (f32[1,28672]{1,0:T(1,128)S(1)}, f32[1,28672]{1,0:T(1,128)S(1)}, u32[]{:S(2)}, u32[]{:S(2)}) collective-permute-start(f32[1,28672]{1,0:T(1,128)S(1)} %get-tuple-element.175), channel_id=1, source_target_pairs={{4,0},{8,4},{12,8},{16,12},{20,16},{24,20},{28,24},{5,1},{9,5},{13... | collective-permute-start | bytes 344072 | tf_op jit(solution)/shard_map/ppermute | solution.py:21
  8.0 8.8 %collective-permute-start.10 = (f32[2,28672]{1,0:T(2,128)S(1)}, f32[2,28672]{1,0:T(2,128)S(1)}, u32[]{:S(2)}, u32[]{:S(2)}) collective-permute-start(f32[2,28672]{1,0:T(2,128)S(1)} %get-tuple-element.182), channel_id=1, source_target_pairs={{0,1},{1,2},{2,3},{4,5},{5,6},{6,7},{8,9},{9,10},{10,11},{12,13},{... | collective-permute-start | bytes 688136 | tf_op jit(solution)/shard_map/ppermute | solution.py:24
  12.4 9.2 %collective-permute-start.11 = (f32[2,28672]{1,0:T(2,128)S(1)}, f32[2,28672]{1,0:T(2,128)S(1)}, u32[]{:S(2)}, u32[]{:S(2)}) collective-permute-start(f32[2,28672]{1,0:T(2,128)S(1)} %get-tuple-element.183), channel_id=1, source_target_pairs={{1,0},{2,1},{3,2},{5,4},{6,5},{7,6},{9,8},{10,9},{11,10},{13,12},{... | collective-permute-start | bytes 688136 | tf_op jit(solution)/shard_map/ppermute | solution.py:25
  14.8 8.5 %copy-start.18 = (s32[4]{0:T(128)S(1)}, s32[4]{0:T(128)}, u32[]{:S(2)}) copy-start(s32[4]{0:T(128)} %constant.45) | copy-start | bytes 52
  17.0 6.4 %copy-start.10 = (f32[2,1,28672]{2,1,0:T(1,128)}, f32[2,1,28672]{2,1,0:T(1,128)S(1)}, u32[]{:S(2)}) copy-start(f32[2,1,28672]{2,1,0:T(1,128)S(1)} %stack.58) | copy-start | bytes 688132
  30.0 14.9 %all-to-all-start.2 = ((f32[32,1,1153]{2,1,0:T(1,128)}), f32[32,1,1153]{2,1,0:T(1,128)}, u32[]{:S(2)}, u32[]{:S(2)}) async-start(f32[32,1,1153]{2,1,0:T(1,128)} %broadcast_in_dim.29), calls=%async_computation.2 | async-start | bytes 327680 | tf_op jit(solution)/shard_map/all_to_all | solution.py:123
  54.7 11.2 %all-to-all-start.3 = ((f32[32,1,1153]{2,1,0:T(1,128)}), f32[32,1,1153]{2,1,0:T(1,128)S(1)}, u32[]{:S(2)}, u32[]{:S(2)}) async-start(f32[32,1,1153]{2,1,0:T(1,128)} %broadcast_in_dim.30), calls=%async_computation.3 | async-start | bytes 327680 | tf_op jit(solution)/shard_map/all_to_all | solution.py:123
  67.6 4.6 %copy-start.3 = (f32[2,4,6,256]{3,2,1,0:T(8,128)}, f32[2,4,6,256]{3,2,1,0:T(8,128)S(1)}, u32[]{:S(2)}) copy-start(f32[2,4,6,256]{3,2,1,0:T(8,128)S(1)} %get-tuple-element.352) | copy-start | bytes 147460 | tf_op jit(solution)/shard_map/while
  67.6 4.6 %copy-start.12 = (f32[2,4,6,384]{3,2,1,0:T(8,128)}, f32[2,4,6,384]{3,2,1,0:T(8,128)S(1)}, u32[]{:S(2)}) copy-start(f32[2,4,6,384]{3,2,1,0:T(8,128)S(1)} %get-tuple-element.351) | copy-start | bytes 221188 | tf_op jit(solution)/shard_map/while
  67.6 24.0 %copy-start.5 = (f32[2,6,1024]{2,1,0:T(8,128)}, f32[2,6,1024]{2,1,0:T(8,128)S(1)}, u32[]{:S(2)}) copy-start(f32[2,6,1024]{2,1,0:T(8,128)S(1)} %get-tuple-element.355) | copy-start | bytes 147460 | tf_op jit(solution)/shard_map/while
  75.3 9.5 %collective-permute-start.3 = (f32[1,96,256]{2,1,0:T(8,128)S(1)}, f32[1,96,256]{2,1,0:T(8,128)S(1)}, u32[]{:S(2)}, u32[]{:S(2)}) collective-permute-start(f32[1,96,256]{2,1,0:T(8,128)S(1)} %get-tuple-element.298), channel_id=1, source_target_pairs={{0,4},{4,8},{8,12},{12,16},{16,20},{20,24},{24,28},{1,5},{5,9},{9,... | collective-permute-start | bytes 294920 | tf_op jit(solution)/shard_map/while/body/eval_jaxpr/ppermute | solution.py:20
  77.6 7.2 %collective-permute-start.2 = (f32[1,96,256]{2,1,0:T(8,128)S(1)}, f32[1,96,256]{2,1,0:T(8,128)S(1)}, u32[]{:S(2)}, u32[]{:S(2)}) collective-permute-start(f32[1,96,256]{2,1,0:T(8,128)S(1)} %get-tuple-element.295), channel_id=1, source_target_pairs={{4,0},{8,4},{12,8},{16,12},{20,16},{24,20},{28,24},{5,1},{9,5},{13... | collective-permute-start | bytes 294920 | tf_op jit(solution)/shard_map/while/body/eval_jaxpr/ppermute | solution.py:21
  78.9 9.5 %collective-permute-start = (f32[2,96,256]{2,1,0:T(8,128)S(1)}, f32[2,96,256]{2,1,0:T(8,128)S(1)}, u32[]{:S(2)}, u32[]{:S(2)}) collective-permute-start(f32[2,96,256]{2,1,0:T(8,128)S(1)} %get-tuple-element.293), channel_id=1, source_target_pairs={{1,0},{2,1},{3,2},{5,4},{6,5},{7,6},{9,8},{10,9},{11,10},{13,12},{... | collective-permute-start | bytes 589832 | tf_op jit(solution)/shard_map/while/body/eval_jaxpr/ppermute | solution.py:25
  80.2 9.7 %collective-permute-start.1 = (f32[2,96,256]{2,1,0:T(8,128)S(1)}, f32[2,96,256]{2,1,0:T(8,128)S(1)}, u32[]{:S(2)}, u32[]{:S(2)}) collective-permute-start(f32[2,96,256]{2,1,0:T(8,128)S(1)} %get-tuple-element.294), channel_id=1, source_target_pairs={{0,1},{1,2},{2,3},{4,5},{5,6},{6,7},{8,9},{9,10},{10,11},{12,13},{... | collective-permute-start | bytes 589832 | tf_op jit(solution)/shard_map/while/body/eval_jaxpr/ppermute | solution.py:24
  94.1 12.7 %all-to-all-start = ((f32[32,1,1248]{2,1,0:T(1,128)}), f32[32,1,1248]{2,1,0:T(1,128)S(1)}, u32[]{:S(2)}, u32[]{:S(2)}) async-start(f32[32,1,1248]{2,1,0:T(1,128)} %broadcast_in_dim.73), calls=%async_computation | async-start | bytes 327680 | tf_op jit(solution)/shard_map/while/body/eval_jaxpr/all_to_all | solution.py:123
  118.1 9.5 %collective-permute-start.7 = (f32[1,96,256]{2,1,0:T(8,128)S(1)}, f32[1,96,256]{2,1,0:T(8,128)S(1)}, u32[]{:S(2)}, u32[]{:S(2)}) collective-permute-start(f32[1,96,256]{2,1,0:T(8,128)S(1)} %get-tuple-element.306), channel_id=1, source_target_pairs={{0,4},{4,8},{8,12},{12,16},{16,20},{20,24},{24,28},{1,5},{5,9},{9,... | collective-permute-start | bytes 294920 | tf_op jit(solution)/shard_map/while/body/eval_jaxpr/ppermute | solution.py:20
  120.5 7.2 %collective-permute-start.6 = (f32[1,96,256]{2,1,0:T(8,128)S(1)}, f32[1,96,256]{2,1,0:T(8,128)S(1)}, u32[]{:S(2)}, u32[]{:S(2)}) collective-permute-start(f32[1,96,256]{2,1,0:T(8,128)S(1)} %get-tuple-element.303), channel_id=1, source_target_pairs={{4,0},{8,4},{12,8},{16,12},{20,16},{24,20},{28,24},{5,1},{9,5},{13... | collective-permute-start | bytes 294920 | tf_op jit(solution)/shard_map/while/body/eval_jaxpr/ppermute | solution.py:21
  121.8 9.5 %collective-permute-start.4 = (f32[2,96,256]{2,1,0:T(8,128)S(1)}, f32[2,96,256]{2,1,0:T(8,128)S(1)}, u32[]{:S(2)}, u32[]{:S(2)}) collective-permute-start(f32[2,96,256]{2,1,0:T(8,128)S(1)} %get-tuple-element.301), channel_id=1, source_target_pairs={{1,0},{2,1},{3,2},{5,4},{6,5},{7,6},{9,8},{10,9},{11,10},{13,12},{... | collective-permute-start | bytes 589832 | tf_op jit(solution)/shard_map/while/body/eval_jaxpr/ppermute | solution.py:25
  123.1 9.7 %collective-permute-start.5 = (f32[2,96,256]{2,1,0:T(8,128)S(1)}, f32[2,96,256]{2,1,0:T(8,128)S(1)}, u32[]{:S(2)}, u32[]{:S(2)}) collective-permute-start(f32[2,96,256]{2,1,0:T(8,128)S(1)} %get-tuple-element.302), channel_id=1, source_target_pairs={{0,1},{1,2},{2,3},{4,5},{5,6},{6,7},{8,9},{9,10},{10,11},{12,13},{... | collective-permute-start | bytes 589832 | tf_op jit(solution)/shard_map/while/body/eval_jaxpr/ppermute | solution.py:24
  137.1 12.7 %all-to-all-start.1 = ((f32[32,1,1248]{2,1,0:T(1,128)}), f32[32,1,1248]{2,1,0:T(1,128)S(1)}, u32[]{:S(2)}, u32[]{:S(2)}) async-start(f32[32,1,1248]{2,1,0:T(1,128)} %broadcast_in_dim.74), calls=%async_computation.1 | async-start | bytes 327680 | tf_op jit(solution)/shard_map/while/body/eval_jaxpr/all_to_all | solution.py:123
  153.2 24.0 %copy-start.5 = (f32[2,6,1024]{2,1,0:T(8,128)}, f32[2,6,1024]{2,1,0:T(8,128)S(1)}, u32[]{:S(2)}) copy-start(f32[2,6,1024]{2,1,0:T(8,128)S(1)} %get-tuple-element.355) | copy-start | bytes 147460 | tf_op jit(solution)/shard_map/while
  160.9 9.5 %collective-permute-start.3 = (f32[1,96,256]{2,1,0:T(8,128)S(1)}, f32[1,96,256]{2,1,0:T(8,128)S(1)}, u32[]{:S(2)}, u32[]{:S(2)}) collective-permute-start(f32[1,96,256]{2,1,0:T(8,128)S(1)} %get-tuple-element.298), channel_id=1, source_target_pairs={{0,4},{4,8},{8,12},{12,16},{16,20},{20,24},{24,28},{1,5},{5,9},{9,... | collective-permute-start | bytes 294920 | tf_op jit(solution)/shard_map/while/body/eval_jaxpr/ppermute | solution.py:20
  163.2 7.2 %collective-permute-start.2 = (f32[1,96,256]{2,1,0:T(8,128)S(1)}, f32[1,96,256]{2,1,0:T(8,128)S(1)}, u32[]{:S(2)}, u32[]{:S(2)}) collective-permute-start(f32[1,96,256]{2,1,0:T(8,128)S(1)} %get-tuple-element.295), channel_id=1, source_target_pairs={{4,0},{8,4},{12,8},{16,12},{20,16},{24,20},{28,24},{5,1},{9,5},{13... | collective-permute-start | bytes 294920 | tf_op jit(solution)/shard_map/while/body/eval_jaxpr/ppermute | solution.py:21
  164.5 9.5 %collective-permute-start = (f32[2,96,256]{2,1,0:T(8,128)S(1)}, f32[2,96,256]{2,1,0:T(8,128)S(1)}, u32[]{:S(2)}, u32[]{:S(2)}) collective-permute-start(f32[2,96,256]{2,1,0:T(8,128)S(1)} %get-tuple-element.293), channel_id=1, source_target_pairs={{1,0},{2,1},{3,2},{5,4},{6,5},{7,6},{9,8},{10,9},{11,10},{13,12},{... | collective-permute-start | bytes 589832 | tf_op jit(solution)/shard_map/while/body/eval_jaxpr/ppermute | solution.py:25
  165.8 9.7 %collective-permute-start.1 = (f32[2,96,256]{2,1,0:T(8,128)S(1)}, f32[2,96,256]{2,1,0:T(8,128)S(1)}, u32[]{:S(2)}, u32[]{:S(2)}) collective-permute-start(f32[2,96,256]{2,1,0:T(8,128)S(1)} %get-tuple-element.294), channel_id=1, source_target_pairs={{0,1},{1,2},{2,3},{4,5},{5,6},{6,7},{8,9},{9,10},{10,11},{12,13},{... | collective-permute-start | bytes 589832 | tf_op jit(solution)/shard_map/while/body/eval_jaxpr/ppermute | solution.py:24
  179.7 12.8 %all-to-all-start = ((f32[32,1,1248]{2,1,0:T(1,128)}), f32[32,1,1248]{2,1,0:T(1,128)S(1)}, u32[]{:S(2)}, u32[]{:S(2)}) async-start(f32[32,1,1248]{2,1,0:T(1,128)} %broadcast_in_dim.73), calls=%async_computation | async-start | bytes 327680 | tf_op jit(solution)/shard_map/while/body/eval_jaxpr/all_to_all | solution.py:123
  203.7 9.5 %collective-permute-start.7 = (f32[1,96,256]{2,1,0:T(8,128)S(1)}, f32[1,96,256]{2,1,0:T(8,128)S(1)}, u32[]{:S(2)}, u32[]{:S(2)}) collective-permute-start(f32[1,96,256]{2,1,0:T(8,128)S(1)} %get-tuple-element.306), channel_id=1, source_target_pairs={{0,4},{4,8},{8,12},{12,16},{16,20},{20,24},{24,28},{1,5},{5,9},{9,... | collective-permute-start | bytes 294920 | tf_op jit(solution)/shard_map/while/body/eval_jaxpr/ppermute | solution.py:20
  206.1 7.2 %collective-permute-start.6 = (f32[1,96,256]{2,1,0:T(8,128)S(1)}, f32[1,96,256]{2,1,0:T(8,128)S(1)}, u32[]{:S(2)}, u32[]{:S(2)}) collective-permute-start(f32[1,96,256]{2,1,0:T(8,128)S(1)} %get-tuple-element.303), channel_id=1, source_target_pairs={{4,0},{8,4},{12,8},{16,12},{20,16},{24,20},{28,24},{5,1},{9,5},{13... | collective-permute-start | bytes 294920 | tf_op jit(solution)/shard_map/while/body/eval_jaxpr/ppermute | solution.py:21
  207.4 9.5 %collective-permute-start.4 = (f32[2,96,256]{2,1,0:T(8,128)S(1)}, f32[2,96,256]{2,1,0:T(8,128)S(1)}, u32[]{:S(2)}, u32[]{:S(2)}) collective-permute-start(f32[2,96,256]{2,1,0:T(8,128)S(1)} %get-tuple-element.301), channel_id=1, source_target_pairs={{1,0},{2,1},{3,2},{5,4},{6,5},{7,6},{9,8},{10,9},{11,10},{13,12},{... | collective-permute-start | bytes 589832 | tf_op jit(solution)/shard_map/while/body/eval_jaxpr/ppermute | solution.py:25
  208.7 9.7 %collective-permute-start.5 = (f32[2,96,256]{2,1,0:T(8,128)S(1)}, f32[2,96,256]{2,1,0:T(8,128)S(1)}, u32[]{:S(2)}, u32[]{:S(2)}) collective-permute-start(f32[2,96,256]{2,1,0:T(8,128)S(1)} %get-tuple-element.302), channel_id=1, source_target_pairs={{0,1},{1,2},{2,3},{4,5},{5,6},{6,7},{8,9},{9,10},{10,11},{12,13},{... | collective-permute-start | bytes 589832 | tf_op jit(solution)/shard_map/while/body/eval_jaxpr/ppermute | solution.py:24
  222.7 12.7 %all-to-all-start.1 = ((f32[32,1,1248]{2,1,0:T(1,128)}), f32[32,1,1248]{2,1,0:T(1,128)S(1)}, u32[]{:S(2)}, u32[]{:S(2)}) async-start(f32[32,1,1248]{2,1,0:T(1,128)} %broadcast_in_dim.74), calls=%async_computation.1 | async-start | bytes 327680 | tf_op jit(solution)/shard_map/while/body/eval_jaxpr/all_to_all | solution.py:123
  (22 other events, 49.5 us)

commit v5 on v3

--- a/solution.py
+++ b/solution.py
@@ -4,6 +4,7 @@
 from jax.sharding import PartitionSpec as P
 
 MODES = 6
+ROWS = 8
 ITERS = 2
 
 
@@ -61,8 +62,19 @@
     )
     slot_weight = jnp.repeat(face_weight, quarter, axis=1)
     weighted_modes = own_modes * slot_weight[:, None, :]
+    padding = ROWS - MODES
+    weighted_padded = jnp.pad(weighted_modes, ((0, 0), (0, padding), (0, 0)))
     rows_here = coarse_op[0].reshape(subdomains * MODES, -1)
     coarse_total = rows_here.shape[1]
+    subdomain_count = coarse_total // MODES
+
+    def pad_columns(rows):
+        lead = rows.shape[:-1]
+        split = rows.reshape(lead + (subdomain_count, MODES))
+        widths = [(0, 0)] * len(lead) + [(0, 0), (0, padding)]
+        return jnp.pad(split, widths).reshape(lead + (subdomain_count * ROWS,))
+
+    rows_padded = pad_columns(rows_here)
 
     gap_faces = face_split(vectors)
     mode_faces = face_split(own_modes)
@@ -105,6 +117,8 @@
         return jnp.einsum("sfcq,sfqr->sfcr", raw, permutes, precision=HIGHEST)
 
     partner_modes = to_mine(partner_raw_modes)
+    partner_slot_modes = jnp.moveaxis(partner_modes, 1, 2).reshape(subdomains, MODES, width)
+    partner_rows_padded = pad_columns(partner_rows)
 
     def partner_values(raw, shape):
         return jnp.moveaxis(to_mine(raw), 1, 2).reshape(shape)
@@ -114,36 +128,40 @@
         return values - partner_values(raw, values.shape)
 
     def coefficients(values):
-        return jnp.einsum("skm,snm->skn", weighted_modes, values, precision=HIGHEST)
-
-    def gathered(coeffs, extra):
-        payload = jnp.concatenate([coeffs.reshape(-1), extra.reshape(-1)])
+        return jnp.einsum("skm,snm->skn", weighted_padded, values, precision=HIGHEST)
+
+    def gathered(coeffs, extra=None):
+        pieces = [] if coeffs is None else [coeffs.reshape(-1, columns)]
+        if extra is not None:
+            pieces.append(jnp.pad(extra[None], ((0, ROWS - 1), (0, 0))))
+        payload = jnp.concatenate(pieces, axis=0)
         devices = lax.axis_size("grp") * lax.axis_size("sub")
-        copies = jnp.broadcast_to(payload[None], (devices, payload.shape[0]))
+        copies = jnp.broadcast_to(payload[None], (devices,) + payload.shape)
         everything = lax.all_to_all(copies, ("grp", "sub"), 0, 0, tiled=True)
-        count = coeffs.size
-        extras = jnp.sum(everything[:, count:], axis=0)
-        if count == 0:
+        extras = None if extra is None else jnp.sum(everything[:, -ROWS], axis=0)
+        if coeffs is None:
             return None, extras
-        flat = everything[:, :count].reshape(-1, columns)
+        flat = everything[:, : subdomains * ROWS].reshape(-1, columns)
         return flat, extras
 
     def lift(flat):
-        amounts = jnp.dot(rows_here, flat, precision=HIGHEST, preferred_element_type=jnp.float32)
+        amounts = jnp.dot(rows_padded, flat, precision=HIGHEST, preferred_element_type=jnp.float32)
         shaped = amounts.reshape(subdomains, MODES, columns)
-        own_part = jnp.einsum("skm,skn->snm", own_modes, shaped, precision=HIGHEST)
-        far_amounts = jnp.einsum("sfkc,cn->sfkn", partner_rows, flat, precision=HIGHEST)
-        far_part = jnp.einsum("sfkm,sfkn->snfm", partner_modes, far_amounts, precision=HIGHEST)
-        return own_part - far_part.reshape(subdomains, columns, width)
+        far_amounts = jnp.einsum(
+            "sfkc,cn->skfn", partner_rows_padded, flat, precision=HIGHEST
+        )
+        far_spread = jnp.repeat(jnp.swapaxes(far_amounts, 2, 3), quarter, axis=3)
+        own_part = own_modes[:, :, None, :] * shaped[:, :, :, None]
+        far_part = partner_slot_modes[:, :, None, :] * far_spread
+        return jnp.sum(own_part - far_part, axis=1)
 
     def project_with(values, flat):
         return values - lift(flat)
 
-    nothing = jnp.zeros((1,), jnp.float32)
     dual = vectors - partner_values(partner_gaps, vectors.shape)
-    flat_dual, _ = gathered(coefficients(dual), nothing)
+    flat_dual, _ = gathered(coefficients(dual))
     residual = project_with(dual, flat_dual)
-    flat_residual, _ = gathered(coefficients(residual), nothing)
+    flat_residual, _ = gathered(coefficients(residual))
     multipliers = jnp.zeros_like(dual)
     direction = jnp.zeros_like(dual)
     rho_prev = jnp.ones((columns,), jnp.float32)
@@ -162,7 +180,7 @@
         if step_index + 1 < ITERS:
             flat_image, curvature = gathered(coefficients(image), partial_dot)
         else:
-            _, curvature = gathered(jnp.zeros((0,), jnp.float32), partial_dot)
+            _, curvature = gathered(None, partial_dot)
         step_len = rho_now / curvature
         multipliers = multipliers + step_len[None, :, None] * direction
         residual = residual - step_len[None, :, None] * image

time: 214 us -> 224 us (1.047)
  blocking collectives: 46 us -> 60.4 us
  other arithmetic: 11.1 us -> 22.1 us
  matrix products: 31.5 us -> 20.7 us
  waiting for transfers between devices: 53.2 us -> 50 us
  local copies, waits for them, and re-layouts: 23.5 us -> 20.8 us
    all_to_all x4, blocking collectives: 46 us -> 60.4 us  [gathered(): everything = lax.all_to_all(copies, ('grp', 'sub'), 0, 0, tiled=True)]
    dot_general x25 -> x15, matrix products: 19.2 us -> 7.32 us  [the longest x5 3.7 us: coefficients(): jnp.einsum('skm,snm->skn', weighted_padded, values, precision=HIGHEST)]
    reduce_sum x4 -> x9, other arithmetic: 0.81 us -> 7.54 us  [the longest x5 5.4 us: lift(): return jnp.sum(own_part - far_part, axis=1)]
    unnamed x65 -> x60, local copies, waits for them, and re-layouts: 10.4 us -> 3.95 us
    ppermute x5, starting transfers between devices: 11 us -> 15.1 us  [neighbors(): from_below = lax.ppermute(d3, 'grp', up_grp)]
    another operation x1 -> x2, local copies, waits for them, and re-layouts: 0.01 us -> 4.01 us  [pad_columns(): split = rows.reshape(lead + (subdomain_count, MODES))]
    ppermute x5, starting transfers between devices: 11.5 us -> 8.36 us  [neighbors(): left_dev = lax.ppermute(d1[-1:], 'sub', up_sub)]
    sub x0 -> x4, other arithmetic: none -> 3.1 us  [project_with(): return values - lift(flat)]
  transfers between devices with their start and end apart: 22 -> 22, of which waited for: 12 -> 11; matrix products, arithmetic and copies ran while one was open for 2% -> 6% of each run, Pallas kernels for 0% -> 0%
where the time goes in v5:
time: 224 us; the launch traced here: 222 us
  blocking collectives  60.4 us (27%)
  waiting for transfers between devices  50 us (22%)
  starting transfers between devices  46.6 us (21%)
  other arithmetic  22.1 us (10%)
  local copies, waits for them, and re-layouts  20.8 us (9%)
  matrix products  20.7 us (9%)
    all_to_all x4, blocking collectives, gathered(): everything = lax.all_to_all(copies, ('grp', 'sub'), 0, 0, tiled=True)  60.4 us
    ppermute x5, waiting for transfers between devices, neighbors(): from_above = lax.ppermute(d2, 'grp', down_grp)  22.9 us
    ppermute x5, starting transfers between devices, neighbors(): from_below = lax.ppermute(d3, 'grp', up_grp)  15.1 us
    ppermute x5, waiting for transfers between devices, neighbors(): from_below = lax.ppermute(d3, 'grp', up_grp)  14.8 us
    all_to_all x2, waiting for transfers between devices, gathered(): everything = lax.all_to_all(copies, ('grp', 'sub'), 0, 0, tiled=True)  12.2 us
    all_to_all x2, starting transfers between devices, gathered(): everything = lax.all_to_all(copies, ('grp', 'sub'), 0, 0, tiled=True)  9.98 us
    dot_general x6, matrix products, to_mine(): return jnp.einsum('sfcq,sfqr->sfcr', raw, permutes, precision=HIGHEST)  9.2 us
    ppermute x5, starting transfers between devices, neighbors(): left_dev = lax.ppermute(d1[-1:], 'sub', up_sub)  8.36 us
  transfers between devices with their start and end apart: 22, of which 11 were waited for; matrix products, arithmetic and copies ran while one was open for 6% of the time, Pallas kernels for 0%

profile of v5, /device:TPU:0, one launch (start us, length us, event | category | flops | bytes accessed | tf_op | source)
XLA Modules:
  0.0 222.4 jit_solution(13165997075829277305)
XLA Ops:
  5.6 2.4 %collective-permute-start = (f32[1,28672]{1,0:T(1,128)S(1)}, f32[1,28672]{1,0:T(1,128)S(1)}, u32[]{:S(2)}, u32[]{:S(2)}) collective-permute-start(f32[1,28672]{1,0:T(1,128)S(1)} %get-tuple-element.38), channel_id=1, source_target_pairs={{0,4},{4,8},{8,12},{12,16},{16,20},{20,24},{24,28},{1,5},{5,9},{9,... | collective-permute-start | bytes 344072 | tf_op jit(solution)/shard_map/ppermute | solution.py:21
  9.4 4.3 %collective-permute-start.2 = (f32[2,28672]{1,0:T(2,128)S(1)}, f32[2,28672]{1,0:T(2,128)S(1)}, u32[]{:S(2)}, u32[]{:S(2)}) collective-permute-start(f32[2,28672]{1,0:T(2,128)S(1)} %get-tuple-element.48), channel_id=1, source_target_pairs={{0,1},{1,2},{2,3},{4,5},{5,6},{6,7},{8,9},{9,10},{10,11},{12,13},{... | collective-permute-start | bytes 688136 | tf_op jit(solution)/shard_map/ppermute | solution.py:25
  18.4 4.6 %collective-permute-done.3 = f32[2,28672]{1,0:T(2,128)S(1)} collective-permute-done((f32[2,28672]{1,0:T(2,128)S(1)}, f32[2,28672]{1,0:T(2,128)S(1)}, u32[]{:S(2)}, u32[]{:S(2)}) %collective-permute-start.3) | collective-permute-done | bytes 229408 | tf_op jit(solution)/shard_map/ppermute | solution.py:26
  25.7 2.6 %reshape.246 = f32[2,4,96,256]{3,2,1,0:T(8,128)} reshape(f32[2,4,24576]{2,1,0:T(4,128)} %slice.248) | data formatting | bytes 1572864 | tf_op jit(solution)/shard_map/reshape | solution.py:97
  29.3 2.5 %convolution_bitcast_fusion.4 = f32[2,4,12,8,256]{4,3,2,1,0:T(8,128)S(1)} fusion(f32[2,4,96,256]{3,2,1,0:T(8,128)} %reshape.246, f32[2,4,256,256]{3,2,1,0:T(8,128)S(1)} %fusion.8), kind=kOutput, calls=%fused_computation.20 | convolution fusion | flops 603979776 | bytes 3670016 | tf_op jit(solution)/shard_map/sfcq,sfqr->sfcr/dot_general | solution.py:117
  33.5 6.4 %all-to-all-start = ((f32[32,16,96]{2,1,0:T(8,128)}), f32[32,16,96]{2,1,0:T(8,128)S(1)}, u32[]{:S(2)}, u32[]{:S(2)}) async-start(f32[32,16,96]{2,1,0:T(8,128)} %broadcast_in_dim.100), calls=%async_computation | async-start | bytes 524288 | tf_op jit(solution)/shard_map/all_to_all | solution.py:140
  40.8 3.7 %reshape_reshape.3 = f32[2,4,6,64,6]{4,3,2,1,0:T(8,128)} reshape(f32[2,4,2304]{2,1,0:T(4,128)} %pad_maximum_fusion.11) | data formatting | bytes 147456 | tf_op jit(solution)/shard_map/reshape;reshape | solution.py:73
  44.4 2.7 %pad.27 = f32[2,4,6,64,8]{4,3,2,1,0:T(8,128)} pad(f32[2,4,6,64,6]{4,3,2,1,0:T(8,128)} %reshape_reshape.3, f32[]{:T(128)} %constant.27.clone.1), padding=0_0x0_0x0_0x0_0x0_2 | pad | bytes 172036 | tf_op jit(solution)/shard_map/jit(_pad)/pad | solution.py:75
  47.2 2.2 %reshape.271 = f32[2,4,6,512]{3,2,1,0:T(8,128)S(1)} reshape(f32[2,4,6,64,8]{4,3,2,1,0:T(8,128)} %pad.27) | data formatting | bytes 196608 | tf_op jit(solution)/shard_map/reshape | solution.py:75
  52.3 1.5 fusion.27
  54.7 16.1 %all_to_all.30 = f32[32,16,96]{2,1,0:T(8,128)S(1)} all-to-all(f32[32,16,96]{2,1,0:T(8,128)S(1)} %broadcast_in_dim.103), channel_id=1, replica_groups=mesh['sub'=8,'grp'=4] {'grp','sub'}, dimensions={0} | all-to-all | bytes 393216 | tf_op jit(solution)/shard_map/all_to_all | solution.py:140
  74.4 1.8 collective-permute-start.4
  77.5 2.3 %collective-permute-start.6 = (f32[2,96,256]{2,1,0:T(8,128)S(1)}, f32[2,96,256]{2,1,0:T(8,128)S(1)}, u32[]{:S(2)}, u32[]{:S(2)}) collective-permute-start(f32[2,96,256]{2,1,0:T(8,128)S(1)} %get-tuple-element.32), channel_id=1, source_target_pairs={{0,1},{1,2},{2,3},{4,5},{5,6},{6,7},{8,9},{9,10},{10,11},{12,13},{... | collective-permute-start | bytes 589832 | tf_op jit(solution)/shard_map/ppermute | solution.py:25
  81.2 3.7 %collective-permute-done.6 = f32[2,96,256]{2,1,0:T(8,128)S(1)} collective-permute-done((f32[2,96,256]{2,1,0:T(8,128)S(1)}, f32[2,96,256]{2,1,0:T(8,128)S(1)}, u32[]{:S(2)}, u32[]{:S(2)}) %collective-permute-start.6) | collective-permute-done | bytes 196640 | tf_op jit(solution)/shard_map/ppermute | solution.py:25
  84.9 4.4 %collective-permute-done.7 = f32[2,96,256]{2,1,0:T(8,128)S(1)} collective-permute-done((f32[2,96,256]{2,1,0:T(8,128)S(1)}, f32[2,96,256]{2,1,0:T(8,128)S(1)}, u32[]{:S(2)}, u32[]{:S(2)}) %collective-permute-start.7) | collective-permute-done | bytes 196640 | tf_op jit(solution)/shard_map/ppermute | solution.py:26
  91.9 16.4 %all_to_all.31 = f32[32,24,96]{2,1,0:T(8,128)S(1)} all-to-all(f32[32,24,96]{2,1,0:T(8,128)S(1)} %broadcast_in_dim.106), channel_id=1, replica_groups=mesh['sub'=8,'grp'=4] {'grp','sub'}, dimensions={0} | all-to-all | bytes 589824 | tf_op jit(solution)/shard_map/all_to_all | solution.py:140
  113.8 2.8 %collective-permute-start.10 = (f32[2,96,256]{2,1,0:T(8,128)S(1)}, f32[2,96,256]{2,1,0:T(8,128)S(1)}, u32[]{:S(2)}, u32[]{:S(2)}) collective-permute-start(f32[2,96,256]{2,1,0:T(8,128)S(1)} %get-tuple-element.26), channel_id=1, source_target_pairs={{0,1},{1,2},{2,3},{4,5},{5,6},{6,7},{8,9},{9,10},{10,11},{12,13},{... | collective-permute-start | bytes 589832 | tf_op jit(solution)/shard_map/ppermute | solution.py:25
  116.7 1.5 collective-permute-start.11
  118.2 3.1 %collective-permute-done.10 = f32[2,96,256]{2,1,0:T(8,128)S(1)} collective-permute-done((f32[2,96,256]{2,1,0:T(8,128)S(1)}, f32[2,96,256]{2,1,0:T(8,128)S(1)}, u32[]{:S(2)}, u32[]{:S(2)}) %collective-permute-start.10) | collective-permute-done | bytes 196640 | tf_op jit(solution)/shard_map/ppermute | solution.py:25
  121.4 4.6 %collective-permute-done.11 = f32[2,96,256]{2,1,0:T(8,128)S(1)} collective-permute-done((f32[2,96,256]{2,1,0:T(8,128)S(1)}, f32[2,96,256]{2,1,0:T(8,128)S(1)}, u32[]{:S(2)}, u32[]{:S(2)}) %collective-permute-start.11) | collective-permute-done | bytes 196640 | tf_op jit(solution)/shard_map/ppermute | solution.py:26
  130.2 3.6 %all-to-all-start.3 = ((f32[32,24,96]{2,1,0:T(8,128)}), f32[32,24,96]{2,1,0:T(8,128)}, u32[]{:S(2)}, u32[]{:S(2)}) async-start(f32[32,24,96]{2,1,0:T(8,128)} %broadcast_in_dim.109), calls=%async_computation.3 | async-start | bytes 786432 | tf_op jit(solution)/shard_map/all_to_all | solution.py:140
  134.7 12.2 %all-to-all-done.3 = f32[32,24,96]{2,1,0:T(8,128)} async-done(((f32[32,24,96]{2,1,0:T(8,128)}), f32[32,24,96]{2,1,0:T(8,128)}, u32[]{:S(2)}, u32[]{:S(2)}) %all-to-all-start.3) | async-done | bytes 294944 | tf_op jit(solution)/shard_map/all_to_all | solution.py:140
  155.9 2.8 %collective-permute-start.14 = (f32[2,96,256]{2,1,0:T(8,128)S(1)}, f32[2,96,256]{2,1,0:T(8,128)S(1)}, u32[]{:S(2)}, u32[]{:S(2)}) collective-permute-start(f32[2,96,256]{2,1,0:T(8,128)S(1)} %get-tuple-element.20), channel_id=1, source_target_pairs={{0,1},{1,2},{2,3},{4,5},{5,6},{6,7},{8,9},{9,10},{10,11},{12,13},{... | collective-permute-start | bytes 589832 | tf_op jit(solution)/shard_map/ppermute | solution.py:25
  160.1 3.4 %collective-permute-done.14 = f32[2,96,256]{2,1,0:T(8,128)S(1)} collective-permute-done((f32[2,96,256]{2,1,0:T(8,128)S(1)}, f32[2,96,256]{2,1,0:T(8,128)S(1)}, u32[]{:S(2)}, u32[]{:S(2)}) %collective-permute-start.14) | collective-permute-done | bytes 196640 | tf_op jit(solution)/shard_map/ppermute | solution.py:25
  163.5 4.6 %collective-permute-done.15 = f32[2,96,256]{2,1,0:T(8,128)S(1)} collective-permute-done((f32[2,96,256]{2,1,0:T(8,128)S(1)}, f32[2,96,256]{2,1,0:T(8,128)S(1)}, u32[]{:S(2)}, u32[]{:S(2)}) %collective-permute-start.15) | collective-permute-done | bytes 196640 | tf_op jit(solution)/shard_map/ppermute | solution.py:26
  170.6 16.4 %all_to_all.32 = f32[32,24,96]{2,1,0:T(8,128)S(1)} all-to-all(f32[32,24,96]{2,1,0:T(8,128)S(1)} %broadcast_in_dim.112), channel_id=1, replica_groups=mesh['sub'=8,'grp'=4] {'grp','sub'}, dimensions={0} | all-to-all | bytes 589824 | tf_op jit(solution)/shard_map/all_to_all | solution.py:140
  192.8 2.8 %collective-permute-start.18 = (f32[2,96,256]{2,1,0:T(8,128)S(1)}, f32[2,96,256]{2,1,0:T(8,128)S(1)}, u32[]{:S(2)}, u32[]{:S(2)}) collective-permute-start(f32[2,96,256]{2,1,0:T(8,128)S(1)} %get-tuple-element.14), channel_id=1, source_target_pairs={{0,1},{1,2},{2,3},{4,5},{5,6},{6,7},{8,9},{9,10},{10,11},{12,13},{... | collective-permute-start | bytes 589832 | tf_op jit(solution)/shard_map/ppermute | solution.py:25
  197.0 3.4 %collective-permute-done.18 = f32[2,96,256]{2,1,0:T(8,128)S(1)} collective-permute-done((f32[2,96,256]{2,1,0:T(8,128)S(1)}, f32[2,96,256]{2,1,0:T(8,128)S(1)}, u32[]{:S(2)}, u32[]{:S(2)}) %collective-permute-start.18) | collective-permute-done | bytes 196640 | tf_op jit(solution)/shard_map/ppermute | solution.py:25
  200.3 4.6 %collective-permute-done.19 = f32[2,96,256]{2,1,0:T(8,128)S(1)} collective-permute-done((f32[2,96,256]{2,1,0:T(8,128)S(1)}, f32[2,96,256]{2,1,0:T(8,128)S(1)}, u32[]{:S(2)}, u32[]{:S(2)}) %collective-permute-start.19) | collective-permute-done | bytes 196640 | tf_op jit(solution)/shard_map/ppermute | solution.py:26
  205.0 1.4 convolution_bitcast_fusion
  207.7 11.5 %all_to_all.33 = f32[32,8,96]{2,1,0:T(8,128)S(1)} all-to-all(f32[32,8,96]{2,1,0:T(8,128)S(1)} %broadcast_in_dim.115), channel_id=1, replica_groups=mesh['sub'=8,'grp'=4] {'grp','sub'}, dimensions={0} | all-to-all | bytes 196608 | tf_op jit(solution)/shard_map/all_to_all | solution.py:140
  219.3 3.2 %subtract_bitcast_fusion = (f32[1,2,96,1024]{3,2,1,0:T(8,128)}, f32[1,2,96,1024]{3,2,1,0:T(8,128)}) fusion(f32[2,96,1024]{2,1,0:T(8,128)} %get-tuple-element.3, f32[96]{0:T(128)S(1)} %div.27, f32[2,96,1024]{2,1,0:T(8,128)S(1)} %fusion.27, f32[2,96,1024]{2,1,0:T(8,128)S(1)} %copy-done.8, f32[96]{0:T(128)S(1)} %div.25, f32[2,96,1024]{2,1,0:T(8,128)} %copy-done.9, ...), kind=kLoop, calls=%fused_computation.43 | loop fusion | flops 1376256 | bytes 5505792 | tf_op jit(solution)/shard_map/broadcast_in_dim | solution.py:190
  (203 shorter events, 60.8 us)
Async XLA Ops:
  5.4 19.3 %copy-start.22 = (s32[4]{0:T(128)S(1)}, s32[4]{0:T(128)}, u32[]{:S(2)}) copy-start(s32[4]{0:T(128)} %constant.51) | copy-start | bytes 52
  5.6 10.7 %collective-permute-start = (f32[1,28672]{1,0:T(1,128)S(1)}, f32[1,28672]{1,0:T(1,128)S(1)}, u32[]{:S(2)}, u32[]{:S(2)}) collective-permute-start(f32[1,28672]{1,0:T(1,128)S(1)} %get-tuple-element.38), channel_id=1, source_target_pairs={{0,4},{4,8},{8,12},{12,16},{16,20},{20,24},{24,28},{1,5},{5,9},{9,... | collective-permute-start | bytes 344072 | tf_op jit(solution)/shard_map/ppermute | solution.py:21
  8.1 8.3 %collective-permute-start.1 = (f32[1,28672]{1,0:T(1,128)S(1)}, f32[1,28672]{1,0:T(1,128)S(1)}, u32[]{:S(2)}, u32[]{:S(2)}) collective-permute-start(f32[1,28672]{1,0:T(1,128)S(1)} %get-tuple-element.41), channel_id=1, source_target_pairs={{4,0},{8,4},{12,8},{16,12},{20,16},{24,20},{28,24},{5,1},{9,5},{13... | collective-permute-start | bytes 344072 | tf_op jit(solution)/shard_map/ppermute | solution.py:22
  9.4 8.8 %collective-permute-start.2 = (f32[2,28672]{1,0:T(2,128)S(1)}, f32[2,28672]{1,0:T(2,128)S(1)}, u32[]{:S(2)}, u32[]{:S(2)}) collective-permute-start(f32[2,28672]{1,0:T(2,128)S(1)} %get-tuple-element.48), channel_id=1, source_target_pairs={{0,1},{1,2},{2,3},{4,5},{5,6},{6,7},{8,9},{9,10},{10,11},{12,13},{... | collective-permute-start | bytes 688136 | tf_op jit(solution)/shard_map/ppermute | solution.py:25
  13.8 9.2 %collective-permute-start.3 = (f32[2,28672]{1,0:T(2,128)S(1)}, f32[2,28672]{1,0:T(2,128)S(1)}, u32[]{:S(2)}, u32[]{:S(2)}) collective-permute-start(f32[2,28672]{1,0:T(2,128)S(1)} %get-tuple-element.49), channel_id=1, source_target_pairs={{1,0},{2,1},{3,2},{5,4},{6,5},{7,6},{9,8},{10,9},{11,10},{13,12},{... | collective-permute-start | bytes 688136 | tf_op jit(solution)/shard_map/ppermute | solution.py:26
  33.5 17.0 %all-to-all-start = ((f32[32,16,96]{2,1,0:T(8,128)}), f32[32,16,96]{2,1,0:T(8,128)S(1)}, u32[]{:S(2)}, u32[]{:S(2)}) async-start(f32[32,16,96]{2,1,0:T(8,128)} %broadcast_in_dim.100), calls=%async_computation | async-start | bytes 524288 | tf_op jit(solution)/shard_map/all_to_all | solution.py:140
  53.9 19.6 %copy-start.3 = (bf16[1,2,1024,1024]{3,2,1,0:T(8,128)(2,1)S(1)}, bf16[1,2,1024,1024]{3,2,1,0:T(8,128)(2,1)}, u32[]{:S(2)}) copy-start(bf16[1,2,1024,1024]{3,2,1,0:T(8,128)(2,1)} %param.9) | copy-start | bytes 12582916
  74.4 6.8 %collective-permute-start.4 = (f32[1,96,256]{2,1,0:T(8,128)S(1)}, f32[1,96,256]{2,1,0:T(8,128)S(1)}, u32[]{:S(2)}, u32[]{:S(2)}) collective-permute-start(f32[1,96,256]{2,1,0:T(8,128)S(1)} %get-tuple-element.28), channel_id=1, source_target_pairs={{0,4},{4,8},{8,12},{12,16},{16,20},{20,24},{24,28},{1,5},{5,9},{9,... | collective-permute-start | bytes 294920 | tf_op jit(solution)/shard_map/ppermute | solution.py:21
  76.2 4.9 %collective-permute-start.5 = (f32[1,96,256]{2,1,0:T(8,128)S(1)}, f32[1,96,256]{2,1,0:T(8,128)S(1)}, u32[]{:S(2)}, u32[]{:S(2)}) collective-permute-start(f32[1,96,256]{2,1,0:T(8,128)S(1)} %get-tuple-element.29), channel_id=1, source_target_pairs={{4,0},{8,4},{12,8},{16,12},{20,16},{24,20},{28,24},{5,1},{9,5},{13... | collective-permute-start | bytes 294920 | tf_op jit(solution)/shard_map/ppermute | solution.py:22
  77.5 7.4 %collective-permute-start.6 = (f32[2,96,256]{2,1,0:T(8,128)S(1)}, f32[2,96,256]{2,1,0:T(8,128)S(1)}, u32[]{:S(2)}, u32[]{:S(2)}) collective-permute-start(f32[2,96,256]{2,1,0:T(8,128)S(1)} %get-tuple-element.32), channel_id=1, source_target_pairs={{0,1},{1,2},{2,3},{4,5},{5,6},{6,7},{8,9},{9,10},{10,11},{12,13},{... | collective-permute-start | bytes 589832 | tf_op jit(solution)/shard_map/ppermute | solution.py:25
  79.8 9.5 %collective-permute-start.7 = (f32[2,96,256]{2,1,0:T(8,128)S(1)}, f32[2,96,256]{2,1,0:T(8,128)S(1)}, u32[]{:S(2)}, u32[]{:S(2)}) collective-permute-start(f32[2,96,256]{2,1,0:T(8,128)S(1)} %get-tuple-element.33), channel_id=1, source_target_pairs={{1,0},{2,1},{3,2},{5,4},{6,5},{7,6},{9,8},{10,9},{11,10},{13,12},{... | collective-permute-start | bytes 589832 | tf_op jit(solution)/shard_map/ppermute | solution.py:26
  90.8 17.8 %copy-start.17 = (f32[2,4,6,512]{3,2,1,0:T(8,128)S(1)}, f32[2,4,6,512]{3,2,1,0:T(8,128)}, u32[]{:S(2)}) copy-start(f32[2,4,6,512]{3,2,1,0:T(8,128)} %copy-done.16) | copy-start | bytes 294916
  91.1 19.1 %copy-start.5 = (bf16[1,2,1024,1024]{3,2,1,0:T(8,128)(2,1)S(1)}, bf16[1,2,1024,1024]{3,2,1,0:T(8,128)(2,1)}, u32[]{:S(2)}) copy-start(bf16[1,2,1024,1024]{3,2,1,0:T(8,128)(2,1)} %param.8) | copy-start | bytes 12582916
  110.2 17.3 %copy-start = (f32[2,96,1024]{2,1,0:T(8,128)}, f32[2,96,1024]{2,1,0:T(8,128)S(1)}, u32[]{:S(2)}) copy-start(f32[2,96,1024]{2,1,0:T(8,128)S(1)} %sub.94) | copy-start | bytes 2359300
  111.1 7.1 %collective-permute-start.8 = (f32[1,96,256]{2,1,0:T(8,128)S(1)}, f32[1,96,256]{2,1,0:T(8,128)S(1)}, u32[]{:S(2)}, u32[]{:S(2)}) collective-permute-start(f32[1,96,256]{2,1,0:T(8,128)S(1)} %get-tuple-element.22), channel_id=1, source_target_pairs={{0,4},{4,8},{8,12},{12,16},{16,20},{20,24},{24,28},{1,5},{5,9},{9,... | collective-permute-start | bytes 294920 | tf_op jit(solution)/shard_map/ppermute | solution.py:21
  112.5 5.7 %collective-permute-start.9 = (f32[1,96,256]{2,1,0:T(8,128)S(1)}, f32[1,96,256]{2,1,0:T(8,128)S(1)}, u32[]{:S(2)}, u32[]{:S(2)}) collective-permute-start(f32[1,96,256]{2,1,0:T(8,128)S(1)} %get-tuple-element.23), channel_id=1, source_target_pairs={{4,0},{8,4},{12,8},{16,12},{20,16},{24,20},{28,24},{5,1},{9,5},{13... | collective-permute-start | bytes 294920 | tf_op jit(solution)/shard_map/ppermute | solution.py:22
  113.8 7.6 %collective-permute-start.10 = (f32[2,96,256]{2,1,0:T(8,128)S(1)}, f32[2,96,256]{2,1,0:T(8,128)S(1)}, u32[]{:S(2)}, u32[]{:S(2)}) collective-permute-start(f32[2,96,256]{2,1,0:T(8,128)S(1)} %get-tuple-element.26), channel_id=1, source_target_pairs={{0,1},{1,2},{2,3},{4,5},{5,6},{6,7},{8,9},{9,10},{10,11},{12,13},{... | collective-permute-start | bytes 589832 | tf_op jit(solution)/shard_map/ppermute | solution.py:25
  116.7 9.4 %collective-permute-start.11 = (f32[2,96,256]{2,1,0:T(8,128)S(1)}, f32[2,96,256]{2,1,0:T(8,128)S(1)}, u32[]{:S(2)}, u32[]{:S(2)}) collective-permute-start(f32[2,96,256]{2,1,0:T(8,128)S(1)} %get-tuple-element.27), channel_id=1, source_target_pairs={{1,0},{2,1},{3,2},{5,4},{6,5},{7,6},{9,8},{10,9},{11,10},{13,12},{... | collective-permute-start | bytes 589832 | tf_op jit(solution)/shard_map/ppermute | solution.py:26
  127.4 22.1 %copy-start.18 = (f32[2,4,6,512]{3,2,1,0:T(8,128)S(1)}, f32[2,4,6,512]{3,2,1,0:T(8,128)}, u32[]{:S(2)}) copy-start(f32[2,4,6,512]{3,2,1,0:T(8,128)} %copy-done.16) | copy-start | bytes 294916
  130.2 16.8 %all-to-all-start.3 = ((f32[32,24,96]{2,1,0:T(8,128)}), f32[32,24,96]{2,1,0:T(8,128)}, u32[]{:S(2)}, u32[]{:S(2)}) async-start(f32[32,24,96]{2,1,0:T(8,128)} %broadcast_in_dim.109), calls=%async_computation.3 | async-start | bytes 786432 | tf_op jit(solution)/shard_map/all_to_all | solution.py:140
  153.2 6.9 %collective-permute-start.12 = (f32[1,96,256]{2,1,0:T(8,128)S(1)}, f32[1,96,256]{2,1,0:T(8,128)S(1)}, u32[]{:S(2)}, u32[]{:S(2)}) collective-permute-start(f32[1,96,256]{2,1,0:T(8,128)S(1)} %get-tuple-element.16), channel_id=1, source_target_pairs={{0,4},{4,8},{8,12},{12,16},{16,20},{20,24},{24,28},{1,5},{5,9},{9,... | collective-permute-start | bytes 294920 | tf_op jit(solution)/shard_map/ppermute | solution.py:21
  154.6 5.5 %collective-permute-start.13 = (f32[1,96,256]{2,1,0:T(8,128)S(1)}, f32[1,96,256]{2,1,0:T(8,128)S(1)}, u32[]{:S(2)}, u32[]{:S(2)}) collective-permute-start(f32[1,96,256]{2,1,0:T(8,128)S(1)} %get-tuple-element.17), channel_id=1, source_target_pairs={{4,0},{8,4},{12,8},{16,12},{20,16},{24,20},{28,24},{5,1},{9,5},{13... | collective-permute-start | bytes 294920 | tf_op jit(solution)/shard_map/ppermute | solution.py:22
  155.9 7.6 %collective-permute-start.14 = (f32[2,96,256]{2,1,0:T(8,128)S(1)}, f32[2,96,256]{2,1,0:T(8,128)S(1)}, u32[]{:S(2)}, u32[]{:S(2)}) collective-permute-start(f32[2,96,256]{2,1,0:T(8,128)S(1)} %get-tuple-element.20), channel_id=1, source_target_pairs={{0,1},{1,2},{2,3},{4,5},{5,6},{6,7},{8,9},{9,10},{10,11},{12,13},{... | collective-permute-start | bytes 589832 | tf_op jit(solution)/shard_map/ppermute | solution.py:25
  158.8 9.4 %collective-permute-start.15 = (f32[2,96,256]{2,1,0:T(8,128)S(1)}, f32[2,96,256]{2,1,0:T(8,128)S(1)}, u32[]{:S(2)}, u32[]{:S(2)}) collective-permute-start(f32[2,96,256]{2,1,0:T(8,128)S(1)} %get-tuple-element.21), channel_id=1, source_target_pairs={{1,0},{2,1},{3,2},{5,4},{6,5},{7,6},{9,8},{10,9},{11,10},{13,12},{... | collective-permute-start | bytes 589832 | tf_op jit(solution)/shard_map/ppermute | solution.py:26
  169.5 17.9 %copy-start.19 = (f32[2,4,6,512]{3,2,1,0:T(8,128)S(1)}, f32[2,4,6,512]{3,2,1,0:T(8,128)}, u32[]{:S(2)}) copy-start(f32[2,4,6,512]{3,2,1,0:T(8,128)} %copy-done.16) | copy-start | bytes 294916
  169.6 19.3 %copy-start.1 = (f32[2,96,1024]{2,1,0:T(8,128)S(1)}, f32[2,96,1024]{2,1,0:T(8,128)}, u32[]{:S(2)}) copy-start(f32[2,96,1024]{2,1,0:T(8,128)} %copy-done) | copy-start | bytes 2359300
  170.6 18.6 %copy-start.6 = (bf16[1,2,1024,1024]{3,2,1,0:T(8,128)(2,1)S(1)}, bf16[1,2,1024,1024]{3,2,1,0:T(8,128)(2,1)}, u32[]{:S(2)}) copy-start(bf16[1,2,1024,1024]{3,2,1,0:T(8,128)(2,1)} %param.8) | copy-start | bytes 12582916
  189.2 17.3 %copy-start.9 = (f32[2,96,1024]{2,1,0:T(8,128)}, f32[2,96,1024]{2,1,0:T(8,128)S(1)}, u32[]{:S(2)}) copy-start(f32[2,96,1024]{2,1,0:T(8,128)S(1)} %multiply_add_fusion) | copy-start | bytes 2359300
  190.0 6.9 %collective-permute-start.16 = (f32[1,96,256]{2,1,0:T(8,128)S(1)}, f32[1,96,256]{2,1,0:T(8,128)S(1)}, u32[]{:S(2)}, u32[]{:S(2)}) collective-permute-start(f32[1,96,256]{2,1,0:T(8,128)S(1)} %get-tuple-element.10), channel_id=1, source_target_pairs={{0,4},{4,8},{8,12},{12,16},{16,20},{20,24},{24,28},{1,5},{5,9},{9,... | collective-permute-start | bytes 294920 | tf_op jit(solution)/shard_map/ppermute | solution.py:21
  191.5 5.5 %collective-permute-start.17 = (f32[1,96,256]{2,1,0:T(8,128)S(1)}, f32[1,96,256]{2,1,0:T(8,128)S(1)}, u32[]{:S(2)}, u32[]{:S(2)}) collective-permute-start(f32[1,96,256]{2,1,0:T(8,128)S(1)} %get-tuple-element.11), channel_id=1, source_target_pairs={{4,0},{8,4},{12,8},{16,12},{20,16},{24,20},{28,24},{5,1},{9,5},{13... | collective-permute-start | bytes 294920 | tf_op jit(solution)/shard_map/ppermute | solution.py:22
  192.8 7.6 %collective-permute-start.18 = (f32[2,96,256]{2,1,0:T(8,128)S(1)}, f32[2,96,256]{2,1,0:T(8,128)S(1)}, u32[]{:S(2)}, u32[]{:S(2)}) collective-permute-start(f32[2,96,256]{2,1,0:T(8,128)S(1)} %get-tuple-element.14), channel_id=1, source_target_pairs={{0,1},{1,2},{2,3},{4,5},{5,6},{6,7},{8,9},{9,10},{10,11},{12,13},{... | collective-permute-start | bytes 589832 | tf_op jit(solution)/shard_map/ppermute | solution.py:25
  195.6 9.4 %collective-permute-start.19 = (f32[2,96,256]{2,1,0:T(8,128)S(1)}, f32[2,96,256]{2,1,0:T(8,128)S(1)}, u32[]{:S(2)}, u32[]{:S(2)}) collective-permute-start(f32[2,96,256]{2,1,0:T(8,128)S(1)} %get-tuple-element.15), channel_id=1, source_target_pairs={{1,0},{2,1},{3,2},{5,4},{6,5},{7,6},{9,8},{10,9},{11,10},{13,12},{... | collective-permute-start | bytes 589832 | tf_op jit(solution)/shard_map/ppermute | solution.py:26
  (13 other events, 98.8 us)

commit v6 on v3

--- a/solution.py
+++ b/solution.py
@@ -105,6 +105,7 @@
         return jnp.einsum("sfcq,sfqr->sfcr", raw, permutes, precision=HIGHEST)
 
     partner_modes = to_mine(partner_raw_modes)
+    partner_slot_modes = jnp.moveaxis(partner_modes, 1, 2).reshape(subdomains, MODES, width)
 
     def partner_values(raw, shape):
         return jnp.moveaxis(to_mine(raw), 1, 2).reshape(shape)
@@ -131,10 +132,11 @@
     def lift(flat):
         amounts = jnp.dot(rows_here, flat, precision=HIGHEST, preferred_element_type=jnp.float32)
         shaped = amounts.reshape(subdomains, MODES, columns)
-        own_part = jnp.einsum("skm,skn->snm", own_modes, shaped, precision=HIGHEST)
-        far_amounts = jnp.einsum("sfkc,cn->sfkn", partner_rows, flat, precision=HIGHEST)
-        far_part = jnp.einsum("sfkm,sfkn->snfm", partner_modes, far_amounts, precision=HIGHEST)
-        return own_part - far_part.reshape(subdomains, columns, width)
+        far_amounts = jnp.einsum("sfkc,cn->skfn", partner_rows, flat, precision=HIGHEST)
+        far_spread = jnp.repeat(jnp.swapaxes(far_amounts, 2, 3), quarter, axis=3)
+        own_part = own_modes[:, :, None, :] * shaped[:, :, :, None]
+        far_part = partner_slot_modes[:, :, None, :] * far_spread
+        return jnp.sum(own_part - far_part, axis=1)
 
     def project_with(values, flat):
         return values - lift(flat)

time: 214 us -> 213 us (level)
  other arithmetic: 11.1 us -> 22.1 us
  matrix products: 31.5 us -> 23.3 us
  local copies, waits for them, and re-layouts: 23.5 us -> 19.7 us
    dot_general x15 -> x5, matrix products: 14.3 us -> 4.97 us  [lift(): jnp.einsum('sfkc,cn->skfn', partner_rows, flat, precision=HIGHEST)]
    reduce_sum x0 -> x5, other arithmetic: none -> 5.41 us  [lift(): return jnp.sum(own_part - far_part, axis=1)]
    sub x0 -> x4, other arithmetic: none -> 4.36 us  [project_with(): return values - lift(flat)]
    unnamed x65 -> x55, local copies, waits for them, and re-layouts: 10.4 us -> 8.12 us
where the time goes in v6:
time: 213 us; the launch traced here: 212 us
  waiting for transfers between devices  53.1 us (25%)
  blocking collectives  46 us (22%)
  starting transfers between devices  45.9 us (22%)
  matrix products  23.3 us (11%)
  other arithmetic  22.1 us (10%)
  local copies, waits for them, and re-layouts  19.7 us (9%)
    all_to_all x4, blocking collectives, gathered(): everything = lax.all_to_all(copies, ('grp', 'sub'), 0, 0, tiled=True)  46 us
    ppermute x5, waiting for transfers between devices, neighbors(): from_above = lax.ppermute(d2, 'grp', down_grp)  23 us
    ppermute x5, waiting for transfers between devices, neighbors(): from_below = lax.ppermute(d3, 'grp', up_grp)  15.7 us
    all_to_all x2, waiting for transfers between devices, gathered(): everything = lax.all_to_all(copies, ('grp', 'sub'), 0, 0, tiled=True)  14.4 us
    ppermute x5, starting transfers between devices, neighbors(): left_dev = lax.ppermute(d1[-1:], 'sub', up_sub)  11.6 us
    ppermute x5, starting transfers between devices, neighbors(): from_below = lax.ppermute(d3, 'grp', up_grp)  11 us
    all_to_all x2, starting transfers between devices, gathered(): everything = lax.all_to_all(copies, ('grp', 'sub'), 0, 0, tiled=True)  10.2 us
    dot_general x6, matrix products, to_mine(): return jnp.einsum('sfcq,sfqr->sfcr', raw, permutes, precision=HIGHEST)  9.2 us
  transfers between devices with their start and end apart: 22, of which 12 were waited for; matrix products, arithmetic and copies ran while one was open for 2% of the time, Pallas kernels for 0%

profile of v6, /device:TPU:0, one launch (start us, length us, event | category | flops | bytes accessed | tf_op | source)
XLA Modules:
  0.0 212.0 jit_solution(9462734848735834984)
XLA Ops:
  5.4 2.4 %collective-permute-start = (f32[1,28672]{1,0:T(1,128)S(1)}, f32[1,28672]{1,0:T(1,128)S(1)}, u32[]{:S(2)}, u32[]{:S(2)}) collective-permute-start(f32[1,28672]{1,0:T(1,128)S(1)} %get-tuple-element.38), channel_id=1, source_target_pairs={{0,4},{4,8},{8,12},{12,16},{16,20},{20,24},{24,28},{1,5},{5,9},{9,... | collective-permute-start | bytes 344072 | tf_op jit(solution)/shard_map/ppermute | solution.py:20
  9.3 4.3 %collective-permute-start.2 = (f32[2,28672]{1,0:T(2,128)S(1)}, f32[2,28672]{1,0:T(2,128)S(1)}, u32[]{:S(2)}, u32[]{:S(2)}) collective-permute-start(f32[2,28672]{1,0:T(2,128)S(1)} %get-tuple-element.48), channel_id=1, source_target_pairs={{0,1},{1,2},{2,3},{4,5},{5,6},{6,7},{8,9},{9,10},{10,11},{12,13},{... | collective-permute-start | bytes 688136 | tf_op jit(solution)/shard_map/ppermute | solution.py:24
  16.3 1.8 collective-permute-done.2
  18.3 4.6 %collective-permute-done.3 = f32[2,28672]{1,0:T(2,128)S(1)} collective-permute-done((f32[2,28672]{1,0:T(2,128)S(1)}, f32[2,28672]{1,0:T(2,128)S(1)}, u32[]{:S(2)}, u32[]{:S(2)}) %collective-permute-start.3) | collective-permute-done | bytes 229408 | tf_op jit(solution)/shard_map/ppermute | solution.py:25
  26.5 2.5 %convolution_bitcast_fusion.4 = f32[2,4,12,8,256]{4,3,2,1,0:T(8,128)S(1)} fusion(f32[2,4,96,256]{3,2,1,0:T(8,128)} %reshape.244, f32[2,4,256,256]{3,2,1,0:T(8,128)S(1)} %fusion.8), kind=kOutput, calls=%fused_computation.20 | convolution fusion | flops 603979776 | bytes 3670016 | tf_op jit(solution)/shard_map/sfcq,sfqr->sfcr/dot_general | solution.py:105
  31.6 6.2 %all-to-all-start = ((f32[32,1,1153]{2,1,0:T(1,128)}), f32[32,1,1153]{2,1,0:T(1,128)S(1)}, u32[]{:S(2)}, u32[]{:S(2)}) async-start(f32[32,1,1153]{2,1,0:T(1,128)} %broadcast_in_dim.41), calls=%async_computation | async-start | bytes 327680 | tf_op jit(solution)/shard_map/all_to_all | solution.py:124
  39.8 6.6 %all-to-all-done = f32[32,1,1153]{2,1,0:T(1,128)S(1)} async-done(((f32[32,1,1153]{2,1,0:T(1,128)}), f32[32,1,1153]{2,1,0:T(1,128)S(1)}, u32[]{:S(2)}, u32[]{:S(2)}) %all-to-all-start) | async-done | bytes 147616 | tf_op jit(solution)/shard_map/all_to_all | solution.py:124
  48.3 1.5 fusion.37
  50.8 10.7 %all_to_all.51 = f32[32,1,1153]{2,1,0:T(1,128)S(1)} all-to-all(f32[32,1,1153]{2,1,0:T(1,128)S(1)} %broadcast_in_dim.43), channel_id=1, replica_groups=mesh['sub'=8,'grp'=4] {'grp','sub'}, dimensions={0} | all-to-all | bytes 295168 | tf_op jit(solution)/shard_map/all_to_all | solution.py:124
  67.7 2.3 %collective-permute-start.4 = (f32[1,96,256]{2,1,0:T(8,128)S(1)}, f32[1,96,256]{2,1,0:T(8,128)S(1)}, u32[]{:S(2)}, u32[]{:S(2)}) collective-permute-start(f32[1,96,256]{2,1,0:T(8,128)S(1)} %get-tuple-element.28), channel_id=1, source_target_pairs={{0,4},{4,8},{8,12},{12,16},{16,20},{20,24},{24,28},{1,5},{5,9},{9,... | collective-permute-start | bytes 294920 | tf_op jit(solution)/shard_map/ppermute | solution.py:20
  71.3 1.7 collective-permute-start.6
  74.4 3.5 %collective-permute-done.6 = f32[2,96,256]{2,1,0:T(8,128)S(1)} collective-permute-done((f32[2,96,256]{2,1,0:T(8,128)S(1)}, f32[2,96,256]{2,1,0:T(8,128)S(1)}, u32[]{:S(2)}, u32[]{:S(2)}) %collective-permute-start.6) | collective-permute-done | bytes 196640 | tf_op jit(solution)/shard_map/ppermute | solution.py:24
  77.9 4.6 %collective-permute-done.7 = f32[2,96,256]{2,1,0:T(8,128)S(1)} collective-permute-done((f32[2,96,256]{2,1,0:T(8,128)S(1)}, f32[2,96,256]{2,1,0:T(8,128)S(1)}, u32[]{:S(2)}, u32[]{:S(2)}) %collective-permute-start.7) | collective-permute-done | bytes 196640 | tf_op jit(solution)/shard_map/ppermute | solution.py:25
  86.0 12.2 %all_to_all.52 = f32[32,1,1248]{2,1,0:T(1,128)S(1)} all-to-all(f32[32,1,1248]{2,1,0:T(1,128)S(1)} %broadcast_in_dim.45), channel_id=1, replica_groups=mesh['sub'=8,'grp'=4] {'grp','sub'}, dimensions={0} | all-to-all | bytes 319488 | tf_op jit(solution)/shard_map/all_to_all | solution.py:124
  105.5 2.3 %collective-permute-start.8 = (f32[1,96,256]{2,1,0:T(8,128)S(1)}, f32[1,96,256]{2,1,0:T(8,128)S(1)}, u32[]{:S(2)}, u32[]{:S(2)}) collective-permute-start(f32[1,96,256]{2,1,0:T(8,128)S(1)} %get-tuple-element.22), channel_id=1, source_target_pairs={{0,4},{4,8},{8,12},{12,16},{16,20},{20,24},{24,28},{1,5},{5,9},{9,... | collective-permute-start | bytes 294920 | tf_op jit(solution)/shard_map/ppermute | solution.py:20
  109.1 1.7 collective-permute-start.10
  112.1 3.5 %collective-permute-done.10 = f32[2,96,256]{2,1,0:T(8,128)S(1)} collective-permute-done((f32[2,96,256]{2,1,0:T(8,128)S(1)}, f32[2,96,256]{2,1,0:T(8,128)S(1)}, u32[]{:S(2)}, u32[]{:S(2)}) %collective-permute-start.10) | collective-permute-done | bytes 196640 | tf_op jit(solution)/shard_map/ppermute | solution.py:24
  115.7 4.6 %collective-permute-done.11 = f32[2,96,256]{2,1,0:T(8,128)S(1)} collective-permute-done((f32[2,96,256]{2,1,0:T(8,128)S(1)}, f32[2,96,256]{2,1,0:T(8,128)S(1)}, u32[]{:S(2)}, u32[]{:S(2)}) %collective-permute-start.11) | collective-permute-done | bytes 196640 | tf_op jit(solution)/shard_map/ppermute | solution.py:25
  124.5 4.0 %all-to-all-start.3 = ((f32[32,1,1248]{2,1,0:T(1,128)}), f32[32,1,1248]{2,1,0:T(1,128)}, u32[]{:S(2)}, u32[]{:S(2)}) async-start(f32[32,1,1248]{2,1,0:T(1,128)} %broadcast_in_dim.47), calls=%async_computation.3 | async-start | bytes 327680 | tf_op jit(solution)/shard_map/all_to_all | solution.py:124
  129.2 7.8 %all-to-all-done.3 = f32[32,1,1248]{2,1,0:T(1,128)} async-done(((f32[32,1,1248]{2,1,0:T(1,128)}), f32[32,1,1248]{2,1,0:T(1,128)}, u32[]{:S(2)}, u32[]{:S(2)}) %all-to-all-start.3) | async-done | bytes 159776 | tf_op jit(solution)/shard_map/all_to_all | solution.py:124
  144.7 2.3 %collective-permute-start.12 = (f32[1,96,256]{2,1,0:T(8,128)S(1)}, f32[1,96,256]{2,1,0:T(8,128)S(1)}, u32[]{:S(2)}, u32[]{:S(2)}) collective-permute-start(f32[1,96,256]{2,1,0:T(8,128)S(1)} %get-tuple-element.16), channel_id=1, source_target_pairs={{0,4},{4,8},{8,12},{12,16},{16,20},{20,24},{24,28},{1,5},{5,9},{9,... | collective-permute-start | bytes 294920 | tf_op jit(solution)/shard_map/ppermute | solution.py:20
  148.3 1.7 collective-permute-start.14
  151.6 3.3 %collective-permute-done.14 = f32[2,96,256]{2,1,0:T(8,128)S(1)} collective-permute-done((f32[2,96,256]{2,1,0:T(8,128)S(1)}, f32[2,96,256]{2,1,0:T(8,128)S(1)}, u32[]{:S(2)}, u32[]{:S(2)}) %collective-permute-start.14) | collective-permute-done | bytes 196640 | tf_op jit(solution)/shard_map/ppermute | solution.py:24
  154.9 4.6 %collective-permute-done.15 = f32[2,96,256]{2,1,0:T(8,128)S(1)} collective-permute-done((f32[2,96,256]{2,1,0:T(8,128)S(1)}, f32[2,96,256]{2,1,0:T(8,128)S(1)}, u32[]{:S(2)}, u32[]{:S(2)}) %collective-permute-start.15) | collective-permute-done | bytes 196640 | tf_op jit(solution)/shard_map/ppermute | solution.py:25
  163.0 12.2 %all_to_all.53 = f32[32,1,1248]{2,1,0:T(1,128)S(1)} all-to-all(f32[32,1,1248]{2,1,0:T(1,128)S(1)} %broadcast_in_dim.93), channel_id=1, replica_groups=mesh['sub'=8,'grp'=4] {'grp','sub'}, dimensions={0} | all-to-all | bytes 319488 | tf_op jit(solution)/shard_map/all_to_all | solution.py:124
  178.1 1.6 multiply_add_fusion
  180.5 2.3 %collective-permute-start.16 = (f32[1,96,256]{2,1,0:T(8,128)S(1)}, f32[1,96,256]{2,1,0:T(8,128)S(1)}, u32[]{:S(2)}, u32[]{:S(2)}) collective-permute-start(f32[1,96,256]{2,1,0:T(8,128)S(1)} %get-tuple-element.10), channel_id=1, source_target_pairs={{0,4},{4,8},{8,12},{12,16},{16,20},{20,24},{24,28},{1,5},{5,9},{9,... | collective-permute-start | bytes 294920 | tf_op jit(solution)/shard_map/ppermute | solution.py:20
  184.2 1.7 collective-permute-start.18
  187.2 3.5 %collective-permute-done.18 = f32[2,96,256]{2,1,0:T(8,128)S(1)} collective-permute-done((f32[2,96,256]{2,1,0:T(8,128)S(1)}, f32[2,96,256]{2,1,0:T(8,128)S(1)}, u32[]{:S(2)}, u32[]{:S(2)}) %collective-permute-start.18) | collective-permute-done | bytes 196640 | tf_op jit(solution)/shard_map/ppermute | solution.py:24
  190.7 4.6 %collective-permute-done.19 = f32[2,96,256]{2,1,0:T(8,128)S(1)} collective-permute-done((f32[2,96,256]{2,1,0:T(8,128)S(1)}, f32[2,96,256]{2,1,0:T(8,128)S(1)}, u32[]{:S(2)}, u32[]{:S(2)}) %collective-permute-start.19) | collective-permute-done | bytes 196640 | tf_op jit(solution)/shard_map/ppermute | solution.py:25
  198.1 10.8 %all_to_all.54 = f32[32,1,96]{2,1,0:T(1,128)S(1)} all-to-all(f32[32,1,96]{2,1,0:T(1,128)S(1)} %broadcast_in_dim.95), channel_id=1, replica_groups=mesh['sub'=8,'grp'=4] {'grp','sub'}, dimensions={0} | all-to-all | bytes 24576 | tf_op jit(solution)/shard_map/all_to_all | solution.py:124
  208.9 3.0 %subtract_bitcast_fusion = (f32[1,2,96,1024]{3,2,1,0:T(8,128)}, f32[1,2,96,1024]{3,2,1,0:T(8,128)}) fusion(f32[2,96,1024]{2,1,0:T(8,128)} %get-tuple-element.3, f32[96]{0:T(128)S(1)} %div.27, f32[2,96,1024]{2,1,0:T(8,128)S(1)} %fusion.37, f32[2,96,1024]{2,1,0:T(8,128)S(1)} %copy-done.7, f32[96]{0:T(128)S(1)} %div.25, f32[2,96,1024]{2,1,0:T(8,128)} %copy-done.8, ...), kind=kLoop, calls=%fused_computation.43 | loop fusion | flops 1376256 | bytes 5505792 | tf_op jit(solution)/shard_map/broadcast_in_dim | solution.py:174
  (214 shorter events, 69.6 us)
Async XLA Ops:
  0.6 14.3 %copy-start.19 = (s32[1,2,1024]{2,1,0:T(2,128)S(1)}, s32[1,2,1024]{2,1,0:T(2,128)}, u32[]{:S(2)}) copy-start(s32[1,2,1024]{2,1,0:T(2,128)} %param.12) | copy-start | bytes 24580
  0.6 14.4 %copy-start.16 = (f32[1,2,6,1024]{3,1,2,0:T(2,128)S(1)}, f32[1,2,6,1024]{3,1,2,0:T(2,128)}, u32[]{:S(2)}) copy-start(f32[1,2,6,1024]{3,1,2,0:T(2,128)} %param.10) | copy-start | bytes 147460
  0.7 14.3 %copy-start.18 = (f32[1,2,6,384]{3,1,2,0:T(2,128)S(1)}, f32[1,2,6,384]{3,1,2,0:T(2,128)}, u32[]{:S(2)}) copy-start(f32[1,2,6,384]{3,1,2,0:T(2,128)} %param.11) | copy-start | bytes 55300
  4.1 19.8 %copy-start.20 = (s32[4]{0:T(128)S(1)}, s32[4]{0:T(128)}, u32[]{:S(2)}) copy-start(s32[4]{0:T(128)} %constant.38) | copy-start | bytes 52
  5.4 10.1 %collective-permute-start = (f32[1,28672]{1,0:T(1,128)S(1)}, f32[1,28672]{1,0:T(1,128)S(1)}, u32[]{:S(2)}, u32[]{:S(2)}) collective-permute-start(f32[1,28672]{1,0:T(1,128)S(1)} %get-tuple-element.38), channel_id=1, source_target_pairs={{0,4},{4,8},{8,12},{12,16},{16,20},{20,24},{24,28},{1,5},{5,9},{9,... | collective-permute-start | bytes 344072 | tf_op jit(solution)/shard_map/ppermute | solution.py:20
  8.0 7.7 %collective-permute-start.1 = (f32[1,28672]{1,0:T(1,128)S(1)}, f32[1,28672]{1,0:T(1,128)S(1)}, u32[]{:S(2)}, u32[]{:S(2)}) collective-permute-start(f32[1,28672]{1,0:T(1,128)S(1)} %get-tuple-element.41), channel_id=1, source_target_pairs={{4,0},{8,4},{12,8},{16,12},{20,16},{24,20},{28,24},{5,1},{9,5},{13... | collective-permute-start | bytes 344072 | tf_op jit(solution)/shard_map/ppermute | solution.py:21
  9.3 8.8 %collective-permute-start.2 = (f32[2,28672]{1,0:T(2,128)S(1)}, f32[2,28672]{1,0:T(2,128)S(1)}, u32[]{:S(2)}, u32[]{:S(2)}) collective-permute-start(f32[2,28672]{1,0:T(2,128)S(1)} %get-tuple-element.48), channel_id=1, source_target_pairs={{0,1},{1,2},{2,3},{4,5},{5,6},{6,7},{8,9},{9,10},{10,11},{12,13},{... | collective-permute-start | bytes 688136 | tf_op jit(solution)/shard_map/ppermute | solution.py:24
  13.6 9.2 %collective-permute-start.3 = (f32[2,28672]{1,0:T(2,128)S(1)}, f32[2,28672]{1,0:T(2,128)S(1)}, u32[]{:S(2)}, u32[]{:S(2)}) collective-permute-start(f32[2,28672]{1,0:T(2,128)S(1)} %get-tuple-element.49), channel_id=1, source_target_pairs={{1,0},{2,1},{3,2},{5,4},{6,5},{7,6},{9,8},{10,9},{11,10},{13,12},{... | collective-permute-start | bytes 688136 | tf_op jit(solution)/shard_map/ppermute | solution.py:25
  24.1 5.9 %copy-start.9 = (f32[1,2,96,1024]{3,2,1,0:T(8,128)S(1)}, f32[1,2,96,1024]{3,2,1,0:T(8,128)}, u32[]{:S(2)}) copy-start(f32[1,2,96,1024]{3,2,1,0:T(8,128)} %param.7) | copy-start | bytes 2359300
  31.6 14.8 %all-to-all-start = ((f32[32,1,1153]{2,1,0:T(1,128)}), f32[32,1,1153]{2,1,0:T(1,128)S(1)}, u32[]{:S(2)}, u32[]{:S(2)}) async-start(f32[32,1,1153]{2,1,0:T(1,128)} %broadcast_in_dim.41), calls=%async_computation | async-start | bytes 327680 | tf_op jit(solution)/shard_map/all_to_all | solution.py:124
  38.7 9.6 %copy-start.17 = (f32[2,4,6,384]{3,2,1,0:T(8,128)}, f32[2,4,6,384]{3,2,1,0:T(8,128)S(1)}, u32[]{:S(2)}) copy-start(f32[2,4,6,384]{3,2,1,0:T(8,128)S(1)} %reshape.249) | copy-start | bytes 221188
  67.7 6.6 %collective-permute-start.4 = (f32[1,96,256]{2,1,0:T(8,128)S(1)}, f32[1,96,256]{2,1,0:T(8,128)S(1)}, u32[]{:S(2)}, u32[]{:S(2)}) collective-permute-start(f32[1,96,256]{2,1,0:T(8,128)S(1)} %get-tuple-element.28), channel_id=1, source_target_pairs={{0,4},{4,8},{8,12},{12,16},{16,20},{20,24},{24,28},{1,5},{5,9},{9,... | collective-permute-start | bytes 294920 | tf_op jit(solution)/shard_map/ppermute | solution.py:20
  70.0 4.3 %collective-permute-start.5 = (f32[1,96,256]{2,1,0:T(8,128)S(1)}, f32[1,96,256]{2,1,0:T(8,128)S(1)}, u32[]{:S(2)}, u32[]{:S(2)}) collective-permute-start(f32[1,96,256]{2,1,0:T(8,128)S(1)} %get-tuple-element.29), channel_id=1, source_target_pairs={{4,0},{8,4},{12,8},{16,12},{20,16},{24,20},{28,24},{5,1},{9,5},{13... | collective-permute-start | bytes 294920 | tf_op jit(solution)/shard_map/ppermute | solution.py:21
  71.3 6.6 %collective-permute-start.6 = (f32[2,96,256]{2,1,0:T(8,128)S(1)}, f32[2,96,256]{2,1,0:T(8,128)S(1)}, u32[]{:S(2)}, u32[]{:S(2)}) collective-permute-start(f32[2,96,256]{2,1,0:T(8,128)S(1)} %get-tuple-element.32), channel_id=1, source_target_pairs={{0,1},{1,2},{2,3},{4,5},{5,6},{6,7},{8,9},{9,10},{10,11},{12,13},{... | collective-permute-start | bytes 589832 | tf_op jit(solution)/shard_map/ppermute | solution.py:24
  73.0 9.5 %collective-permute-start.7 = (f32[2,96,256]{2,1,0:T(8,128)S(1)}, f32[2,96,256]{2,1,0:T(8,128)S(1)}, u32[]{:S(2)}, u32[]{:S(2)}) collective-permute-start(f32[2,96,256]{2,1,0:T(8,128)S(1)} %get-tuple-element.33), channel_id=1, source_target_pairs={{1,0},{2,1},{3,2},{5,4},{6,5},{7,6},{9,8},{10,9},{11,10},{13,12},{... | collective-permute-start | bytes 589832 | tf_op jit(solution)/shard_map/ppermute | solution.py:25
  104.6 17.2 %copy-start = (f32[2,96,1024]{2,1,0:T(8,128)}, f32[2,96,1024]{2,1,0:T(8,128)S(1)}, u32[]{:S(2)}) copy-start(f32[2,96,1024]{2,1,0:T(8,128)S(1)} %sub.94) | copy-start | bytes 2359300
  105.5 6.6 %collective-permute-start.8 = (f32[1,96,256]{2,1,0:T(8,128)S(1)}, f32[1,96,256]{2,1,0:T(8,128)S(1)}, u32[]{:S(2)}, u32[]{:S(2)}) collective-permute-start(f32[1,96,256]{2,1,0:T(8,128)S(1)} %get-tuple-element.22), channel_id=1, source_target_pairs={{0,4},{4,8},{8,12},{12,16},{16,20},{20,24},{24,28},{1,5},{5,9},{9,... | collective-permute-start | bytes 294920 | tf_op jit(solution)/shard_map/ppermute | solution.py:20
  107.8 4.3 %collective-permute-start.9 = (f32[1,96,256]{2,1,0:T(8,128)S(1)}, f32[1,96,256]{2,1,0:T(8,128)S(1)}, u32[]{:S(2)}, u32[]{:S(2)}) collective-permute-start(f32[1,96,256]{2,1,0:T(8,128)S(1)} %get-tuple-element.23), channel_id=1, source_target_pairs={{4,0},{8,4},{12,8},{16,12},{20,16},{24,20},{28,24},{5,1},{9,5},{13... | collective-permute-start | bytes 294920 | tf_op jit(solution)/shard_map/ppermute | solution.py:21
  109.1 6.6 %collective-permute-start.10 = (f32[2,96,256]{2,1,0:T(8,128)S(1)}, f32[2,96,256]{2,1,0:T(8,128)S(1)}, u32[]{:S(2)}, u32[]{:S(2)}) collective-permute-start(f32[2,96,256]{2,1,0:T(8,128)S(1)} %get-tuple-element.26), channel_id=1, source_target_pairs={{0,1},{1,2},{2,3},{4,5},{5,6},{6,7},{8,9},{9,10},{10,11},{12,13},{... | collective-permute-start | bytes 589832 | tf_op jit(solution)/shard_map/ppermute | solution.py:24
  110.8 9.5 %collective-permute-start.11 = (f32[2,96,256]{2,1,0:T(8,128)S(1)}, f32[2,96,256]{2,1,0:T(8,128)S(1)}, u32[]{:S(2)}, u32[]{:S(2)}) collective-permute-start(f32[2,96,256]{2,1,0:T(8,128)S(1)} %get-tuple-element.27), channel_id=1, source_target_pairs={{1,0},{2,1},{3,2},{5,4},{6,5},{7,6},{9,8},{10,9},{11,10},{13,12},{... | collective-permute-start | bytes 589832 | tf_op jit(solution)/shard_map/ppermute | solution.py:25
  124.5 12.5 %all-to-all-start.3 = ((f32[32,1,1248]{2,1,0:T(1,128)}), f32[32,1,1248]{2,1,0:T(1,128)}, u32[]{:S(2)}, u32[]{:S(2)}) async-start(f32[32,1,1248]{2,1,0:T(1,128)} %broadcast_in_dim.47), calls=%async_computation.3 | async-start | bytes 327680 | tf_op jit(solution)/shard_map/all_to_all | solution.py:124
  144.7 6.8 %collective-permute-start.12 = (f32[1,96,256]{2,1,0:T(8,128)S(1)}, f32[1,96,256]{2,1,0:T(8,128)S(1)}, u32[]{:S(2)}, u32[]{:S(2)}) collective-permute-start(f32[1,96,256]{2,1,0:T(8,128)S(1)} %get-tuple-element.16), channel_id=1, source_target_pairs={{0,4},{4,8},{8,12},{12,16},{16,20},{20,24},{24,28},{1,5},{5,9},{9,... | collective-permute-start | bytes 294920 | tf_op jit(solution)/shard_map/ppermute | solution.py:20
  147.0 4.5 %collective-permute-start.13 = (f32[1,96,256]{2,1,0:T(8,128)S(1)}, f32[1,96,256]{2,1,0:T(8,128)S(1)}, u32[]{:S(2)}, u32[]{:S(2)}) collective-permute-start(f32[1,96,256]{2,1,0:T(8,128)S(1)} %get-tuple-element.17), channel_id=1, source_target_pairs={{4,0},{8,4},{12,8},{16,12},{20,16},{24,20},{28,24},{5,1},{9,5},{13... | collective-permute-start | bytes 294920 | tf_op jit(solution)/shard_map/ppermute | solution.py:21
  148.3 6.6 %collective-permute-start.14 = (f32[2,96,256]{2,1,0:T(8,128)S(1)}, f32[2,96,256]{2,1,0:T(8,128)S(1)}, u32[]{:S(2)}, u32[]{:S(2)}) collective-permute-start(f32[2,96,256]{2,1,0:T(8,128)S(1)} %get-tuple-element.20), channel_id=1, source_target_pairs={{0,1},{1,2},{2,3},{4,5},{5,6},{6,7},{8,9},{9,10},{10,11},{12,13},{... | collective-permute-start | bytes 589832 | tf_op jit(solution)/shard_map/ppermute | solution.py:24
  150.0 9.5 %collective-permute-start.15 = (f32[2,96,256]{2,1,0:T(8,128)S(1)}, f32[2,96,256]{2,1,0:T(8,128)S(1)}, u32[]{:S(2)}, u32[]{:S(2)}) collective-permute-start(f32[2,96,256]{2,1,0:T(8,128)S(1)} %get-tuple-element.21), channel_id=1, source_target_pairs={{1,0},{2,1},{3,2},{5,4},{6,5},{7,6},{9,8},{10,9},{11,10},{13,12},{... | collective-permute-start | bytes 589832 | tf_op jit(solution)/shard_map/ppermute | solution.py:25
  179.7 17.2 %copy-start.8 = (f32[2,96,1024]{2,1,0:T(8,128)}, f32[2,96,1024]{2,1,0:T(8,128)S(1)}, u32[]{:S(2)}) copy-start(f32[2,96,1024]{2,1,0:T(8,128)S(1)} %multiply_add_fusion) | copy-start | bytes 2359300
  180.5 6.6 %collective-permute-start.16 = (f32[1,96,256]{2,1,0:T(8,128)S(1)}, f32[1,96,256]{2,1,0:T(8,128)S(1)}, u32[]{:S(2)}, u32[]{:S(2)}) collective-permute-start(f32[1,96,256]{2,1,0:T(8,128)S(1)} %get-tuple-element.10), channel_id=1, source_target_pairs={{0,4},{4,8},{8,12},{12,16},{16,20},{20,24},{24,28},{1,5},{5,9},{9,... | collective-permute-start | bytes 294920 | tf_op jit(solution)/shard_map/ppermute | solution.py:20
  182.9 4.3 %collective-permute-start.17 = (f32[1,96,256]{2,1,0:T(8,128)S(1)}, f32[1,96,256]{2,1,0:T(8,128)S(1)}, u32[]{:S(2)}, u32[]{:S(2)}) collective-permute-start(f32[1,96,256]{2,1,0:T(8,128)S(1)} %get-tuple-element.11), channel_id=1, source_target_pairs={{4,0},{8,4},{12,8},{16,12},{20,16},{24,20},{28,24},{5,1},{9,5},{13... | collective-permute-start | bytes 294920 | tf_op jit(solution)/shard_map/ppermute | solution.py:21
  184.2 6.6 %collective-permute-start.18 = (f32[2,96,256]{2,1,0:T(8,128)S(1)}, f32[2,96,256]{2,1,0:T(8,128)S(1)}, u32[]{:S(2)}, u32[]{:S(2)}) collective-permute-start(f32[2,96,256]{2,1,0:T(8,128)S(1)} %get-tuple-element.14), channel_id=1, source_target_pairs={{0,1},{1,2},{2,3},{4,5},{5,6},{6,7},{8,9},{9,10},{10,11},{12,13},{... | collective-permute-start | bytes 589832 | tf_op jit(solution)/shard_map/ppermute | solution.py:24
  185.9 9.5 %collective-permute-start.19 = (f32[2,96,256]{2,1,0:T(8,128)S(1)}, f32[2,96,256]{2,1,0:T(8,128)S(1)}, u32[]{:S(2)}, u32[]{:S(2)}) collective-permute-start(f32[2,96,256]{2,1,0:T(8,128)S(1)} %get-tuple-element.15), channel_id=1, source_target_pairs={{1,0},{2,1},{3,2},{5,4},{6,5},{7,6},{9,8},{10,9},{11,10},{13,12},{... | collective-permute-start | bytes 589832 | tf_op jit(solution)/shard_map/ppermute | solution.py:25
  196.8 12.2 %copy-start.1 = (f32[2,96,1024]{2,1,0:T(8,128)S(1)}, f32[2,96,1024]{2,1,0:T(8,128)}, u32[]{:S(2)}) copy-start(f32[2,96,1024]{2,1,0:T(8,128)} %copy-done) | copy-start | bytes 2359300
  196.8 12.2 %copy-start.7 = (f32[2,96,1024]{2,1,0:T(8,128)S(1)}, f32[2,96,1024]{2,1,0:T(8,128)}, u32[]{:S(2)}) copy-start(f32[2,96,1024]{2,1,0:T(8,128)} %copy-done.6) | copy-start | bytes 2359300
  (11 other events, 21.1 us)

commit v7 on v6

--- a/solution.py
+++ b/solution.py
@@ -67,26 +67,16 @@
     gap_faces = face_split(vectors)
     mode_faces = face_split(own_modes)
     map_faces = face_split(maps.astype(jnp.float32)[:, None, :])
-    own_rows = coarse_op[0]
-    gap_size = columns * quarter
+    own_rows = coarse_op[0].reshape(subdomains, -1, quarter)
     packs = [
-        jnp.concatenate(
-            [
-                gap_faces[g].reshape(subdomains, -1),
-                mode_faces[g].reshape(subdomains, -1),
-                map_faces[g].reshape(subdomains, -1),
-                own_rows.reshape(subdomains, -1),
-            ],
-            axis=1,
-        )
+        jnp.concatenate([gap_faces[g], mode_faces[g], map_faces[g], own_rows], axis=1)
         for g in range(4)
     ]
     partner_pack = neighbors(*packs)
-    partner_gaps = partner_pack[:, :, :gap_size].reshape(subdomains, 4, columns, quarter)
-    partner_pack = partner_pack[:, :, gap_size:]
-    partner_raw_modes = partner_pack[:, :, : MODES * quarter].reshape(subdomains, 4, MODES, quarter)
-    partner_map = partner_pack[:, :, MODES * quarter:(MODES + 1) * quarter]
-    partner_rows = partner_pack[:, :, (MODES + 1) * quarter:].reshape(
+    partner_gaps = partner_pack[:, :, :columns]
+    partner_raw_modes = partner_pack[:, :, columns:columns + MODES]
+    partner_map = partner_pack[:, :, columns + MODES]
+    partner_rows = partner_pack[:, :, columns + MODES + 1:].reshape(
         subdomains, 4, MODES, coarse_total
     )
 

time: 213 us -> 206 us (0.967)
  matrix products: 23.3 us -> 18.6 us
  other arithmetic: 22.1 us -> 19.1 us
    dot_general x5, matrix products: 4.97 us -> 1.4 us  [lift(): jnp.einsum('sfkc,cn->skfn', partner_rows, flat, precision=HIGHEST)]
    unnamed x55 -> x46, local copies, waits for them, and re-layouts: 8.12 us -> 7.74 us
where the time goes in v7:
time: 206 us; the launch traced here: 205 us
  waiting for transfers between devices  54.4 us (26%)
  blocking collectives  45.9 us (22%)
  starting transfers between devices  45.6 us (22%)
  local copies, waits for them, and re-layouts  19.6 us (10%)
  other arithmetic  19.1 us (9%)
  matrix products  18.6 us (9%)
    all_to_all x4, blocking collectives, gathered(): everything = lax.all_to_all(copies, ('grp', 'sub'), 0, 0, tiled=True)  45.9 us
    ppermute x5, waiting for transfers between devices, neighbors(): from_above = lax.ppermute(d2, 'grp', down_grp)  23.2 us
    ppermute x5, waiting for transfers between devices, neighbors(): from_below = lax.ppermute(d3, 'grp', up_grp)  16.7 us
    all_to_all x2, waiting for transfers between devices, gathered(): everything = lax.all_to_all(copies, ('grp', 'sub'), 0, 0, tiled=True)  14.6 us
    ppermute x5, starting transfers between devices, neighbors(): left_dev = lax.ppermute(d1[-1:], 'sub', up_sub)  11.5 us
    ppermute x5, starting transfers between devices, neighbors(): from_below = lax.ppermute(d3, 'grp', up_grp)  11 us
    all_to_all x2, starting transfers between devices, gathered(): everything = lax.all_to_all(copies, ('grp', 'sub'), 0, 0, tiled=True)  10.2 us
    dot_general x6, matrix products, to_mine(): return jnp.einsum('sfcq,sfqr->sfcr', raw, permutes, precision=HIGHEST)  8.1 us
  transfers between devices with their start and end apart: 22, of which 12 were waited for; matrix products, arithmetic and copies ran while one was open for 2% of the time, Pallas kernels for 0%

profile of v7, /device:TPU:0, one launch (start us, length us, event | category | flops | bytes accessed | tf_op | source)
XLA Modules:
  0.0 205.1 jit_solution(1860661704032412449)
XLA Ops:
  4.4 2.4 %collective-permute-start = (f32[1,112,256]{2,1,0:T(8,128)S(1)}, f32[1,112,256]{2,1,0:T(8,128)S(1)}, u32[]{:S(2)}, u32[]{:S(2)}) collective-permute-start(f32[1,112,256]{2,1,0:T(8,128)S(1)} %get-tuple-element.38), channel_id=1, source_target_pairs={{0,4},{4,8},{8,12},{12,16},{16,20},{20,24},{24,28},{1,5},{5,9},{9,... | collective-permute-start | bytes 344072 | tf_op jit(solution)/shard_map/ppermute | solution.py:20
  8.1 4.3 %collective-permute-start.2 = (f32[2,112,256]{2,1,0:T(8,128)S(1)}, f32[2,112,256]{2,1,0:T(8,128)S(1)}, u32[]{:S(2)}, u32[]{:S(2)}) collective-permute-start(f32[2,112,256]{2,1,0:T(8,128)S(1)} %get-tuple-element.48), channel_id=1, source_target_pairs={{0,1},{1,2},{2,3},{4,5},{5,6},{6,7},{8,9},{9,10},{10,11},{12,13},{... | collective-permute-start | bytes 688136 | tf_op jit(solution)/shard_map/ppermute | solution.py:24
  14.3 2.6 %collective-permute-done.2 = f32[2,112,256]{2,1,0:T(8,128)S(1)} collective-permute-done((f32[2,112,256]{2,1,0:T(8,128)S(1)}, f32[2,112,256]{2,1,0:T(8,128)S(1)}, u32[]{:S(2)}, u32[]{:S(2)}) %collective-permute-start.2) | collective-permute-done | bytes 229408 | tf_op jit(solution)/shard_map/ppermute | solution.py:24
  16.9 4.7 %collective-permute-done.3 = f32[2,112,256]{2,1,0:T(8,128)S(1)} collective-permute-done((f32[2,112,256]{2,1,0:T(8,128)S(1)}, f32[2,112,256]{2,1,0:T(8,128)S(1)}, u32[]{:S(2)}, u32[]{:S(2)}) %collective-permute-start.3) | collective-permute-done | bytes 229408 | tf_op jit(solution)/shard_map/ppermute | solution.py:25
  26.8 6.2 %all-to-all-start = ((f32[32,1,1153]{2,1,0:T(1,128)}), f32[32,1,1153]{2,1,0:T(1,128)S(1)}, u32[]{:S(2)}, u32[]{:S(2)}) async-start(f32[32,1,1153]{2,1,0:T(1,128)} %broadcast_in_dim.41), calls=%async_computation | async-start | bytes 327680 | tf_op jit(solution)/shard_map/all_to_all | solution.py:114
  34.8 6.8 %all-to-all-done = f32[32,1,1153]{2,1,0:T(1,128)S(1)} async-done(((f32[32,1,1153]{2,1,0:T(1,128)}), f32[32,1,1153]{2,1,0:T(1,128)S(1)}, u32[]{:S(2)}, u32[]{:S(2)}) %all-to-all-start) | async-done | bytes 147616 | tf_op jit(solution)/shard_map/all_to_all | solution.py:114
  43.5 1.5 fusion.50
  46.0 10.7 %all_to_all.51 = f32[32,1,1153]{2,1,0:T(1,128)S(1)} all-to-all(f32[32,1,1153]{2,1,0:T(1,128)S(1)} %broadcast_in_dim.43), channel_id=1, replica_groups=mesh['sub'=8,'grp'=4] {'grp','sub'}, dimensions={0} | all-to-all | bytes 295168 | tf_op jit(solution)/shard_map/all_to_all | solution.py:114
  62.0 2.3 %collective-permute-start.4 = (f32[1,96,256]{2,1,0:T(8,128)S(1)}, f32[1,96,256]{2,1,0:T(8,128)S(1)}, u32[]{:S(2)}, u32[]{:S(2)}) collective-permute-start(f32[1,96,256]{2,1,0:T(8,128)S(1)} %get-tuple-element.28), channel_id=1, source_target_pairs={{0,4},{4,8},{8,12},{12,16},{16,20},{20,24},{24,28},{1,5},{5,9},{9,... | collective-permute-start | bytes 294920 | tf_op jit(solution)/shard_map/ppermute | solution.py:20
  65.7 1.7 collective-permute-start.6
  68.7 3.5 %collective-permute-done.6 = f32[2,96,256]{2,1,0:T(8,128)S(1)} collective-permute-done((f32[2,96,256]{2,1,0:T(8,128)S(1)}, f32[2,96,256]{2,1,0:T(8,128)S(1)}, u32[]{:S(2)}, u32[]{:S(2)}) %collective-permute-start.6) | collective-permute-done | bytes 196640 | tf_op jit(solution)/shard_map/ppermute | solution.py:24
  72.2 4.6 %collective-permute-done.7 = f32[2,96,256]{2,1,0:T(8,128)S(1)} collective-permute-done((f32[2,96,256]{2,1,0:T(8,128)S(1)}, f32[2,96,256]{2,1,0:T(8,128)S(1)}, u32[]{:S(2)}, u32[]{:S(2)}) %collective-permute-start.7) | collective-permute-done | bytes 196640 | tf_op jit(solution)/shard_map/ppermute | solution.py:25
  80.4 12.2 %all_to_all.52 = f32[32,1,1248]{2,1,0:T(1,128)S(1)} all-to-all(f32[32,1,1248]{2,1,0:T(1,128)S(1)} %broadcast_in_dim.45), channel_id=1, replica_groups=mesh['sub'=8,'grp'=4] {'grp','sub'}, dimensions={0} | all-to-all | bytes 319488 | tf_op jit(solution)/shard_map/all_to_all | solution.py:114
  98.9 2.3 %collective-permute-start.8 = (f32[1,96,256]{2,1,0:T(8,128)S(1)}, f32[1,96,256]{2,1,0:T(8,128)S(1)}, u32[]{:S(2)}, u32[]{:S(2)}) collective-permute-start(f32[1,96,256]{2,1,0:T(8,128)S(1)} %get-tuple-element.22), channel_id=1, source_target_pairs={{0,4},{4,8},{8,12},{12,16},{16,20},{20,24},{24,28},{1,5},{5,9},{9,... | collective-permute-start | bytes 294920 | tf_op jit(solution)/shard_map/ppermute | solution.py:20
  102.5 1.7 collective-permute-start.10
  105.6 3.5 %collective-permute-done.10 = f32[2,96,256]{2,1,0:T(8,128)S(1)} collective-permute-done((f32[2,96,256]{2,1,0:T(8,128)S(1)}, f32[2,96,256]{2,1,0:T(8,128)S(1)}, u32[]{:S(2)}, u32[]{:S(2)}) %collective-permute-start.10) | collective-permute-done | bytes 196640 | tf_op jit(solution)/shard_map/ppermute | solution.py:24
  109.1 4.6 %collective-permute-done.11 = f32[2,96,256]{2,1,0:T(8,128)S(1)} collective-permute-done((f32[2,96,256]{2,1,0:T(8,128)S(1)}, f32[2,96,256]{2,1,0:T(8,128)S(1)}, u32[]{:S(2)}, u32[]{:S(2)}) %collective-permute-start.11) | collective-permute-done | bytes 196640 | tf_op jit(solution)/shard_map/ppermute | solution.py:25
  117.9 4.0 %all-to-all-start.3 = ((f32[32,1,1248]{2,1,0:T(1,128)}), f32[32,1,1248]{2,1,0:T(1,128)}, u32[]{:S(2)}, u32[]{:S(2)}) async-start(f32[32,1,1248]{2,1,0:T(1,128)} %broadcast_in_dim.47), calls=%async_computation.3 | async-start | bytes 327680 | tf_op jit(solution)/shard_map/all_to_all | solution.py:114
  122.6 7.8 %all-to-all-done.3 = f32[32,1,1248]{2,1,0:T(1,128)} async-done(((f32[32,1,1248]{2,1,0:T(1,128)}), f32[32,1,1248]{2,1,0:T(1,128)}, u32[]{:S(2)}, u32[]{:S(2)}) %all-to-all-start.3) | async-done | bytes 159776 | tf_op jit(solution)/shard_map/all_to_all | solution.py:114
  134.9 1.4 fusion.26
  137.2 2.3 %collective-permute-start.12 = (f32[1,96,256]{2,1,0:T(8,128)S(1)}, f32[1,96,256]{2,1,0:T(8,128)S(1)}, u32[]{:S(2)}, u32[]{:S(2)}) collective-permute-start(f32[1,96,256]{2,1,0:T(8,128)S(1)} %get-tuple-element.16), channel_id=1, source_target_pairs={{0,4},{4,8},{8,12},{12,16},{16,20},{20,24},{24,28},{1,5},{5,9},{9,... | collective-permute-start | bytes 294920 | tf_op jit(solution)/shard_map/ppermute | solution.py:20
  140.8 1.7 collective-permute-start.14
  143.9 3.5 %collective-permute-done.14 = f32[2,96,256]{2,1,0:T(8,128)S(1)} collective-permute-done((f32[2,96,256]{2,1,0:T(8,128)S(1)}, f32[2,96,256]{2,1,0:T(8,128)S(1)}, u32[]{:S(2)}, u32[]{:S(2)}) %collective-permute-start.14) | collective-permute-done | bytes 196640 | tf_op jit(solution)/shard_map/ppermute | solution.py:24
  147.4 4.6 %collective-permute-done.15 = f32[2,96,256]{2,1,0:T(8,128)S(1)} collective-permute-done((f32[2,96,256]{2,1,0:T(8,128)S(1)}, f32[2,96,256]{2,1,0:T(8,128)S(1)}, u32[]{:S(2)}, u32[]{:S(2)}) %collective-permute-start.15) | collective-permute-done | bytes 196640 | tf_op jit(solution)/shard_map/ppermute | solution.py:25
  155.5 12.2 %all_to_all.53 = f32[32,1,1248]{2,1,0:T(1,128)S(1)} all-to-all(f32[32,1,1248]{2,1,0:T(1,128)S(1)} %broadcast_in_dim.93), channel_id=1, replica_groups=mesh['sub'=8,'grp'=4] {'grp','sub'}, dimensions={0} | all-to-all | bytes 319488 | tf_op jit(solution)/shard_map/all_to_all | solution.py:114
  171.3 1.6 multiply_add_fusion
  173.7 2.3 %collective-permute-start.16 = (f32[1,96,256]{2,1,0:T(8,128)S(1)}, f32[1,96,256]{2,1,0:T(8,128)S(1)}, u32[]{:S(2)}, u32[]{:S(2)}) collective-permute-start(f32[1,96,256]{2,1,0:T(8,128)S(1)} %get-tuple-element.10), channel_id=1, source_target_pairs={{0,4},{4,8},{8,12},{12,16},{16,20},{20,24},{24,28},{1,5},{5,9},{9,... | collective-permute-start | bytes 294920 | tf_op jit(solution)/shard_map/ppermute | solution.py:20
  177.4 1.7 collective-permute-start.18
  180.4 3.5 %collective-permute-done.18 = f32[2,96,256]{2,1,0:T(8,128)S(1)} collective-permute-done((f32[2,96,256]{2,1,0:T(8,128)S(1)}, f32[2,96,256]{2,1,0:T(8,128)S(1)}, u32[]{:S(2)}, u32[]{:S(2)}) %collective-permute-start.18) | collective-permute-done | bytes 196640 | tf_op jit(solution)/shard_map/ppermute | solution.py:24
  183.9 4.6 %collective-permute-done.19 = f32[2,96,256]{2,1,0:T(8,128)S(1)} collective-permute-done((f32[2,96,256]{2,1,0:T(8,128)S(1)}, f32[2,96,256]{2,1,0:T(8,128)S(1)}, u32[]{:S(2)}, u32[]{:S(2)}) %collective-permute-start.19) | collective-permute-done | bytes 196640 | tf_op jit(solution)/shard_map/ppermute | solution.py:25
  191.3 10.8 %all_to_all.54 = f32[32,1,96]{2,1,0:T(1,128)S(1)} all-to-all(f32[32,1,96]{2,1,0:T(1,128)S(1)} %broadcast_in_dim.95), channel_id=1, replica_groups=mesh['sub'=8,'grp'=4] {'grp','sub'}, dimensions={0} | all-to-all | bytes 24576 | tf_op jit(solution)/shard_map/all_to_all | solution.py:114
  202.1 3.0 %subtract_bitcast_fusion = (f32[1,2,96,1024]{3,2,1,0:T(8,128)}, f32[1,2,96,1024]{3,2,1,0:T(8,128)}) fusion(f32[2,96,1024]{2,1,0:T(8,128)} %get-tuple-element.3, f32[96]{0:T(128)S(1)} %div.27, f32[2,96,1024]{2,1,0:T(8,128)S(1)} %fusion.50, f32[2,96,1024]{2,1,0:T(8,128)S(1)} %copy-done.7, f32[96]{0:T(128)S(1)} %div.25, f32[2,96,1024]{2,1,0:T(8,128)} %copy-done.8, ...), kind=kLoop, calls=%fused_computation.44 | loop fusion | flops 1376256 | bytes 5505792 | tf_op jit(solution)/shard_map/broadcast_in_dim | solution.py:164
  (199 shorter events, 62.6 us)
Async XLA Ops:
  0.6 13.1 %copy-start.16 = (s32[1,2,1024]{2,1,0:T(2,128)S(1)}, s32[1,2,1024]{2,1,0:T(2,128)}, u32[]{:S(2)}) copy-start(s32[1,2,1024]{2,1,0:T(2,128)} %param.12) | copy-start | bytes 24580
  0.6 13.2 %copy-start.13 = (f32[1,2,6,1024]{3,1,2,0:T(2,128)S(1)}, f32[1,2,6,1024]{3,1,2,0:T(2,128)}, u32[]{:S(2)}) copy-start(f32[1,2,6,1024]{3,1,2,0:T(2,128)} %param.10) | copy-start | bytes 147460
  3.0 18.8 %copy-start.17 = (s32[4]{0:T(128)S(1)}, s32[4]{0:T(128)}, u32[]{:S(2)}) copy-start(s32[4]{0:T(128)} %constant.38) | copy-start | bytes 52
  4.4 9.9 %collective-permute-start = (f32[1,112,256]{2,1,0:T(8,128)S(1)}, f32[1,112,256]{2,1,0:T(8,128)S(1)}, u32[]{:S(2)}, u32[]{:S(2)}) collective-permute-start(f32[1,112,256]{2,1,0:T(8,128)S(1)} %get-tuple-element.38), channel_id=1, source_target_pairs={{0,4},{4,8},{8,12},{12,16},{16,20},{20,24},{24,28},{1,5},{5,9},{9,... | collective-permute-start | bytes 344072 | tf_op jit(solution)/shard_map/ppermute | solution.py:20
  6.8 7.5 %collective-permute-start.1 = (f32[1,112,256]{2,1,0:T(8,128)S(1)}, f32[1,112,256]{2,1,0:T(8,128)S(1)}, u32[]{:S(2)}, u32[]{:S(2)}) collective-permute-start(f32[1,112,256]{2,1,0:T(8,128)S(1)} %get-tuple-element.41), channel_id=1, source_target_pairs={{4,0},{8,4},{12,8},{16,12},{20,16},{24,20},{28,24},{5,1},{9,5},{13... | collective-permute-start | bytes 344072 | tf_op jit(solution)/shard_map/ppermute | solution.py:21
  8.1 8.8 %collective-permute-start.2 = (f32[2,112,256]{2,1,0:T(8,128)S(1)}, f32[2,112,256]{2,1,0:T(8,128)S(1)}, u32[]{:S(2)}, u32[]{:S(2)}) collective-permute-start(f32[2,112,256]{2,1,0:T(8,128)S(1)} %get-tuple-element.48), channel_id=1, source_target_pairs={{0,1},{1,2},{2,3},{4,5},{5,6},{6,7},{8,9},{9,10},{10,11},{12,13},{... | collective-permute-start | bytes 688136 | tf_op jit(solution)/shard_map/ppermute | solution.py:24
  12.5 9.2 %collective-permute-start.3 = (f32[2,112,256]{2,1,0:T(8,128)S(1)}, f32[2,112,256]{2,1,0:T(8,128)S(1)}, u32[]{:S(2)}, u32[]{:S(2)}) collective-permute-start(f32[2,112,256]{2,1,0:T(8,128)S(1)} %get-tuple-element.49), channel_id=1, source_target_pairs={{1,0},{2,1},{3,2},{5,4},{6,5},{7,6},{9,8},{10,9},{11,10},{13,12},{... | collective-permute-start | bytes 688136 | tf_op jit(solution)/shard_map/ppermute | solution.py:25
  21.7 3.5 %copy-start.9 = (f32[1,2,96,1024]{3,2,1,0:T(8,128)S(1)}, f32[1,2,96,1024]{3,2,1,0:T(8,128)}, u32[]{:S(2)}) copy-start(f32[1,2,96,1024]{3,2,1,0:T(8,128)} %param.7) | copy-start | bytes 2359300
  26.8 14.8 %all-to-all-start = ((f32[32,1,1153]{2,1,0:T(1,128)}), f32[32,1,1153]{2,1,0:T(1,128)S(1)}, u32[]{:S(2)}, u32[]{:S(2)}) async-start(f32[32,1,1153]{2,1,0:T(1,128)} %broadcast_in_dim.41), calls=%async_computation | async-start | bytes 327680 | tf_op jit(solution)/shard_map/all_to_all | solution.py:114
  33.7 8.3 %copy-start.15 = (f32[2,4,6,384]{3,2,1,0:T(8,128)S(1)}, f32[2,4,6,384]{3,2,1,0:T(8,128)}, u32[]{:S(2)}) copy-start(f32[2,4,6,384]{3,2,1,0:T(8,128)} %reshape.199) | copy-start | bytes 221188
  62.0 6.6 %collective-permute-start.4 = (f32[1,96,256]{2,1,0:T(8,128)S(1)}, f32[1,96,256]{2,1,0:T(8,128)S(1)}, u32[]{:S(2)}, u32[]{:S(2)}) collective-permute-start(f32[1,96,256]{2,1,0:T(8,128)S(1)} %get-tuple-element.28), channel_id=1, source_target_pairs={{0,4},{4,8},{8,12},{12,16},{16,20},{20,24},{24,28},{1,5},{5,9},{9,... | collective-permute-start | bytes 294920 | tf_op jit(solution)/shard_map/ppermute | solution.py:20
  64.4 4.3 %collective-permute-start.5 = (f32[1,96,256]{2,1,0:T(8,128)S(1)}, f32[1,96,256]{2,1,0:T(8,128)S(1)}, u32[]{:S(2)}, u32[]{:S(2)}) collective-permute-start(f32[1,96,256]{2,1,0:T(8,128)S(1)} %get-tuple-element.29), channel_id=1, source_target_pairs={{4,0},{8,4},{12,8},{16,12},{20,16},{24,20},{28,24},{5,1},{9,5},{13... | collective-permute-start | bytes 294920 | tf_op jit(solution)/shard_map/ppermute | solution.py:21
  65.7 6.6 %collective-permute-start.6 = (f32[2,96,256]{2,1,0:T(8,128)S(1)}, f32[2,96,256]{2,1,0:T(8,128)S(1)}, u32[]{:S(2)}, u32[]{:S(2)}) collective-permute-start(f32[2,96,256]{2,1,0:T(8,128)S(1)} %get-tuple-element.32), channel_id=1, source_target_pairs={{0,1},{1,2},{2,3},{4,5},{5,6},{6,7},{8,9},{9,10},{10,11},{12,13},{... | collective-permute-start | bytes 589832 | tf_op jit(solution)/shard_map/ppermute | solution.py:24
  67.3 9.5 %collective-permute-start.7 = (f32[2,96,256]{2,1,0:T(8,128)S(1)}, f32[2,96,256]{2,1,0:T(8,128)S(1)}, u32[]{:S(2)}, u32[]{:S(2)}) collective-permute-start(f32[2,96,256]{2,1,0:T(8,128)S(1)} %get-tuple-element.33), channel_id=1, source_target_pairs={{1,0},{2,1},{3,2},{5,4},{6,5},{7,6},{9,8},{10,9},{11,10},{13,12},{... | collective-permute-start | bytes 589832 | tf_op jit(solution)/shard_map/ppermute | solution.py:25
  98.0 17.2 %copy-start = (f32[2,96,1024]{2,1,0:T(8,128)}, f32[2,96,1024]{2,1,0:T(8,128)S(1)}, u32[]{:S(2)}) copy-start(f32[2,96,1024]{2,1,0:T(8,128)S(1)} %sub.98) | copy-start | bytes 2359300
  98.9 6.6 %collective-permute-start.8 = (f32[1,96,256]{2,1,0:T(8,128)S(1)}, f32[1,96,256]{2,1,0:T(8,128)S(1)}, u32[]{:S(2)}, u32[]{:S(2)}) collective-permute-start(f32[1,96,256]{2,1,0:T(8,128)S(1)} %get-tuple-element.22), channel_id=1, source_target_pairs={{0,4},{4,8},{8,12},{12,16},{16,20},{20,24},{24,28},{1,5},{5,9},{9,... | collective-permute-start | bytes 294920 | tf_op jit(solution)/shard_map/ppermute | solution.py:20
  101.2 4.3 %collective-permute-start.9 = (f32[1,96,256]{2,1,0:T(8,128)S(1)}, f32[1,96,256]{2,1,0:T(8,128)S(1)}, u32[]{:S(2)}, u32[]{:S(2)}) collective-permute-start(f32[1,96,256]{2,1,0:T(8,128)S(1)} %get-tuple-element.23), channel_id=1, source_target_pairs={{4,0},{8,4},{12,8},{16,12},{20,16},{24,20},{28,24},{5,1},{9,5},{13... | collective-permute-start | bytes 294920 | tf_op jit(solution)/shard_map/ppermute | solution.py:21
  102.5 6.6 %collective-permute-start.10 = (f32[2,96,256]{2,1,0:T(8,128)S(1)}, f32[2,96,256]{2,1,0:T(8,128)S(1)}, u32[]{:S(2)}, u32[]{:S(2)}) collective-permute-start(f32[2,96,256]{2,1,0:T(8,128)S(1)} %get-tuple-element.26), channel_id=1, source_target_pairs={{0,1},{1,2},{2,3},{4,5},{5,6},{6,7},{8,9},{9,10},{10,11},{12,13},{... | collective-permute-start | bytes 589832 | tf_op jit(solution)/shard_map/ppermute | solution.py:24
  104.2 9.5 %collective-permute-start.11 = (f32[2,96,256]{2,1,0:T(8,128)S(1)}, f32[2,96,256]{2,1,0:T(8,128)S(1)}, u32[]{:S(2)}, u32[]{:S(2)}) collective-permute-start(f32[2,96,256]{2,1,0:T(8,128)S(1)} %get-tuple-element.27), channel_id=1, source_target_pairs={{1,0},{2,1},{3,2},{5,4},{6,5},{7,6},{9,8},{10,9},{11,10},{13,12},{... | collective-permute-start | bytes 589832 | tf_op jit(solution)/shard_map/ppermute | solution.py:25
  117.9 12.5 %all-to-all-start.3 = ((f32[32,1,1248]{2,1,0:T(1,128)}), f32[32,1,1248]{2,1,0:T(1,128)}, u32[]{:S(2)}, u32[]{:S(2)}) async-start(f32[32,1,1248]{2,1,0:T(1,128)} %broadcast_in_dim.47), calls=%async_computation.3 | async-start | bytes 327680 | tf_op jit(solution)/shard_map/all_to_all | solution.py:114
  137.2 6.6 %collective-permute-start.12 = (f32[1,96,256]{2,1,0:T(8,128)S(1)}, f32[1,96,256]{2,1,0:T(8,128)S(1)}, u32[]{:S(2)}, u32[]{:S(2)}) collective-permute-start(f32[1,96,256]{2,1,0:T(8,128)S(1)} %get-tuple-element.16), channel_id=1, source_target_pairs={{0,4},{4,8},{8,12},{12,16},{16,20},{20,24},{24,28},{1,5},{5,9},{9,... | collective-permute-start | bytes 294920 | tf_op jit(solution)/shard_map/ppermute | solution.py:20
  139.5 4.3 %collective-permute-start.13 = (f32[1,96,256]{2,1,0:T(8,128)S(1)}, f32[1,96,256]{2,1,0:T(8,128)S(1)}, u32[]{:S(2)}, u32[]{:S(2)}) collective-permute-start(f32[1,96,256]{2,1,0:T(8,128)S(1)} %get-tuple-element.17), channel_id=1, source_target_pairs={{4,0},{8,4},{12,8},{16,12},{20,16},{24,20},{28,24},{5,1},{9,5},{13... | collective-permute-start | bytes 294920 | tf_op jit(solution)/shard_map/ppermute | solution.py:21
  140.8 6.6 %collective-permute-start.14 = (f32[2,96,256]{2,1,0:T(8,128)S(1)}, f32[2,96,256]{2,1,0:T(8,128)S(1)}, u32[]{:S(2)}, u32[]{:S(2)}) collective-permute-start(f32[2,96,256]{2,1,0:T(8,128)S(1)} %get-tuple-element.20), channel_id=1, source_target_pairs={{0,1},{1,2},{2,3},{4,5},{5,6},{6,7},{8,9},{9,10},{10,11},{12,13},{... | collective-permute-start | bytes 589832 | tf_op jit(solution)/shard_map/ppermute | solution.py:24
  142.5 9.5 %collective-permute-start.15 = (f32[2,96,256]{2,1,0:T(8,128)S(1)}, f32[2,96,256]{2,1,0:T(8,128)S(1)}, u32[]{:S(2)}, u32[]{:S(2)}) collective-permute-start(f32[2,96,256]{2,1,0:T(8,128)S(1)} %get-tuple-element.21), channel_id=1, source_target_pairs={{1,0},{2,1},{3,2},{5,4},{6,5},{7,6},{9,8},{10,9},{11,10},{13,12},{... | collective-permute-start | bytes 589832 | tf_op jit(solution)/shard_map/ppermute | solution.py:25
  170.1 2.8 %copy-start.5 = (bf16[1,2,1024,1024]{3,2,1,0:T(8,128)(2,1)S(1)}, bf16[1,2,1024,1024]{3,2,1,0:T(8,128)(2,1)}, u32[]{:S(2)}) copy-start(bf16[1,2,1024,1024]{3,2,1,0:T(8,128)(2,1)} %param.8) | copy-start | bytes 12582916
  172.9 17.2 %copy-start.8 = (f32[2,96,1024]{2,1,0:T(8,128)}, f32[2,96,1024]{2,1,0:T(8,128)S(1)}, u32[]{:S(2)}) copy-start(f32[2,96,1024]{2,1,0:T(8,128)S(1)} %multiply_add_fusion) | copy-start | bytes 2359300
  173.7 6.6 %collective-permute-start.16 = (f32[1,96,256]{2,1,0:T(8,128)S(1)}, f32[1,96,256]{2,1,0:T(8,128)S(1)}, u32[]{:S(2)}, u32[]{:S(2)}) collective-permute-start(f32[1,96,256]{2,1,0:T(8,128)S(1)} %get-tuple-element.10), channel_id=1, source_target_pairs={{0,4},{4,8},{8,12},{12,16},{16,20},{20,24},{24,28},{1,5},{5,9},{9,... | collective-permute-start | bytes 294920 | tf_op jit(solution)/shard_map/ppermute | solution.py:20
  176.1 4.3 %collective-permute-start.17 = (f32[1,96,256]{2,1,0:T(8,128)S(1)}, f32[1,96,256]{2,1,0:T(8,128)S(1)}, u32[]{:S(2)}, u32[]{:S(2)}) collective-permute-start(f32[1,96,256]{2,1,0:T(8,128)S(1)} %get-tuple-element.11), channel_id=1, source_target_pairs={{4,0},{8,4},{12,8},{16,12},{20,16},{24,20},{28,24},{5,1},{9,5},{13... | collective-permute-start | bytes 294920 | tf_op jit(solution)/shard_map/ppermute | solution.py:21
  177.4 6.6 %collective-permute-start.18 = (f32[2,96,256]{2,1,0:T(8,128)S(1)}, f32[2,96,256]{2,1,0:T(8,128)S(1)}, u32[]{:S(2)}, u32[]{:S(2)}) collective-permute-start(f32[2,96,256]{2,1,0:T(8,128)S(1)} %get-tuple-element.14), channel_id=1, source_target_pairs={{0,1},{1,2},{2,3},{4,5},{5,6},{6,7},{8,9},{9,10},{10,11},{12,13},{... | collective-permute-start | bytes 589832 | tf_op jit(solution)/shard_map/ppermute | solution.py:24
  179.0 9.5 %collective-permute-start.19 = (f32[2,96,256]{2,1,0:T(8,128)S(1)}, f32[2,96,256]{2,1,0:T(8,128)S(1)}, u32[]{:S(2)}, u32[]{:S(2)}) collective-permute-start(f32[2,96,256]{2,1,0:T(8,128)S(1)} %get-tuple-element.15), channel_id=1, source_target_pairs={{1,0},{2,1},{3,2},{5,4},{6,5},{7,6},{9,8},{10,9},{11,10},{13,12},{... | collective-permute-start | bytes 589832 | tf_op jit(solution)/shard_map/ppermute | solution.py:25
  189.9 12.2 %copy-start.1 = (f32[2,96,1024]{2,1,0:T(8,128)S(1)}, f32[2,96,1024]{2,1,0:T(8,128)}, u32[]{:S(2)}) copy-start(f32[2,96,1024]{2,1,0:T(8,128)} %copy-done) | copy-start | bytes 2359300
  190.0 12.2 %copy-start.7 = (f32[2,96,1024]{2,1,0:T(8,128)S(1)}, f32[2,96,1024]{2,1,0:T(8,128)}, u32[]{:S(2)}) copy-start(f32[2,96,1024]{2,1,0:T(8,128)} %copy-done.6) | copy-start | bytes 2359300
  (8 other events, 11.5 us)

commit v8 on v7

--- a/solution.py
+++ b/solution.py
@@ -91,8 +91,20 @@
         "sfmt,sfmi->sfti", partner_hot, mine_hot, preferred_element_type=jnp.float32
     )
 
+    permutes_b = permutes.astype(jnp.bfloat16)
+
     def to_mine(raw):
-        return jnp.einsum("sfcq,sfqr->sfcr", raw, permutes, precision=HIGHEST)
+        hi = raw.astype(jnp.bfloat16)
+        rest = raw - hi.astype(jnp.float32)
+        mid = rest.astype(jnp.bfloat16)
+        lo = (rest - mid.astype(jnp.float32)).astype(jnp.bfloat16)
+
+        def moved(part):
+            return jnp.einsum(
+                "sfcq,sfqr->sfcr", part, permutes_b, preferred_element_type=jnp.float32
+            )
+
+        return (moved(hi) + moved(mid)) + moved(lo)
 
     partner_modes = to_mine(partner_raw_modes)
     partner_slot_modes = jnp.moveaxis(partner_modes, 1, 2).reshape(subdomains, MODES, width)

time: 206 us -> 225 us (1.092)
  local copies, waits for them, and re-layouts: 19.6 us -> 27.2 us
  matrix products: 18.6 us -> 25.4 us
  other arithmetic: 19.1 us -> 24.3 us
    dot_general x5, matrix products: 1.19 us -> 4.39 us  [lift(): jnp.dot(rows_here, flat, precision=HIGHEST, preferred_element_type=jnp.fl...]
    sub x4, other arithmetic: 4.36 us -> 1.24 us  [project_with(): return values - lift(flat)]
    dot_general x5, matrix products: 1.4 us -> 4.26 us  [lift(): jnp.einsum('sfkc,cn->skfn', partner_rows, flat, precision=HIGHEST)]
    unnamed x46 -> x62, local copies, waits for them, and re-layouts: 7.74 us -> 9.9 us
    dot_general x6 -> x18, matrix products: 8.1 us -> 6.85 us  [moved(): jnp.einsum('sfcq,sfqr->sfcr', part, permutes_b, preferred_element_type=jn...]
where the time goes in v8:
time: 225 us; the launch traced here: 223 us
  waiting for transfers between devices  52.2 us (23%)
  blocking collectives  46 us (20%)
  starting transfers between devices  45.9 us (20%)
  local copies, waits for them, and re-layouts  27.2 us (12%)
  matrix products  25.4 us (11%)
  other arithmetic  24.3 us (11%)
    all_to_all x4, blocking collectives, gathered(): everything = lax.all_to_all(copies, ('grp', 'sub'), 0, 0, tiled=True)  46 us
    ppermute x5, waiting for transfers between devices, neighbors(): from_above = lax.ppermute(d2, 'grp', down_grp)  23.2 us
    ppermute x5, waiting for transfers between devices, neighbors(): from_below = lax.ppermute(d3, 'grp', up_grp)  16.7 us
    all_to_all x2, waiting for transfers between devices, gathered(): everything = lax.all_to_all(copies, ('grp', 'sub'), 0, 0, tiled=True)  12.3 us
    ppermute x5, starting transfers between devices, neighbors(): left_dev = lax.ppermute(d1[-1:], 'sub', up_sub)  11.7 us
    ppermute x5, starting transfers between devices, neighbors(): from_below = lax.ppermute(d3, 'grp', up_grp)  11 us
    all_to_all x2, starting transfers between devices, gathered(): everything = lax.all_to_all(copies, ('grp', 'sub'), 0, 0, tiled=True)  10.3 us
    unnamed x62, local copies, waits for them, and re-layouts  9.9 us
  transfers between devices with their start and end apart: 22, of which 12 were waited for; matrix products, arithmetic and copies ran while one was open for 2% of the time, Pallas kernels for 0%

profile of v8, /device:TPU:0, one launch (start us, length us, event | category | flops | bytes accessed | tf_op | source)
XLA Modules:
  0.0 222.8 jit_solution(13262253762994115677)
XLA Ops:
  4.4 2.4 %collective-permute-start = (f32[1,112,256]{2,1,0:T(8,128)S(1)}, f32[1,112,256]{2,1,0:T(8,128)S(1)}, u32[]{:S(2)}, u32[]{:S(2)}) collective-permute-start(f32[1,112,256]{2,1,0:T(8,128)S(1)} %get-tuple-element.46), channel_id=1, source_target_pairs={{0,4},{4,8},{8,12},{12,16},{16,20},{20,24},{24,28},{1,5},{5,9},{9,... | collective-permute-start | bytes 344072 | tf_op jit(solution)/shard_map/ppermute | solution.py:20
  8.1 4.3 %collective-permute-start.2 = (f32[2,112,256]{2,1,0:T(8,128)S(1)}, f32[2,112,256]{2,1,0:T(8,128)S(1)}, u32[]{:S(2)}, u32[]{:S(2)}) collective-permute-start(f32[2,112,256]{2,1,0:T(8,128)S(1)} %get-tuple-element.56), channel_id=1, source_target_pairs={{0,1},{1,2},{2,3},{4,5},{5,6},{6,7},{8,9},{9,10},{10,11},{12,13},{... | collective-permute-start | bytes 688136 | tf_op jit(solution)/shard_map/ppermute | solution.py:24
  14.4 2.6 %collective-permute-done.2 = f32[2,112,256]{2,1,0:T(8,128)S(1)} collective-permute-done((f32[2,112,256]{2,1,0:T(8,128)S(1)}, f32[2,112,256]{2,1,0:T(8,128)S(1)}, u32[]{:S(2)}, u32[]{:S(2)}) %collective-permute-start.2) | collective-permute-done | bytes 229408 | tf_op jit(solution)/shard_map/ppermute | solution.py:24
  16.9 4.7 %collective-permute-done.3 = f32[2,112,256]{2,1,0:T(8,128)S(1)} collective-permute-done((f32[2,112,256]{2,1,0:T(8,128)S(1)}, f32[2,112,256]{2,1,0:T(8,128)S(1)}, u32[]{:S(2)}, u32[]{:S(2)}) %collective-permute-start.3) | collective-permute-done | bytes 229408 | tf_op jit(solution)/shard_map/ppermute | solution.py:25
  27.6 6.3 %all-to-all-start = ((f32[32,1,1153]{2,1,0:T(1,128)}), f32[32,1,1153]{2,1,0:T(1,128)}, u32[]{:S(2)}, u32[]{:S(2)}) async-start(f32[32,1,1153]{2,1,0:T(1,128)} %broadcast_in_dim.41), calls=%async_computation | async-start | bytes 327680 | tf_op jit(solution)/shard_map/all_to_all | solution.py:126
  37.5 5.0 %all-to-all-done = f32[32,1,1153]{2,1,0:T(1,128)} async-done(((f32[32,1,1153]{2,1,0:T(1,128)}), f32[32,1,1153]{2,1,0:T(1,128)}, u32[]{:S(2)}, u32[]{:S(2)}) %all-to-all-start) | async-done | bytes 147616 | tf_op jit(solution)/shard_map/all_to_all | solution.py:126
  45.3 1.8 subtract_reduce_fusion.4
  49.0 10.7 %all_to_all.51 = f32[32,1,1153]{2,1,0:T(1,128)S(1)} all-to-all(f32[32,1,1153]{2,1,0:T(1,128)S(1)} %broadcast_in_dim.43), channel_id=1, replica_groups=mesh['sub'=8,'grp'=4] {'grp','sub'}, dimensions={0} | all-to-all | bytes 295168 | tf_op jit(solution)/shard_map/all_to_all | solution.py:126
  65.8 2.3 %collective-permute-start.4 = (f32[1,96,256]{2,1,0:T(8,128)S(1)}, f32[1,96,256]{2,1,0:T(8,128)S(1)}, u32[]{:S(2)}, u32[]{:S(2)}) collective-permute-start(f32[1,96,256]{2,1,0:T(8,128)S(1)} %get-tuple-element.36), channel_id=1, source_target_pairs={{0,4},{4,8},{8,12},{12,16},{16,20},{20,24},{24,28},{1,5},{5,9},{9,... | collective-permute-start | bytes 294920 | tf_op jit(solution)/shard_map/ppermute | solution.py:20
  72.5 3.5 %collective-permute-done.6 = f32[2,96,256]{2,1,0:T(8,128)S(1)} collective-permute-done((f32[2,96,256]{2,1,0:T(8,128)S(1)}, f32[2,96,256]{2,1,0:T(8,128)S(1)}, u32[]{:S(2)}, u32[]{:S(2)}) %collective-permute-start.6) | collective-permute-done | bytes 196640 | tf_op jit(solution)/shard_map/ppermute | solution.py:24
  76.0 4.6 %collective-permute-done.7 = f32[2,96,256]{2,1,0:T(8,128)S(1)} collective-permute-done((f32[2,96,256]{2,1,0:T(8,128)S(1)}, f32[2,96,256]{2,1,0:T(8,128)S(1)}, u32[]{:S(2)}, u32[]{:S(2)}) %collective-permute-start.7) | collective-permute-done | bytes 196640 | tf_op jit(solution)/shard_map/ppermute | solution.py:25
  83.0 12.2 %all_to_all.52 = f32[32,1,1248]{2,1,0:T(1,128)S(1)} all-to-all(f32[32,1,1248]{2,1,0:T(1,128)S(1)} %broadcast_in_dim.45), channel_id=1, replica_groups=mesh['sub'=8,'grp'=4] {'grp','sub'}, dimensions={0} | all-to-all | bytes 319488 | tf_op jit(solution)/shard_map/all_to_all | solution.py:126
  99.6 2.5 %collective-permute-start.8 = (f32[1,96,256]{2,1,0:T(8,128)S(1)}, f32[1,96,256]{2,1,0:T(8,128)S(1)}, u32[]{:S(2)}, u32[]{:S(2)}) collective-permute-start(f32[1,96,256]{2,1,0:T(8,128)S(1)} %get-tuple-element.28), channel_id=1, source_target_pairs={{0,4},{4,8},{8,12},{12,16},{16,20},{20,24},{24,28},{1,5},{5,9},{9,... | collective-permute-start | bytes 294920 | tf_op jit(solution)/shard_map/ppermute | solution.py:20
  106.5 3.5 %collective-permute-done.10 = f32[2,96,256]{2,1,0:T(8,128)S(1)} collective-permute-done((f32[2,96,256]{2,1,0:T(8,128)S(1)}, f32[2,96,256]{2,1,0:T(8,128)S(1)}, u32[]{:S(2)}, u32[]{:S(2)}) %collective-permute-start.10) | collective-permute-done | bytes 196640 | tf_op jit(solution)/shard_map/ppermute | solution.py:24
  110.0 4.6 %collective-permute-done.11 = f32[2,96,256]{2,1,0:T(8,128)S(1)} collective-permute-done((f32[2,96,256]{2,1,0:T(8,128)S(1)}, f32[2,96,256]{2,1,0:T(8,128)S(1)}, u32[]{:S(2)}, u32[]{:S(2)}) %collective-permute-start.11) | collective-permute-done | bytes 196640 | tf_op jit(solution)/shard_map/ppermute | solution.py:25
  120.8 4.0 %all-to-all-start.3 = ((f32[32,1,1248]{2,1,0:T(1,128)}), f32[32,1,1248]{2,1,0:T(1,128)}, u32[]{:S(2)}, u32[]{:S(2)}) async-start(f32[32,1,1248]{2,1,0:T(1,128)} %broadcast_in_dim.47), calls=%async_computation.3 | async-start | bytes 327680 | tf_op jit(solution)/shard_map/all_to_all | solution.py:126
  126.1 7.3 %all-to-all-done.3 = f32[32,1,1248]{2,1,0:T(1,128)} async-done(((f32[32,1,1248]{2,1,0:T(1,128)}), f32[32,1,1248]{2,1,0:T(1,128)}, u32[]{:S(2)}, u32[]{:S(2)}) %all-to-all-start.3) | async-done | bytes 159776 | tf_op jit(solution)/shard_map/all_to_all | solution.py:126
  138.1 1.7 fusion.48
  139.8 1.7 sub.146
  141.5 1.8 convolution_bitcast_fusion.6
  146.5 1.9 subtract_reduce_fusion.1
  150.2 2.3 %collective-permute-start.12 = (f32[1,96,256]{2,1,0:T(8,128)S(1)}, f32[1,96,256]{2,1,0:T(8,128)S(1)}, u32[]{:S(2)}, u32[]{:S(2)}) collective-permute-start(f32[1,96,256]{2,1,0:T(8,128)S(1)} %get-tuple-element.20), channel_id=1, source_target_pairs={{0,4},{4,8},{8,12},{12,16},{16,20},{20,24},{24,28},{1,5},{5,9},{9,... | collective-permute-start | bytes 294920 | tf_op jit(solution)/shard_map/ppermute | solution.py:20
  156.9 3.5 %collective-permute-done.14 = f32[2,96,256]{2,1,0:T(8,128)S(1)} collective-permute-done((f32[2,96,256]{2,1,0:T(8,128)S(1)}, f32[2,96,256]{2,1,0:T(8,128)S(1)}, u32[]{:S(2)}, u32[]{:S(2)}) %collective-permute-start.14) | collective-permute-done | bytes 196640 | tf_op jit(solution)/shard_map/ppermute | solution.py:24
  160.4 4.6 %collective-permute-done.15 = f32[2,96,256]{2,1,0:T(8,128)S(1)} collective-permute-done((f32[2,96,256]{2,1,0:T(8,128)S(1)}, f32[2,96,256]{2,1,0:T(8,128)S(1)}, u32[]{:S(2)}, u32[]{:S(2)}) %collective-permute-start.15) | collective-permute-done | bytes 196640 | tf_op jit(solution)/shard_map/ppermute | solution.py:25
  170.5 12.2 %all_to_all.53 = f32[32,1,1248]{2,1,0:T(1,128)S(1)} all-to-all(f32[32,1,1248]{2,1,0:T(1,128)S(1)} %broadcast_in_dim.93), channel_id=1, replica_groups=mesh['sub'=8,'grp'=4] {'grp','sub'}, dimensions={0} | all-to-all | bytes 319488 | tf_op jit(solution)/shard_map/all_to_all | solution.py:126
  183.5 1.7 reshape.209
  191.7 2.3 %collective-permute-start.16 = (f32[1,96,256]{2,1,0:T(8,128)S(1)}, f32[1,96,256]{2,1,0:T(8,128)S(1)}, u32[]{:S(2)}, u32[]{:S(2)}) collective-permute-start(f32[1,96,256]{2,1,0:T(8,128)S(1)} %get-tuple-element.12), channel_id=1, source_target_pairs={{0,4},{4,8},{8,12},{12,16},{16,20},{20,24},{24,28},{1,5},{5,9},{9,... | collective-permute-start | bytes 294920 | tf_op jit(solution)/shard_map/ppermute | solution.py:20
  195.4 1.7 collective-permute-start.18
  198.4 3.5 %collective-permute-done.18 = f32[2,96,256]{2,1,0:T(8,128)S(1)} collective-permute-done((f32[2,96,256]{2,1,0:T(8,128)S(1)}, f32[2,96,256]{2,1,0:T(8,128)S(1)}, u32[]{:S(2)}, u32[]{:S(2)}) %collective-permute-start.18) | collective-permute-done | bytes 196640 | tf_op jit(solution)/shard_map/ppermute | solution.py:24
  201.9 4.6 %collective-permute-done.19 = f32[2,96,256]{2,1,0:T(8,128)S(1)} collective-permute-done((f32[2,96,256]{2,1,0:T(8,128)S(1)}, f32[2,96,256]{2,1,0:T(8,128)S(1)}, u32[]{:S(2)}, u32[]{:S(2)}) %collective-permute-start.19) | collective-permute-done | bytes 196640 | tf_op jit(solution)/shard_map/ppermute | solution.py:25
  208.9 10.8 %all_to_all.54 = f32[32,1,96]{2,1,0:T(1,128)S(1)} all-to-all(f32[32,1,96]{2,1,0:T(1,128)S(1)} %broadcast_in_dim.95), channel_id=1, replica_groups=mesh['sub'=8,'grp'=4] {'grp','sub'}, dimensions={0} | all-to-all | bytes 24576 | tf_op jit(solution)/shard_map/all_to_all | solution.py:126
  219.8 3.0 %subtract_bitcast_fusion = (f32[1,2,96,1024]{3,2,1,0:T(8,128)}, f32[1,2,96,1024]{3,2,1,0:T(8,128)}) fusion(f32[2,96,1024]{2,1,0:T(8,128)} %get-tuple-element.3, f32[96]{0:T(128)S(1)} %div.27, f32[2,96,1024]{2,1,0:T(8,128)S(1)} %fusion.75, f32[2,96,1024]{2,1,0:T(8,128)S(1)} %get-tuple-element.7, f32[96]{0:T(128)S(1)} %copy-done.22, ...), kind=kLoop, calls=%fused_computation.52 | loop fusion | flops 1376256 | bytes 5505792 | tf_op jit(solution)/shard_map/broadcast_in_dim | solution.py:176
  (232 shorter events, 81.3 us)
Async XLA Ops:
  0.6 13.1 %copy-start.20 = (s32[1,2,1024]{2,1,0:T(2,128)S(1)}, s32[1,2,1024]{2,1,0:T(2,128)}, u32[]{:S(2)}) copy-start(s32[1,2,1024]{2,1,0:T(2,128)} %param.12) | copy-start | bytes 24580
  0.6 13.2 %copy-start.7 = (f32[1,2,6,1024]{3,1,2,0:T(2,128)S(1)}, f32[1,2,6,1024]{3,1,2,0:T(2,128)}, u32[]{:S(2)}) copy-start(f32[1,2,6,1024]{3,1,2,0:T(2,128)} %param.10) | copy-start | bytes 147460
  4.3 18.1 %copy-start.23 = (s32[4]{0:T(128)S(1)}, s32[4]{0:T(128)}, u32[]{:S(2)}) copy-start(s32[4]{0:T(128)} %constant.38) | copy-start | bytes 52
  4.4 9.9 %collective-permute-start = (f32[1,112,256]{2,1,0:T(8,128)S(1)}, f32[1,112,256]{2,1,0:T(8,128)S(1)}, u32[]{:S(2)}, u32[]{:S(2)}) collective-permute-start(f32[1,112,256]{2,1,0:T(8,128)S(1)} %get-tuple-element.46), channel_id=1, source_target_pairs={{0,4},{4,8},{8,12},{12,16},{16,20},{20,24},{24,28},{1,5},{5,9},{9,... | collective-permute-start | bytes 344072 | tf_op jit(solution)/shard_map/ppermute | solution.py:20
  6.8 7.5 %collective-permute-start.1 = (f32[1,112,256]{2,1,0:T(8,128)S(1)}, f32[1,112,256]{2,1,0:T(8,128)S(1)}, u32[]{:S(2)}, u32[]{:S(2)}) collective-permute-start(f32[1,112,256]{2,1,0:T(8,128)S(1)} %get-tuple-element.49), channel_id=1, source_target_pairs={{4,0},{8,4},{12,8},{16,12},{20,16},{24,20},{28,24},{5,1},{9,5},{13... | collective-permute-start | bytes 344072 | tf_op jit(solution)/shard_map/ppermute | solution.py:21
  8.1 8.8 %collective-permute-start.2 = (f32[2,112,256]{2,1,0:T(8,128)S(1)}, f32[2,112,256]{2,1,0:T(8,128)S(1)}, u32[]{:S(2)}, u32[]{:S(2)}) collective-permute-start(f32[2,112,256]{2,1,0:T(8,128)S(1)} %get-tuple-element.56), channel_id=1, source_target_pairs={{0,1},{1,2},{2,3},{4,5},{5,6},{6,7},{8,9},{9,10},{10,11},{12,13},{... | collective-permute-start | bytes 688136 | tf_op jit(solution)/shard_map/ppermute | solution.py:24
  12.5 9.2 %collective-permute-start.3 = (f32[2,112,256]{2,1,0:T(8,128)S(1)}, f32[2,112,256]{2,1,0:T(8,128)S(1)}, u32[]{:S(2)}, u32[]{:S(2)}) collective-permute-start(f32[2,112,256]{2,1,0:T(8,128)S(1)} %get-tuple-element.57), channel_id=1, source_target_pairs={{1,0},{2,1},{3,2},{5,4},{6,5},{7,6},{9,8},{10,9},{11,10},{13,12},{... | collective-permute-start | bytes 688136 | tf_op jit(solution)/shard_map/ppermute | solution.py:25
  13.8 29.8 %copy-start.10 = (f32[12,384]{1,0:T(8,128)}, f32[12,384]{1,0:T(8,128)S(1)}, u32[]{:S(2)}) copy-start(f32[12,384]{1,0:T(8,128)S(1)} %reshape_squeeze.11) | copy-start | bytes 55300
  14.2 11.4 %copy-start.14 = (f32[1,2,4,256]{3,1,2,0:T(2,128)}, f32[1,2,4,256]{3,1,2,0:T(2,128)S(1)}, u32[]{:S(2)}) copy-start(f32[1,2,4,256]{3,1,2,0:T(2,128)S(1)} %copy.220) | copy-start | bytes 24580
  27.6 14.9 %all-to-all-start = ((f32[32,1,1153]{2,1,0:T(1,128)}), f32[32,1,1153]{2,1,0:T(1,128)}, u32[]{:S(2)}, u32[]{:S(2)}) async-start(f32[32,1,1153]{2,1,0:T(1,128)} %broadcast_in_dim.41), calls=%async_computation | async-start | bytes 327680 | tf_op jit(solution)/shard_map/all_to_all | solution.py:126
  65.8 6.6 %collective-permute-start.4 = (f32[1,96,256]{2,1,0:T(8,128)S(1)}, f32[1,96,256]{2,1,0:T(8,128)S(1)}, u32[]{:S(2)}, u32[]{:S(2)}) collective-permute-start(f32[1,96,256]{2,1,0:T(8,128)S(1)} %get-tuple-element.36), channel_id=1, source_target_pairs={{0,4},{4,8},{8,12},{12,16},{16,20},{20,24},{24,28},{1,5},{5,9},{9,... | collective-permute-start | bytes 294920 | tf_op jit(solution)/shard_map/ppermute | solution.py:20
  68.1 4.3 %collective-permute-start.5 = (f32[1,96,256]{2,1,0:T(8,128)S(1)}, f32[1,96,256]{2,1,0:T(8,128)S(1)}, u32[]{:S(2)}, u32[]{:S(2)}) collective-permute-start(f32[1,96,256]{2,1,0:T(8,128)S(1)} %get-tuple-element.37), channel_id=1, source_target_pairs={{4,0},{8,4},{12,8},{16,12},{20,16},{24,20},{28,24},{5,1},{9,5},{13... | collective-permute-start | bytes 294920 | tf_op jit(solution)/shard_map/ppermute | solution.py:21
  69.4 6.6 %collective-permute-start.6 = (f32[2,96,256]{2,1,0:T(8,128)S(1)}, f32[2,96,256]{2,1,0:T(8,128)S(1)}, u32[]{:S(2)}, u32[]{:S(2)}) collective-permute-start(f32[2,96,256]{2,1,0:T(8,128)S(1)} %get-tuple-element.40), channel_id=1, source_target_pairs={{0,1},{1,2},{2,3},{4,5},{5,6},{6,7},{8,9},{9,10},{10,11},{12,13},{... | collective-permute-start | bytes 589832 | tf_op jit(solution)/shard_map/ppermute | solution.py:24
  71.1 9.5 %collective-permute-start.7 = (f32[2,96,256]{2,1,0:T(8,128)S(1)}, f32[2,96,256]{2,1,0:T(8,128)S(1)}, u32[]{:S(2)}, u32[]{:S(2)}) collective-permute-start(f32[2,96,256]{2,1,0:T(8,128)S(1)} %get-tuple-element.41), channel_id=1, source_target_pairs={{1,0},{2,1},{3,2},{5,4},{6,5},{7,6},{9,8},{10,9},{11,10},{13,12},{... | collective-permute-start | bytes 589832 | tf_op jit(solution)/shard_map/ppermute | solution.py:25
  81.6 14.4 %copy-start.11 = (f32[12,384]{1,0:T(8,128)S(1)}, f32[12,384]{1,0:T(8,128)}, u32[]{:S(2)}) copy-start(f32[12,384]{1,0:T(8,128)} %copy-done.10) | copy-start | bytes 55300
  81.7 14.6 %copy-start.19 = (f32[2,4,6,384]{3,2,1,0:T(8,128)S(1)}, f32[2,4,6,384]{3,2,1,0:T(8,128)}, u32[]{:S(2)}) copy-start(f32[2,4,6,384]{3,2,1,0:T(8,128)} %copy-done.18) | copy-start | bytes 221188
  99.6 6.8 %collective-permute-start.8 = (f32[1,96,256]{2,1,0:T(8,128)S(1)}, f32[1,96,256]{2,1,0:T(8,128)S(1)}, u32[]{:S(2)}, u32[]{:S(2)}) collective-permute-start(f32[1,96,256]{2,1,0:T(8,128)S(1)} %get-tuple-element.28), channel_id=1, source_target_pairs={{0,4},{4,8},{8,12},{12,16},{16,20},{20,24},{24,28},{1,5},{5,9},{9,... | collective-permute-start | bytes 294920 | tf_op jit(solution)/shard_map/ppermute | solution.py:20
  102.2 4.3 %collective-permute-start.9 = (f32[1,96,256]{2,1,0:T(8,128)S(1)}, f32[1,96,256]{2,1,0:T(8,128)S(1)}, u32[]{:S(2)}, u32[]{:S(2)}) collective-permute-start(f32[1,96,256]{2,1,0:T(8,128)S(1)} %get-tuple-element.29), channel_id=1, source_target_pairs={{4,0},{8,4},{12,8},{16,12},{20,16},{24,20},{28,24},{5,1},{9,5},{13... | collective-permute-start | bytes 294920 | tf_op jit(solution)/shard_map/ppermute | solution.py:21
  103.5 6.6 %collective-permute-start.10 = (f32[2,96,256]{2,1,0:T(8,128)S(1)}, f32[2,96,256]{2,1,0:T(8,128)S(1)}, u32[]{:S(2)}, u32[]{:S(2)}) collective-permute-start(f32[2,96,256]{2,1,0:T(8,128)S(1)} %get-tuple-element.32), channel_id=1, source_target_pairs={{0,1},{1,2},{2,3},{4,5},{5,6},{6,7},{8,9},{9,10},{10,11},{12,13},{... | collective-permute-start | bytes 589832 | tf_op jit(solution)/shard_map/ppermute | solution.py:24
  105.1 9.5 %collective-permute-start.11 = (f32[2,96,256]{2,1,0:T(8,128)S(1)}, f32[2,96,256]{2,1,0:T(8,128)S(1)}, u32[]{:S(2)}, u32[]{:S(2)}) collective-permute-start(f32[2,96,256]{2,1,0:T(8,128)S(1)} %get-tuple-element.33), channel_id=1, source_target_pairs={{1,0},{2,1},{3,2},{5,4},{6,5},{7,6},{9,8},{10,9},{11,10},{13,12},{... | collective-permute-start | bytes 589832 | tf_op jit(solution)/shard_map/ppermute | solution.py:25
  120.8 12.5 %all-to-all-start.3 = ((f32[32,1,1248]{2,1,0:T(1,128)}), f32[32,1,1248]{2,1,0:T(1,128)}, u32[]{:S(2)}, u32[]{:S(2)}) async-start(f32[32,1,1248]{2,1,0:T(1,128)} %broadcast_in_dim.47), calls=%async_computation.3 | async-start | bytes 327680 | tf_op jit(solution)/shard_map/all_to_all | solution.py:126
  150.2 6.6 %collective-permute-start.12 = (f32[1,96,256]{2,1,0:T(8,128)S(1)}, f32[1,96,256]{2,1,0:T(8,128)S(1)}, u32[]{:S(2)}, u32[]{:S(2)}) collective-permute-start(f32[1,96,256]{2,1,0:T(8,128)S(1)} %get-tuple-element.20), channel_id=1, source_target_pairs={{0,4},{4,8},{8,12},{12,16},{16,20},{20,24},{24,28},{1,5},{5,9},{9,... | collective-permute-start | bytes 294920 | tf_op jit(solution)/shard_map/ppermute | solution.py:20
  152.6 4.3 %collective-permute-start.13 = (f32[1,96,256]{2,1,0:T(8,128)S(1)}, f32[1,96,256]{2,1,0:T(8,128)S(1)}, u32[]{:S(2)}, u32[]{:S(2)}) collective-permute-start(f32[1,96,256]{2,1,0:T(8,128)S(1)} %get-tuple-element.21), channel_id=1, source_target_pairs={{4,0},{8,4},{12,8},{16,12},{20,16},{24,20},{28,24},{5,1},{9,5},{13... | collective-permute-start | bytes 294920 | tf_op jit(solution)/shard_map/ppermute | solution.py:21
  153.9 6.6 %collective-permute-start.14 = (f32[2,96,256]{2,1,0:T(8,128)S(1)}, f32[2,96,256]{2,1,0:T(8,128)S(1)}, u32[]{:S(2)}, u32[]{:S(2)}) collective-permute-start(f32[2,96,256]{2,1,0:T(8,128)S(1)} %get-tuple-element.24), channel_id=1, source_target_pairs={{0,1},{1,2},{2,3},{4,5},{5,6},{6,7},{8,9},{9,10},{10,11},{12,13},{... | collective-permute-start | bytes 589832 | tf_op jit(solution)/shard_map/ppermute | solution.py:24
  155.5 9.5 %collective-permute-start.15 = (f32[2,96,256]{2,1,0:T(8,128)S(1)}, f32[2,96,256]{2,1,0:T(8,128)S(1)}, u32[]{:S(2)}, u32[]{:S(2)}) collective-permute-start(f32[2,96,256]{2,1,0:T(8,128)S(1)} %get-tuple-element.25), channel_id=1, source_target_pairs={{1,0},{2,1},{3,2},{5,4},{6,5},{7,6},{9,8},{10,9},{11,10},{13,12},{... | collective-permute-start | bytes 589832 | tf_op jit(solution)/shard_map/ppermute | solution.py:25
  190.9 16.8 %copy-start.4 = (f32[2,96,1024]{2,1,0:T(8,128)}, f32[2,96,1024]{2,1,0:T(8,128)S(1)}, u32[]{:S(2)}) copy-start(f32[2,96,1024]{2,1,0:T(8,128)S(1)} %multiply_add_fusion) | copy-start | bytes 2359300
  191.7 6.6 %collective-permute-start.16 = (f32[1,96,256]{2,1,0:T(8,128)S(1)}, f32[1,96,256]{2,1,0:T(8,128)S(1)}, u32[]{:S(2)}, u32[]{:S(2)}) collective-permute-start(f32[1,96,256]{2,1,0:T(8,128)S(1)} %get-tuple-element.12), channel_id=1, source_target_pairs={{0,4},{4,8},{8,12},{12,16},{16,20},{20,24},{24,28},{1,5},{5,9},{9,... | collective-permute-start | bytes 294920 | tf_op jit(solution)/shard_map/ppermute | solution.py:20
  194.1 4.3 %collective-permute-start.17 = (f32[1,96,256]{2,1,0:T(8,128)S(1)}, f32[1,96,256]{2,1,0:T(8,128)S(1)}, u32[]{:S(2)}, u32[]{:S(2)}) collective-permute-start(f32[1,96,256]{2,1,0:T(8,128)S(1)} %get-tuple-element.13), channel_id=1, source_target_pairs={{4,0},{8,4},{12,8},{16,12},{20,16},{24,20},{28,24},{5,1},{9,5},{13... | collective-permute-start | bytes 294920 | tf_op jit(solution)/shard_map/ppermute | solution.py:21
  195.4 6.6 %collective-permute-start.18 = (f32[2,96,256]{2,1,0:T(8,128)S(1)}, f32[2,96,256]{2,1,0:T(8,128)S(1)}, u32[]{:S(2)}, u32[]{:S(2)}) collective-permute-start(f32[2,96,256]{2,1,0:T(8,128)S(1)} %get-tuple-element.16), channel_id=1, source_target_pairs={{0,1},{1,2},{2,3},{4,5},{5,6},{6,7},{8,9},{9,10},{10,11},{12,13},{... | collective-permute-start | bytes 589832 | tf_op jit(solution)/shard_map/ppermute | solution.py:24
  197.0 9.5 %collective-permute-start.19 = (f32[2,96,256]{2,1,0:T(8,128)S(1)}, f32[2,96,256]{2,1,0:T(8,128)S(1)}, u32[]{:S(2)}, u32[]{:S(2)}) collective-permute-start(f32[2,96,256]{2,1,0:T(8,128)S(1)} %get-tuple-element.17), channel_id=1, source_target_pairs={{1,0},{2,1},{3,2},{5,4},{6,5},{7,6},{9,8},{10,9},{11,10},{13,12},{... | collective-permute-start | bytes 589832 | tf_op jit(solution)/shard_map/ppermute | solution.py:25
  207.3 12.5 %copy-start.25 = (f32[96]{0:T(128)S(1)}, f32[96]{0:T(128)}, u32[]{:S(2)}) copy-start(f32[96]{0:T(128)} %copy-done.24) | copy-start | bytes 1156
  207.3 12.5 %copy-start.22 = (f32[96]{0:T(128)S(1)}, f32[96]{0:T(128)}, u32[]{:S(2)}) copy-start(f32[96]{0:T(128)} %copy-done.21) | copy-start | bytes 1156
  (16 other events, 36.4 us)

commit v9 on v7

--- a/solution.py
+++ b/solution.py
@@ -113,7 +113,7 @@
         copies = jnp.broadcast_to(payload[None], (devices, payload.shape[0]))
         everything = lax.all_to_all(copies, ("grp", "sub"), 0, 0, tiled=True)
         count = coeffs.size
-        extras = jnp.sum(everything[:, count:], axis=0)
+        extras = jnp.sum(everything[:, count:], axis=0) if extra.size else None
         if count == 0:
             return None, extras
         flat = everything[:, :count].reshape(-1, columns)
@@ -131,7 +131,7 @@
     def project_with(values, flat):
         return values - lift(flat)
 
-    nothing = jnp.zeros((1,), jnp.float32)
+    nothing = jnp.zeros((0,), jnp.float32)
     dual = vectors - partner_values(partner_gaps, vectors.shape)
     flat_dual, _ = gathered(coefficients(dual), nothing)
     residual = project_with(dual, flat_dual)

time: 206 us -> 211 us (1.024)
  matrix products: 18.6 us -> 23 us
    dot_general x5, matrix products: 1.4 us -> 5.86 us  [lift(): jnp.einsum('sfkc,cn->skfn', partner_rows, flat, precision=HIGHEST)]
    unnamed x46 -> x42, local copies, waits for them, and re-layouts: 7.74 us -> 7.75 us
where the time goes in v9:
time: 211 us; the launch traced here: 210 us
  waiting for transfers between devices  54.1 us (26%)
  starting transfers between devices  45.8 us (22%)
  blocking collectives  45.5 us (22%)
  matrix products  23 us (11%)
  other arithmetic  20.4 us (10%)
  local copies, waits for them, and re-layouts  19 us (9%)
    all_to_all x4, blocking collectives, gathered(): everything = lax.all_to_all(copies, ('grp', 'sub'), 0, 0, tiled=True)  45.5 us
    ppermute x5, waiting for transfers between devices, neighbors(): from_above = lax.ppermute(d2, 'grp', down_grp)  23.2 us
    ppermute x5, waiting for transfers between devices, neighbors(): from_below = lax.ppermute(d3, 'grp', up_grp)  16.5 us
    all_to_all x2, waiting for transfers between devices, gathered(): everything = lax.all_to_all(copies, ('grp', 'sub'), 0, 0, tiled=True)  14.4 us
    ppermute x5, starting transfers between devices, neighbors(): left_dev = lax.ppermute(d1[-1:], 'sub', up_sub)  11.4 us
    ppermute x5, starting transfers between devices, neighbors(): from_below = lax.ppermute(d3, 'grp', up_grp)  11 us
    all_to_all x2, starting transfers between devices, gathered(): everything = lax.all_to_all(copies, ('grp', 'sub'), 0, 0, tiled=True)  10.2 us
    dot_general x6, matrix products, to_mine(): return jnp.einsum('sfcq,sfqr->sfcr', raw, permutes, precision=HIGHEST)  8.09 us
  transfers between devices with their start and end apart: 22, of which 12 were waited for; matrix products, arithmetic and copies ran while one was open for 2% of the time, Pallas kernels for 0%

profile of v9, /device:TPU:0, one launch (start us, length us, event | category | flops | bytes accessed | tf_op | source)
XLA Modules:
  0.0 209.6 jit_solution(8324377258872047548)
XLA Ops:
  4.4 2.4 %collective-permute-start = (f32[1,112,256]{2,1,0:T(8,128)S(1)}, f32[1,112,256]{2,1,0:T(8,128)S(1)}, u32[]{:S(2)}, u32[]{:S(2)}) collective-permute-start(f32[1,112,256]{2,1,0:T(8,128)S(1)} %get-tuple-element.38), channel_id=1, source_target_pairs={{0,4},{4,8},{8,12},{12,16},{16,20},{20,24},{24,28},{1,5},{5,9},{9,... | collective-permute-start | bytes 344072 | tf_op jit(solution)/shard_map/ppermute | solution.py:20
  8.1 4.3 %collective-permute-start.2 = (f32[2,112,256]{2,1,0:T(8,128)S(1)}, f32[2,112,256]{2,1,0:T(8,128)S(1)}, u32[]{:S(2)}, u32[]{:S(2)}) collective-permute-start(f32[2,112,256]{2,1,0:T(8,128)S(1)} %get-tuple-element.48), channel_id=1, source_target_pairs={{0,1},{1,2},{2,3},{4,5},{5,6},{6,7},{8,9},{9,10},{10,11},{12,13},{... | collective-permute-start | bytes 688136 | tf_op jit(solution)/shard_map/ppermute | solution.py:24
  14.3 2.6 %collective-permute-done.2 = f32[2,112,256]{2,1,0:T(8,128)S(1)} collective-permute-done((f32[2,112,256]{2,1,0:T(8,128)S(1)}, f32[2,112,256]{2,1,0:T(8,128)S(1)}, u32[]{:S(2)}, u32[]{:S(2)}) %collective-permute-start.2) | collective-permute-done | bytes 229408 | tf_op jit(solution)/shard_map/ppermute | solution.py:24
  16.9 4.7 %collective-permute-done.3 = f32[2,112,256]{2,1,0:T(8,128)S(1)} collective-permute-done((f32[2,112,256]{2,1,0:T(8,128)S(1)}, f32[2,112,256]{2,1,0:T(8,128)S(1)}, u32[]{:S(2)}, u32[]{:S(2)}) %collective-permute-start.3) | collective-permute-done | bytes 229408 | tf_op jit(solution)/shard_map/ppermute | solution.py:25
  26.8 6.2 %all-to-all-start = ((f32[32,1,1152]{2,1,0:T(1,128)}), f32[32,1,1152]{2,1,0:T(1,128)S(1)}, u32[]{:S(2)}, u32[]{:S(2)}) async-start(f32[32,1,1152]{2,1,0:T(1,128)} %broadcast_in_dim.88), calls=%async_computation | async-start | bytes 294912 | tf_op jit(solution)/shard_map/all_to_all | solution.py:114
  34.8 6.6 %all-to-all-done = f32[32,1,1152]{2,1,0:T(1,128)S(1)} async-done(((f32[32,1,1152]{2,1,0:T(1,128)}), f32[32,1,1152]{2,1,0:T(1,128)S(1)}, u32[]{:S(2)}, u32[]{:S(2)}) %all-to-all-start) | async-done | bytes 147488 | tf_op jit(solution)/shard_map/all_to_all | solution.py:114
  44.5 1.5 fusion.50
  47.0 10.4 %all_to_all.48 = f32[32,1,1152]{2,1,0:T(1,128)S(1)} all-to-all(f32[32,1,1152]{2,1,0:T(1,128)S(1)} %broadcast_in_dim.91), channel_id=1, replica_groups=mesh['sub'=8,'grp'=4] {'grp','sub'}, dimensions={0} | all-to-all | bytes 294912 | tf_op jit(solution)/shard_map/all_to_all | solution.py:114
  63.9 2.2 %collective-permute-start.4 = (f32[1,96,256]{2,1,0:T(8,128)S(1)}, f32[1,96,256]{2,1,0:T(8,128)S(1)}, u32[]{:S(2)}, u32[]{:S(2)}) collective-permute-start(f32[1,96,256]{2,1,0:T(8,128)S(1)} %get-tuple-element.28), channel_id=1, source_target_pairs={{0,4},{4,8},{8,12},{12,16},{16,20},{20,24},{24,28},{1,5},{5,9},{9,... | collective-permute-start | bytes 294920 | tf_op jit(solution)/shard_map/ppermute | solution.py:20
  67.4 1.7 collective-permute-start.6
  69.1 1.5 collective-permute-start.7
  70.7 3.4 %collective-permute-done.6 = f32[2,96,256]{2,1,0:T(8,128)S(1)} collective-permute-done((f32[2,96,256]{2,1,0:T(8,128)S(1)}, f32[2,96,256]{2,1,0:T(8,128)S(1)}, u32[]{:S(2)}, u32[]{:S(2)}) %collective-permute-start.6) | collective-permute-done | bytes 196640 | tf_op jit(solution)/shard_map/ppermute | solution.py:24
  74.1 4.6 %collective-permute-done.7 = f32[2,96,256]{2,1,0:T(8,128)S(1)} collective-permute-done((f32[2,96,256]{2,1,0:T(8,128)S(1)}, f32[2,96,256]{2,1,0:T(8,128)S(1)}, u32[]{:S(2)}, u32[]{:S(2)}) %collective-permute-start.7) | collective-permute-done | bytes 196640 | tf_op jit(solution)/shard_map/ppermute | solution.py:25
  82.2 12.1 %all_to_all.49 = f32[32,1,1248]{2,1,0:T(1,128)S(1)} all-to-all(f32[32,1,1248]{2,1,0:T(1,128)S(1)} %broadcast_in_dim.93), channel_id=1, replica_groups=mesh['sub'=8,'grp'=4] {'grp','sub'}, dimensions={0} | all-to-all | bytes 319488 | tf_op jit(solution)/shard_map/all_to_all | solution.py:114
  101.5 2.3 %collective-permute-start.8 = (f32[1,96,256]{2,1,0:T(8,128)S(1)}, f32[1,96,256]{2,1,0:T(8,128)S(1)}, u32[]{:S(2)}, u32[]{:S(2)}) collective-permute-start(f32[1,96,256]{2,1,0:T(8,128)S(1)} %get-tuple-element.22), channel_id=1, source_target_pairs={{0,4},{4,8},{8,12},{12,16},{16,20},{20,24},{24,28},{1,5},{5,9},{9,... | collective-permute-start | bytes 294920 | tf_op jit(solution)/shard_map/ppermute | solution.py:20
  105.1 1.7 collective-permute-start.10
  108.2 3.5 %collective-permute-done.10 = f32[2,96,256]{2,1,0:T(8,128)S(1)} collective-permute-done((f32[2,96,256]{2,1,0:T(8,128)S(1)}, f32[2,96,256]{2,1,0:T(8,128)S(1)}, u32[]{:S(2)}, u32[]{:S(2)}) %collective-permute-start.10) | collective-permute-done | bytes 196640 | tf_op jit(solution)/shard_map/ppermute | solution.py:24
  111.7 4.6 %collective-permute-done.11 = f32[2,96,256]{2,1,0:T(8,128)S(1)} collective-permute-done((f32[2,96,256]{2,1,0:T(8,128)S(1)}, f32[2,96,256]{2,1,0:T(8,128)S(1)}, u32[]{:S(2)}, u32[]{:S(2)}) %collective-permute-start.11) | collective-permute-done | bytes 196640 | tf_op jit(solution)/shard_map/ppermute | solution.py:25
  120.5 4.0 %all-to-all-start.3 = ((f32[32,1,1248]{2,1,0:T(1,128)}), f32[32,1,1248]{2,1,0:T(1,128)}, u32[]{:S(2)}, u32[]{:S(2)}) async-start(f32[32,1,1248]{2,1,0:T(1,128)} %broadcast_in_dim.95), calls=%async_computation.3 | async-start | bytes 327680 | tf_op jit(solution)/shard_map/all_to_all | solution.py:114
  125.2 7.8 %all-to-all-done.3 = f32[32,1,1248]{2,1,0:T(1,128)} async-done(((f32[32,1,1248]{2,1,0:T(1,128)}), f32[32,1,1248]{2,1,0:T(1,128)}, u32[]{:S(2)}, u32[]{:S(2)}) %all-to-all-start.3) | async-done | bytes 159776 | tf_op jit(solution)/shard_map/all_to_all | solution.py:114
  140.7 2.3 %collective-permute-start.12 = (f32[1,96,256]{2,1,0:T(8,128)S(1)}, f32[1,96,256]{2,1,0:T(8,128)S(1)}, u32[]{:S(2)}, u32[]{:S(2)}) collective-permute-start(f32[1,96,256]{2,1,0:T(8,128)S(1)} %get-tuple-element.16), channel_id=1, source_target_pairs={{0,4},{4,8},{8,12},{12,16},{16,20},{20,24},{24,28},{1,5},{5,9},{9,... | collective-permute-start | bytes 294920 | tf_op jit(solution)/shard_map/ppermute | solution.py:20
  144.3 1.7 collective-permute-start.14
  147.4 3.5 %collective-permute-done.14 = f32[2,96,256]{2,1,0:T(8,128)S(1)} collective-permute-done((f32[2,96,256]{2,1,0:T(8,128)S(1)}, f32[2,96,256]{2,1,0:T(8,128)S(1)}, u32[]{:S(2)}, u32[]{:S(2)}) %collective-permute-start.14) | collective-permute-done | bytes 196640 | tf_op jit(solution)/shard_map/ppermute | solution.py:24
  150.9 4.6 %collective-permute-done.15 = f32[2,96,256]{2,1,0:T(8,128)S(1)} collective-permute-done((f32[2,96,256]{2,1,0:T(8,128)S(1)}, f32[2,96,256]{2,1,0:T(8,128)S(1)}, u32[]{:S(2)}, u32[]{:S(2)}) %collective-permute-start.15) | collective-permute-done | bytes 196640 | tf_op jit(solution)/shard_map/ppermute | solution.py:25
  159.1 12.2 %all_to_all.50 = f32[32,1,1248]{2,1,0:T(1,128)S(1)} all-to-all(f32[32,1,1248]{2,1,0:T(1,128)S(1)} %broadcast_in_dim.97), channel_id=1, replica_groups=mesh['sub'=8,'grp'=4] {'grp','sub'}, dimensions={0} | all-to-all | bytes 319488 | tf_op jit(solution)/shard_map/all_to_all | solution.py:114
  175.7 1.6 multiply_add_fusion
  178.2 2.3 %collective-permute-start.16 = (f32[1,96,256]{2,1,0:T(8,128)S(1)}, f32[1,96,256]{2,1,0:T(8,128)S(1)}, u32[]{:S(2)}, u32[]{:S(2)}) collective-permute-start(f32[1,96,256]{2,1,0:T(8,128)S(1)} %get-tuple-element.10), channel_id=1, source_target_pairs={{0,4},{4,8},{8,12},{12,16},{16,20},{20,24},{24,28},{1,5},{5,9},{9,... | collective-permute-start | bytes 294920 | tf_op jit(solution)/shard_map/ppermute | solution.py:20
  181.8 1.7 collective-permute-start.18
  184.8 3.5 %collective-permute-done.18 = f32[2,96,256]{2,1,0:T(8,128)S(1)} collective-permute-done((f32[2,96,256]{2,1,0:T(8,128)S(1)}, f32[2,96,256]{2,1,0:T(8,128)S(1)}, u32[]{:S(2)}, u32[]{:S(2)}) %collective-permute-start.18) | collective-permute-done | bytes 196640 | tf_op jit(solution)/shard_map/ppermute | solution.py:24
  188.4 4.6 %collective-permute-done.19 = f32[2,96,256]{2,1,0:T(8,128)S(1)} collective-permute-done((f32[2,96,256]{2,1,0:T(8,128)S(1)}, f32[2,96,256]{2,1,0:T(8,128)S(1)}, u32[]{:S(2)}, u32[]{:S(2)}) %collective-permute-start.19) | collective-permute-done | bytes 196640 | tf_op jit(solution)/shard_map/ppermute | solution.py:25
  195.7 10.8 %all_to_all.51 = f32[32,1,96]{2,1,0:T(1,128)S(1)} all-to-all(f32[32,1,96]{2,1,0:T(1,128)S(1)} %broadcast_in_dim.99), channel_id=1, replica_groups=mesh['sub'=8,'grp'=4] {'grp','sub'}, dimensions={0} | all-to-all | bytes 24576 | tf_op jit(solution)/shard_map/all_to_all | solution.py:114
  206.6 3.0 %subtract_bitcast_fusion = (f32[1,2,96,1024]{3,2,1,0:T(8,128)}, f32[1,2,96,1024]{3,2,1,0:T(8,128)}) fusion(f32[2,96,1024]{2,1,0:T(8,128)} %get-tuple-element.3, f32[96]{0:T(128)S(1)} %div.27, f32[2,96,1024]{2,1,0:T(8,128)S(1)} %fusion.50, f32[2,96,1024]{2,1,0:T(8,128)S(1)} %copy-done.7, f32[96]{0:T(128)S(1)} %div.25, f32[2,96,1024]{2,1,0:T(8,128)} %copy-done.8, ...), kind=kLoop, calls=%fused_computation.44 | loop fusion | flops 1376256 | bytes 5505792 | tf_op jit(solution)/shard_map/broadcast_in_dim | solution.py:164
  (193 shorter events, 67.9 us)
Async XLA Ops:
  0.6 13.1 %copy-start.15 = (s32[1,2,1024]{2,1,0:T(2,128)S(1)}, s32[1,2,1024]{2,1,0:T(2,128)}, u32[]{:S(2)}) copy-start(s32[1,2,1024]{2,1,0:T(2,128)} %param.12) | copy-start | bytes 24580
  0.6 13.2 %copy-start.13 = (f32[1,2,6,1024]{3,1,2,0:T(2,128)S(1)}, f32[1,2,6,1024]{3,1,2,0:T(2,128)}, u32[]{:S(2)}) copy-start(f32[1,2,6,1024]{3,1,2,0:T(2,128)} %param.10) | copy-start | bytes 147460
  3.0 18.8 %copy-start.16 = (s32[4]{0:T(128)S(1)}, s32[4]{0:T(128)}, u32[]{:S(2)}) copy-start(s32[4]{0:T(128)} %constant.36) | copy-start | bytes 52
  4.4 9.9 %collective-permute-start = (f32[1,112,256]{2,1,0:T(8,128)S(1)}, f32[1,112,256]{2,1,0:T(8,128)S(1)}, u32[]{:S(2)}, u32[]{:S(2)}) collective-permute-start(f32[1,112,256]{2,1,0:T(8,128)S(1)} %get-tuple-element.38), channel_id=1, source_target_pairs={{0,4},{4,8},{8,12},{12,16},{16,20},{20,24},{24,28},{1,5},{5,9},{9,... | collective-permute-start | bytes 344072 | tf_op jit(solution)/shard_map/ppermute | solution.py:20
  6.8 7.5 %collective-permute-start.1 = (f32[1,112,256]{2,1,0:T(8,128)S(1)}, f32[1,112,256]{2,1,0:T(8,128)S(1)}, u32[]{:S(2)}, u32[]{:S(2)}) collective-permute-start(f32[1,112,256]{2,1,0:T(8,128)S(1)} %get-tuple-element.41), channel_id=1, source_target_pairs={{4,0},{8,4},{12,8},{16,12},{20,16},{24,20},{28,24},{5,1},{9,5},{13... | collective-permute-start | bytes 344072 | tf_op jit(solution)/shard_map/ppermute | solution.py:21
  8.1 8.8 %collective-permute-start.2 = (f32[2,112,256]{2,1,0:T(8,128)S(1)}, f32[2,112,256]{2,1,0:T(8,128)S(1)}, u32[]{:S(2)}, u32[]{:S(2)}) collective-permute-start(f32[2,112,256]{2,1,0:T(8,128)S(1)} %get-tuple-element.48), channel_id=1, source_target_pairs={{0,1},{1,2},{2,3},{4,5},{5,6},{6,7},{8,9},{9,10},{10,11},{12,13},{... | collective-permute-start | bytes 688136 | tf_op jit(solution)/shard_map/ppermute | solution.py:24
  12.5 9.2 %collective-permute-start.3 = (f32[2,112,256]{2,1,0:T(8,128)S(1)}, f32[2,112,256]{2,1,0:T(8,128)S(1)}, u32[]{:S(2)}, u32[]{:S(2)}) collective-permute-start(f32[2,112,256]{2,1,0:T(8,128)S(1)} %get-tuple-element.49), channel_id=1, source_target_pairs={{1,0},{2,1},{3,2},{5,4},{6,5},{7,6},{9,8},{10,9},{11,10},{13,12},{... | collective-permute-start | bytes 688136 | tf_op jit(solution)/shard_map/ppermute | solution.py:25
  21.7 3.5 %copy-start.9 = (f32[1,2,96,1024]{3,2,1,0:T(8,128)S(1)}, f32[1,2,96,1024]{3,2,1,0:T(8,128)}, u32[]{:S(2)}) copy-start(f32[1,2,96,1024]{3,2,1,0:T(8,128)} %param.7) | copy-start | bytes 2359300
  26.8 14.6 %all-to-all-start = ((f32[32,1,1152]{2,1,0:T(1,128)}), f32[32,1,1152]{2,1,0:T(1,128)S(1)}, u32[]{:S(2)}, u32[]{:S(2)}) async-start(f32[32,1,1152]{2,1,0:T(1,128)} %broadcast_in_dim.88), calls=%async_computation | async-start | bytes 294912 | tf_op jit(solution)/shard_map/all_to_all | solution.py:114
  63.9 6.7 %collective-permute-start.4 = (f32[1,96,256]{2,1,0:T(8,128)S(1)}, f32[1,96,256]{2,1,0:T(8,128)S(1)}, u32[]{:S(2)}, u32[]{:S(2)}) collective-permute-start(f32[1,96,256]{2,1,0:T(8,128)S(1)} %get-tuple-element.28), channel_id=1, source_target_pairs={{0,4},{4,8},{8,12},{12,16},{16,20},{20,24},{24,28},{1,5},{5,9},{9,... | collective-permute-start | bytes 294920 | tf_op jit(solution)/shard_map/ppermute | solution.py:20
  66.1 4.5 %collective-permute-start.5 = (f32[1,96,256]{2,1,0:T(8,128)S(1)}, f32[1,96,256]{2,1,0:T(8,128)S(1)}, u32[]{:S(2)}, u32[]{:S(2)}) collective-permute-start(f32[1,96,256]{2,1,0:T(8,128)S(1)} %get-tuple-element.29), channel_id=1, source_target_pairs={{4,0},{8,4},{12,8},{16,12},{20,16},{24,20},{28,24},{5,1},{9,5},{13... | collective-permute-start | bytes 294920 | tf_op jit(solution)/shard_map/ppermute | solution.py:21
  67.4 6.6 %collective-permute-start.6 = (f32[2,96,256]{2,1,0:T(8,128)S(1)}, f32[2,96,256]{2,1,0:T(8,128)S(1)}, u32[]{:S(2)}, u32[]{:S(2)}) collective-permute-start(f32[2,96,256]{2,1,0:T(8,128)S(1)} %get-tuple-element.32), channel_id=1, source_target_pairs={{0,1},{1,2},{2,3},{4,5},{5,6},{6,7},{8,9},{9,10},{10,11},{12,13},{... | collective-permute-start | bytes 589832 | tf_op jit(solution)/shard_map/ppermute | solution.py:24
  69.1 9.5 %collective-permute-start.7 = (f32[2,96,256]{2,1,0:T(8,128)S(1)}, f32[2,96,256]{2,1,0:T(8,128)S(1)}, u32[]{:S(2)}, u32[]{:S(2)}) collective-permute-start(f32[2,96,256]{2,1,0:T(8,128)S(1)} %get-tuple-element.33), channel_id=1, source_target_pairs={{1,0},{2,1},{3,2},{5,4},{6,5},{7,6},{9,8},{10,9},{11,10},{13,12},{... | collective-permute-start | bytes 589832 | tf_op jit(solution)/shard_map/ppermute | solution.py:25
  100.6 17.2 %copy-start = (f32[2,96,1024]{2,1,0:T(8,128)}, f32[2,96,1024]{2,1,0:T(8,128)S(1)}, u32[]{:S(2)}) copy-start(f32[2,96,1024]{2,1,0:T(8,128)S(1)} %sub.98) | copy-start | bytes 2359300
  101.5 6.6 %collective-permute-start.8 = (f32[1,96,256]{2,1,0:T(8,128)S(1)}, f32[1,96,256]{2,1,0:T(8,128)S(1)}, u32[]{:S(2)}, u32[]{:S(2)}) collective-permute-start(f32[1,96,256]{2,1,0:T(8,128)S(1)} %get-tuple-element.22), channel_id=1, source_target_pairs={{0,4},{4,8},{8,12},{12,16},{16,20},{20,24},{24,28},{1,5},{5,9},{9,... | collective-permute-start | bytes 294920 | tf_op jit(solution)/shard_map/ppermute | solution.py:20
  103.8 4.3 %collective-permute-start.9 = (f32[1,96,256]{2,1,0:T(8,128)S(1)}, f32[1,96,256]{2,1,0:T(8,128)S(1)}, u32[]{:S(2)}, u32[]{:S(2)}) collective-permute-start(f32[1,96,256]{2,1,0:T(8,128)S(1)} %get-tuple-element.23), channel_id=1, source_target_pairs={{4,0},{8,4},{12,8},{16,12},{20,16},{24,20},{28,24},{5,1},{9,5},{13... | collective-permute-start | bytes 294920 | tf_op jit(solution)/shard_map/ppermute | solution.py:21
  105.1 6.6 %collective-permute-start.10 = (f32[2,96,256]{2,1,0:T(8,128)S(1)}, f32[2,96,256]{2,1,0:T(8,128)S(1)}, u32[]{:S(2)}, u32[]{:S(2)}) collective-permute-start(f32[2,96,256]{2,1,0:T(8,128)S(1)} %get-tuple-element.26), channel_id=1, source_target_pairs={{0,1},{1,2},{2,3},{4,5},{5,6},{6,7},{8,9},{9,10},{10,11},{12,13},{... | collective-permute-start | bytes 589832 | tf_op jit(solution)/shard_map/ppermute | solution.py:24
  106.8 9.5 %collective-permute-start.11 = (f32[2,96,256]{2,1,0:T(8,128)S(1)}, f32[2,96,256]{2,1,0:T(8,128)S(1)}, u32[]{:S(2)}, u32[]{:S(2)}) collective-permute-start(f32[2,96,256]{2,1,0:T(8,128)S(1)} %get-tuple-element.27), channel_id=1, source_target_pairs={{1,0},{2,1},{3,2},{5,4},{6,5},{7,6},{9,8},{10,9},{11,10},{13,12},{... | collective-permute-start | bytes 589832 | tf_op jit(solution)/shard_map/ppermute | solution.py:25
  120.5 12.5 %all-to-all-start.3 = ((f32[32,1,1248]{2,1,0:T(1,128)}), f32[32,1,1248]{2,1,0:T(1,128)}, u32[]{:S(2)}, u32[]{:S(2)}) async-start(f32[32,1,1248]{2,1,0:T(1,128)} %broadcast_in_dim.95), calls=%async_computation.3 | async-start | bytes 327680 | tf_op jit(solution)/shard_map/all_to_all | solution.py:114
  137.3 2.6 %copy-start.3 = (bf16[1,2,1024,1024]{3,2,1,0:T(8,128)(2,1)S(1)}, bf16[1,2,1024,1024]{3,2,1,0:T(8,128)(2,1)}, u32[]{:S(2)}) copy-start(bf16[1,2,1024,1024]{3,2,1,0:T(8,128)(2,1)} %param.9) | copy-start | bytes 12582916
  140.7 6.6 %collective-permute-start.12 = (f32[1,96,256]{2,1,0:T(8,128)S(1)}, f32[1,96,256]{2,1,0:T(8,128)S(1)}, u32[]{:S(2)}, u32[]{:S(2)}) collective-permute-start(f32[1,96,256]{2,1,0:T(8,128)S(1)} %get-tuple-element.16), channel_id=1, source_target_pairs={{0,4},{4,8},{8,12},{12,16},{16,20},{20,24},{24,28},{1,5},{5,9},{9,... | collective-permute-start | bytes 294920 | tf_op jit(solution)/shard_map/ppermute | solution.py:20
  143.1 4.3 %collective-permute-start.13 = (f32[1,96,256]{2,1,0:T(8,128)S(1)}, f32[1,96,256]{2,1,0:T(8,128)S(1)}, u32[]{:S(2)}, u32[]{:S(2)}) collective-permute-start(f32[1,96,256]{2,1,0:T(8,128)S(1)} %get-tuple-element.17), channel_id=1, source_target_pairs={{4,0},{8,4},{12,8},{16,12},{20,16},{24,20},{28,24},{5,1},{9,5},{13... | collective-permute-start | bytes 294920 | tf_op jit(solution)/shard_map/ppermute | solution.py:21
  144.3 6.6 %collective-permute-start.14 = (f32[2,96,256]{2,1,0:T(8,128)S(1)}, f32[2,96,256]{2,1,0:T(8,128)S(1)}, u32[]{:S(2)}, u32[]{:S(2)}) collective-permute-start(f32[2,96,256]{2,1,0:T(8,128)S(1)} %get-tuple-element.20), channel_id=1, source_target_pairs={{0,1},{1,2},{2,3},{4,5},{5,6},{6,7},{8,9},{9,10},{10,11},{12,13},{... | collective-permute-start | bytes 589832 | tf_op jit(solution)/shard_map/ppermute | solution.py:24
  146.0 9.5 %collective-permute-start.15 = (f32[2,96,256]{2,1,0:T(8,128)S(1)}, f32[2,96,256]{2,1,0:T(8,128)S(1)}, u32[]{:S(2)}, u32[]{:S(2)}) collective-permute-start(f32[2,96,256]{2,1,0:T(8,128)S(1)} %get-tuple-element.21), channel_id=1, source_target_pairs={{1,0},{2,1},{3,2},{5,4},{6,5},{7,6},{9,8},{10,9},{11,10},{13,12},{... | collective-permute-start | bytes 589832 | tf_op jit(solution)/shard_map/ppermute | solution.py:25
  174.5 2.8 %copy-start.5 = (bf16[1,2,1024,1024]{3,2,1,0:T(8,128)(2,1)S(1)}, bf16[1,2,1024,1024]{3,2,1,0:T(8,128)(2,1)}, u32[]{:S(2)}) copy-start(bf16[1,2,1024,1024]{3,2,1,0:T(8,128)(2,1)} %param.8) | copy-start | bytes 12582916
  177.3 17.2 %copy-start.8 = (f32[2,96,1024]{2,1,0:T(8,128)}, f32[2,96,1024]{2,1,0:T(8,128)S(1)}, u32[]{:S(2)}) copy-start(f32[2,96,1024]{2,1,0:T(8,128)S(1)} %multiply_add_fusion) | copy-start | bytes 2359300
  178.2 6.6 %collective-permute-start.16 = (f32[1,96,256]{2,1,0:T(8,128)S(1)}, f32[1,96,256]{2,1,0:T(8,128)S(1)}, u32[]{:S(2)}, u32[]{:S(2)}) collective-permute-start(f32[1,96,256]{2,1,0:T(8,128)S(1)} %get-tuple-element.10), channel_id=1, source_target_pairs={{0,4},{4,8},{8,12},{12,16},{16,20},{20,24},{24,28},{1,5},{5,9},{9,... | collective-permute-start | bytes 294920 | tf_op jit(solution)/shard_map/ppermute | solution.py:20
  180.5 4.3 %collective-permute-start.17 = (f32[1,96,256]{2,1,0:T(8,128)S(1)}, f32[1,96,256]{2,1,0:T(8,128)S(1)}, u32[]{:S(2)}, u32[]{:S(2)}) collective-permute-start(f32[1,96,256]{2,1,0:T(8,128)S(1)} %get-tuple-element.11), channel_id=1, source_target_pairs={{4,0},{8,4},{12,8},{16,12},{20,16},{24,20},{28,24},{5,1},{9,5},{13... | collective-permute-start | bytes 294920 | tf_op jit(solution)/shard_map/ppermute | solution.py:21
  181.8 6.6 %collective-permute-start.18 = (f32[2,96,256]{2,1,0:T(8,128)S(1)}, f32[2,96,256]{2,1,0:T(8,128)S(1)}, u32[]{:S(2)}, u32[]{:S(2)}) collective-permute-start(f32[2,96,256]{2,1,0:T(8,128)S(1)} %get-tuple-element.14), channel_id=1, source_target_pairs={{0,1},{1,2},{2,3},{4,5},{5,6},{6,7},{8,9},{9,10},{10,11},{12,13},{... | collective-permute-start | bytes 589832 | tf_op jit(solution)/shard_map/ppermute | solution.py:24
  183.5 9.5 %collective-permute-start.19 = (f32[2,96,256]{2,1,0:T(8,128)S(1)}, f32[2,96,256]{2,1,0:T(8,128)S(1)}, u32[]{:S(2)}, u32[]{:S(2)}) collective-permute-start(f32[2,96,256]{2,1,0:T(8,128)S(1)} %get-tuple-element.15), channel_id=1, source_target_pairs={{1,0},{2,1},{3,2},{5,4},{6,5},{7,6},{9,8},{10,9},{11,10},{13,12},{... | collective-permute-start | bytes 589832 | tf_op jit(solution)/shard_map/ppermute | solution.py:25
  194.4 12.2 %copy-start.1 = (f32[2,96,1024]{2,1,0:T(8,128)S(1)}, f32[2,96,1024]{2,1,0:T(8,128)}, u32[]{:S(2)}) copy-start(f32[2,96,1024]{2,1,0:T(8,128)} %copy-done) | copy-start | bytes 2359300
  194.4 12.2 %copy-start.7 = (f32[2,96,1024]{2,1,0:T(8,128)S(1)}, f32[2,96,1024]{2,1,0:T(8,128)}, u32[]{:S(2)}) copy-start(f32[2,96,1024]{2,1,0:T(8,128)} %copy-done.6) | copy-start | bytes 2359300
  (7 other events, 8.9 us)

commit v10 on v7

--- a/solution.py
+++ b/solution.py
@@ -149,12 +149,15 @@
         if step_index > 0:
             search = search + (rho_now / rho_prev)[None, :, None] * direction
         direction = search
-        image = jump(apply_blocks(direction, stiffness))
-        partial_dot = jnp.sum(direction * image, axis=(0, 2))
         if step_index + 1 < ITERS:
+            image = jump(apply_blocks(direction, stiffness))
+            partial_dot = jnp.sum(direction * image, axis=(0, 2))
             flat_image, curvature = gathered(coefficients(image), partial_dot)
         else:
+            product = apply_blocks(direction, stiffness)
+            partial_dot = jnp.sum(slot_weight[:, None, :] * direction * product, axis=(0, 2))
             _, curvature = gathered(jnp.zeros((0,), jnp.float32), partial_dot)
+            image = jump(product)
         step_len = rho_now / curvature
         multipliers = multipliers + step_len[None, :, None] * direction
         residual = residual - step_len[None, :, None] * image

time: 206 us -> 206 us (level)
  blocking collectives: 45.9 us -> 35.2 us
  matrix products: 18.6 us -> 24 us
  starting transfers between devices: 45.6 us -> 50.4 us
  waiting for transfers between devices: 54.4 us -> 51.7 us
  local copies, waits for them, and re-layouts: 19.6 us -> 22.1 us
    all_to_all x4 -> x3, blocking collectives: 45.9 us -> 35.2 us  [gathered(): everything = lax.all_to_all(copies, ('grp', 'sub'), 0, 0, tiled=True)]
    dot_general x5, matrix products: 1.4 us -> 4.97 us  [lift(): jnp.einsum('sfkc,cn->skfn', partner_rows, flat, precision=HIGHEST)]
    all_to_all x2 -> x3, starting transfers between devices: 10.2 us -> 12.6 us  [gathered(): everything = lax.all_to_all(copies, ('grp', 'sub'), 0, 0, tiled=True)]
    all_to_all x2 -> x3, waiting for transfers between devices: 14.6 us -> 13.7 us  [gathered(): everything = lax.all_to_all(copies, ('grp', 'sub'), 0, 0, tiled=True)]
    unnamed x46 -> x54, local copies, waits for them, and re-layouts: 7.74 us -> 8.36 us
  transfers between devices with their start and end apart: 22 -> 23, of which waited for: 12 -> 12; matrix products, arithmetic and copies ran while one was open for 2% -> 5% of each run, Pallas kernels for 0% -> 0%
where the time goes in v10:
time: 206 us; the launch traced here: 204 us
  waiting for transfers between devices  51.7 us (25%)
  starting transfers between devices  50.4 us (24%)
  blocking collectives  35.2 us (17%)
  matrix products  24 us (12%)
  local copies, waits for them, and re-layouts  22.1 us (11%)
  other arithmetic  19.3 us (9%)
    all_to_all x3, blocking collectives, gathered(): everything = lax.all_to_all(copies, ('grp', 'sub'), 0, 0, tiled=True)  35.2 us
    ppermute x5, waiting for transfers between devices, neighbors(): from_above = lax.ppermute(d2, 'grp', down_grp)  23.1 us
    ppermute x5, waiting for transfers between devices, neighbors(): from_below = lax.ppermute(d3, 'grp', up_grp)  14.9 us
    all_to_all x3, waiting for transfers between devices, gathered(): everything = lax.all_to_all(copies, ('grp', 'sub'), 0, 0, tiled=True)  13.7 us
    ppermute x5, starting transfers between devices, neighbors(): from_below = lax.ppermute(d3, 'grp', up_grp)  12.9 us
    all_to_all x3, starting transfers between devices, gathered(): everything = lax.all_to_all(copies, ('grp', 'sub'), 0, 0, tiled=True)  12.6 us
    ppermute x5, starting transfers between devices, neighbors(): left_dev = lax.ppermute(d1[-1:], 'sub', up_sub)  12 us
    dot_general x6, matrix products, to_mine(): return jnp.einsum('sfcq,sfqr->sfcr', raw, permutes, precision=HIGHEST)  8.85 us
  transfers between devices with their start and end apart: 23, of which 12 were waited for; matrix products, arithmetic and copies ran while one was open for 5% of the time, Pallas kernels for 0%

profile of v10, /device:TPU:0, one launch (start us, length us, event | category | flops | bytes accessed | tf_op | source)
XLA Modules:
  0.0 204.5 jit_solution(17953823438659126827)
XLA Ops:
  4.4 2.4 %collective-permute-start = (f32[1,112,256]{2,1,0:T(8,128)S(1)}, f32[1,112,256]{2,1,0:T(8,128)S(1)}, u32[]{:S(2)}, u32[]{:S(2)}) collective-permute-start(f32[1,112,256]{2,1,0:T(8,128)S(1)} %get-tuple-element.36), channel_id=1, source_target_pairs={{0,4},{4,8},{8,12},{12,16},{16,20},{20,24},{24,28},{1,5},{5,9},{9,... | collective-permute-start | bytes 344072 | tf_op jit(solution)/shard_map/ppermute | solution.py:20
  8.1 4.3 %collective-permute-start.2 = (f32[2,112,256]{2,1,0:T(8,128)S(1)}, f32[2,112,256]{2,1,0:T(8,128)S(1)}, u32[]{:S(2)}, u32[]{:S(2)}) collective-permute-start(f32[2,112,256]{2,1,0:T(8,128)S(1)} %get-tuple-element.46), channel_id=1, source_target_pairs={{0,1},{1,2},{2,3},{4,5},{5,6},{6,7},{8,9},{9,10},{10,11},{12,13},{... | collective-permute-start | bytes 688136 | tf_op jit(solution)/shard_map/ppermute | solution.py:24
  14.3 2.6 %collective-permute-done.2 = f32[2,112,256]{2,1,0:T(8,128)S(1)} collective-permute-done((f32[2,112,256]{2,1,0:T(8,128)S(1)}, f32[2,112,256]{2,1,0:T(8,128)S(1)}, u32[]{:S(2)}, u32[]{:S(2)}) %collective-permute-start.2) | collective-permute-done | bytes 229408 | tf_op jit(solution)/shard_map/ppermute | solution.py:24
  16.9 4.7 %collective-permute-done.3 = f32[2,112,256]{2,1,0:T(8,128)S(1)} collective-permute-done((f32[2,112,256]{2,1,0:T(8,128)S(1)}, f32[2,112,256]{2,1,0:T(8,128)S(1)}, u32[]{:S(2)}, u32[]{:S(2)}) %collective-permute-start.3) | collective-permute-done | bytes 229408 | tf_op jit(solution)/shard_map/ppermute | solution.py:25
  27.4 6.2 %all-to-all-start = ((f32[32,1,1153]{2,1,0:T(1,128)}), f32[32,1,1153]{2,1,0:T(1,128)S(1)}, u32[]{:S(2)}, u32[]{:S(2)}) async-start(f32[32,1,1153]{2,1,0:T(1,128)} %broadcast_in_dim.41), calls=%async_computation | async-start | bytes 327680 | tf_op jit(solution)/shard_map/all_to_all | solution.py:114
  34.4 1.9 convolution_bitcast_fusion.5
  36.3 5.8 %all-to-all-done = f32[32,1,1153]{2,1,0:T(1,128)S(1)} async-done(((f32[32,1,1153]{2,1,0:T(1,128)}), f32[32,1,1153]{2,1,0:T(1,128)S(1)}, u32[]{:S(2)}, u32[]{:S(2)}) %all-to-all-start) | async-done | bytes 147616 | tf_op jit(solution)/shard_map/all_to_all | solution.py:114
  46.6 10.7 %all_to_all.51 = f32[32,1,1153]{2,1,0:T(1,128)S(1)} all-to-all(f32[32,1,1153]{2,1,0:T(1,128)S(1)} %broadcast_in_dim.43), channel_id=1, replica_groups=mesh['sub'=8,'grp'=4] {'grp','sub'}, dimensions={0} | all-to-all | bytes 295168 | tf_op jit(solution)/shard_map/all_to_all | solution.py:114
  63.5 2.3 %collective-permute-start.4 = (f32[1,96,256]{2,1,0:T(8,128)S(1)}, f32[1,96,256]{2,1,0:T(8,128)S(1)}, u32[]{:S(2)}, u32[]{:S(2)}) collective-permute-start(f32[1,96,256]{2,1,0:T(8,128)S(1)} %get-tuple-element.26), channel_id=1, source_target_pairs={{0,4},{4,8},{8,12},{12,16},{16,20},{20,24},{24,28},{1,5},{5,9},{9,... | collective-permute-start | bytes 294920 | tf_op jit(solution)/shard_map/ppermute | solution.py:20
  67.1 1.7 collective-permute-start.6
  70.2 3.5 %collective-permute-done.6 = f32[2,96,256]{2,1,0:T(8,128)S(1)} collective-permute-done((f32[2,96,256]{2,1,0:T(8,128)S(1)}, f32[2,96,256]{2,1,0:T(8,128)S(1)}, u32[]{:S(2)}, u32[]{:S(2)}) %collective-permute-start.6) | collective-permute-done | bytes 196640 | tf_op jit(solution)/shard_map/ppermute | solution.py:24
  73.7 4.6 %collective-permute-done.7 = f32[2,96,256]{2,1,0:T(8,128)S(1)} collective-permute-done((f32[2,96,256]{2,1,0:T(8,128)S(1)}, f32[2,96,256]{2,1,0:T(8,128)S(1)}, u32[]{:S(2)}, u32[]{:S(2)}) %collective-permute-start.7) | collective-permute-done | bytes 196640 | tf_op jit(solution)/shard_map/ppermute | solution.py:25
  81.8 12.2 %all_to_all.52 = f32[32,1,1248]{2,1,0:T(1,128)S(1)} all-to-all(f32[32,1,1248]{2,1,0:T(1,128)S(1)} %broadcast_in_dim.45), channel_id=1, replica_groups=mesh['sub'=8,'grp'=4] {'grp','sub'}, dimensions={0} | all-to-all | bytes 319488 | tf_op jit(solution)/shard_map/all_to_all | solution.py:114
  101.2 2.3 %collective-permute-start.8 = (f32[1,96,256]{2,1,0:T(8,128)S(1)}, f32[1,96,256]{2,1,0:T(8,128)S(1)}, u32[]{:S(2)}, u32[]{:S(2)}) collective-permute-start(f32[1,96,256]{2,1,0:T(8,128)S(1)} %get-tuple-element.20), channel_id=1, source_target_pairs={{0,4},{4,8},{8,12},{12,16},{16,20},{20,24},{24,28},{1,5},{5,9},{9,... | collective-permute-start | bytes 294920 | tf_op jit(solution)/shard_map/ppermute | solution.py:20
  107.9 3.5 %collective-permute-done.10 = f32[2,96,256]{2,1,0:T(8,128)S(1)} collective-permute-done((f32[2,96,256]{2,1,0:T(8,128)S(1)}, f32[2,96,256]{2,1,0:T(8,128)S(1)}, u32[]{:S(2)}, u32[]{:S(2)}) %collective-permute-start.10) | collective-permute-done | bytes 196640 | tf_op jit(solution)/shard_map/ppermute | solution.py:24
  111.4 4.6 %collective-permute-done.11 = f32[2,96,256]{2,1,0:T(8,128)S(1)} collective-permute-done((f32[2,96,256]{2,1,0:T(8,128)S(1)}, f32[2,96,256]{2,1,0:T(8,128)S(1)}, u32[]{:S(2)}, u32[]{:S(2)}) %collective-permute-start.11) | collective-permute-done | bytes 196640 | tf_op jit(solution)/shard_map/ppermute | solution.py:25
  120.2 4.0 %all-to-all-start.3 = ((f32[32,1,1248]{2,1,0:T(1,128)}), f32[32,1,1248]{2,1,0:T(1,128)}, u32[]{:S(2)}, u32[]{:S(2)}) async-start(f32[32,1,1248]{2,1,0:T(1,128)} %broadcast_in_dim.47), calls=%async_computation.3 | async-start | bytes 327680 | tf_op jit(solution)/shard_map/all_to_all | solution.py:114
  124.9 7.8 %all-to-all-done.3 = f32[32,1,1248]{2,1,0:T(1,128)} async-done(((f32[32,1,1248]{2,1,0:T(1,128)}), f32[32,1,1248]{2,1,0:T(1,128)}, u32[]{:S(2)}, u32[]{:S(2)}) %all-to-all-start.3) | async-done | bytes 159776 | tf_op jit(solution)/shard_map/all_to_all | solution.py:114
  140.4 2.3 %collective-permute-start.12 = (f32[1,96,256]{2,1,0:T(8,128)S(1)}, f32[1,96,256]{2,1,0:T(8,128)S(1)}, u32[]{:S(2)}, u32[]{:S(2)}) collective-permute-start(f32[1,96,256]{2,1,0:T(8,128)S(1)} %get-tuple-element.14), channel_id=1, source_target_pairs={{0,4},{4,8},{8,12},{12,16},{16,20},{20,24},{24,28},{1,5},{5,9},{9,... | collective-permute-start | bytes 294920 | tf_op jit(solution)/shard_map/ppermute | solution.py:20
  144.1 1.7 collective-permute-start.14
  147.1 3.5 %collective-permute-done.14 = f32[2,96,256]{2,1,0:T(8,128)S(1)} collective-permute-done((f32[2,96,256]{2,1,0:T(8,128)S(1)}, f32[2,96,256]{2,1,0:T(8,128)S(1)}, u32[]{:S(2)}, u32[]{:S(2)}) %collective-permute-start.14) | collective-permute-done | bytes 196640 | tf_op jit(solution)/shard_map/ppermute | solution.py:24
  150.6 4.6 %collective-permute-done.15 = f32[2,96,256]{2,1,0:T(8,128)S(1)} collective-permute-done((f32[2,96,256]{2,1,0:T(8,128)S(1)}, f32[2,96,256]{2,1,0:T(8,128)S(1)}, u32[]{:S(2)}, u32[]{:S(2)}) %collective-permute-start.15) | collective-permute-done | bytes 196640 | tf_op jit(solution)/shard_map/ppermute | solution.py:25
  158.8 12.2 %all_to_all.53 = f32[32,1,1248]{2,1,0:T(1,128)S(1)} all-to-all(f32[32,1,1248]{2,1,0:T(1,128)S(1)} %broadcast_in_dim.93), channel_id=1, replica_groups=mesh['sub'=8,'grp'=4] {'grp','sub'}, dimensions={0} | all-to-all | bytes 319488 | tf_op jit(solution)/shard_map/all_to_all | solution.py:114
  175.5 1.9 multiply_reduce_fusion
  178.0 2.5 %all-to-all-start.5 = ((f32[32,1,96]{2,1,0:T(1,128)}), f32[32,1,96]{2,1,0:T(1,128)S(1)}, u32[]{:S(2)}, u32[]{:S(2)}) async-start(f32[32,1,96]{2,1,0:T(1,128)} %broadcast_in_dim.95), calls=%async_computation.5 | async-start | bytes 32768 | tf_op jit(solution)/shard_map/all_to_all | solution.py:114
  180.4 1.8 fusion.51
  182.2 2.7 %collective-permute-start.16 = (f32[1,96,256]{2,1,0:T(8,128)}, f32[1,96,256]{2,1,0:T(8,128)}, u32[]{:S(2)}, u32[]{:S(2)}) collective-permute-start(f32[1,96,256]{2,1,0:T(8,128)} %get-tuple-element.8), channel_id=1, source_target_pairs={{0,4},{4,8},{8,12},{12,16},{16,20},{20,24},{24,28},{1,5},{5,9},{9,... | collective-permute-start | bytes 294920 | tf_op jit(solution)/shard_map/ppermute | solution.py:20
  184.9 1.8 fusion.52
  188.0 3.6 %collective-permute-start.18 = (f32[2,96,256]{2,1,0:T(8,128)}, f32[2,96,256]{2,1,0:T(8,128)S(1)}, u32[]{:S(2)}, u32[]{:S(2)}) collective-permute-start(f32[2,96,256]{2,1,0:T(8,128)} %get-tuple-element.12), channel_id=1, source_target_pairs={{0,1},{1,2},{2,3},{4,5},{5,6},{6,7},{8,9},{9,10},{10,11},{12,13},{... | collective-permute-start | bytes 589832 | tf_op jit(solution)/shard_map/ppermute | solution.py:24
  195.0 1.8 collective-permute-done.18
  196.8 4.5 %collective-permute-done.19 = f32[2,96,256]{2,1,0:T(8,128)S(1)} collective-permute-done((f32[2,96,256]{2,1,0:T(8,128)}, f32[2,96,256]{2,1,0:T(8,128)S(1)}, u32[]{:S(2)}, u32[]{:S(2)}) %collective-permute-start.19) | collective-permute-done | bytes 196640 | tf_op jit(solution)/shard_map/ppermute | solution.py:25
  202.8 1.7 subtract_bitcast_fusion
  (207 shorter events, 71.0 us)
Async XLA Ops:
  0.6 13.1 %copy-start.20 = (s32[1,2,1024]{2,1,0:T(2,128)S(1)}, s32[1,2,1024]{2,1,0:T(2,128)}, u32[]{:S(2)}) copy-start(s32[1,2,1024]{2,1,0:T(2,128)} %param.12) | copy-start | bytes 24580
  0.6 13.2 %copy-start.15 = (f32[1,2,6,1024]{3,1,2,0:T(2,128)S(1)}, f32[1,2,6,1024]{3,1,2,0:T(2,128)}, u32[]{:S(2)}) copy-start(f32[1,2,6,1024]{3,1,2,0:T(2,128)} %param.10) | copy-start | bytes 147460
  3.0 19.3 %copy-start.21 = (s32[4]{0:T(128)S(1)}, s32[4]{0:T(128)}, u32[]{:S(2)}) copy-start(s32[4]{0:T(128)} %constant.38) | copy-start | bytes 52
  4.4 9.9 %collective-permute-start = (f32[1,112,256]{2,1,0:T(8,128)S(1)}, f32[1,112,256]{2,1,0:T(8,128)S(1)}, u32[]{:S(2)}, u32[]{:S(2)}) collective-permute-start(f32[1,112,256]{2,1,0:T(8,128)S(1)} %get-tuple-element.36), channel_id=1, source_target_pairs={{0,4},{4,8},{8,12},{12,16},{16,20},{20,24},{24,28},{1,5},{5,9},{9,... | collective-permute-start | bytes 344072 | tf_op jit(solution)/shard_map/ppermute | solution.py:20
  6.8 7.5 %collective-permute-start.1 = (f32[1,112,256]{2,1,0:T(8,128)S(1)}, f32[1,112,256]{2,1,0:T(8,128)S(1)}, u32[]{:S(2)}, u32[]{:S(2)}) collective-permute-start(f32[1,112,256]{2,1,0:T(8,128)S(1)} %get-tuple-element.39), channel_id=1, source_target_pairs={{4,0},{8,4},{12,8},{16,12},{20,16},{24,20},{28,24},{5,1},{9,5},{13... | collective-permute-start | bytes 344072 | tf_op jit(solution)/shard_map/ppermute | solution.py:21
  8.1 8.8 %collective-permute-start.2 = (f32[2,112,256]{2,1,0:T(8,128)S(1)}, f32[2,112,256]{2,1,0:T(8,128)S(1)}, u32[]{:S(2)}, u32[]{:S(2)}) collective-permute-start(f32[2,112,256]{2,1,0:T(8,128)S(1)} %get-tuple-element.46), channel_id=1, source_target_pairs={{0,1},{1,2},{2,3},{4,5},{5,6},{6,7},{8,9},{9,10},{10,11},{12,13},{... | collective-permute-start | bytes 688136 | tf_op jit(solution)/shard_map/ppermute | solution.py:24
  12.4 9.2 %collective-permute-start.3 = (f32[2,112,256]{2,1,0:T(8,128)S(1)}, f32[2,112,256]{2,1,0:T(8,128)S(1)}, u32[]{:S(2)}, u32[]{:S(2)}) collective-permute-start(f32[2,112,256]{2,1,0:T(8,128)S(1)} %get-tuple-element.47), channel_id=1, source_target_pairs={{1,0},{2,1},{3,2},{5,4},{6,5},{7,6},{9,8},{10,9},{11,10},{13,12},{... | collective-permute-start | bytes 688136 | tf_op jit(solution)/shard_map/ppermute | solution.py:25
  27.4 14.8 %all-to-all-start = ((f32[32,1,1153]{2,1,0:T(1,128)}), f32[32,1,1153]{2,1,0:T(1,128)S(1)}, u32[]{:S(2)}, u32[]{:S(2)}) async-start(f32[32,1,1153]{2,1,0:T(1,128)} %broadcast_in_dim.41), calls=%async_computation | async-start | bytes 327680 | tf_op jit(solution)/shard_map/all_to_all | solution.py:114
  34.4 8.5 %copy-start.19 = (f32[2,4,6,384]{3,2,1,0:T(8,128)}, f32[2,4,6,384]{3,2,1,0:T(8,128)S(1)}, u32[]{:S(2)}) copy-start(f32[2,4,6,384]{3,2,1,0:T(8,128)S(1)} %reshape.199) | copy-start | bytes 221188
  63.5 6.6 %collective-permute-start.4 = (f32[1,96,256]{2,1,0:T(8,128)S(1)}, f32[1,96,256]{2,1,0:T(8,128)S(1)}, u32[]{:S(2)}, u32[]{:S(2)}) collective-permute-start(f32[1,96,256]{2,1,0:T(8,128)S(1)} %get-tuple-element.26), channel_id=1, source_target_pairs={{0,4},{4,8},{8,12},{12,16},{16,20},{20,24},{24,28},{1,5},{5,9},{9,... | collective-permute-start | bytes 294920 | tf_op jit(solution)/shard_map/ppermute | solution.py:20
  65.8 4.3 %collective-permute-start.5 = (f32[1,96,256]{2,1,0:T(8,128)S(1)}, f32[1,96,256]{2,1,0:T(8,128)S(1)}, u32[]{:S(2)}, u32[]{:S(2)}) collective-permute-start(f32[1,96,256]{2,1,0:T(8,128)S(1)} %get-tuple-element.27), channel_id=1, source_target_pairs={{4,0},{8,4},{12,8},{16,12},{20,16},{24,20},{28,24},{5,1},{9,5},{13... | collective-permute-start | bytes 294920 | tf_op jit(solution)/shard_map/ppermute | solution.py:21
  67.1 6.6 %collective-permute-start.6 = (f32[2,96,256]{2,1,0:T(8,128)S(1)}, f32[2,96,256]{2,1,0:T(8,128)S(1)}, u32[]{:S(2)}, u32[]{:S(2)}) collective-permute-start(f32[2,96,256]{2,1,0:T(8,128)S(1)} %get-tuple-element.30), channel_id=1, source_target_pairs={{0,1},{1,2},{2,3},{4,5},{5,6},{6,7},{8,9},{9,10},{10,11},{12,13},{... | collective-permute-start | bytes 589832 | tf_op jit(solution)/shard_map/ppermute | solution.py:24
  68.8 9.5 %collective-permute-start.7 = (f32[2,96,256]{2,1,0:T(8,128)S(1)}, f32[2,96,256]{2,1,0:T(8,128)S(1)}, u32[]{:S(2)}, u32[]{:S(2)}) collective-permute-start(f32[2,96,256]{2,1,0:T(8,128)S(1)} %get-tuple-element.31), channel_id=1, source_target_pairs={{1,0},{2,1},{3,2},{5,4},{6,5},{7,6},{9,8},{10,9},{11,10},{13,12},{... | collective-permute-start | bytes 589832 | tf_op jit(solution)/shard_map/ppermute | solution.py:25
  100.4 17.2 %copy-start = (f32[2,96,1024]{2,1,0:T(8,128)}, f32[2,96,1024]{2,1,0:T(8,128)S(1)}, u32[]{:S(2)}) copy-start(f32[2,96,1024]{2,1,0:T(8,128)S(1)} %sub.98) | copy-start | bytes 2359300
  101.2 6.6 %collective-permute-start.8 = (f32[1,96,256]{2,1,0:T(8,128)S(1)}, f32[1,96,256]{2,1,0:T(8,128)S(1)}, u32[]{:S(2)}, u32[]{:S(2)}) collective-permute-start(f32[1,96,256]{2,1,0:T(8,128)S(1)} %get-tuple-element.20), channel_id=1, source_target_pairs={{0,4},{4,8},{8,12},{12,16},{16,20},{20,24},{24,28},{1,5},{5,9},{9,... | collective-permute-start | bytes 294920 | tf_op jit(solution)/shard_map/ppermute | solution.py:20
  103.6 4.3 %collective-permute-start.9 = (f32[1,96,256]{2,1,0:T(8,128)S(1)}, f32[1,96,256]{2,1,0:T(8,128)S(1)}, u32[]{:S(2)}, u32[]{:S(2)}) collective-permute-start(f32[1,96,256]{2,1,0:T(8,128)S(1)} %get-tuple-element.21), channel_id=1, source_target_pairs={{4,0},{8,4},{12,8},{16,12},{20,16},{24,20},{28,24},{5,1},{9,5},{13... | collective-permute-start | bytes 294920 | tf_op jit(solution)/shard_map/ppermute | solution.py:21
  104.9 6.6 %collective-permute-start.10 = (f32[2,96,256]{2,1,0:T(8,128)S(1)}, f32[2,96,256]{2,1,0:T(8,128)S(1)}, u32[]{:S(2)}, u32[]{:S(2)}) collective-permute-start(f32[2,96,256]{2,1,0:T(8,128)S(1)} %get-tuple-element.24), channel_id=1, source_target_pairs={{0,1},{1,2},{2,3},{4,5},{5,6},{6,7},{8,9},{9,10},{10,11},{12,13},{... | collective-permute-start | bytes 589832 | tf_op jit(solution)/shard_map/ppermute | solution.py:24
  106.5 9.5 %collective-permute-start.11 = (f32[2,96,256]{2,1,0:T(8,128)S(1)}, f32[2,96,256]{2,1,0:T(8,128)S(1)}, u32[]{:S(2)}, u32[]{:S(2)}) collective-permute-start(f32[2,96,256]{2,1,0:T(8,128)S(1)} %get-tuple-element.25), channel_id=1, source_target_pairs={{1,0},{2,1},{3,2},{5,4},{6,5},{7,6},{9,8},{10,9},{11,10},{13,12},{... | collective-permute-start | bytes 589832 | tf_op jit(solution)/shard_map/ppermute | solution.py:25
  120.2 12.5 %all-to-all-start.3 = ((f32[32,1,1248]{2,1,0:T(1,128)}), f32[32,1,1248]{2,1,0:T(1,128)}, u32[]{:S(2)}, u32[]{:S(2)}) async-start(f32[32,1,1248]{2,1,0:T(1,128)} %broadcast_in_dim.47), calls=%async_computation.3 | async-start | bytes 327680 | tf_op jit(solution)/shard_map/all_to_all | solution.py:114
  140.4 6.6 %collective-permute-start.12 = (f32[1,96,256]{2,1,0:T(8,128)S(1)}, f32[1,96,256]{2,1,0:T(8,128)S(1)}, u32[]{:S(2)}, u32[]{:S(2)}) collective-permute-start(f32[1,96,256]{2,1,0:T(8,128)S(1)} %get-tuple-element.14), channel_id=1, source_target_pairs={{0,4},{4,8},{8,12},{12,16},{16,20},{20,24},{24,28},{1,5},{5,9},{9,... | collective-permute-start | bytes 294920 | tf_op jit(solution)/shard_map/ppermute | solution.py:20
  142.8 4.3 %collective-permute-start.13 = (f32[1,96,256]{2,1,0:T(8,128)S(1)}, f32[1,96,256]{2,1,0:T(8,128)S(1)}, u32[]{:S(2)}, u32[]{:S(2)}) collective-permute-start(f32[1,96,256]{2,1,0:T(8,128)S(1)} %get-tuple-element.15), channel_id=1, source_target_pairs={{4,0},{8,4},{12,8},{16,12},{20,16},{24,20},{28,24},{5,1},{9,5},{13... | collective-permute-start | bytes 294920 | tf_op jit(solution)/shard_map/ppermute | solution.py:21
  144.1 6.6 %collective-permute-start.14 = (f32[2,96,256]{2,1,0:T(8,128)S(1)}, f32[2,96,256]{2,1,0:T(8,128)S(1)}, u32[]{:S(2)}, u32[]{:S(2)}) collective-permute-start(f32[2,96,256]{2,1,0:T(8,128)S(1)} %get-tuple-element.18), channel_id=1, source_target_pairs={{0,1},{1,2},{2,3},{4,5},{5,6},{6,7},{8,9},{9,10},{10,11},{12,13},{... | collective-permute-start | bytes 589832 | tf_op jit(solution)/shard_map/ppermute | solution.py:24
  145.7 9.5 %collective-permute-start.15 = (f32[2,96,256]{2,1,0:T(8,128)S(1)}, f32[2,96,256]{2,1,0:T(8,128)S(1)}, u32[]{:S(2)}, u32[]{:S(2)}) collective-permute-start(f32[2,96,256]{2,1,0:T(8,128)S(1)} %get-tuple-element.19), channel_id=1, source_target_pairs={{1,0},{2,1},{3,2},{5,4},{6,5},{7,6},{9,8},{10,9},{11,10},{13,12},{... | collective-permute-start | bytes 589832 | tf_op jit(solution)/shard_map/ppermute | solution.py:25
  178.0 14.9 %all-to-all-start.5 = ((f32[32,1,96]{2,1,0:T(1,128)}), f32[32,1,96]{2,1,0:T(1,128)S(1)}, u32[]{:S(2)}, u32[]{:S(2)}) async-start(f32[32,1,96]{2,1,0:T(1,128)} %broadcast_in_dim.95), calls=%async_computation.5 | async-start | bytes 32768 | tf_op jit(solution)/shard_map/all_to_all | solution.py:114
  182.2 10.8 %collective-permute-start.16 = (f32[1,96,256]{2,1,0:T(8,128)}, f32[1,96,256]{2,1,0:T(8,128)}, u32[]{:S(2)}, u32[]{:S(2)}) collective-permute-start(f32[1,96,256]{2,1,0:T(8,128)} %get-tuple-element.8), channel_id=1, source_target_pairs={{0,4},{4,8},{8,12},{12,16},{16,20},{20,24},{24,28},{1,5},{5,9},{9,... | collective-permute-start | bytes 294920 | tf_op jit(solution)/shard_map/ppermute | solution.py:20
  186.7 7.3 %collective-permute-start.17 = (f32[1,96,256]{2,1,0:T(8,128)}, f32[1,96,256]{2,1,0:T(8,128)}, u32[]{:S(2)}, u32[]{:S(2)}) collective-permute-start(f32[1,96,256]{2,1,0:T(8,128)} %get-tuple-element.9), channel_id=1, source_target_pairs={{4,0},{8,4},{12,8},{16,12},{20,16},{24,20},{28,24},{5,1},{9,5},{13... | collective-permute-start | bytes 294920 | tf_op jit(solution)/shard_map/ppermute | solution.py:21
  188.0 8.7 %collective-permute-start.18 = (f32[2,96,256]{2,1,0:T(8,128)}, f32[2,96,256]{2,1,0:T(8,128)S(1)}, u32[]{:S(2)}, u32[]{:S(2)}) collective-permute-start(f32[2,96,256]{2,1,0:T(8,128)} %get-tuple-element.12), channel_id=1, source_target_pairs={{0,1},{1,2},{2,3},{4,5},{5,6},{6,7},{8,9},{9,10},{10,11},{12,13},{... | collective-permute-start | bytes 589832 | tf_op jit(solution)/shard_map/ppermute | solution.py:24
  191.6 9.7 %collective-permute-start.19 = (f32[2,96,256]{2,1,0:T(8,128)}, f32[2,96,256]{2,1,0:T(8,128)S(1)}, u32[]{:S(2)}, u32[]{:S(2)}) collective-permute-start(f32[2,96,256]{2,1,0:T(8,128)} %get-tuple-element.13), channel_id=1, source_target_pairs={{1,0},{2,1},{3,2},{5,4},{6,5},{7,6},{9,8},{10,9},{11,10},{13,12},{... | collective-permute-start | bytes 589832 | tf_op jit(solution)/shard_map/ppermute | solution.py:25
  192.9 9.8 %copy-start.1 = (f32[2,96,1024]{2,1,0:T(8,128)S(1)}, f32[2,96,1024]{2,1,0:T(8,128)}, u32[]{:S(2)}) copy-start(f32[2,96,1024]{2,1,0:T(8,128)} %copy-done) | copy-start | bytes 2359300
  192.9 9.8 %copy-start.7 = (f32[2,96,1024]{2,1,0:T(8,128)S(1)}, f32[2,96,1024]{2,1,0:T(8,128)}, u32[]{:S(2)}) copy-start(f32[2,96,1024]{2,1,0:T(8,128)} %copy-done.6) | copy-start | bytes 2359300
  192.9 9.8 %copy-start.10 = (f32[2,96,1024]{2,1,0:T(8,128)S(1)}, f32[2,96,1024]{2,1,0:T(8,128)}, u32[]{:S(2)}) copy-start(f32[2,96,1024]{2,1,0:T(8,128)} %get-tuple-element.55) | copy-start | bytes 2359300
  192.9 9.8 %copy-start.14 = (f32[2,96,1024]{2,1,0:T(8,128)S(1)}, f32[2,96,1024]{2,1,0:T(8,128)}, u32[]{:S(2)}) copy-start(f32[2,96,1024]{2,1,0:T(8,128)} %copy-done.13) | copy-start | bytes 2359300
  (13 other events, 25.8 us)

commit v11 on v7

--- a/solution.py
+++ b/solution.py
@@ -119,10 +119,13 @@
         flat = everything[:, :count].reshape(-1, columns)
         return flat, extras
 
+    all_rows = jnp.concatenate([rows_here, partner_rows.reshape(-1, coarse_total)], axis=0)
+    own_count = subdomains * MODES
+
     def lift(flat):
-        amounts = jnp.dot(rows_here, flat, precision=HIGHEST, preferred_element_type=jnp.float32)
-        shaped = amounts.reshape(subdomains, MODES, columns)
-        far_amounts = jnp.einsum("sfkc,cn->skfn", partner_rows, flat, precision=HIGHEST)
+        both = jnp.dot(all_rows, flat, precision=HIGHEST, preferred_element_type=jnp.float32)
+        shaped = both[:own_count].reshape(subdomains, MODES, columns)
+        far_amounts = jnp.swapaxes(both[own_count:].reshape(subdomains, 4, MODES, columns), 1, 2)
         far_spread = jnp.repeat(jnp.swapaxes(far_amounts, 2, 3), quarter, axis=3)
         own_part = own_modes[:, :, None, :] * shaped[:, :, :, None]
         far_part = partner_slot_modes[:, :, None, :] * far_spread

time: 206 us -> 209 us (1.015)
  local copies, waits for them, and re-layouts: 19.6 us -> 22.6 us
    reshape x4 -> x5, local copies, waits for them, and re-layouts: 3.21 us -> 5.58 us  [gathered(): flat = everything[:, :count].reshape(-1, columns)]
    unnamed x46 -> x42, local copies, waits for them, and re-layouts: 7.74 us -> 7.07 us
where the time goes in v11:
time: 209 us; the launch traced here: 208 us
  waiting for transfers between devices  54.2 us (26%)
  blocking collectives  46 us (22%)
  starting transfers between devices  45.6 us (22%)
  local copies, waits for them, and re-layouts  22.6 us (11%)
  matrix products  19.2 us (9%)
  other arithmetic  18.3 us (9%)
    all_to_all x4, blocking collectives, gathered(): everything = lax.all_to_all(copies, ('grp', 'sub'), 0, 0, tiled=True)  46 us
    ppermute x5, waiting for transfers between devices, neighbors(): from_above = lax.ppermute(d2, 'grp', down_grp)  23.2 us
    ppermute x5, waiting for transfers between devices, neighbors(): from_below = lax.ppermute(d3, 'grp', up_grp)  16.7 us
    all_to_all x2, waiting for transfers between devices, gathered(): everything = lax.all_to_all(copies, ('grp', 'sub'), 0, 0, tiled=True)  14.4 us
    ppermute x5, starting transfers between devices, neighbors(): left_dev = lax.ppermute(d1[-1:], 'sub', up_sub)  11.6 us
    ppermute x5, starting transfers between devices, neighbors(): from_below = lax.ppermute(d3, 'grp', up_grp)  11 us
    all_to_all x2, starting transfers between devices, gathered(): everything = lax.all_to_all(copies, ('grp', 'sub'), 0, 0, tiled=True)  10.2 us
    dot_general x6, matrix products, to_mine(): return jnp.einsum('sfcq,sfqr->sfcr', raw, permutes, precision=HIGHEST)  8.09 us
  transfers between devices with their start and end apart: 22, of which 12 were waited for; matrix products, arithmetic and copies ran while one was open for 2% of the time, Pallas kernels for 0%

profile of v11, /device:TPU:0, one launch (start us, length us, event | category | flops | bytes accessed | tf_op | source)
XLA Modules:
  0.0 207.7 jit_solution(2828676806487358343)
XLA Ops:
  4.4 2.4 %collective-permute-start = (f32[1,112,256]{2,1,0:T(8,128)S(1)}, f32[1,112,256]{2,1,0:T(8,128)S(1)}, u32[]{:S(2)}, u32[]{:S(2)}) collective-permute-start(f32[1,112,256]{2,1,0:T(8,128)S(1)} %get-tuple-element.38), channel_id=1, source_target_pairs={{0,4},{4,8},{8,12},{12,16},{16,20},{20,24},{24,28},{1,5},{5,9},{9,... | collective-permute-start | bytes 344072 | tf_op jit(solution)/shard_map/ppermute | solution.py:20
  8.1 4.3 %collective-permute-start.2 = (f32[2,112,256]{2,1,0:T(8,128)S(1)}, f32[2,112,256]{2,1,0:T(8,128)S(1)}, u32[]{:S(2)}, u32[]{:S(2)}) collective-permute-start(f32[2,112,256]{2,1,0:T(8,128)S(1)} %get-tuple-element.48), channel_id=1, source_target_pairs={{0,1},{1,2},{2,3},{4,5},{5,6},{6,7},{8,9},{9,10},{10,11},{12,13},{... | collective-permute-start | bytes 688136 | tf_op jit(solution)/shard_map/ppermute | solution.py:24
  14.3 2.6 %collective-permute-done.2 = f32[2,112,256]{2,1,0:T(8,128)S(1)} collective-permute-done((f32[2,112,256]{2,1,0:T(8,128)S(1)}, f32[2,112,256]{2,1,0:T(8,128)S(1)}, u32[]{:S(2)}, u32[]{:S(2)}) %collective-permute-start.2) | collective-permute-done | bytes 229408 | tf_op jit(solution)/shard_map/ppermute | solution.py:24
  16.9 4.7 %collective-permute-done.3 = f32[2,112,256]{2,1,0:T(8,128)S(1)} collective-permute-done((f32[2,112,256]{2,1,0:T(8,128)S(1)}, f32[2,112,256]{2,1,0:T(8,128)S(1)}, u32[]{:S(2)}, u32[]{:S(2)}) %collective-permute-start.3) | collective-permute-done | bytes 229408 | tf_op jit(solution)/shard_map/ppermute | solution.py:25
  26.8 6.2 %all-to-all-start = ((f32[32,1,1153]{2,1,0:T(1,128)}), f32[32,1,1153]{2,1,0:T(1,128)S(1)}, u32[]{:S(2)}, u32[]{:S(2)}) async-start(f32[32,1,1153]{2,1,0:T(1,128)} %broadcast_in_dim.41), calls=%async_computation | async-start | bytes 327680 | tf_op jit(solution)/shard_map/all_to_all | solution.py:114
  35.7 5.9 %all-to-all-done = f32[32,1,1153]{2,1,0:T(1,128)S(1)} async-done(((f32[32,1,1153]{2,1,0:T(1,128)}), f32[32,1,1153]{2,1,0:T(1,128)S(1)}, u32[]{:S(2)}, u32[]{:S(2)}) %all-to-all-start) | async-done | bytes 147616 | tf_op jit(solution)/shard_map/all_to_all | solution.py:114
  45.8 10.7 %all_to_all.51 = f32[32,1,1153]{2,1,0:T(1,128)S(1)} all-to-all(f32[32,1,1153]{2,1,0:T(1,128)S(1)} %broadcast_in_dim.43), channel_id=1, replica_groups=mesh['sub'=8,'grp'=4] {'grp','sub'}, dimensions={0} | all-to-all | bytes 295168 | tf_op jit(solution)/shard_map/all_to_all | solution.py:114
  61.5 2.3 %collective-permute-start.4 = (f32[1,96,256]{2,1,0:T(8,128)S(1)}, f32[1,96,256]{2,1,0:T(8,128)S(1)}, u32[]{:S(2)}, u32[]{:S(2)}) collective-permute-start(f32[1,96,256]{2,1,0:T(8,128)S(1)} %get-tuple-element.28), channel_id=1, source_target_pairs={{0,4},{4,8},{8,12},{12,16},{16,20},{20,24},{24,28},{1,5},{5,9},{9,... | collective-permute-start | bytes 294920 | tf_op jit(solution)/shard_map/ppermute | solution.py:20
  65.2 1.7 collective-permute-start.6
  68.2 3.5 %collective-permute-done.6 = f32[2,96,256]{2,1,0:T(8,128)S(1)} collective-permute-done((f32[2,96,256]{2,1,0:T(8,128)S(1)}, f32[2,96,256]{2,1,0:T(8,128)S(1)}, u32[]{:S(2)}, u32[]{:S(2)}) %collective-permute-start.6) | collective-permute-done | bytes 196640 | tf_op jit(solution)/shard_map/ppermute | solution.py:24
  71.7 4.6 %collective-permute-done.7 = f32[2,96,256]{2,1,0:T(8,128)S(1)} collective-permute-done((f32[2,96,256]{2,1,0:T(8,128)S(1)}, f32[2,96,256]{2,1,0:T(8,128)S(1)}, u32[]{:S(2)}, u32[]{:S(2)}) %collective-permute-start.7) | collective-permute-done | bytes 196640 | tf_op jit(solution)/shard_map/ppermute | solution.py:25
  79.9 12.2 %all_to_all.52 = f32[32,1,1248]{2,1,0:T(1,128)S(1)} all-to-all(f32[32,1,1248]{2,1,0:T(1,128)S(1)} %broadcast_in_dim.45), channel_id=1, replica_groups=mesh['sub'=8,'grp'=4] {'grp','sub'}, dimensions={0} | all-to-all | bytes 319488 | tf_op jit(solution)/shard_map/all_to_all | solution.py:114
  92.8 1.7 reshape.215
  100.4 2.3 %collective-permute-start.8 = (f32[1,96,256]{2,1,0:T(8,128)S(1)}, f32[1,96,256]{2,1,0:T(8,128)S(1)}, u32[]{:S(2)}, u32[]{:S(2)}) collective-permute-start(f32[1,96,256]{2,1,0:T(8,128)S(1)} %get-tuple-element.22), channel_id=1, source_target_pairs={{0,4},{4,8},{8,12},{12,16},{16,20},{20,24},{24,28},{1,5},{5,9},{9,... | collective-permute-start | bytes 294920 | tf_op jit(solution)/shard_map/ppermute | solution.py:20
  104.1 1.7 collective-permute-start.10
  107.1 3.5 %collective-permute-done.10 = f32[2,96,256]{2,1,0:T(8,128)S(1)} collective-permute-done((f32[2,96,256]{2,1,0:T(8,128)S(1)}, f32[2,96,256]{2,1,0:T(8,128)S(1)}, u32[]{:S(2)}, u32[]{:S(2)}) %collective-permute-start.10) | collective-permute-done | bytes 196640 | tf_op jit(solution)/shard_map/ppermute | solution.py:24
  110.6 4.6 %collective-permute-done.11 = f32[2,96,256]{2,1,0:T(8,128)S(1)} collective-permute-done((f32[2,96,256]{2,1,0:T(8,128)S(1)}, f32[2,96,256]{2,1,0:T(8,128)S(1)}, u32[]{:S(2)}, u32[]{:S(2)}) %collective-permute-start.11) | collective-permute-done | bytes 196640 | tf_op jit(solution)/shard_map/ppermute | solution.py:25
  119.4 4.0 %all-to-all-start.3 = ((f32[32,1,1248]{2,1,0:T(1,128)}), f32[32,1,1248]{2,1,0:T(1,128)}, u32[]{:S(2)}, u32[]{:S(2)}) async-start(f32[32,1,1248]{2,1,0:T(1,128)} %broadcast_in_dim.47), calls=%async_computation.3 | async-start | bytes 327680 | tf_op jit(solution)/shard_map/all_to_all | solution.py:114
  123.4 8.5 %all-to-all-done.3 = f32[32,1,1248]{2,1,0:T(1,128)} async-done(((f32[32,1,1248]{2,1,0:T(1,128)}), f32[32,1,1248]{2,1,0:T(1,128)}, u32[]{:S(2)}, u32[]{:S(2)}) %all-to-all-start.3) | async-done | bytes 159776 | tf_op jit(solution)/shard_map/all_to_all | solution.py:114
  133.6 1.7 reshape.219
  140.0 2.3 %collective-permute-start.12 = (f32[1,96,256]{2,1,0:T(8,128)S(1)}, f32[1,96,256]{2,1,0:T(8,128)S(1)}, u32[]{:S(2)}, u32[]{:S(2)}) collective-permute-start(f32[1,96,256]{2,1,0:T(8,128)S(1)} %get-tuple-element.16), channel_id=1, source_target_pairs={{0,4},{4,8},{8,12},{12,16},{16,20},{20,24},{24,28},{1,5},{5,9},{9,... | collective-permute-start | bytes 294920 | tf_op jit(solution)/shard_map/ppermute | solution.py:20
  143.6 1.7 collective-permute-start.14
  146.7 3.5 %collective-permute-done.14 = f32[2,96,256]{2,1,0:T(8,128)S(1)} collective-permute-done((f32[2,96,256]{2,1,0:T(8,128)S(1)}, f32[2,96,256]{2,1,0:T(8,128)S(1)}, u32[]{:S(2)}, u32[]{:S(2)}) %collective-permute-start.14) | collective-permute-done | bytes 196640 | tf_op jit(solution)/shard_map/ppermute | solution.py:24
  150.2 4.6 %collective-permute-done.15 = f32[2,96,256]{2,1,0:T(8,128)S(1)} collective-permute-done((f32[2,96,256]{2,1,0:T(8,128)S(1)}, f32[2,96,256]{2,1,0:T(8,128)S(1)}, u32[]{:S(2)}, u32[]{:S(2)}) %collective-permute-start.15) | collective-permute-done | bytes 196640 | tf_op jit(solution)/shard_map/ppermute | solution.py:25
  158.3 12.2 %all_to_all.53 = f32[32,1,1248]{2,1,0:T(1,128)S(1)} all-to-all(f32[32,1,1248]{2,1,0:T(1,128)S(1)} %broadcast_in_dim.93), channel_id=1, replica_groups=mesh['sub'=8,'grp'=4] {'grp','sub'}, dimensions={0} | all-to-all | bytes 319488 | tf_op jit(solution)/shard_map/all_to_all | solution.py:114
  173.8 1.6 multiply_add_fusion
  176.3 2.3 %collective-permute-start.16 = (f32[1,96,256]{2,1,0:T(8,128)S(1)}, f32[1,96,256]{2,1,0:T(8,128)S(1)}, u32[]{:S(2)}, u32[]{:S(2)}) collective-permute-start(f32[1,96,256]{2,1,0:T(8,128)S(1)} %get-tuple-element.10), channel_id=1, source_target_pairs={{0,4},{4,8},{8,12},{12,16},{16,20},{20,24},{24,28},{1,5},{5,9},{9,... | collective-permute-start | bytes 294920 | tf_op jit(solution)/shard_map/ppermute | solution.py:20
  179.9 1.7 collective-permute-start.18
  183.0 3.5 %collective-permute-done.18 = f32[2,96,256]{2,1,0:T(8,128)S(1)} collective-permute-done((f32[2,96,256]{2,1,0:T(8,128)S(1)}, f32[2,96,256]{2,1,0:T(8,128)S(1)}, u32[]{:S(2)}, u32[]{:S(2)}) %collective-permute-start.18) | collective-permute-done | bytes 196640 | tf_op jit(solution)/shard_map/ppermute | solution.py:24
  186.5 4.6 %collective-permute-done.19 = f32[2,96,256]{2,1,0:T(8,128)S(1)} collective-permute-done((f32[2,96,256]{2,1,0:T(8,128)S(1)}, f32[2,96,256]{2,1,0:T(8,128)S(1)}, u32[]{:S(2)}, u32[]{:S(2)}) %collective-permute-start.19) | collective-permute-done | bytes 196640 | tf_op jit(solution)/shard_map/ppermute | solution.py:25
  193.8 10.8 %all_to_all.54 = f32[32,1,96]{2,1,0:T(1,128)S(1)} all-to-all(f32[32,1,96]{2,1,0:T(1,128)S(1)} %broadcast_in_dim.95), channel_id=1, replica_groups=mesh['sub'=8,'grp'=4] {'grp','sub'}, dimensions={0} | all-to-all | bytes 24576 | tf_op jit(solution)/shard_map/all_to_all | solution.py:114
  204.7 3.0 %subtract_bitcast_fusion = (f32[1,2,96,1024]{3,2,1,0:T(8,128)}, f32[1,2,96,1024]{3,2,1,0:T(8,128)}) fusion(f32[2,96,1024]{2,1,0:T(8,128)} %get-tuple-element.3, f32[96]{0:T(128)S(1)} %div.27, f32[2,96,1024]{2,1,0:T(8,128)S(1)} %fusion.57, f32[2,96,1024]{2,1,0:T(8,128)S(1)} %copy-done.7, f32[96]{0:T(128)S(1)} %div.25, f32[2,96,1024]{2,1,0:T(8,128)} %copy-done.8, ...), kind=kLoop, calls=%fused_computation.34 | loop fusion | flops 1376256 | bytes 5505792 | tf_op jit(solution)/shard_map/broadcast_in_dim | solution.py:167
  (203 shorter events, 65.0 us)
Async XLA Ops:
  0.6 13.1 %copy-start.14 = (s32[1,2,1024]{2,1,0:T(2,128)S(1)}, s32[1,2,1024]{2,1,0:T(2,128)}, u32[]{:S(2)}) copy-start(s32[1,2,1024]{2,1,0:T(2,128)} %param.12) | copy-start | bytes 24580
  0.6 13.2 %copy-start.13 = (f32[1,2,6,1024]{3,1,2,0:T(2,128)S(1)}, f32[1,2,6,1024]{3,1,2,0:T(2,128)}, u32[]{:S(2)}) copy-start(f32[1,2,6,1024]{3,1,2,0:T(2,128)} %param.10) | copy-start | bytes 147460
  3.0 18.8 %copy-start.15 = (s32[4]{0:T(128)S(1)}, s32[4]{0:T(128)}, u32[]{:S(2)}) copy-start(s32[4]{0:T(128)} %constant.38) | copy-start | bytes 52
  4.4 9.9 %collective-permute-start = (f32[1,112,256]{2,1,0:T(8,128)S(1)}, f32[1,112,256]{2,1,0:T(8,128)S(1)}, u32[]{:S(2)}, u32[]{:S(2)}) collective-permute-start(f32[1,112,256]{2,1,0:T(8,128)S(1)} %get-tuple-element.38), channel_id=1, source_target_pairs={{0,4},{4,8},{8,12},{12,16},{16,20},{20,24},{24,28},{1,5},{5,9},{9,... | collective-permute-start | bytes 344072 | tf_op jit(solution)/shard_map/ppermute | solution.py:20
  6.8 7.5 %collective-permute-start.1 = (f32[1,112,256]{2,1,0:T(8,128)S(1)}, f32[1,112,256]{2,1,0:T(8,128)S(1)}, u32[]{:S(2)}, u32[]{:S(2)}) collective-permute-start(f32[1,112,256]{2,1,0:T(8,128)S(1)} %get-tuple-element.41), channel_id=1, source_target_pairs={{4,0},{8,4},{12,8},{16,12},{20,16},{24,20},{28,24},{5,1},{9,5},{13... | collective-permute-start | bytes 344072 | tf_op jit(solution)/shard_map/ppermute | solution.py:21
  8.1 8.8 %collective-permute-start.2 = (f32[2,112,256]{2,1,0:T(8,128)S(1)}, f32[2,112,256]{2,1,0:T(8,128)S(1)}, u32[]{:S(2)}, u32[]{:S(2)}) collective-permute-start(f32[2,112,256]{2,1,0:T(8,128)S(1)} %get-tuple-element.48), channel_id=1, source_target_pairs={{0,1},{1,2},{2,3},{4,5},{5,6},{6,7},{8,9},{9,10},{10,11},{12,13},{... | collective-permute-start | bytes 688136 | tf_op jit(solution)/shard_map/ppermute | solution.py:24
  12.4 9.2 %collective-permute-start.3 = (f32[2,112,256]{2,1,0:T(8,128)S(1)}, f32[2,112,256]{2,1,0:T(8,128)S(1)}, u32[]{:S(2)}, u32[]{:S(2)}) collective-permute-start(f32[2,112,256]{2,1,0:T(8,128)S(1)} %get-tuple-element.49), channel_id=1, source_target_pairs={{1,0},{2,1},{3,2},{5,4},{6,5},{7,6},{9,8},{10,9},{11,10},{13,12},{... | collective-permute-start | bytes 688136 | tf_op jit(solution)/shard_map/ppermute | solution.py:25
  21.7 3.5 %copy-start.9 = (f32[1,2,96,1024]{3,2,1,0:T(8,128)S(1)}, f32[1,2,96,1024]{3,2,1,0:T(8,128)}, u32[]{:S(2)}) copy-start(f32[1,2,96,1024]{3,2,1,0:T(8,128)} %param.7) | copy-start | bytes 2359300
  26.8 14.8 %all-to-all-start = ((f32[32,1,1153]{2,1,0:T(1,128)}), f32[32,1,1153]{2,1,0:T(1,128)S(1)}, u32[]{:S(2)}, u32[]{:S(2)}) async-start(f32[32,1,1153]{2,1,0:T(1,128)} %broadcast_in_dim.41), calls=%async_computation | async-start | bytes 327680 | tf_op jit(solution)/shard_map/all_to_all | solution.py:114
  61.5 6.6 %collective-permute-start.4 = (f32[1,96,256]{2,1,0:T(8,128)S(1)}, f32[1,96,256]{2,1,0:T(8,128)S(1)}, u32[]{:S(2)}, u32[]{:S(2)}) collective-permute-start(f32[1,96,256]{2,1,0:T(8,128)S(1)} %get-tuple-element.28), channel_id=1, source_target_pairs={{0,4},{4,8},{8,12},{12,16},{16,20},{20,24},{24,28},{1,5},{5,9},{9,... | collective-permute-start | bytes 294920 | tf_op jit(solution)/shard_map/ppermute | solution.py:20
  63.9 4.3 %collective-permute-start.5 = (f32[1,96,256]{2,1,0:T(8,128)S(1)}, f32[1,96,256]{2,1,0:T(8,128)S(1)}, u32[]{:S(2)}, u32[]{:S(2)}) collective-permute-start(f32[1,96,256]{2,1,0:T(8,128)S(1)} %get-tuple-element.29), channel_id=1, source_target_pairs={{4,0},{8,4},{12,8},{16,12},{20,16},{24,20},{28,24},{5,1},{9,5},{13... | collective-permute-start | bytes 294920 | tf_op jit(solution)/shard_map/ppermute | solution.py:21
  65.2 6.6 %collective-permute-start.6 = (f32[2,96,256]{2,1,0:T(8,128)S(1)}, f32[2,96,256]{2,1,0:T(8,128)S(1)}, u32[]{:S(2)}, u32[]{:S(2)}) collective-permute-start(f32[2,96,256]{2,1,0:T(8,128)S(1)} %get-tuple-element.32), channel_id=1, source_target_pairs={{0,1},{1,2},{2,3},{4,5},{5,6},{6,7},{8,9},{9,10},{10,11},{12,13},{... | collective-permute-start | bytes 589832 | tf_op jit(solution)/shard_map/ppermute | solution.py:24
  66.9 9.5 %collective-permute-start.7 = (f32[2,96,256]{2,1,0:T(8,128)S(1)}, f32[2,96,256]{2,1,0:T(8,128)S(1)}, u32[]{:S(2)}, u32[]{:S(2)}) collective-permute-start(f32[2,96,256]{2,1,0:T(8,128)S(1)} %get-tuple-element.33), channel_id=1, source_target_pairs={{1,0},{2,1},{3,2},{5,4},{6,5},{7,6},{9,8},{10,9},{11,10},{13,12},{... | collective-permute-start | bytes 589832 | tf_op jit(solution)/shard_map/ppermute | solution.py:25
  99.6 17.2 %copy-start = (f32[2,96,1024]{2,1,0:T(8,128)}, f32[2,96,1024]{2,1,0:T(8,128)S(1)}, u32[]{:S(2)}) copy-start(f32[2,96,1024]{2,1,0:T(8,128)S(1)} %sub.94) | copy-start | bytes 2359300
  100.4 6.6 %collective-permute-start.8 = (f32[1,96,256]{2,1,0:T(8,128)S(1)}, f32[1,96,256]{2,1,0:T(8,128)S(1)}, u32[]{:S(2)}, u32[]{:S(2)}) collective-permute-start(f32[1,96,256]{2,1,0:T(8,128)S(1)} %get-tuple-element.22), channel_id=1, source_target_pairs={{0,4},{4,8},{8,12},{12,16},{16,20},{20,24},{24,28},{1,5},{5,9},{9,... | collective-permute-start | bytes 294920 | tf_op jit(solution)/shard_map/ppermute | solution.py:20
  102.8 4.3 %collective-permute-start.9 = (f32[1,96,256]{2,1,0:T(8,128)S(1)}, f32[1,96,256]{2,1,0:T(8,128)S(1)}, u32[]{:S(2)}, u32[]{:S(2)}) collective-permute-start(f32[1,96,256]{2,1,0:T(8,128)S(1)} %get-tuple-element.23), channel_id=1, source_target_pairs={{4,0},{8,4},{12,8},{16,12},{20,16},{24,20},{28,24},{5,1},{9,5},{13... | collective-permute-start | bytes 294920 | tf_op jit(solution)/shard_map/ppermute | solution.py:21
  104.1 6.6 %collective-permute-start.10 = (f32[2,96,256]{2,1,0:T(8,128)S(1)}, f32[2,96,256]{2,1,0:T(8,128)S(1)}, u32[]{:S(2)}, u32[]{:S(2)}) collective-permute-start(f32[2,96,256]{2,1,0:T(8,128)S(1)} %get-tuple-element.26), channel_id=1, source_target_pairs={{0,1},{1,2},{2,3},{4,5},{5,6},{6,7},{8,9},{9,10},{10,11},{12,13},{... | collective-permute-start | bytes 589832 | tf_op jit(solution)/shard_map/ppermute | solution.py:24
  105.7 9.5 %collective-permute-start.11 = (f32[2,96,256]{2,1,0:T(8,128)S(1)}, f32[2,96,256]{2,1,0:T(8,128)S(1)}, u32[]{:S(2)}, u32[]{:S(2)}) collective-permute-start(f32[2,96,256]{2,1,0:T(8,128)S(1)} %get-tuple-element.27), channel_id=1, source_target_pairs={{1,0},{2,1},{3,2},{5,4},{6,5},{7,6},{9,8},{10,9},{11,10},{13,12},{... | collective-permute-start | bytes 589832 | tf_op jit(solution)/shard_map/ppermute | solution.py:25
  119.4 12.5 %all-to-all-start.3 = ((f32[32,1,1248]{2,1,0:T(1,128)}), f32[32,1,1248]{2,1,0:T(1,128)}, u32[]{:S(2)}, u32[]{:S(2)}) async-start(f32[32,1,1248]{2,1,0:T(1,128)} %broadcast_in_dim.47), calls=%async_computation.3 | async-start | bytes 327680 | tf_op jit(solution)/shard_map/all_to_all | solution.py:114
  136.5 2.6 %copy-start.3 = (bf16[1,2,1024,1024]{3,2,1,0:T(8,128)(2,1)S(1)}, bf16[1,2,1024,1024]{3,2,1,0:T(8,128)(2,1)}, u32[]{:S(2)}) copy-start(bf16[1,2,1024,1024]{3,2,1,0:T(8,128)(2,1)} %param.9) | copy-start | bytes 12582916
  140.0 6.6 %collective-permute-start.12 = (f32[1,96,256]{2,1,0:T(8,128)S(1)}, f32[1,96,256]{2,1,0:T(8,128)S(1)}, u32[]{:S(2)}, u32[]{:S(2)}) collective-permute-start(f32[1,96,256]{2,1,0:T(8,128)S(1)} %get-tuple-element.16), channel_id=1, source_target_pairs={{0,4},{4,8},{8,12},{12,16},{16,20},{20,24},{24,28},{1,5},{5,9},{9,... | collective-permute-start | bytes 294920 | tf_op jit(solution)/shard_map/ppermute | solution.py:20
  142.3 4.3 %collective-permute-start.13 = (f32[1,96,256]{2,1,0:T(8,128)S(1)}, f32[1,96,256]{2,1,0:T(8,128)S(1)}, u32[]{:S(2)}, u32[]{:S(2)}) collective-permute-start(f32[1,96,256]{2,1,0:T(8,128)S(1)} %get-tuple-element.17), channel_id=1, source_target_pairs={{4,0},{8,4},{12,8},{16,12},{20,16},{24,20},{28,24},{5,1},{9,5},{13... | collective-permute-start | bytes 294920 | tf_op jit(solution)/shard_map/ppermute | solution.py:21
  143.6 6.6 %collective-permute-start.14 = (f32[2,96,256]{2,1,0:T(8,128)S(1)}, f32[2,96,256]{2,1,0:T(8,128)S(1)}, u32[]{:S(2)}, u32[]{:S(2)}) collective-permute-start(f32[2,96,256]{2,1,0:T(8,128)S(1)} %get-tuple-element.20), channel_id=1, source_target_pairs={{0,1},{1,2},{2,3},{4,5},{5,6},{6,7},{8,9},{9,10},{10,11},{12,13},{... | collective-permute-start | bytes 589832 | tf_op jit(solution)/shard_map/ppermute | solution.py:24
  145.3 9.5 %collective-permute-start.15 = (f32[2,96,256]{2,1,0:T(8,128)S(1)}, f32[2,96,256]{2,1,0:T(8,128)S(1)}, u32[]{:S(2)}, u32[]{:S(2)}) collective-permute-start(f32[2,96,256]{2,1,0:T(8,128)S(1)} %get-tuple-element.21), channel_id=1, source_target_pairs={{1,0},{2,1},{3,2},{5,4},{6,5},{7,6},{9,8},{10,9},{11,10},{13,12},{... | collective-permute-start | bytes 589832 | tf_op jit(solution)/shard_map/ppermute | solution.py:25
  172.6 2.8 %copy-start.5 = (bf16[1,2,1024,1024]{3,2,1,0:T(8,128)(2,1)S(1)}, bf16[1,2,1024,1024]{3,2,1,0:T(8,128)(2,1)}, u32[]{:S(2)}) copy-start(bf16[1,2,1024,1024]{3,2,1,0:T(8,128)(2,1)} %param.8) | copy-start | bytes 12582916
  175.4 17.2 %copy-start.8 = (f32[2,96,1024]{2,1,0:T(8,128)}, f32[2,96,1024]{2,1,0:T(8,128)S(1)}, u32[]{:S(2)}) copy-start(f32[2,96,1024]{2,1,0:T(8,128)S(1)} %multiply_add_fusion) | copy-start | bytes 2359300
  176.3 6.6 %collective-permute-start.16 = (f32[1,96,256]{2,1,0:T(8,128)S(1)}, f32[1,96,256]{2,1,0:T(8,128)S(1)}, u32[]{:S(2)}, u32[]{:S(2)}) collective-permute-start(f32[1,96,256]{2,1,0:T(8,128)S(1)} %get-tuple-element.10), channel_id=1, source_target_pairs={{0,4},{4,8},{8,12},{12,16},{16,20},{20,24},{24,28},{1,5},{5,9},{9,... | collective-permute-start | bytes 294920 | tf_op jit(solution)/shard_map/ppermute | solution.py:20
  178.6 4.3 %collective-permute-start.17 = (f32[1,96,256]{2,1,0:T(8,128)S(1)}, f32[1,96,256]{2,1,0:T(8,128)S(1)}, u32[]{:S(2)}, u32[]{:S(2)}) collective-permute-start(f32[1,96,256]{2,1,0:T(8,128)S(1)} %get-tuple-element.11), channel_id=1, source_target_pairs={{4,0},{8,4},{12,8},{16,12},{20,16},{24,20},{28,24},{5,1},{9,5},{13... | collective-permute-start | bytes 294920 | tf_op jit(solution)/shard_map/ppermute | solution.py:21
  179.9 6.6 %collective-permute-start.18 = (f32[2,96,256]{2,1,0:T(8,128)S(1)}, f32[2,96,256]{2,1,0:T(8,128)S(1)}, u32[]{:S(2)}, u32[]{:S(2)}) collective-permute-start(f32[2,96,256]{2,1,0:T(8,128)S(1)} %get-tuple-element.14), channel_id=1, source_target_pairs={{0,1},{1,2},{2,3},{4,5},{5,6},{6,7},{8,9},{9,10},{10,11},{12,13},{... | collective-permute-start | bytes 589832 | tf_op jit(solution)/shard_map/ppermute | solution.py:24
  181.6 9.5 %collective-permute-start.19 = (f32[2,96,256]{2,1,0:T(8,128)S(1)}, f32[2,96,256]{2,1,0:T(8,128)S(1)}, u32[]{:S(2)}, u32[]{:S(2)}) collective-permute-start(f32[2,96,256]{2,1,0:T(8,128)S(1)} %get-tuple-element.15), channel_id=1, source_target_pairs={{1,0},{2,1},{3,2},{5,4},{6,5},{7,6},{9,8},{10,9},{11,10},{13,12},{... | collective-permute-start | bytes 589832 | tf_op jit(solution)/shard_map/ppermute | solution.py:25
  192.5 12.2 %copy-start.1 = (f32[2,96,1024]{2,1,0:T(8,128)S(1)}, f32[2,96,1024]{2,1,0:T(8,128)}, u32[]{:S(2)}) copy-start(f32[2,96,1024]{2,1,0:T(8,128)} %copy-done) | copy-start | bytes 2359300
  192.5 12.2 %copy-start.7 = (f32[2,96,1024]{2,1,0:T(8,128)S(1)}, f32[2,96,1024]{2,1,0:T(8,128)}, u32[]{:S(2)}) copy-start(f32[2,96,1024]{2,1,0:T(8,128)} %copy-done.6) | copy-start | bytes 2359300
  (6 other events, 8.2 us)

commit v12 on v7

--- a/solution.py
+++ b/solution.py
@@ -11,6 +11,10 @@
 
 
 def neighbors(d0, d1, d2, d3):
+    return jnp.stack(neighbor_parts(d0, d1, d2, d3), axis=1)
+
+
+def neighbor_parts(d0, d1, d2, d3):
     sub_count = lax.axis_size("sub")
     grp_count = lax.axis_size("grp")
     up_sub = [(i, i + 1) for i in range(sub_count - 1)]
@@ -23,7 +27,7 @@
     from_right = jnp.concatenate([d0[1:], right_dev], axis=0)
     from_below = lax.ppermute(d3, "grp", up_grp)
     from_above = lax.ppermute(d2, "grp", down_grp)
-    return jnp.stack([from_left, from_right, from_below, from_above], axis=1)
+    return [from_left, from_right, from_below, from_above]
 
 
 def face_split(values):
@@ -101,8 +105,15 @@
         return jnp.moveaxis(to_mine(raw), 1, 2).reshape(shape)
 
     def jump(values):
-        raw = neighbors(*face_split(values))
-        return values - partner_values(raw, values.shape)
+        parts = neighbor_parts(*face_split(values))
+        beside = jnp.einsum(
+            "sfcq,sfqr->sfcr", jnp.stack(parts[:2], axis=1), permutes[:, :2], precision=HIGHEST
+        )
+        across = jnp.einsum(
+            "sfcq,sfqr->sfcr", jnp.stack(parts[2:], axis=1), permutes[:, 2:], precision=HIGHEST
+        )
+        partner = jnp.concatenate([beside, across], axis=1)
+        return values - jnp.moveaxis(partner, 1, 2).reshape(values.shape)
 
     def coefficients(values):
         return jnp.einsum("skm,snm->skn", weighted_modes, values, precision=HIGHEST)

time: 206 us -> 205 us (level)
  matrix products: 18.6 us -> 23.5 us
  waiting for transfers between devices: 54.4 us -> 50.2 us
  local copies, waits for them, and re-layouts: 19.6 us -> 16.4 us
    dot_general x0 -> x8, matrix products: none -> 6.14 us  [the longest x4 3.07 us: jump(): jnp.einsum('sfcq,sfqr->sfcr', jnp.stack(parts[:2], axis=1), permutes[:, :...]
    dot_general x6 -> x2, matrix products: 8.1 us -> 3.27 us  [to_mine(): return jnp.einsum('sfcq,sfqr->sfcr', raw, permutes, precision=HIGHEST)]
    dot_general x5, matrix products: 1.4 us -> 4.97 us  [lift(): jnp.einsum('sfkc,cn->skfn', partner_rows, flat, precision=HIGHEST)]
    ppermute x20, waiting for transfers between devices: 39.9 us -> 36.6 us  [the longest x5 23.2 us: neighbor_parts(): from_above = lax.ppermute(d2, 'grp', down_grp)]
    unnamed x46 -> x50, local copies, waits for them, and re-layouts: 7.74 us -> 8.33 us
  transfers between devices with their start and end apart: 22 -> 22, of which waited for: 12 -> 12; matrix products, arithmetic and copies ran while one was open for 2% -> 4% of each run, Pallas kernels for 0% -> 0%
where the time goes in v12:
time: 205 us; the launch traced here: 203 us
  waiting for transfers between devices  50.2 us (24%)
  blocking collectives  46 us (22%)
  starting transfers between devices  45.8 us (22%)
  matrix products  23.5 us (11%)
  other arithmetic  19.5 us (10%)
  local copies, waits for them, and re-layouts  16.4 us (8%)
    all_to_all x4, blocking collectives, gathered(): everything = lax.all_to_all(copies, ('grp', 'sub'), 0, 0, tiled=True)  46 us
    ppermute x5, waiting for transfers between devices, neighbor_parts(): from_above = lax.ppermute(d2, 'grp', down_grp)  23.2 us
    all_to_all x2, waiting for transfers between devices, gathered(): everything = lax.all_to_all(copies, ('grp', 'sub'), 0, 0, tiled=True)  13.6 us
    ppermute x5, waiting for transfers between devices, neighbor_parts(): from_below = lax.ppermute(d3, 'grp', up_grp)  13.4 us
    ppermute x5, starting transfers between devices, neighbor_parts(): left_dev = lax.ppermute(d1[-1:], 'sub', up_sub)  11.6 us
    ppermute x5, starting transfers between devices, neighbor_parts(): from_below = lax.ppermute(d3, 'grp', up_grp)  11 us
    all_to_all x2, starting transfers between devices, gathered(): everything = lax.all_to_all(copies, ('grp', 'sub'), 0, 0, tiled=True)  10.2 us
    unnamed x50, local copies, waits for them, and re-layouts  8.33 us
  transfers between devices with their start and end apart: 22, of which 12 were waited for; matrix products, arithmetic and copies ran while one was open for 4% of the time, Pallas kernels for 0%

profile of v12, /device:TPU:0, one launch (start us, length us, event | category | flops | bytes accessed | tf_op | source)
XLA Modules:
  0.0 203.3 jit_solution(11675323552896482975)
XLA Ops:
  4.4 2.4 %collective-permute-start = (f32[1,112,256]{2,1,0:T(8,128)S(1)}, f32[1,112,256]{2,1,0:T(8,128)S(1)}, u32[]{:S(2)}, u32[]{:S(2)}) collective-permute-start(f32[1,112,256]{2,1,0:T(8,128)S(1)} %get-tuple-element.38), channel_id=1, source_target_pairs={{0,4},{4,8},{8,12},{12,16},{16,20},{20,24},{24,28},{1,5},{5,9},{9,... | collective-permute-start | bytes 344072 | tf_op jit(solution)/shard_map/ppermute | solution.py:24
  8.1 4.3 %collective-permute-start.2 = (f32[2,112,256]{2,1,0:T(8,128)S(1)}, f32[2,112,256]{2,1,0:T(8,128)S(1)}, u32[]{:S(2)}, u32[]{:S(2)}) collective-permute-start(f32[2,112,256]{2,1,0:T(8,128)S(1)} %get-tuple-element.48), channel_id=1, source_target_pairs={{0,1},{1,2},{2,3},{4,5},{5,6},{6,7},{8,9},{9,10},{10,11},{12,13},{... | collective-permute-start | bytes 688136 | tf_op jit(solution)/shard_map/ppermute | solution.py:28
  14.3 2.6 %collective-permute-done.2 = f32[2,112,256]{2,1,0:T(8,128)S(1)} collective-permute-done((f32[2,112,256]{2,1,0:T(8,128)S(1)}, f32[2,112,256]{2,1,0:T(8,128)S(1)}, u32[]{:S(2)}, u32[]{:S(2)}) %collective-permute-start.2) | collective-permute-done | bytes 229408 | tf_op jit(solution)/shard_map/ppermute | solution.py:28
  16.9 4.7 %collective-permute-done.3 = f32[2,112,256]{2,1,0:T(8,128)S(1)} collective-permute-done((f32[2,112,256]{2,1,0:T(8,128)S(1)}, f32[2,112,256]{2,1,0:T(8,128)S(1)}, u32[]{:S(2)}, u32[]{:S(2)}) %collective-permute-start.3) | collective-permute-done | bytes 229408 | tf_op jit(solution)/shard_map/ppermute | solution.py:29
  27.4 6.2 %all-to-all-start = ((f32[32,1,1153]{2,1,0:T(1,128)}), f32[32,1,1153]{2,1,0:T(1,128)S(1)}, u32[]{:S(2)}, u32[]{:S(2)}) async-start(f32[32,1,1153]{2,1,0:T(1,128)} %broadcast_in_dim.41), calls=%async_computation | async-start | bytes 327680 | tf_op jit(solution)/shard_map/all_to_all | solution.py:125
  34.5 1.9 convolution_bitcast_fusion.1
  36.4 5.8 %all-to-all-done = f32[32,1,1153]{2,1,0:T(1,128)S(1)} async-done(((f32[32,1,1153]{2,1,0:T(1,128)}), f32[32,1,1153]{2,1,0:T(1,128)S(1)}, u32[]{:S(2)}, u32[]{:S(2)}) %all-to-all-start) | async-done | bytes 147616 | tf_op jit(solution)/shard_map/all_to_all | solution.py:125
  44.1 1.5 fusion.70
  46.6 10.7 %all_to_all.51 = f32[32,1,1153]{2,1,0:T(1,128)S(1)} all-to-all(f32[32,1,1153]{2,1,0:T(1,128)S(1)} %broadcast_in_dim.43), channel_id=1, replica_groups=mesh['sub'=8,'grp'=4] {'grp','sub'}, dimensions={0} | all-to-all | bytes 295168 | tf_op jit(solution)/shard_map/all_to_all | solution.py:125
  63.5 2.3 %collective-permute-start.4 = (f32[1,96,256]{2,1,0:T(8,128)S(1)}, f32[1,96,256]{2,1,0:T(8,128)S(1)}, u32[]{:S(2)}, u32[]{:S(2)}) collective-permute-start(f32[1,96,256]{2,1,0:T(8,128)S(1)} %get-tuple-element.28), channel_id=1, source_target_pairs={{0,4},{4,8},{8,12},{12,16},{16,20},{20,24},{24,28},{1,5},{5,9},{9,... | collective-permute-start | bytes 294920 | tf_op jit(solution)/shard_map/ppermute | solution.py:24
  67.2 1.7 collective-permute-start.6
  71.0 2.8 %collective-permute-done.6 = f32[2,96,256]{2,1,0:T(8,128)S(1)} collective-permute-done((f32[2,96,256]{2,1,0:T(8,128)S(1)}, f32[2,96,256]{2,1,0:T(8,128)S(1)}, u32[]{:S(2)}, u32[]{:S(2)}) %collective-permute-start.6) | collective-permute-done | bytes 196640 | tf_op jit(solution)/shard_map/ppermute | solution.py:28
  73.7 4.6 %collective-permute-done.7 = f32[2,96,256]{2,1,0:T(8,128)S(1)} collective-permute-done((f32[2,96,256]{2,1,0:T(8,128)S(1)}, f32[2,96,256]{2,1,0:T(8,128)S(1)}, u32[]{:S(2)}, u32[]{:S(2)}) %collective-permute-start.7) | collective-permute-done | bytes 196640 | tf_op jit(solution)/shard_map/ppermute | solution.py:29
  81.3 12.2 %all_to_all.52 = f32[32,1,1248]{2,1,0:T(1,128)S(1)} all-to-all(f32[32,1,1248]{2,1,0:T(1,128)S(1)} %broadcast_in_dim.45), channel_id=1, replica_groups=mesh['sub'=8,'grp'=4] {'grp','sub'}, dimensions={0} | all-to-all | bytes 319488 | tf_op jit(solution)/shard_map/all_to_all | solution.py:125
  99.1 2.3 %collective-permute-start.8 = (f32[1,96,256]{2,1,0:T(8,128)S(1)}, f32[1,96,256]{2,1,0:T(8,128)S(1)}, u32[]{:S(2)}, u32[]{:S(2)}) collective-permute-start(f32[1,96,256]{2,1,0:T(8,128)S(1)} %get-tuple-element.22), channel_id=1, source_target_pairs={{0,4},{4,8},{8,12},{12,16},{16,20},{20,24},{24,28},{1,5},{5,9},{9,... | collective-permute-start | bytes 294920 | tf_op jit(solution)/shard_map/ppermute | solution.py:24
  102.8 1.7 collective-permute-start.10
  106.6 2.7 %collective-permute-done.10 = f32[2,96,256]{2,1,0:T(8,128)S(1)} collective-permute-done((f32[2,96,256]{2,1,0:T(8,128)S(1)}, f32[2,96,256]{2,1,0:T(8,128)S(1)}, u32[]{:S(2)}, u32[]{:S(2)}) %collective-permute-start.10) | collective-permute-done | bytes 196640 | tf_op jit(solution)/shard_map/ppermute | solution.py:28
  109.3 4.6 %collective-permute-done.11 = f32[2,96,256]{2,1,0:T(8,128)S(1)} collective-permute-done((f32[2,96,256]{2,1,0:T(8,128)S(1)}, f32[2,96,256]{2,1,0:T(8,128)S(1)}, u32[]{:S(2)}, u32[]{:S(2)}) %collective-permute-start.11) | collective-permute-done | bytes 196640 | tf_op jit(solution)/shard_map/ppermute | solution.py:29
  117.6 3.9 %all-to-all-start.3 = ((f32[32,1,1248]{2,1,0:T(1,128)}), f32[32,1,1248]{2,1,0:T(1,128)}, u32[]{:S(2)}, u32[]{:S(2)}) async-start(f32[32,1,1248]{2,1,0:T(1,128)} %broadcast_in_dim.47), calls=%async_computation.3 | async-start | bytes 327680 | tf_op jit(solution)/shard_map/all_to_all | solution.py:125
  122.3 7.8 %all-to-all-done.3 = f32[32,1,1248]{2,1,0:T(1,128)} async-done(((f32[32,1,1248]{2,1,0:T(1,128)}), f32[32,1,1248]{2,1,0:T(1,128)}, u32[]{:S(2)}, u32[]{:S(2)}) %all-to-all-start.3) | async-done | bytes 159776 | tf_op jit(solution)/shard_map/all_to_all | solution.py:125
  137.8 2.3 %collective-permute-start.12 = (f32[1,96,256]{2,1,0:T(8,128)S(1)}, f32[1,96,256]{2,1,0:T(8,128)S(1)}, u32[]{:S(2)}, u32[]{:S(2)}) collective-permute-start(f32[1,96,256]{2,1,0:T(8,128)S(1)} %get-tuple-element.16), channel_id=1, source_target_pairs={{0,4},{4,8},{8,12},{12,16},{16,20},{20,24},{24,28},{1,5},{5,9},{9,... | collective-permute-start | bytes 294920 | tf_op jit(solution)/shard_map/ppermute | solution.py:24
  141.4 1.7 collective-permute-start.14
  145.2 2.8 %collective-permute-done.14 = f32[2,96,256]{2,1,0:T(8,128)S(1)} collective-permute-done((f32[2,96,256]{2,1,0:T(8,128)S(1)}, f32[2,96,256]{2,1,0:T(8,128)S(1)}, u32[]{:S(2)}, u32[]{:S(2)}) %collective-permute-start.14) | collective-permute-done | bytes 196640 | tf_op jit(solution)/shard_map/ppermute | solution.py:28
  148.0 4.6 %collective-permute-done.15 = f32[2,96,256]{2,1,0:T(8,128)S(1)} collective-permute-done((f32[2,96,256]{2,1,0:T(8,128)S(1)}, f32[2,96,256]{2,1,0:T(8,128)S(1)}, u32[]{:S(2)}, u32[]{:S(2)}) %collective-permute-start.15) | collective-permute-done | bytes 196640 | tf_op jit(solution)/shard_map/ppermute | solution.py:29
  155.5 12.2 %all_to_all.53 = f32[32,1,1248]{2,1,0:T(1,128)S(1)} all-to-all(f32[32,1,1248]{2,1,0:T(1,128)S(1)} %broadcast_in_dim.93), channel_id=1, replica_groups=mesh['sub'=8,'grp'=4] {'grp','sub'}, dimensions={0} | all-to-all | bytes 319488 | tf_op jit(solution)/shard_map/all_to_all | solution.py:125
  170.6 1.6 multiply_add_fusion
  173.0 2.3 %collective-permute-start.16 = (f32[1,96,256]{2,1,0:T(8,128)S(1)}, f32[1,96,256]{2,1,0:T(8,128)S(1)}, u32[]{:S(2)}, u32[]{:S(2)}) collective-permute-start(f32[1,96,256]{2,1,0:T(8,128)S(1)} %get-tuple-element.10), channel_id=1, source_target_pairs={{0,4},{4,8},{8,12},{12,16},{16,20},{20,24},{24,28},{1,5},{5,9},{9,... | collective-permute-start | bytes 294920 | tf_op jit(solution)/shard_map/ppermute | solution.py:24
  176.7 1.7 collective-permute-start.18
  180.7 2.5 %collective-permute-done.18 = f32[2,96,256]{2,1,0:T(8,128)S(1)} collective-permute-done((f32[2,96,256]{2,1,0:T(8,128)S(1)}, f32[2,96,256]{2,1,0:T(8,128)S(1)}, u32[]{:S(2)}, u32[]{:S(2)}) %collective-permute-start.18) | collective-permute-done | bytes 196640 | tf_op jit(solution)/shard_map/ppermute | solution.py:28
  183.2 4.6 %collective-permute-done.19 = f32[2,96,256]{2,1,0:T(8,128)S(1)} collective-permute-done((f32[2,96,256]{2,1,0:T(8,128)S(1)}, f32[2,96,256]{2,1,0:T(8,128)S(1)}, u32[]{:S(2)}, u32[]{:S(2)}) %collective-permute-start.19) | collective-permute-done | bytes 196640 | tf_op jit(solution)/shard_map/ppermute | solution.py:29
  189.1 10.8 %all_to_all.54 = f32[32,1,96]{2,1,0:T(1,128)S(1)} all-to-all(f32[32,1,96]{2,1,0:T(1,128)S(1)} %broadcast_in_dim.95), channel_id=1, replica_groups=mesh['sub'=8,'grp'=4] {'grp','sub'}, dimensions={0} | all-to-all | bytes 24576 | tf_op jit(solution)/shard_map/all_to_all | solution.py:125
  199.9 3.4 %subtract_bitcast_fusion = (f32[1,2,96,1024]{3,2,1,0:T(8,128)}, f32[1,2,96,1024]{3,2,1,0:T(8,128)}) fusion(f32[2,96,1024]{2,1,0:T(8,128)S(1)} %get-tuple-element.3, f32[96]{0:T(128)S(1)} %div.27, f32[2,96,1024]{2,1,0:T(8,128)S(1)} %fusion.70, f32[2,96,1024]{2,1,0:T(8,128)} %copy-done.5, f32[96]{0:T(128)S(1)} %div.25, f32[2,96,1024]{2,1,0:T(8,128)} %copy-done.6, ...), kind=kLoop, calls=%fused_computation.52 | loop fusion | flops 1376256 | bytes 5505792 | tf_op jit(solution)/shard_map/broadcast_in_dim | solution.py:175
  (211 shorter events, 64.2 us)
Async XLA Ops:
  0.6 13.1 %copy-start.18 = (s32[1,2,1024]{2,1,0:T(2,128)S(1)}, s32[1,2,1024]{2,1,0:T(2,128)}, u32[]{:S(2)}) copy-start(s32[1,2,1024]{2,1,0:T(2,128)} %param.12) | copy-start | bytes 24580
  0.6 13.2 %copy-start.11 = (f32[1,2,6,1024]{3,1,2,0:T(2,128)S(1)}, f32[1,2,6,1024]{3,1,2,0:T(2,128)}, u32[]{:S(2)}) copy-start(f32[1,2,6,1024]{3,1,2,0:T(2,128)} %param.10) | copy-start | bytes 147460
  3.0 19.3 %copy-start.19 = (s32[4]{0:T(128)S(1)}, s32[4]{0:T(128)}, u32[]{:S(2)}) copy-start(s32[4]{0:T(128)} %constant.38) | copy-start | bytes 52
  4.4 9.9 %collective-permute-start = (f32[1,112,256]{2,1,0:T(8,128)S(1)}, f32[1,112,256]{2,1,0:T(8,128)S(1)}, u32[]{:S(2)}, u32[]{:S(2)}) collective-permute-start(f32[1,112,256]{2,1,0:T(8,128)S(1)} %get-tuple-element.38), channel_id=1, source_target_pairs={{0,4},{4,8},{8,12},{12,16},{16,20},{20,24},{24,28},{1,5},{5,9},{9,... | collective-permute-start | bytes 344072 | tf_op jit(solution)/shard_map/ppermute | solution.py:24
  6.8 7.5 %collective-permute-start.1 = (f32[1,112,256]{2,1,0:T(8,128)S(1)}, f32[1,112,256]{2,1,0:T(8,128)S(1)}, u32[]{:S(2)}, u32[]{:S(2)}) collective-permute-start(f32[1,112,256]{2,1,0:T(8,128)S(1)} %get-tuple-element.41), channel_id=1, source_target_pairs={{4,0},{8,4},{12,8},{16,12},{20,16},{24,20},{28,24},{5,1},{9,5},{13... | collective-permute-start | bytes 344072 | tf_op jit(solution)/shard_map/ppermute | solution.py:25
  8.1 8.8 %collective-permute-start.2 = (f32[2,112,256]{2,1,0:T(8,128)S(1)}, f32[2,112,256]{2,1,0:T(8,128)S(1)}, u32[]{:S(2)}, u32[]{:S(2)}) collective-permute-start(f32[2,112,256]{2,1,0:T(8,128)S(1)} %get-tuple-element.48), channel_id=1, source_target_pairs={{0,1},{1,2},{2,3},{4,5},{5,6},{6,7},{8,9},{9,10},{10,11},{12,13},{... | collective-permute-start | bytes 688136 | tf_op jit(solution)/shard_map/ppermute | solution.py:28
  12.4 9.2 %collective-permute-start.3 = (f32[2,112,256]{2,1,0:T(8,128)S(1)}, f32[2,112,256]{2,1,0:T(8,128)S(1)}, u32[]{:S(2)}, u32[]{:S(2)}) collective-permute-start(f32[2,112,256]{2,1,0:T(8,128)S(1)} %get-tuple-element.49), channel_id=1, source_target_pairs={{1,0},{2,1},{3,2},{5,4},{6,5},{7,6},{9,8},{10,9},{11,10},{13,12},{... | collective-permute-start | bytes 688136 | tf_op jit(solution)/shard_map/ppermute | solution.py:29
  16.9 4.8 %copy-start.12 = (f32[2,112,256]{2,1,0:T(8,128)}, f32[2,112,256]{2,1,0:T(8,128)S(1)}, u32[]{:S(2)}) copy-start(f32[2,112,256]{2,1,0:T(8,128)S(1)} %collective-permute-done.2) | copy-start | bytes 688132
  21.7 4.1 %copy-start.7 = (f32[1,2,96,1024]{3,2,1,0:T(8,128)S(1)}, f32[1,2,96,1024]{3,2,1,0:T(8,128)}, u32[]{:S(2)}) copy-start(f32[1,2,96,1024]{3,2,1,0:T(8,128)} %param.7) | copy-start | bytes 2359300
  27.4 14.8 %all-to-all-start = ((f32[32,1,1153]{2,1,0:T(1,128)}), f32[32,1,1153]{2,1,0:T(1,128)S(1)}, u32[]{:S(2)}, u32[]{:S(2)}) async-start(f32[32,1,1153]{2,1,0:T(1,128)} %broadcast_in_dim.41), calls=%async_computation | async-start | bytes 327680 | tf_op jit(solution)/shard_map/all_to_all | solution.py:125
  34.4 8.4 %copy-start.17 = (f32[2,4,6,384]{3,2,1,0:T(8,128)}, f32[2,4,6,384]{3,2,1,0:T(8,128)S(1)}, u32[]{:S(2)}) copy-start(f32[2,4,6,384]{3,2,1,0:T(8,128)S(1)} %reshape.199) | copy-start | bytes 221188
  57.3 6.2 %copy-start.14 = (f32[32,1,1153]{2,0,1:T(8,128)}, f32[32,1,1153]{2,0,1:T(8,128)S(1)}, u32[]{:S(2)}) copy-start(f32[32,1,1153]{2,0,1:T(8,128)S(1)} %copy.254) | copy-start | bytes 442756
  63.5 6.6 %collective-permute-start.4 = (f32[1,96,256]{2,1,0:T(8,128)S(1)}, f32[1,96,256]{2,1,0:T(8,128)S(1)}, u32[]{:S(2)}, u32[]{:S(2)}) collective-permute-start(f32[1,96,256]{2,1,0:T(8,128)S(1)} %get-tuple-element.28), channel_id=1, source_target_pairs={{0,4},{4,8},{8,12},{12,16},{16,20},{20,24},{24,28},{1,5},{5,9},{9,... | collective-permute-start | bytes 294920 | tf_op jit(solution)/shard_map/ppermute | solution.py:24
  65.9 4.3 %collective-permute-start.5 = (f32[1,96,256]{2,1,0:T(8,128)S(1)}, f32[1,96,256]{2,1,0:T(8,128)S(1)}, u32[]{:S(2)}, u32[]{:S(2)}) collective-permute-start(f32[1,96,256]{2,1,0:T(8,128)S(1)} %get-tuple-element.29), channel_id=1, source_target_pairs={{4,0},{8,4},{12,8},{16,12},{20,16},{24,20},{28,24},{5,1},{9,5},{13... | collective-permute-start | bytes 294920 | tf_op jit(solution)/shard_map/ppermute | solution.py:25
  67.2 6.6 %collective-permute-start.6 = (f32[2,96,256]{2,1,0:T(8,128)S(1)}, f32[2,96,256]{2,1,0:T(8,128)S(1)}, u32[]{:S(2)}, u32[]{:S(2)}) collective-permute-start(f32[2,96,256]{2,1,0:T(8,128)S(1)} %get-tuple-element.32), channel_id=1, source_target_pairs={{0,1},{1,2},{2,3},{4,5},{5,6},{6,7},{8,9},{9,10},{10,11},{12,13},{... | collective-permute-start | bytes 589832 | tf_op jit(solution)/shard_map/ppermute | solution.py:28
  68.8 9.5 %collective-permute-start.7 = (f32[2,96,256]{2,1,0:T(8,128)S(1)}, f32[2,96,256]{2,1,0:T(8,128)S(1)}, u32[]{:S(2)}, u32[]{:S(2)}) collective-permute-start(f32[2,96,256]{2,1,0:T(8,128)S(1)} %get-tuple-element.33), channel_id=1, source_target_pairs={{1,0},{2,1},{3,2},{5,4},{6,5},{7,6},{9,8},{10,9},{11,10},{13,12},{... | collective-permute-start | bytes 589832 | tf_op jit(solution)/shard_map/ppermute | solution.py:29
  98.3 16.6 %copy-start = (f32[2,96,1024]{2,1,0:T(8,128)}, f32[2,96,1024]{2,1,0:T(8,128)S(1)}, u32[]{:S(2)}) copy-start(f32[2,96,1024]{2,1,0:T(8,128)S(1)} %sub.98) | copy-start | bytes 2359300
  99.1 6.6 %collective-permute-start.8 = (f32[1,96,256]{2,1,0:T(8,128)S(1)}, f32[1,96,256]{2,1,0:T(8,128)S(1)}, u32[]{:S(2)}, u32[]{:S(2)}) collective-permute-start(f32[1,96,256]{2,1,0:T(8,128)S(1)} %get-tuple-element.22), channel_id=1, source_target_pairs={{0,4},{4,8},{8,12},{12,16},{16,20},{20,24},{24,28},{1,5},{5,9},{9,... | collective-permute-start | bytes 294920 | tf_op jit(solution)/shard_map/ppermute | solution.py:24
  101.5 4.3 %collective-permute-start.9 = (f32[1,96,256]{2,1,0:T(8,128)S(1)}, f32[1,96,256]{2,1,0:T(8,128)S(1)}, u32[]{:S(2)}, u32[]{:S(2)}) collective-permute-start(f32[1,96,256]{2,1,0:T(8,128)S(1)} %get-tuple-element.23), channel_id=1, source_target_pairs={{4,0},{8,4},{12,8},{16,12},{20,16},{24,20},{28,24},{5,1},{9,5},{13... | collective-permute-start | bytes 294920 | tf_op jit(solution)/shard_map/ppermute | solution.py:25
  102.8 6.6 %collective-permute-start.10 = (f32[2,96,256]{2,1,0:T(8,128)S(1)}, f32[2,96,256]{2,1,0:T(8,128)S(1)}, u32[]{:S(2)}, u32[]{:S(2)}) collective-permute-start(f32[2,96,256]{2,1,0:T(8,128)S(1)} %get-tuple-element.26), channel_id=1, source_target_pairs={{0,1},{1,2},{2,3},{4,5},{5,6},{6,7},{8,9},{9,10},{10,11},{12,13},{... | collective-permute-start | bytes 589832 | tf_op jit(solution)/shard_map/ppermute | solution.py:28
  104.4 9.5 %collective-permute-start.11 = (f32[2,96,256]{2,1,0:T(8,128)S(1)}, f32[2,96,256]{2,1,0:T(8,128)S(1)}, u32[]{:S(2)}, u32[]{:S(2)}) collective-permute-start(f32[2,96,256]{2,1,0:T(8,128)S(1)} %get-tuple-element.27), channel_id=1, source_target_pairs={{1,0},{2,1},{3,2},{5,4},{6,5},{7,6},{9,8},{10,9},{11,10},{13,12},{... | collective-permute-start | bytes 589832 | tf_op jit(solution)/shard_map/ppermute | solution.py:29
  114.8 16.4 %copy-start.15 = (f32[32,1,1153]{2,0,1:T(8,128)S(1)}, f32[32,1,1153]{2,0,1:T(8,128)}, u32[]{:S(2)}) copy-start(f32[32,1,1153]{2,0,1:T(8,128)} %copy-done.14) | copy-start | bytes 442756
  117.6 12.5 %all-to-all-start.3 = ((f32[32,1,1248]{2,1,0:T(1,128)}), f32[32,1,1248]{2,1,0:T(1,128)}, u32[]{:S(2)}, u32[]{:S(2)}) async-start(f32[32,1,1248]{2,1,0:T(1,128)} %broadcast_in_dim.47), calls=%async_computation.3 | async-start | bytes 327680 | tf_op jit(solution)/shard_map/all_to_all | solution.py:125
  137.8 6.6 %collective-permute-start.12 = (f32[1,96,256]{2,1,0:T(8,128)S(1)}, f32[1,96,256]{2,1,0:T(8,128)S(1)}, u32[]{:S(2)}, u32[]{:S(2)}) collective-permute-start(f32[1,96,256]{2,1,0:T(8,128)S(1)} %get-tuple-element.16), channel_id=1, source_target_pairs={{0,4},{4,8},{8,12},{12,16},{16,20},{20,24},{24,28},{1,5},{5,9},{9,... | collective-permute-start | bytes 294920 | tf_op jit(solution)/shard_map/ppermute | solution.py:24
  140.1 4.3 %collective-permute-start.13 = (f32[1,96,256]{2,1,0:T(8,128)S(1)}, f32[1,96,256]{2,1,0:T(8,128)S(1)}, u32[]{:S(2)}, u32[]{:S(2)}) collective-permute-start(f32[1,96,256]{2,1,0:T(8,128)S(1)} %get-tuple-element.17), channel_id=1, source_target_pairs={{4,0},{8,4},{12,8},{16,12},{20,16},{24,20},{28,24},{5,1},{9,5},{13... | collective-permute-start | bytes 294920 | tf_op jit(solution)/shard_map/ppermute | solution.py:25
  141.4 6.6 %collective-permute-start.14 = (f32[2,96,256]{2,1,0:T(8,128)S(1)}, f32[2,96,256]{2,1,0:T(8,128)S(1)}, u32[]{:S(2)}, u32[]{:S(2)}) collective-permute-start(f32[2,96,256]{2,1,0:T(8,128)S(1)} %get-tuple-element.20), channel_id=1, source_target_pairs={{0,1},{1,2},{2,3},{4,5},{5,6},{6,7},{8,9},{9,10},{10,11},{12,13},{... | collective-permute-start | bytes 589832 | tf_op jit(solution)/shard_map/ppermute | solution.py:28
  143.1 9.5 %collective-permute-start.15 = (f32[2,96,256]{2,1,0:T(8,128)S(1)}, f32[2,96,256]{2,1,0:T(8,128)S(1)}, u32[]{:S(2)}, u32[]{:S(2)}) collective-permute-start(f32[2,96,256]{2,1,0:T(8,128)S(1)} %get-tuple-element.21), channel_id=1, source_target_pairs={{1,0},{2,1},{3,2},{5,4},{6,5},{7,6},{9,8},{10,9},{11,10},{13,12},{... | collective-permute-start | bytes 589832 | tf_op jit(solution)/shard_map/ppermute | solution.py:29
  172.2 16.6 %copy-start.6 = (f32[2,96,1024]{2,1,0:T(8,128)}, f32[2,96,1024]{2,1,0:T(8,128)S(1)}, u32[]{:S(2)}) copy-start(f32[2,96,1024]{2,1,0:T(8,128)S(1)} %multiply_add_fusion) | copy-start | bytes 2359300
  173.0 6.8 %collective-permute-start.16 = (f32[1,96,256]{2,1,0:T(8,128)S(1)}, f32[1,96,256]{2,1,0:T(8,128)S(1)}, u32[]{:S(2)}, u32[]{:S(2)}) collective-permute-start(f32[1,96,256]{2,1,0:T(8,128)S(1)} %get-tuple-element.10), channel_id=1, source_target_pairs={{0,4},{4,8},{8,12},{12,16},{16,20},{20,24},{24,28},{1,5},{5,9},{9,... | collective-permute-start | bytes 294920 | tf_op jit(solution)/shard_map/ppermute | solution.py:24
  175.4 4.5 %collective-permute-start.17 = (f32[1,96,256]{2,1,0:T(8,128)S(1)}, f32[1,96,256]{2,1,0:T(8,128)S(1)}, u32[]{:S(2)}, u32[]{:S(2)}) collective-permute-start(f32[1,96,256]{2,1,0:T(8,128)S(1)} %get-tuple-element.11), channel_id=1, source_target_pairs={{4,0},{8,4},{12,8},{16,12},{20,16},{24,20},{28,24},{5,1},{9,5},{13... | collective-permute-start | bytes 294920 | tf_op jit(solution)/shard_map/ppermute | solution.py:25
  176.7 6.6 %collective-permute-start.18 = (f32[2,96,256]{2,1,0:T(8,128)S(1)}, f32[2,96,256]{2,1,0:T(8,128)S(1)}, u32[]{:S(2)}, u32[]{:S(2)}) collective-permute-start(f32[2,96,256]{2,1,0:T(8,128)S(1)} %get-tuple-element.14), channel_id=1, source_target_pairs={{0,1},{1,2},{2,3},{4,5},{5,6},{6,7},{8,9},{9,10},{10,11},{12,13},{... | collective-permute-start | bytes 589832 | tf_op jit(solution)/shard_map/ppermute | solution.py:28
  178.4 9.5 %collective-permute-start.19 = (f32[2,96,256]{2,1,0:T(8,128)S(1)}, f32[2,96,256]{2,1,0:T(8,128)S(1)}, u32[]{:S(2)}, u32[]{:S(2)}) collective-permute-start(f32[2,96,256]{2,1,0:T(8,128)S(1)} %get-tuple-element.15), channel_id=1, source_target_pairs={{1,0},{2,1},{3,2},{5,4},{6,5},{7,6},{9,8},{10,9},{11,10},{13,12},{... | collective-permute-start | bytes 589832 | tf_op jit(solution)/shard_map/ppermute | solution.py:29
  (10 other events, 15.0 us)

commit v13 on v12

--- a/solution.py
+++ b/solution.py
@@ -76,23 +76,35 @@
         jnp.concatenate([gap_faces[g], mode_faces[g], map_faces[g], own_rows], axis=1)
         for g in range(4)
     ]
-    partner_pack = neighbors(*packs)
-    partner_gaps = partner_pack[:, :, :columns]
-    partner_raw_modes = partner_pack[:, :, columns:columns + MODES]
-    partner_map = partner_pack[:, :, columns + MODES]
-    partner_rows = partner_pack[:, :, columns + MODES + 1:].reshape(
-        subdomains, 4, MODES, coarse_total
-    )
+    pack_parts = neighbor_parts(*packs)
 
     opposite = jnp.array([1, 0, 3, 2], jnp.int32)
     offsets = (jnp.arange(4, dtype=jnp.int32) * quarter)[None, :, None]
     my_slot = maps.reshape(subdomains, 4, quarter) - offsets
-    partner_slot = partner_map.astype(jnp.int32) - (opposite * quarter)[None, :, None]
     local = jnp.arange(quarter, dtype=jnp.int32)[None, None, None, :]
     mine_hot = (my_slot[..., None] == local).astype(jnp.bfloat16)
-    partner_hot = (partner_slot[..., None] == local).astype(jnp.bfloat16)
-    permutes = jnp.einsum(
-        "sfmt,sfmi->sfti", partner_hot, mine_hot, preferred_element_type=jnp.float32
+
+    def half_exchange(pieces, faces):
+        pack = jnp.stack(pieces, axis=1)
+        partner_map = pack[:, :, columns + MODES]
+        partner_slot = partner_map.astype(jnp.int32) - (opposite[faces] * quarter)[None, :, None]
+        partner_hot = (partner_slot[..., None] == local).astype(jnp.bfloat16)
+        half_permutes = jnp.einsum(
+            "sfmt,sfmi->sfti", partner_hot, mine_hot[:, faces], preferred_element_type=jnp.float32
+        )
+        gaps_half = jnp.einsum(
+            "sfcq,sfqr->sfcr", pack[:, :, :columns], half_permutes, precision=HIGHEST
+        )
+        return pack, half_permutes, gaps_half
+
+    pack_x, permutes_x, gaps_x = half_exchange(pack_parts[:2], slice(0, 2))
+    pack_y, permutes_y, gaps_y = half_exchange(pack_parts[2:], slice(2, 4))
+    partner_pack = jnp.concatenate([pack_x, pack_y], axis=1)
+    permutes = jnp.concatenate([permutes_x, permutes_y], axis=1)
+    partner_gaps_mine = jnp.concatenate([gaps_x, gaps_y], axis=1)
+    partner_raw_modes = partner_pack[:, :, columns:columns + MODES]
+    partner_rows = partner_pack[:, :, columns + MODES + 1:].reshape(
+        subdomains, 4, MODES, coarse_total
     )
 
     def to_mine(raw):
@@ -143,7 +155,7 @@
         return values - lift(flat)
 
     nothing = jnp.zeros((1,), jnp.float32)
-    dual = vectors - partner_values(partner_gaps, vectors.shape)
+    dual = vectors - jnp.moveaxis(partner_gaps_mine, 1, 2).reshape(vectors.shape)
     flat_dual, _ = gathered(coefficients(dual), nothing)
     residual = project_with(dual, flat_dual)
     flat_residual, _ = gathered(coefficients(residual), nothing)

time: 205 us -> 204 us (level)
    dot_general x1 -> x4, matrix products: 0.98 us -> 3.35 us  [the longest x2 2.56 us: half_exchange(): jnp.einsum('sfcq,sfqr->sfcr', pack[:, :, :columns], half_permutes, precis...]
    unnamed x50 -> x54, local copies, waits for them, and re-layouts: 8.33 us -> 8.44 us
where the time goes in v13:
time: 204 us; the launch traced here: 203 us
  waiting for transfers between devices  48.3 us (24%)
  starting transfers between devices  46 us (23%)
  blocking collectives  46 us (23%)
  matrix products  24.4 us (12%)
  other arithmetic  19.7 us (10%)
  local copies, waits for them, and re-layouts  16.5 us (8%)
    all_to_all x4, blocking collectives, gathered(): everything = lax.all_to_all(copies, ('grp', 'sub'), 0, 0, tiled=True)  46 us
    ppermute x5, waiting for transfers between devices, neighbor_parts(): from_above = lax.ppermute(d2, 'grp', down_grp)  23.2 us
    all_to_all x2, waiting for transfers between devices, gathered(): everything = lax.all_to_all(copies, ('grp', 'sub'), 0, 0, tiled=True)  13.6 us
    ppermute x5, starting transfers between devices, neighbor_parts(): left_dev = lax.ppermute(d1[-1:], 'sub', up_sub)  11.6 us
    ppermute x5, waiting for transfers between devices, neighbor_parts(): from_below = lax.ppermute(d3, 'grp', up_grp)  11.5 us
    ppermute x5, starting transfers between devices, neighbor_parts(): from_below = lax.ppermute(d3, 'grp', up_grp)  11 us
    all_to_all x2, starting transfers between devices, gathered(): everything = lax.all_to_all(copies, ('grp', 'sub'), 0, 0, tiled=True)  10.2 us
    unnamed x54, local copies, waits for them, and re-layouts  8.44 us
  transfers between devices with their start and end apart: 22, of which 12 were waited for; matrix products, arithmetic and copies ran while one was open for 4% of the time, Pallas kernels for 0%

profile of v13, /device:TPU:0, one launch (start us, length us, event | category | flops | bytes accessed | tf_op | source)
XLA Modules:
  0.0 202.9 jit_solution(14267784263067849982)
XLA Ops:
  4.4 2.4 %collective-permute-start = (f32[1,112,256]{2,1,0:T(8,128)S(1)}, f32[1,112,256]{2,1,0:T(8,128)S(1)}, u32[]{:S(2)}, u32[]{:S(2)}) collective-permute-start(f32[1,112,256]{2,1,0:T(8,128)S(1)} %get-tuple-element.38), channel_id=1, source_target_pairs={{0,4},{4,8},{8,12},{12,16},{16,20},{20,24},{24,28},{1,5},{5,9},{9,... | collective-permute-start | bytes 344072 | tf_op jit(solution)/shard_map/ppermute | solution.py:24
  8.1 4.3 %collective-permute-start.2 = (f32[2,112,256]{2,1,0:T(8,128)S(1)}, f32[2,112,256]{2,1,0:T(8,128)S(1)}, u32[]{:S(2)}, u32[]{:S(2)}) collective-permute-start(f32[2,112,256]{2,1,0:T(8,128)S(1)} %get-tuple-element.48), channel_id=1, source_target_pairs={{0,1},{1,2},{2,3},{4,5},{5,6},{6,7},{8,9},{9,10},{10,11},{12,13},{... | collective-permute-start | bytes 688136 | tf_op jit(solution)/shard_map/ppermute | solution.py:28
  16.9 4.7 %collective-permute-done.3 = f32[2,112,256]{2,1,0:T(8,128)S(1)} collective-permute-done((f32[2,112,256]{2,1,0:T(8,128)S(1)}, f32[2,112,256]{2,1,0:T(8,128)S(1)}, u32[]{:S(2)}, u32[]{:S(2)}) %collective-permute-start.3) | collective-permute-done | bytes 229408 | tf_op jit(solution)/shard_map/ppermute | solution.py:29
  22.8 1.8 fusion.22
  27.3 6.2 %all-to-all-start = ((f32[32,1,1153]{2,1,0:T(1,128)}), f32[32,1,1153]{2,1,0:T(1,128)S(1)}, u32[]{:S(2)}, u32[]{:S(2)}) async-start(f32[32,1,1153]{2,1,0:T(1,128)} %broadcast_in_dim.41), calls=%async_computation | async-start | bytes 327680 | tf_op jit(solution)/shard_map/all_to_all | solution.py:137
  34.4 1.9 fusion.12
  36.3 5.8 %all-to-all-done = f32[32,1,1153]{2,1,0:T(1,128)S(1)} async-done(((f32[32,1,1153]{2,1,0:T(1,128)}), f32[32,1,1153]{2,1,0:T(1,128)S(1)}, u32[]{:S(2)}, u32[]{:S(2)}) %all-to-all-start) | async-done | bytes 147616 | tf_op jit(solution)/shard_map/all_to_all | solution.py:137
  44.0 1.5 fusion.81
  46.5 10.7 %all_to_all.51 = f32[32,1,1153]{2,1,0:T(1,128)S(1)} all-to-all(f32[32,1,1153]{2,1,0:T(1,128)S(1)} %broadcast_in_dim.43), channel_id=1, replica_groups=mesh['sub'=8,'grp'=4] {'grp','sub'}, dimensions={0} | all-to-all | bytes 295168 | tf_op jit(solution)/shard_map/all_to_all | solution.py:137
  63.4 2.3 %collective-permute-start.4 = (f32[1,96,256]{2,1,0:T(8,128)S(1)}, f32[1,96,256]{2,1,0:T(8,128)S(1)}, u32[]{:S(2)}, u32[]{:S(2)}) collective-permute-start(f32[1,96,256]{2,1,0:T(8,128)S(1)} %get-tuple-element.28), channel_id=1, source_target_pairs={{0,4},{4,8},{8,12},{12,16},{16,20},{20,24},{24,28},{1,5},{5,9},{9,... | collective-permute-start | bytes 294920 | tf_op jit(solution)/shard_map/ppermute | solution.py:24
  67.1 1.7 collective-permute-start.6
  71.0 2.6 %collective-permute-done.6 = f32[2,96,256]{2,1,0:T(8,128)S(1)} collective-permute-done((f32[2,96,256]{2,1,0:T(8,128)S(1)}, f32[2,96,256]{2,1,0:T(8,128)S(1)}, u32[]{:S(2)}, u32[]{:S(2)}) %collective-permute-start.6) | collective-permute-done | bytes 196640 | tf_op jit(solution)/shard_map/ppermute | solution.py:28
  73.6 4.6 %collective-permute-done.7 = f32[2,96,256]{2,1,0:T(8,128)S(1)} collective-permute-done((f32[2,96,256]{2,1,0:T(8,128)S(1)}, f32[2,96,256]{2,1,0:T(8,128)S(1)}, u32[]{:S(2)}, u32[]{:S(2)}) %collective-permute-start.7) | collective-permute-done | bytes 196640 | tf_op jit(solution)/shard_map/ppermute | solution.py:29
  81.2 12.2 %all_to_all.52 = f32[32,1,1248]{2,1,0:T(1,128)S(1)} all-to-all(f32[32,1,1248]{2,1,0:T(1,128)S(1)} %broadcast_in_dim.45), channel_id=1, replica_groups=mesh['sub'=8,'grp'=4] {'grp','sub'}, dimensions={0} | all-to-all | bytes 319488 | tf_op jit(solution)/shard_map/all_to_all | solution.py:137
  99.0 2.3 %collective-permute-start.8 = (f32[1,96,256]{2,1,0:T(8,128)S(1)}, f32[1,96,256]{2,1,0:T(8,128)S(1)}, u32[]{:S(2)}, u32[]{:S(2)}) collective-permute-start(f32[1,96,256]{2,1,0:T(8,128)S(1)} %get-tuple-element.22), channel_id=1, source_target_pairs={{0,4},{4,8},{8,12},{12,16},{16,20},{20,24},{24,28},{1,5},{5,9},{9,... | collective-permute-start | bytes 294920 | tf_op jit(solution)/shard_map/ppermute | solution.py:24
  102.6 1.7 collective-permute-start.10
  106.5 2.7 %collective-permute-done.10 = f32[2,96,256]{2,1,0:T(8,128)S(1)} collective-permute-done((f32[2,96,256]{2,1,0:T(8,128)S(1)}, f32[2,96,256]{2,1,0:T(8,128)S(1)}, u32[]{:S(2)}, u32[]{:S(2)}) %collective-permute-start.10) | collective-permute-done | bytes 196640 | tf_op jit(solution)/shard_map/ppermute | solution.py:28
  109.2 4.6 %collective-permute-done.11 = f32[2,96,256]{2,1,0:T(8,128)S(1)} collective-permute-done((f32[2,96,256]{2,1,0:T(8,128)S(1)}, f32[2,96,256]{2,1,0:T(8,128)S(1)}, u32[]{:S(2)}, u32[]{:S(2)}) %collective-permute-start.11) | collective-permute-done | bytes 196640 | tf_op jit(solution)/shard_map/ppermute | solution.py:29
  117.5 4.0 %all-to-all-start.3 = ((f32[32,1,1248]{2,1,0:T(1,128)}), f32[32,1,1248]{2,1,0:T(1,128)}, u32[]{:S(2)}, u32[]{:S(2)}) async-start(f32[32,1,1248]{2,1,0:T(1,128)} %broadcast_in_dim.47), calls=%async_computation.3 | async-start | bytes 327680 | tf_op jit(solution)/shard_map/all_to_all | solution.py:137
  122.2 7.8 %all-to-all-done.3 = f32[32,1,1248]{2,1,0:T(1,128)} async-done(((f32[32,1,1248]{2,1,0:T(1,128)}), f32[32,1,1248]{2,1,0:T(1,128)}, u32[]{:S(2)}, u32[]{:S(2)}) %all-to-all-start.3) | async-done | bytes 159776 | tf_op jit(solution)/shard_map/all_to_all | solution.py:137
  137.7 2.3 %collective-permute-start.12 = (f32[1,96,256]{2,1,0:T(8,128)S(1)}, f32[1,96,256]{2,1,0:T(8,128)S(1)}, u32[]{:S(2)}, u32[]{:S(2)}) collective-permute-start(f32[1,96,256]{2,1,0:T(8,128)S(1)} %get-tuple-element.16), channel_id=1, source_target_pairs={{0,4},{4,8},{8,12},{12,16},{16,20},{20,24},{24,28},{1,5},{5,9},{9,... | collective-permute-start | bytes 294920 | tf_op jit(solution)/shard_map/ppermute | solution.py:24
  141.3 1.7 collective-permute-start.14
  145.3 2.5 %collective-permute-done.14 = f32[2,96,256]{2,1,0:T(8,128)S(1)} collective-permute-done((f32[2,96,256]{2,1,0:T(8,128)S(1)}, f32[2,96,256]{2,1,0:T(8,128)S(1)}, u32[]{:S(2)}, u32[]{:S(2)}) %collective-permute-start.14) | collective-permute-done | bytes 196640 | tf_op jit(solution)/shard_map/ppermute | solution.py:28
  147.9 4.6 %collective-permute-done.15 = f32[2,96,256]{2,1,0:T(8,128)S(1)} collective-permute-done((f32[2,96,256]{2,1,0:T(8,128)S(1)}, f32[2,96,256]{2,1,0:T(8,128)S(1)}, u32[]{:S(2)}, u32[]{:S(2)}) %collective-permute-start.15) | collective-permute-done | bytes 196640 | tf_op jit(solution)/shard_map/ppermute | solution.py:29
  155.4 12.2 %all_to_all.53 = f32[32,1,1248]{2,1,0:T(1,128)S(1)} all-to-all(f32[32,1,1248]{2,1,0:T(1,128)S(1)} %broadcast_in_dim.49), channel_id=1, replica_groups=mesh['sub'=8,'grp'=4] {'grp','sub'}, dimensions={0} | all-to-all | bytes 319488 | tf_op jit(solution)/shard_map/all_to_all | solution.py:137
  170.5 1.6 multiply_add_fusion
  172.9 2.3 %collective-permute-start.16 = (f32[1,96,256]{2,1,0:T(8,128)S(1)}, f32[1,96,256]{2,1,0:T(8,128)S(1)}, u32[]{:S(2)}, u32[]{:S(2)}) collective-permute-start(f32[1,96,256]{2,1,0:T(8,128)S(1)} %get-tuple-element.10), channel_id=1, source_target_pairs={{0,4},{4,8},{8,12},{12,16},{16,20},{20,24},{24,28},{1,5},{5,9},{9,... | collective-permute-start | bytes 294920 | tf_op jit(solution)/shard_map/ppermute | solution.py:24
  176.6 1.7 collective-permute-start.18
  180.4 2.7 %collective-permute-done.18 = f32[2,96,256]{2,1,0:T(8,128)S(1)} collective-permute-done((f32[2,96,256]{2,1,0:T(8,128)S(1)}, f32[2,96,256]{2,1,0:T(8,128)S(1)}, u32[]{:S(2)}, u32[]{:S(2)}) %collective-permute-start.18) | collective-permute-done | bytes 196640 | tf_op jit(solution)/shard_map/ppermute | solution.py:28
  183.1 4.6 %collective-permute-done.19 = f32[2,96,256]{2,1,0:T(8,128)S(1)} collective-permute-done((f32[2,96,256]{2,1,0:T(8,128)S(1)}, f32[2,96,256]{2,1,0:T(8,128)S(1)}, u32[]{:S(2)}, u32[]{:S(2)}) %collective-permute-start.19) | collective-permute-done | bytes 196640 | tf_op jit(solution)/shard_map/ppermute | solution.py:29
  188.9 10.8 %all_to_all.54 = f32[32,1,96]{2,1,0:T(1,128)S(1)} all-to-all(f32[32,1,96]{2,1,0:T(1,128)S(1)} %broadcast_in_dim.97), channel_id=1, replica_groups=mesh['sub'=8,'grp'=4] {'grp','sub'}, dimensions={0} | all-to-all | bytes 24576 | tf_op jit(solution)/shard_map/all_to_all | solution.py:137
  199.7 3.2 %subtract_bitcast_fusion = (f32[1,2,96,1024]{3,2,1,0:T(8,128)}, f32[1,2,96,1024]{3,2,1,0:T(8,128)}) fusion(f32[2,96,1024]{2,1,0:T(8,128)S(1)} %get-tuple-element.3, f32[96]{0:T(128)S(1)} %div.27, f32[2,96,1024]{2,1,0:T(8,128)S(1)} %fusion.81, f32[2,96,1024]{2,1,0:T(8,128)} %copy-done.6, f32[96]{0:T(128)S(1)} %div.25, f32[2,96,1024]{2,1,0:T(8,128)} %copy-done.7, ...), kind=kLoop, calls=%fused_computation.40 | loop fusion | flops 1376256 | bytes 5505792 | tf_op jit(solution)/shard_map/broadcast_in_dim | solution.py:187
  (220 shorter events, 65.0 us)
Async XLA Ops:
  0.6 14.1 %copy-start.21 = (s32[2]{0:T(128)S(1)}, s32[2]{0:T(128)}, u32[]{:S(2)}) copy-start(s32[2]{0:T(128)} %constant.42) | copy-start | bytes 28
  0.6 13.1 %copy-start.19 = (s32[1,2,1024]{2,1,0:T(2,128)S(1)}, s32[1,2,1024]{2,1,0:T(2,128)}, u32[]{:S(2)}) copy-start(s32[1,2,1024]{2,1,0:T(2,128)} %param.12) | copy-start | bytes 24580
  4.3 18.0 %copy-start.20 = (s32[2]{0:T(128)S(1)}, s32[2]{0:T(128)}, u32[]{:S(2)}) copy-start(s32[2]{0:T(128)} %constant.43) | copy-start | bytes 28
  4.4 10.2 %collective-permute-start = (f32[1,112,256]{2,1,0:T(8,128)S(1)}, f32[1,112,256]{2,1,0:T(8,128)S(1)}, u32[]{:S(2)}, u32[]{:S(2)}) collective-permute-start(f32[1,112,256]{2,1,0:T(8,128)S(1)} %get-tuple-element.38), channel_id=1, source_target_pairs={{0,4},{4,8},{8,12},{12,16},{16,20},{20,24},{24,28},{1,5},{5,9},{9,... | collective-permute-start | bytes 344072 | tf_op jit(solution)/shard_map/ppermute | solution.py:24
  6.8 7.9 %collective-permute-start.1 = (f32[1,112,256]{2,1,0:T(8,128)S(1)}, f32[1,112,256]{2,1,0:T(8,128)S(1)}, u32[]{:S(2)}, u32[]{:S(2)}) collective-permute-start(f32[1,112,256]{2,1,0:T(8,128)S(1)} %get-tuple-element.41), channel_id=1, source_target_pairs={{4,0},{8,4},{12,8},{16,12},{20,16},{24,20},{28,24},{5,1},{9,5},{13... | collective-permute-start | bytes 344072 | tf_op jit(solution)/shard_map/ppermute | solution.py:25
  8.1 8.8 %collective-permute-start.2 = (f32[2,112,256]{2,1,0:T(8,128)S(1)}, f32[2,112,256]{2,1,0:T(8,128)S(1)}, u32[]{:S(2)}, u32[]{:S(2)}) collective-permute-start(f32[2,112,256]{2,1,0:T(8,128)S(1)} %get-tuple-element.48), channel_id=1, source_target_pairs={{0,1},{1,2},{2,3},{4,5},{5,6},{6,7},{8,9},{9,10},{10,11},{12,13},{... | collective-permute-start | bytes 688136 | tf_op jit(solution)/shard_map/ppermute | solution.py:28
  12.5 9.2 %collective-permute-start.3 = (f32[2,112,256]{2,1,0:T(8,128)S(1)}, f32[2,112,256]{2,1,0:T(8,128)S(1)}, u32[]{:S(2)}, u32[]{:S(2)}) collective-permute-start(f32[2,112,256]{2,1,0:T(8,128)S(1)} %get-tuple-element.49), channel_id=1, source_target_pairs={{1,0},{2,1},{3,2},{5,4},{6,5},{7,6},{9,8},{10,9},{11,10},{13,12},{... | collective-permute-start | bytes 688136 | tf_op jit(solution)/shard_map/ppermute | solution.py:29
  15.2 10.4 %copy-start.8 = (f32[1,2,96,1024]{3,2,1,0:T(8,128)S(1)}, f32[1,2,96,1024]{3,2,1,0:T(8,128)}, u32[]{:S(2)}) copy-start(f32[1,2,96,1024]{3,2,1,0:T(8,128)} %param.7) | copy-start | bytes 2359300
  15.2 10.4 %copy-start.12 = (f32[1,2,6,1024]{3,1,2,0:T(2,128)S(1)}, f32[1,2,6,1024]{3,1,2,0:T(2,128)}, u32[]{:S(2)}) copy-start(f32[1,2,6,1024]{3,1,2,0:T(2,128)} %param.10) | copy-start | bytes 147460
  27.3 14.8 %all-to-all-start = ((f32[32,1,1153]{2,1,0:T(1,128)}), f32[32,1,1153]{2,1,0:T(1,128)S(1)}, u32[]{:S(2)}, u32[]{:S(2)}) async-start(f32[32,1,1153]{2,1,0:T(1,128)} %broadcast_in_dim.41), calls=%async_computation | async-start | bytes 327680 | tf_op jit(solution)/shard_map/all_to_all | solution.py:137
  34.4 8.4 %copy-start.18 = (f32[2,4,6,384]{3,2,1,0:T(8,128)}, f32[2,4,6,384]{3,2,1,0:T(8,128)S(1)}, u32[]{:S(2)}) copy-start(f32[2,4,6,384]{3,2,1,0:T(8,128)S(1)} %reshape.207) | copy-start | bytes 221188
  63.4 6.8 %collective-permute-start.4 = (f32[1,96,256]{2,1,0:T(8,128)S(1)}, f32[1,96,256]{2,1,0:T(8,128)S(1)}, u32[]{:S(2)}, u32[]{:S(2)}) collective-permute-start(f32[1,96,256]{2,1,0:T(8,128)S(1)} %get-tuple-element.28), channel_id=1, source_target_pairs={{0,4},{4,8},{8,12},{12,16},{16,20},{20,24},{24,28},{1,5},{5,9},{9,... | collective-permute-start | bytes 294920 | tf_op jit(solution)/shard_map/ppermute | solution.py:24
  65.8 4.5 %collective-permute-start.5 = (f32[1,96,256]{2,1,0:T(8,128)S(1)}, f32[1,96,256]{2,1,0:T(8,128)S(1)}, u32[]{:S(2)}, u32[]{:S(2)}) collective-permute-start(f32[1,96,256]{2,1,0:T(8,128)S(1)} %get-tuple-element.29), channel_id=1, source_target_pairs={{4,0},{8,4},{12,8},{16,12},{20,16},{24,20},{28,24},{5,1},{9,5},{13... | collective-permute-start | bytes 294920 | tf_op jit(solution)/shard_map/ppermute | solution.py:25
  67.1 6.6 %collective-permute-start.6 = (f32[2,96,256]{2,1,0:T(8,128)S(1)}, f32[2,96,256]{2,1,0:T(8,128)S(1)}, u32[]{:S(2)}, u32[]{:S(2)}) collective-permute-start(f32[2,96,256]{2,1,0:T(8,128)S(1)} %get-tuple-element.32), channel_id=1, source_target_pairs={{0,1},{1,2},{2,3},{4,5},{5,6},{6,7},{8,9},{9,10},{10,11},{12,13},{... | collective-permute-start | bytes 589832 | tf_op jit(solution)/shard_map/ppermute | solution.py:28
  68.7 9.5 %collective-permute-start.7 = (f32[2,96,256]{2,1,0:T(8,128)S(1)}, f32[2,96,256]{2,1,0:T(8,128)S(1)}, u32[]{:S(2)}, u32[]{:S(2)}) collective-permute-start(f32[2,96,256]{2,1,0:T(8,128)S(1)} %get-tuple-element.33), channel_id=1, source_target_pairs={{1,0},{2,1},{3,2},{5,4},{6,5},{7,6},{9,8},{10,9},{11,10},{13,12},{... | collective-permute-start | bytes 589832 | tf_op jit(solution)/shard_map/ppermute | solution.py:29
  98.2 16.6 %copy-start = (f32[2,96,1024]{2,1,0:T(8,128)}, f32[2,96,1024]{2,1,0:T(8,128)S(1)}, u32[]{:S(2)}) copy-start(f32[2,96,1024]{2,1,0:T(8,128)S(1)} %sub.112) | copy-start | bytes 2359300
  99.0 6.6 %collective-permute-start.8 = (f32[1,96,256]{2,1,0:T(8,128)S(1)}, f32[1,96,256]{2,1,0:T(8,128)S(1)}, u32[]{:S(2)}, u32[]{:S(2)}) collective-permute-start(f32[1,96,256]{2,1,0:T(8,128)S(1)} %get-tuple-element.22), channel_id=1, source_target_pairs={{0,4},{4,8},{8,12},{12,16},{16,20},{20,24},{24,28},{1,5},{5,9},{9,... | collective-permute-start | bytes 294920 | tf_op jit(solution)/shard_map/ppermute | solution.py:24
  101.3 4.3 %collective-permute-start.9 = (f32[1,96,256]{2,1,0:T(8,128)S(1)}, f32[1,96,256]{2,1,0:T(8,128)S(1)}, u32[]{:S(2)}, u32[]{:S(2)}) collective-permute-start(f32[1,96,256]{2,1,0:T(8,128)S(1)} %get-tuple-element.23), channel_id=1, source_target_pairs={{4,0},{8,4},{12,8},{16,12},{20,16},{24,20},{28,24},{5,1},{9,5},{13... | collective-permute-start | bytes 294920 | tf_op jit(solution)/shard_map/ppermute | solution.py:25
  102.6 6.6 %collective-permute-start.10 = (f32[2,96,256]{2,1,0:T(8,128)S(1)}, f32[2,96,256]{2,1,0:T(8,128)S(1)}, u32[]{:S(2)}, u32[]{:S(2)}) collective-permute-start(f32[2,96,256]{2,1,0:T(8,128)S(1)} %get-tuple-element.26), channel_id=1, source_target_pairs={{0,1},{1,2},{2,3},{4,5},{5,6},{6,7},{8,9},{9,10},{10,11},{12,13},{... | collective-permute-start | bytes 589832 | tf_op jit(solution)/shard_map/ppermute | solution.py:28
  104.3 9.5 %collective-permute-start.11 = (f32[2,96,256]{2,1,0:T(8,128)S(1)}, f32[2,96,256]{2,1,0:T(8,128)S(1)}, u32[]{:S(2)}, u32[]{:S(2)}) collective-permute-start(f32[2,96,256]{2,1,0:T(8,128)S(1)} %get-tuple-element.27), channel_id=1, source_target_pairs={{1,0},{2,1},{3,2},{5,4},{6,5},{7,6},{9,8},{10,9},{11,10},{13,12},{... | collective-permute-start | bytes 589832 | tf_op jit(solution)/shard_map/ppermute | solution.py:29
  114.6 16.4 %copy-start.16 = (f32[32,1,1153]{2,0,1:T(8,128)S(1)}, f32[32,1,1153]{2,0,1:T(8,128)}, u32[]{:S(2)}) copy-start(f32[32,1,1153]{2,0,1:T(8,128)} %copy-done.15) | copy-start | bytes 442756
  117.5 12.5 %all-to-all-start.3 = ((f32[32,1,1248]{2,1,0:T(1,128)}), f32[32,1,1248]{2,1,0:T(1,128)}, u32[]{:S(2)}, u32[]{:S(2)}) async-start(f32[32,1,1248]{2,1,0:T(1,128)} %broadcast_in_dim.47), calls=%async_computation.3 | async-start | bytes 327680 | tf_op jit(solution)/shard_map/all_to_all | solution.py:137
  137.7 6.8 %collective-permute-start.12 = (f32[1,96,256]{2,1,0:T(8,128)S(1)}, f32[1,96,256]{2,1,0:T(8,128)S(1)}, u32[]{:S(2)}, u32[]{:S(2)}) collective-permute-start(f32[1,96,256]{2,1,0:T(8,128)S(1)} %get-tuple-element.16), channel_id=1, source_target_pairs={{0,4},{4,8},{8,12},{12,16},{16,20},{20,24},{24,28},{1,5},{5,9},{9,... | collective-permute-start | bytes 294920 | tf_op jit(solution)/shard_map/ppermute | solution.py:24
  140.0 4.5 %collective-permute-start.13 = (f32[1,96,256]{2,1,0:T(8,128)S(1)}, f32[1,96,256]{2,1,0:T(8,128)S(1)}, u32[]{:S(2)}, u32[]{:S(2)}) collective-permute-start(f32[1,96,256]{2,1,0:T(8,128)S(1)} %get-tuple-element.17), channel_id=1, source_target_pairs={{4,0},{8,4},{12,8},{16,12},{20,16},{24,20},{28,24},{5,1},{9,5},{13... | collective-permute-start | bytes 294920 | tf_op jit(solution)/shard_map/ppermute | solution.py:25
  141.3 6.6 %collective-permute-start.14 = (f32[2,96,256]{2,1,0:T(8,128)S(1)}, f32[2,96,256]{2,1,0:T(8,128)S(1)}, u32[]{:S(2)}, u32[]{:S(2)}) collective-permute-start(f32[2,96,256]{2,1,0:T(8,128)S(1)} %get-tuple-element.20), channel_id=1, source_target_pairs={{0,1},{1,2},{2,3},{4,5},{5,6},{6,7},{8,9},{9,10},{10,11},{12,13},{... | collective-permute-start | bytes 589832 | tf_op jit(solution)/shard_map/ppermute | solution.py:28
  143.0 9.5 %collective-permute-start.15 = (f32[2,96,256]{2,1,0:T(8,128)S(1)}, f32[2,96,256]{2,1,0:T(8,128)S(1)}, u32[]{:S(2)}, u32[]{:S(2)}) collective-permute-start(f32[2,96,256]{2,1,0:T(8,128)S(1)} %get-tuple-element.21), channel_id=1, source_target_pairs={{1,0},{2,1},{3,2},{5,4},{6,5},{7,6},{9,8},{10,9},{11,10},{13,12},{... | collective-permute-start | bytes 589832 | tf_op jit(solution)/shard_map/ppermute | solution.py:29
  172.1 16.6 %copy-start.7 = (f32[2,96,1024]{2,1,0:T(8,128)}, f32[2,96,1024]{2,1,0:T(8,128)S(1)}, u32[]{:S(2)}) copy-start(f32[2,96,1024]{2,1,0:T(8,128)S(1)} %multiply_add_fusion) | copy-start | bytes 2359300
  172.9 6.6 %collective-permute-start.16 = (f32[1,96,256]{2,1,0:T(8,128)S(1)}, f32[1,96,256]{2,1,0:T(8,128)S(1)}, u32[]{:S(2)}, u32[]{:S(2)}) collective-permute-start(f32[1,96,256]{2,1,0:T(8,128)S(1)} %get-tuple-element.10), channel_id=1, source_target_pairs={{0,4},{4,8},{8,12},{12,16},{16,20},{20,24},{24,28},{1,5},{5,9},{9,... | collective-permute-start | bytes 294920 | tf_op jit(solution)/shard_map/ppermute | solution.py:24
  175.3 4.3 %collective-permute-start.17 = (f32[1,96,256]{2,1,0:T(8,128)S(1)}, f32[1,96,256]{2,1,0:T(8,128)S(1)}, u32[]{:S(2)}, u32[]{:S(2)}) collective-permute-start(f32[1,96,256]{2,1,0:T(8,128)S(1)} %get-tuple-element.11), channel_id=1, source_target_pairs={{4,0},{8,4},{12,8},{16,12},{20,16},{24,20},{28,24},{5,1},{9,5},{13... | collective-permute-start | bytes 294920 | tf_op jit(solution)/shard_map/ppermute | solution.py:25
  176.6 6.6 %collective-permute-start.18 = (f32[2,96,256]{2,1,0:T(8,128)S(1)}, f32[2,96,256]{2,1,0:T(8,128)S(1)}, u32[]{:S(2)}, u32[]{:S(2)}) collective-permute-start(f32[2,96,256]{2,1,0:T(8,128)S(1)} %get-tuple-element.14), channel_id=1, source_target_pairs={{0,1},{1,2},{2,3},{4,5},{5,6},{6,7},{8,9},{9,10},{10,11},{12,13},{... | collective-permute-start | bytes 589832 | tf_op jit(solution)/shard_map/ppermute | solution.py:28
  178.3 9.5 %collective-permute-start.19 = (f32[2,96,256]{2,1,0:T(8,128)S(1)}, f32[2,96,256]{2,1,0:T(8,128)S(1)}, u32[]{:S(2)}, u32[]{:S(2)}) collective-permute-start(f32[2,96,256]{2,1,0:T(8,128)S(1)} %get-tuple-element.15), channel_id=1, source_target_pairs={{1,0},{2,1},{3,2},{5,4},{6,5},{7,6},{9,8},{10,9},{11,10},{13,12},{... | collective-permute-start | bytes 589832 | tf_op jit(solution)/shard_map/ppermute | solution.py:29
  180.4 19.3 %copy-start.1 = (f32[2,96,1024]{2,1,0:T(8,128)S(1)}, f32[2,96,1024]{2,1,0:T(8,128)}, u32[]{:S(2)}) copy-start(f32[2,96,1024]{2,1,0:T(8,128)} %copy-done) | copy-start | bytes 2359300
  (12 other events, 25.9 us)

commit v14 on v13

--- a/solution.py
+++ b/solution.py
@@ -92,16 +92,17 @@
         half_permutes = jnp.einsum(
             "sfmt,sfmi->sfti", partner_hot, mine_hot[:, faces], preferred_element_type=jnp.float32
         )
-        gaps_half = jnp.einsum(
-            "sfcq,sfqr->sfcr", pack[:, :, :columns], half_permutes, precision=HIGHEST
-        )
-        return pack, half_permutes, gaps_half
+        moved = jnp.einsum(
+            "sfcq,sfqr->sfcr", pack[:, :, :columns + MODES], half_permutes, precision=HIGHEST
+        )
+        return pack, half_permutes, moved
 
     pack_x, permutes_x, gaps_x = half_exchange(pack_parts[:2], slice(0, 2))
     pack_y, permutes_y, gaps_y = half_exchange(pack_parts[2:], slice(2, 4))
     partner_pack = jnp.concatenate([pack_x, pack_y], axis=1)
     permutes = jnp.concatenate([permutes_x, permutes_y], axis=1)
-    partner_gaps_mine = jnp.concatenate([gaps_x, gaps_y], axis=1)
+    moved_both = jnp.concatenate([gaps_x, gaps_y], axis=1)
+    partner_gaps_mine = moved_both[:, :, :columns]
     partner_raw_modes = partner_pack[:, :, columns:columns + MODES]
     partner_rows = partner_pack[:, :, columns + MODES + 1:].reshape(
         subdomains, 4, MODES, coarse_total
@@ -110,7 +111,7 @@
     def to_mine(raw):
         return jnp.einsum("sfcq,sfqr->sfcr", raw, permutes, precision=HIGHEST)
 
-    partner_modes = to_mine(partner_raw_modes)
+    partner_modes = moved_both[:, :, columns:columns + MODES]
     partner_slot_modes = jnp.moveaxis(partner_modes, 1, 2).reshape(subdomains, MODES, width)
 
     def partner_values(raw, shape):

time: 204 us -> 204 us (level)
  matrix products: 24.4 us -> 18.9 us
  local copies, waits for them, and re-layouts: 16.5 us -> 18.8 us
    dot_general x5, matrix products: 4.97 us -> 1.41 us  [lift(): jnp.einsum('sfkc,cn->skfn', partner_rows, flat, precision=HIGHEST)]
    dot_general x3 -> x2, matrix products: 4.43 us -> 2.5 us  [half_exchange(): jnp.einsum('sfcq,sfqr->sfcr', pack[:, :, :columns + MODES], half_permutes...]
where the time goes in v14:
time: 204 us; the launch traced here: 203 us
  waiting for transfers between devices  49.8 us (24%)
  blocking collectives  46 us (23%)
  starting transfers between devices  45.9 us (22%)
  other arithmetic  21.3 us (10%)
  matrix products  18.9 us (9%)
  local copies, waits for them, and re-layouts  18.8 us (9%)
    all_to_all x4, blocking collectives, gathered(): everything = lax.all_to_all(copies, ('grp', 'sub'), 0, 0, tiled=True)  46 us
    ppermute x5, waiting for transfers between devices, neighbor_parts(): from_above = lax.ppermute(d2, 'grp', down_grp)  23.1 us
    all_to_all x2, waiting for transfers between devices, gathered(): everything = lax.all_to_all(copies, ('grp', 'sub'), 0, 0, tiled=True)  14.7 us
    ppermute x5, waiting for transfers between devices, neighbor_parts(): from_below = lax.ppermute(d3, 'grp', up_grp)  12 us
    ppermute x5, starting transfers between devices, neighbor_parts(): left_dev = lax.ppermute(d1[-1:], 'sub', up_sub)  11.5 us
    ppermute x5, starting transfers between devices, neighbor_parts(): from_below = lax.ppermute(d3, 'grp', up_grp)  11 us
    all_to_all x2, starting transfers between devices, gathered(): everything = lax.all_to_all(copies, ('grp', 'sub'), 0, 0, tiled=True)  10.2 us
    unnamed x54, local copies, waits for them, and re-layouts  9.17 us
  transfers between devices with their start and end apart: 22, of which 12 were waited for; matrix products, arithmetic and copies ran while one was open for 4% of the time, Pallas kernels for 0%

profile of v14, /device:TPU:0, one launch (start us, length us, event | category | flops | bytes accessed | tf_op | source)
XLA Modules:
  0.0 202.5 jit_solution(890577162839577189)
XLA Ops:
  5.2 2.4 %collective-permute-start = (f32[1,112,256]{2,1,0:T(8,128)S(1)}, f32[1,112,256]{2,1,0:T(8,128)S(1)}, u32[]{:S(2)}, u32[]{:S(2)}) collective-permute-start(f32[1,112,256]{2,1,0:T(8,128)S(1)} %get-tuple-element.38), channel_id=1, source_target_pairs={{0,4},{4,8},{8,12},{12,16},{16,20},{20,24},{24,28},{1,5},{5,9},{9,... | collective-permute-start | bytes 344072 | tf_op jit(solution)/shard_map/ppermute | solution.py:24
  8.9 4.3 %collective-permute-start.2 = (f32[2,112,256]{2,1,0:T(8,128)}, f32[2,112,256]{2,1,0:T(8,128)S(1)}, u32[]{:S(2)}, u32[]{:S(2)}) collective-permute-start(f32[2,112,256]{2,1,0:T(8,128)} %get-tuple-element.48), channel_id=1, source_target_pairs={{0,1},{1,2},{2,3},{4,5},{5,6},{6,7},{8,9},{9,10},{10,11},{12,13},{... | collective-permute-start | bytes 688136 | tf_op jit(solution)/shard_map/ppermute | solution.py:28
  18.0 4.6 %collective-permute-done.3 = f32[2,112,256]{2,1,0:T(8,128)S(1)} collective-permute-done((f32[2,112,256]{2,1,0:T(8,128)}, f32[2,112,256]{2,1,0:T(8,128)S(1)}, u32[]{:S(2)}, u32[]{:S(2)}) %collective-permute-start.3) | collective-permute-done | bytes 229408 | tf_op jit(solution)/shard_map/ppermute | solution.py:29
  23.8 1.8 fusion.17
  29.0 6.2 %all-to-all-start = ((f32[32,1,1153]{2,1,0:T(1,128)}), f32[32,1,1153]{2,1,0:T(1,128)S(1)}, u32[]{:S(2)}, u32[]{:S(2)}) async-start(f32[32,1,1153]{2,1,0:T(1,128)} %broadcast_in_dim.41), calls=%async_computation | async-start | bytes 327680 | tf_op jit(solution)/shard_map/all_to_all | solution.py:138
  36.9 6.8 %all-to-all-done = f32[32,1,1153]{2,1,0:T(1,128)S(1)} async-done(((f32[32,1,1153]{2,1,0:T(1,128)}), f32[32,1,1153]{2,1,0:T(1,128)S(1)}, u32[]{:S(2)}, u32[]{:S(2)}) %all-to-all-start) | async-done | bytes 147616 | tf_op jit(solution)/shard_map/all_to_all | solution.py:138
  45.7 1.5 fusion.69
  48.2 10.7 %all_to_all.51 = f32[32,1,1153]{2,1,0:T(1,128)S(1)} all-to-all(f32[32,1,1153]{2,1,0:T(1,128)S(1)} %broadcast_in_dim.43), channel_id=1, replica_groups=mesh['sub'=8,'grp'=4] {'grp','sub'}, dimensions={0} | all-to-all | bytes 295168 | tf_op jit(solution)/shard_map/all_to_all | solution.py:138
  64.2 2.3 %collective-permute-start.4 = (f32[1,96,256]{2,1,0:T(8,128)S(1)}, f32[1,96,256]{2,1,0:T(8,128)S(1)}, u32[]{:S(2)}, u32[]{:S(2)}) collective-permute-start(f32[1,96,256]{2,1,0:T(8,128)S(1)} %get-tuple-element.28), channel_id=1, source_target_pairs={{0,4},{4,8},{8,12},{12,16},{16,20},{20,24},{24,28},{1,5},{5,9},{9,... | collective-permute-start | bytes 294920 | tf_op jit(solution)/shard_map/ppermute | solution.py:24
  67.8 1.7 collective-permute-start.6
  71.6 2.8 %collective-permute-done.6 = f32[2,96,256]{2,1,0:T(8,128)S(1)} collective-permute-done((f32[2,96,256]{2,1,0:T(8,128)S(1)}, f32[2,96,256]{2,1,0:T(8,128)S(1)}, u32[]{:S(2)}, u32[]{:S(2)}) %collective-permute-start.6) | collective-permute-done | bytes 196640 | tf_op jit(solution)/shard_map/ppermute | solution.py:28
  74.4 4.6 %collective-permute-done.7 = f32[2,96,256]{2,1,0:T(8,128)S(1)} collective-permute-done((f32[2,96,256]{2,1,0:T(8,128)S(1)}, f32[2,96,256]{2,1,0:T(8,128)S(1)}, u32[]{:S(2)}, u32[]{:S(2)}) %collective-permute-start.7) | collective-permute-done | bytes 196640 | tf_op jit(solution)/shard_map/ppermute | solution.py:29
  81.9 12.2 %all_to_all.52 = f32[32,1,1248]{2,1,0:T(1,128)S(1)} all-to-all(f32[32,1,1248]{2,1,0:T(1,128)S(1)} %broadcast_in_dim.45), channel_id=1, replica_groups=mesh['sub'=8,'grp'=4] {'grp','sub'}, dimensions={0} | all-to-all | bytes 319488 | tf_op jit(solution)/shard_map/all_to_all | solution.py:138
  100.5 2.3 %collective-permute-start.8 = (f32[1,96,256]{2,1,0:T(8,128)S(1)}, f32[1,96,256]{2,1,0:T(8,128)S(1)}, u32[]{:S(2)}, u32[]{:S(2)}) collective-permute-start(f32[1,96,256]{2,1,0:T(8,128)S(1)} %get-tuple-element.22), channel_id=1, source_target_pairs={{0,4},{4,8},{8,12},{12,16},{16,20},{20,24},{24,28},{1,5},{5,9},{9,... | collective-permute-start | bytes 294920 | tf_op jit(solution)/shard_map/ppermute | solution.py:24
  104.1 1.7 collective-permute-start.10
  107.9 2.8 %collective-permute-done.10 = f32[2,96,256]{2,1,0:T(8,128)S(1)} collective-permute-done((f32[2,96,256]{2,1,0:T(8,128)S(1)}, f32[2,96,256]{2,1,0:T(8,128)S(1)}, u32[]{:S(2)}, u32[]{:S(2)}) %collective-permute-start.10) | collective-permute-done | bytes 196640 | tf_op jit(solution)/shard_map/ppermute | solution.py:28
  110.7 4.6 %collective-permute-done.11 = f32[2,96,256]{2,1,0:T(8,128)S(1)} collective-permute-done((f32[2,96,256]{2,1,0:T(8,128)S(1)}, f32[2,96,256]{2,1,0:T(8,128)S(1)}, u32[]{:S(2)}, u32[]{:S(2)}) %collective-permute-start.11) | collective-permute-done | bytes 196640 | tf_op jit(solution)/shard_map/ppermute | solution.py:29
  118.9 4.0 %all-to-all-start.3 = ((f32[32,1,1248]{2,1,0:T(1,128)}), f32[32,1,1248]{2,1,0:T(1,128)}, u32[]{:S(2)}, u32[]{:S(2)}) async-start(f32[32,1,1248]{2,1,0:T(1,128)} %broadcast_in_dim.47), calls=%async_computation.3 | async-start | bytes 327680 | tf_op jit(solution)/shard_map/all_to_all | solution.py:138
  123.6 7.8 %all-to-all-done.3 = f32[32,1,1248]{2,1,0:T(1,128)} async-done(((f32[32,1,1248]{2,1,0:T(1,128)}), f32[32,1,1248]{2,1,0:T(1,128)}, u32[]{:S(2)}, u32[]{:S(2)}) %all-to-all-start.3) | async-done | bytes 159776 | tf_op jit(solution)/shard_map/all_to_all | solution.py:138
  138.2 2.3 %collective-permute-start.12 = (f32[1,96,256]{2,1,0:T(8,128)S(1)}, f32[1,96,256]{2,1,0:T(8,128)S(1)}, u32[]{:S(2)}, u32[]{:S(2)}) collective-permute-start(f32[1,96,256]{2,1,0:T(8,128)S(1)} %get-tuple-element.16), channel_id=1, source_target_pairs={{0,4},{4,8},{8,12},{12,16},{16,20},{20,24},{24,28},{1,5},{5,9},{9,... | collective-permute-start | bytes 294920 | tf_op jit(solution)/shard_map/ppermute | solution.py:24
  141.9 1.7 collective-permute-start.14
  145.7 2.8 %collective-permute-done.14 = f32[2,96,256]{2,1,0:T(8,128)S(1)} collective-permute-done((f32[2,96,256]{2,1,0:T(8,128)S(1)}, f32[2,96,256]{2,1,0:T(8,128)S(1)}, u32[]{:S(2)}, u32[]{:S(2)}) %collective-permute-start.14) | collective-permute-done | bytes 196640 | tf_op jit(solution)/shard_map/ppermute | solution.py:28
  148.4 4.6 %collective-permute-done.15 = f32[2,96,256]{2,1,0:T(8,128)S(1)} collective-permute-done((f32[2,96,256]{2,1,0:T(8,128)S(1)}, f32[2,96,256]{2,1,0:T(8,128)S(1)}, u32[]{:S(2)}, u32[]{:S(2)}) %collective-permute-start.15) | collective-permute-done | bytes 196640 | tf_op jit(solution)/shard_map/ppermute | solution.py:29
  156.0 12.2 %all_to_all.53 = f32[32,1,1248]{2,1,0:T(1,128)S(1)} all-to-all(f32[32,1,1248]{2,1,0:T(1,128)S(1)} %broadcast_in_dim.49), channel_id=1, replica_groups=mesh['sub'=8,'grp'=4] {'grp','sub'}, dimensions={0} | all-to-all | bytes 319488 | tf_op jit(solution)/shard_map/all_to_all | solution.py:138
  170.1 1.6 multiply_add_fusion
  172.6 2.3 %collective-permute-start.16 = (f32[1,96,256]{2,1,0:T(8,128)S(1)}, f32[1,96,256]{2,1,0:T(8,128)S(1)}, u32[]{:S(2)}, u32[]{:S(2)}) collective-permute-start(f32[1,96,256]{2,1,0:T(8,128)S(1)} %get-tuple-element.10), channel_id=1, source_target_pairs={{0,4},{4,8},{8,12},{12,16},{16,20},{20,24},{24,28},{1,5},{5,9},{9,... | collective-permute-start | bytes 294920 | tf_op jit(solution)/shard_map/ppermute | solution.py:24
  176.2 1.7 collective-permute-start.18
  177.9 1.5 collective-permute-start.19
  180.3 2.5 %collective-permute-done.18 = f32[2,96,256]{2,1,0:T(8,128)S(1)} collective-permute-done((f32[2,96,256]{2,1,0:T(8,128)S(1)}, f32[2,96,256]{2,1,0:T(8,128)S(1)}, u32[]{:S(2)}, u32[]{:S(2)}) %collective-permute-start.18) | collective-permute-done | bytes 196640 | tf_op jit(solution)/shard_map/ppermute | solution.py:28
  182.8 4.6 %collective-permute-done.19 = f32[2,96,256]{2,1,0:T(8,128)S(1)} collective-permute-done((f32[2,96,256]{2,1,0:T(8,128)S(1)}, f32[2,96,256]{2,1,0:T(8,128)S(1)}, u32[]{:S(2)}, u32[]{:S(2)}) %collective-permute-start.19) | collective-permute-done | bytes 196640 | tf_op jit(solution)/shard_map/ppermute | solution.py:29
  188.6 10.8 %all_to_all.54 = f32[32,1,96]{2,1,0:T(1,128)S(1)} all-to-all(f32[32,1,96]{2,1,0:T(1,128)S(1)} %broadcast_in_dim.97), channel_id=1, replica_groups=mesh['sub'=8,'grp'=4] {'grp','sub'}, dimensions={0} | all-to-all | bytes 24576 | tf_op jit(solution)/shard_map/all_to_all | solution.py:138
  199.4 3.2 %subtract_bitcast_fusion = (f32[1,2,96,1024]{3,2,1,0:T(8,128)}, f32[1,2,96,1024]{3,2,1,0:T(8,128)}) fusion(f32[2,96,1024]{2,1,0:T(8,128)S(1)} %get-tuple-element.3, f32[96]{0:T(128)S(1)} %div.27, f32[2,96,1024]{2,1,0:T(8,128)S(1)} %fusion.69, f32[2,96,1024]{2,1,0:T(8,128)} %copy-done.6, f32[96]{0:T(128)S(1)} %div.25, f32[2,96,1024]{2,1,0:T(8,128)} %copy-done.7, ...), kind=kLoop, calls=%fused_computation.38 | loop fusion | flops 1376256 | bytes 5505792 | tf_op jit(solution)/shard_map/broadcast_in_dim | solution.py:188
  (220 shorter events, 63.9 us)
Async XLA Ops:
  0.6 14.9 %copy-start.21 = (s32[2]{0:T(128)S(1)}, s32[2]{0:T(128)}, u32[]{:S(2)}) copy-start(s32[2]{0:T(128)} %constant.42) | copy-start | bytes 28
  0.6 13.9 %copy-start.19 = (s32[1,2,1024]{2,1,0:T(2,128)S(1)}, s32[1,2,1024]{2,1,0:T(2,128)}, u32[]{:S(2)}) copy-start(s32[1,2,1024]{2,1,0:T(2,128)} %param.12) | copy-start | bytes 24580
  4.3 19.0 %copy-start.20 = (s32[2]{0:T(128)S(1)}, s32[2]{0:T(128)}, u32[]{:S(2)}) copy-start(s32[2]{0:T(128)} %constant.43) | copy-start | bytes 28
  5.2 10.2 %collective-permute-start = (f32[1,112,256]{2,1,0:T(8,128)S(1)}, f32[1,112,256]{2,1,0:T(8,128)S(1)}, u32[]{:S(2)}, u32[]{:S(2)}) collective-permute-start(f32[1,112,256]{2,1,0:T(8,128)S(1)} %get-tuple-element.38), channel_id=1, source_target_pairs={{0,4},{4,8},{8,12},{12,16},{16,20},{20,24},{24,28},{1,5},{5,9},{9,... | collective-permute-start | bytes 344072 | tf_op jit(solution)/shard_map/ppermute | solution.py:24
  7.6 7.9 %collective-permute-start.1 = (f32[1,112,256]{2,1,0:T(8,128)S(1)}, f32[1,112,256]{2,1,0:T(8,128)S(1)}, u32[]{:S(2)}, u32[]{:S(2)}) collective-permute-start(f32[1,112,256]{2,1,0:T(8,128)S(1)} %get-tuple-element.41), channel_id=1, source_target_pairs={{4,0},{8,4},{12,8},{16,12},{20,16},{24,20},{28,24},{5,1},{9,5},{13... | collective-permute-start | bytes 344072 | tf_op jit(solution)/shard_map/ppermute | solution.py:25
  8.9 9.1 %collective-permute-start.2 = (f32[2,112,256]{2,1,0:T(8,128)}, f32[2,112,256]{2,1,0:T(8,128)S(1)}, u32[]{:S(2)}, u32[]{:S(2)}) collective-permute-start(f32[2,112,256]{2,1,0:T(8,128)} %get-tuple-element.48), channel_id=1, source_target_pairs={{0,1},{1,2},{2,3},{4,5},{5,6},{6,7},{8,9},{9,10},{10,11},{12,13},{... | collective-permute-start | bytes 688136 | tf_op jit(solution)/shard_map/ppermute | solution.py:28
  13.2 9.4 %collective-permute-start.3 = (f32[2,112,256]{2,1,0:T(8,128)}, f32[2,112,256]{2,1,0:T(8,128)S(1)}, u32[]{:S(2)}, u32[]{:S(2)}) collective-permute-start(f32[2,112,256]{2,1,0:T(8,128)} %get-tuple-element.49), channel_id=1, source_target_pairs={{1,0},{2,1},{3,2},{5,4},{6,5},{7,6},{9,8},{10,9},{11,10},{13,12},{... | collective-permute-start | bytes 688136 | tf_op jit(solution)/shard_map/ppermute | solution.py:29
  15.4 7.2 %copy-start.14 = (f32[2,1,112,256]{3,2,1,0:T(8,128)}, f32[2,1,112,256]{3,2,1,0:T(8,128)S(1)}, u32[]{:S(2)}) copy-start(f32[2,1,112,256]{3,2,1,0:T(8,128)S(1)} %maximum_bitcast_fusion.4) | copy-start | bytes 688132
  15.5 7.2 %copy-start.15 = (f32[2,1,112,256]{3,2,1,0:T(8,128)}, f32[2,1,112,256]{3,2,1,0:T(8,128)S(1)}, u32[]{:S(2)}) copy-start(f32[2,1,112,256]{3,2,1,0:T(8,128)S(1)} %maximum_bitcast_fusion.5) | copy-start | bytes 688132
  16.0 11.4 %copy-start.8 = (f32[1,2,96,1024]{3,2,1,0:T(8,128)S(1)}, f32[1,2,96,1024]{3,2,1,0:T(8,128)}, u32[]{:S(2)}) copy-start(f32[1,2,96,1024]{3,2,1,0:T(8,128)} %param.7) | copy-start | bytes 2359300
  16.0 11.4 %copy-start.13 = (f32[1,2,6,1024]{3,1,2,0:T(2,128)S(1)}, f32[1,2,6,1024]{3,1,2,0:T(2,128)}, u32[]{:S(2)}) copy-start(f32[1,2,6,1024]{3,1,2,0:T(2,128)} %param.10) | copy-start | bytes 147460
  29.0 14.8 %all-to-all-start = ((f32[32,1,1153]{2,1,0:T(1,128)}), f32[32,1,1153]{2,1,0:T(1,128)S(1)}, u32[]{:S(2)}, u32[]{:S(2)}) async-start(f32[32,1,1153]{2,1,0:T(1,128)} %broadcast_in_dim.41), calls=%async_computation | async-start | bytes 327680 | tf_op jit(solution)/shard_map/all_to_all | solution.py:138
  64.2 6.6 %collective-permute-start.4 = (f32[1,96,256]{2,1,0:T(8,128)S(1)}, f32[1,96,256]{2,1,0:T(8,128)S(1)}, u32[]{:S(2)}, u32[]{:S(2)}) collective-permute-start(f32[1,96,256]{2,1,0:T(8,128)S(1)} %get-tuple-element.28), channel_id=1, source_target_pairs={{0,4},{4,8},{8,12},{12,16},{16,20},{20,24},{24,28},{1,5},{5,9},{9,... | collective-permute-start | bytes 294920 | tf_op jit(solution)/shard_map/ppermute | solution.py:24
  66.5 4.3 %collective-permute-start.5 = (f32[1,96,256]{2,1,0:T(8,128)S(1)}, f32[1,96,256]{2,1,0:T(8,128)S(1)}, u32[]{:S(2)}, u32[]{:S(2)}) collective-permute-start(f32[1,96,256]{2,1,0:T(8,128)S(1)} %get-tuple-element.29), channel_id=1, source_target_pairs={{4,0},{8,4},{12,8},{16,12},{20,16},{24,20},{28,24},{5,1},{9,5},{13... | collective-permute-start | bytes 294920 | tf_op jit(solution)/shard_map/ppermute | solution.py:25
  67.8 6.6 %collective-permute-start.6 = (f32[2,96,256]{2,1,0:T(8,128)S(1)}, f32[2,96,256]{2,1,0:T(8,128)S(1)}, u32[]{:S(2)}, u32[]{:S(2)}) collective-permute-start(f32[2,96,256]{2,1,0:T(8,128)S(1)} %get-tuple-element.32), channel_id=1, source_target_pairs={{0,1},{1,2},{2,3},{4,5},{5,6},{6,7},{8,9},{9,10},{10,11},{12,13},{... | collective-permute-start | bytes 589832 | tf_op jit(solution)/shard_map/ppermute | solution.py:28
  69.5 9.5 %collective-permute-start.7 = (f32[2,96,256]{2,1,0:T(8,128)S(1)}, f32[2,96,256]{2,1,0:T(8,128)S(1)}, u32[]{:S(2)}, u32[]{:S(2)}) collective-permute-start(f32[2,96,256]{2,1,0:T(8,128)S(1)} %get-tuple-element.33), channel_id=1, source_target_pairs={{1,0},{2,1},{3,2},{5,4},{6,5},{7,6},{9,8},{10,9},{11,10},{13,12},{... | collective-permute-start | bytes 589832 | tf_op jit(solution)/shard_map/ppermute | solution.py:29
  99.6 16.6 %copy-start = (f32[2,96,1024]{2,1,0:T(8,128)}, f32[2,96,1024]{2,1,0:T(8,128)S(1)}, u32[]{:S(2)}) copy-start(f32[2,96,1024]{2,1,0:T(8,128)S(1)} %sub.112) | copy-start | bytes 2359300
  100.5 6.6 %collective-permute-start.8 = (f32[1,96,256]{2,1,0:T(8,128)S(1)}, f32[1,96,256]{2,1,0:T(8,128)S(1)}, u32[]{:S(2)}, u32[]{:S(2)}) collective-permute-start(f32[1,96,256]{2,1,0:T(8,128)S(1)} %get-tuple-element.22), channel_id=1, source_target_pairs={{0,4},{4,8},{8,12},{12,16},{16,20},{20,24},{24,28},{1,5},{5,9},{9,... | collective-permute-start | bytes 294920 | tf_op jit(solution)/shard_map/ppermute | solution.py:24
  102.8 4.3 %collective-permute-start.9 = (f32[1,96,256]{2,1,0:T(8,128)S(1)}, f32[1,96,256]{2,1,0:T(8,128)S(1)}, u32[]{:S(2)}, u32[]{:S(2)}) collective-permute-start(f32[1,96,256]{2,1,0:T(8,128)S(1)} %get-tuple-element.23), channel_id=1, source_target_pairs={{4,0},{8,4},{12,8},{16,12},{20,16},{24,20},{28,24},{5,1},{9,5},{13... | collective-permute-start | bytes 294920 | tf_op jit(solution)/shard_map/ppermute | solution.py:25
  104.1 6.6 %collective-permute-start.10 = (f32[2,96,256]{2,1,0:T(8,128)S(1)}, f32[2,96,256]{2,1,0:T(8,128)S(1)}, u32[]{:S(2)}, u32[]{:S(2)}) collective-permute-start(f32[2,96,256]{2,1,0:T(8,128)S(1)} %get-tuple-element.26), channel_id=1, source_target_pairs={{0,1},{1,2},{2,3},{4,5},{5,6},{6,7},{8,9},{9,10},{10,11},{12,13},{... | collective-permute-start | bytes 589832 | tf_op jit(solution)/shard_map/ppermute | solution.py:28
  105.8 9.5 %collective-permute-start.11 = (f32[2,96,256]{2,1,0:T(8,128)S(1)}, f32[2,96,256]{2,1,0:T(8,128)S(1)}, u32[]{:S(2)}, u32[]{:S(2)}) collective-permute-start(f32[2,96,256]{2,1,0:T(8,128)S(1)} %get-tuple-element.27), channel_id=1, source_target_pairs={{1,0},{2,1},{3,2},{5,4},{6,5},{7,6},{9,8},{10,9},{11,10},{13,12},{... | collective-permute-start | bytes 589832 | tf_op jit(solution)/shard_map/ppermute | solution.py:29
  118.9 12.5 %all-to-all-start.3 = ((f32[32,1,1248]{2,1,0:T(1,128)}), f32[32,1,1248]{2,1,0:T(1,128)}, u32[]{:S(2)}, u32[]{:S(2)}) async-start(f32[32,1,1248]{2,1,0:T(1,128)} %broadcast_in_dim.47), calls=%async_computation.3 | async-start | bytes 327680 | tf_op jit(solution)/shard_map/all_to_all | solution.py:138
  138.2 6.6 %collective-permute-start.12 = (f32[1,96,256]{2,1,0:T(8,128)S(1)}, f32[1,96,256]{2,1,0:T(8,128)S(1)}, u32[]{:S(2)}, u32[]{:S(2)}) collective-permute-start(f32[1,96,256]{2,1,0:T(8,128)S(1)} %get-tuple-element.16), channel_id=1, source_target_pairs={{0,4},{4,8},{8,12},{12,16},{16,20},{20,24},{24,28},{1,5},{5,9},{9,... | collective-permute-start | bytes 294920 | tf_op jit(solution)/shard_map/ppermute | solution.py:24
  140.6 4.3 %collective-permute-start.13 = (f32[1,96,256]{2,1,0:T(8,128)S(1)}, f32[1,96,256]{2,1,0:T(8,128)S(1)}, u32[]{:S(2)}, u32[]{:S(2)}) collective-permute-start(f32[1,96,256]{2,1,0:T(8,128)S(1)} %get-tuple-element.17), channel_id=1, source_target_pairs={{4,0},{8,4},{12,8},{16,12},{20,16},{24,20},{28,24},{5,1},{9,5},{13... | collective-permute-start | bytes 294920 | tf_op jit(solution)/shard_map/ppermute | solution.py:25
  141.9 6.6 %collective-permute-start.14 = (f32[2,96,256]{2,1,0:T(8,128)S(1)}, f32[2,96,256]{2,1,0:T(8,128)S(1)}, u32[]{:S(2)}, u32[]{:S(2)}) collective-permute-start(f32[2,96,256]{2,1,0:T(8,128)S(1)} %get-tuple-element.20), channel_id=1, source_target_pairs={{0,1},{1,2},{2,3},{4,5},{5,6},{6,7},{8,9},{9,10},{10,11},{12,13},{... | collective-permute-start | bytes 589832 | tf_op jit(solution)/shard_map/ppermute | solution.py:28
  143.5 9.5 %collective-permute-start.15 = (f32[2,96,256]{2,1,0:T(8,128)S(1)}, f32[2,96,256]{2,1,0:T(8,128)S(1)}, u32[]{:S(2)}, u32[]{:S(2)}) collective-permute-start(f32[2,96,256]{2,1,0:T(8,128)S(1)} %get-tuple-element.21), channel_id=1, source_target_pairs={{1,0},{2,1},{3,2},{5,4},{6,5},{7,6},{9,8},{10,9},{11,10},{13,12},{... | collective-permute-start | bytes 589832 | tf_op jit(solution)/shard_map/ppermute | solution.py:29
  171.7 16.6 %copy-start.7 = (f32[2,96,1024]{2,1,0:T(8,128)}, f32[2,96,1024]{2,1,0:T(8,128)S(1)}, u32[]{:S(2)}) copy-start(f32[2,96,1024]{2,1,0:T(8,128)S(1)} %multiply_add_fusion) | copy-start | bytes 2359300
  172.6 6.8 %collective-permute-start.16 = (f32[1,96,256]{2,1,0:T(8,128)S(1)}, f32[1,96,256]{2,1,0:T(8,128)S(1)}, u32[]{:S(2)}, u32[]{:S(2)}) collective-permute-start(f32[1,96,256]{2,1,0:T(8,128)S(1)} %get-tuple-element.10), channel_id=1, source_target_pairs={{0,4},{4,8},{8,12},{12,16},{16,20},{20,24},{24,28},{1,5},{5,9},{9,... | collective-permute-start | bytes 294920 | tf_op jit(solution)/shard_map/ppermute | solution.py:24
  174.9 4.5 %collective-permute-start.17 = (f32[1,96,256]{2,1,0:T(8,128)S(1)}, f32[1,96,256]{2,1,0:T(8,128)S(1)}, u32[]{:S(2)}, u32[]{:S(2)}) collective-permute-start(f32[1,96,256]{2,1,0:T(8,128)S(1)} %get-tuple-element.11), channel_id=1, source_target_pairs={{4,0},{8,4},{12,8},{16,12},{20,16},{24,20},{28,24},{5,1},{9,5},{13... | collective-permute-start | bytes 294920 | tf_op jit(solution)/shard_map/ppermute | solution.py:25
  176.2 6.6 %collective-permute-start.18 = (f32[2,96,256]{2,1,0:T(8,128)S(1)}, f32[2,96,256]{2,1,0:T(8,128)S(1)}, u32[]{:S(2)}, u32[]{:S(2)}) collective-permute-start(f32[2,96,256]{2,1,0:T(8,128)S(1)} %get-tuple-element.14), channel_id=1, source_target_pairs={{0,1},{1,2},{2,3},{4,5},{5,6},{6,7},{8,9},{9,10},{10,11},{12,13},{... | collective-permute-start | bytes 589832 | tf_op jit(solution)/shard_map/ppermute | solution.py:28
  177.9 9.5 %collective-permute-start.19 = (f32[2,96,256]{2,1,0:T(8,128)S(1)}, f32[2,96,256]{2,1,0:T(8,128)S(1)}, u32[]{:S(2)}, u32[]{:S(2)}) collective-permute-start(f32[2,96,256]{2,1,0:T(8,128)S(1)} %get-tuple-element.15), channel_id=1, source_target_pairs={{1,0},{2,1},{3,2},{5,4},{6,5},{7,6},{9,8},{10,9},{11,10},{13,12},{... | collective-permute-start | bytes 589832 | tf_op jit(solution)/shard_map/ppermute | solution.py:29
  180.3 19.1 %copy-start.1 = (f32[2,96,1024]{2,1,0:T(8,128)S(1)}, f32[2,96,1024]{2,1,0:T(8,128)}, u32[]{:S(2)}) copy-start(f32[2,96,1024]{2,1,0:T(8,128)} %copy-done) | copy-start | bytes 2359300
  (12 other events, 20.4 us)

commit v15 on v13

--- a/solution.py
+++ b/solution.py
@@ -125,7 +125,15 @@
             "sfcq,sfqr->sfcr", jnp.stack(parts[2:], axis=1), permutes[:, 2:], precision=HIGHEST
         )
         partner = jnp.concatenate([beside, across], axis=1)
-        return values - jnp.moveaxis(partner, 1, 2).reshape(values.shape)
+        jumped = values - jnp.moveaxis(partner, 1, 2).reshape(values.shape)
+        face_modes = weighted_modes.reshape(subdomains, MODES, 4, quarter)
+        beside_coeffs = jnp.einsum(
+            "skfq,sfnq->skn", face_modes[:, :, :2], beside, precision=HIGHEST
+        )
+        across_coeffs = jnp.einsum(
+            "skfq,sfnq->skn", face_modes[:, :, 2:], across, precision=HIGHEST
+        )
+        return jumped, coefficients(values) - beside_coeffs - across_coeffs
 
     def coefficients(values):
         return jnp.einsum("skm,snm->skn", weighted_modes, values, precision=HIGHEST)
@@ -164,18 +172,18 @@
     rho_prev = jnp.ones((columns,), jnp.float32)
     for step_index in range(ITERS):
         projected = project_with(residual, flat_residual)
-        precond = jump(apply_blocks(projected, schur_blocks))
+        precond, precond_coeffs = jump(apply_blocks(projected, schur_blocks))
         flat_precond, rho_now = gathered(
-            coefficients(precond), jnp.sum(projected * precond, axis=(0, 2))
+            precond_coeffs, jnp.sum(projected * precond, axis=(0, 2))
         )
         search = project_with(precond, flat_precond)
         if step_index > 0:
             search = search + (rho_now / rho_prev)[None, :, None] * direction
         direction = search
-        image = jump(apply_blocks(direction, stiffness))
+        image, image_coeffs = jump(apply_blocks(direction, stiffness))
         partial_dot = jnp.sum(direction * image, axis=(0, 2))
         if step_index + 1 < ITERS:
-            flat_image, curvature = gathered(coefficients(image), partial_dot)
+            flat_image, curvature = gathered(image_coeffs, partial_dot)
         else:
             _, curvature = gathered(jnp.zeros((0,), jnp.float32), partial_dot)
         step_len = rho_now / curvature

time: 204 us -> 215 us (1.054)
  other arithmetic: 19.7 us -> 29.7 us
  matrix products: 24.4 us -> 27.2 us
    reduce_sum x2, other arithmetic: 0.41 us -> 5.13 us  [shards(): jnp.sum(projected * precond, axis=(0, 2))]
    unnamed x54 -> x56, local copies, waits for them, and re-layouts: 8.44 us -> 4.91 us
    reshape x4, local copies, waits for them, and re-layouts: 0.31 us -> 3.75 us  [jump(): jumped = values - jnp.moveaxis(partner, 1, 2).reshape(values.shape)]
    unnamed x5, other arithmetic: 0.27 us -> 3.02 us
    dot_general x0 -> x6, matrix products: none -> 2.75 us  [the longest x3 1.38 us: jump(): jnp.einsum('skfq,sfnq->skn', face_modes[:, :, 2:], across, precision=HIGH...]
    reduce_sum x2, other arithmetic: 0.41 us -> 2.75 us  [shards(): partial_dot = jnp.sum(direction * image, axis=(0, 2))]
  transfers between devices with their start and end apart: 22 -> 22, of which waited for: 12 -> 12; matrix products, arithmetic and copies ran while one was open for 4% -> 5% of each run, Pallas kernels for 0% -> 0%
where the time goes in v15:
time: 215 us; the launch traced here: 213 us
  waiting for transfers between devices  46.9 us (22%)
  blocking collectives  46 us (21%)
  starting transfers between devices  45.9 us (21%)
  other arithmetic  29.7 us (14%)
  matrix products  27.2 us (13%)
  local copies, waits for them, and re-layouts  15.5 us (7%)
    all_to_all x4, blocking collectives, gathered(): everything = lax.all_to_all(copies, ('grp', 'sub'), 0, 0, tiled=True)  46 us
    ppermute x5, waiting for transfers between devices, neighbor_parts(): from_above = lax.ppermute(d2, 'grp', down_grp)  23.2 us
    all_to_all x2, waiting for transfers between devices, gathered(): everything = lax.all_to_all(copies, ('grp', 'sub'), 0, 0, tiled=True)  13.6 us
    ppermute x5, starting transfers between devices, neighbor_parts(): left_dev = lax.ppermute(d1[-1:], 'sub', up_sub)  11.5 us
    ppermute x5, starting transfers between devices, neighbor_parts(): from_below = lax.ppermute(d3, 'grp', up_grp)  11 us
    ppermute x5, waiting for transfers between devices, neighbor_parts(): from_below = lax.ppermute(d3, 'grp', up_grp)  10.1 us
    all_to_all x2, starting transfers between devices, gathered(): everything = lax.all_to_all(copies, ('grp', 'sub'), 0, 0, tiled=True)  10.1 us
    ppermute x5, starting transfers between devices, neighbor_parts(): from_above = lax.ppermute(d2, 'grp', down_grp)  6.86 us
  transfers between devices with their start and end apart: 22, of which 12 were waited for; matrix products, arithmetic and copies ran while one was open for 5% of the time, Pallas kernels for 0%

profile of v15, /device:TPU:0, one launch (start us, length us, event | category | flops | bytes accessed | tf_op | source)
XLA Modules:
  0.0 213.2 jit_solution(4307238360919557667)
XLA Ops:
  4.4 2.4 %collective-permute-start = (f32[1,112,256]{2,1,0:T(8,128)S(1)}, f32[1,112,256]{2,1,0:T(8,128)S(1)}, u32[]{:S(2)}, u32[]{:S(2)}) collective-permute-start(f32[1,112,256]{2,1,0:T(8,128)S(1)} %get-tuple-element.38), channel_id=1, source_target_pairs={{0,4},{4,8},{8,12},{12,16},{16,20},{20,24},{24,28},{1,5},{5,9},{9,... | collective-permute-start | bytes 344072 | tf_op jit(solution)/shard_map/ppermute | solution.py:24
  8.1 4.3 %collective-permute-start.2 = (f32[2,112,256]{2,1,0:T(8,128)S(1)}, f32[2,112,256]{2,1,0:T(8,128)S(1)}, u32[]{:S(2)}, u32[]{:S(2)}) collective-permute-start(f32[2,112,256]{2,1,0:T(8,128)S(1)} %get-tuple-element.48), channel_id=1, source_target_pairs={{0,1},{1,2},{2,3},{4,5},{5,6},{6,7},{8,9},{9,10},{10,11},{12,13},{... | collective-permute-start | bytes 688136 | tf_op jit(solution)/shard_map/ppermute | solution.py:28
  16.9 4.7 %collective-permute-done.3 = f32[2,112,256]{2,1,0:T(8,128)S(1)} collective-permute-done((f32[2,112,256]{2,1,0:T(8,128)S(1)}, f32[2,112,256]{2,1,0:T(8,128)S(1)}, u32[]{:S(2)}, u32[]{:S(2)}) %collective-permute-start.3) | collective-permute-done | bytes 229408 | tf_op jit(solution)/shard_map/ppermute | solution.py:29
  22.8 1.8 fusion.25
  27.3 6.2 %all-to-all-start = ((f32[32,1,1153]{2,1,0:T(1,128)}), f32[32,1,1153]{2,1,0:T(1,128)S(1)}, u32[]{:S(2)}, u32[]{:S(2)}) async-start(f32[32,1,1153]{2,1,0:T(1,128)} %broadcast_in_dim.41), calls=%async_computation | async-start | bytes 327680 | tf_op jit(solution)/shard_map/all_to_all | solution.py:145
  34.4 1.9 fusion.12
  36.3 5.8 %all-to-all-done = f32[32,1,1153]{2,1,0:T(1,128)S(1)} async-done(((f32[32,1,1153]{2,1,0:T(1,128)}), f32[32,1,1153]{2,1,0:T(1,128)S(1)}, u32[]{:S(2)}, u32[]{:S(2)}) %all-to-all-start) | async-done | bytes 147616 | tf_op jit(solution)/shard_map/all_to_all | solution.py:145
  46.4 10.7 %all_to_all.51 = f32[32,1,1153]{2,1,0:T(1,128)S(1)} all-to-all(f32[32,1,1153]{2,1,0:T(1,128)S(1)} %broadcast_in_dim.43), channel_id=1, replica_groups=mesh['sub'=8,'grp'=4] {'grp','sub'}, dimensions={0} | all-to-all | bytes 295168 | tf_op jit(solution)/shard_map/all_to_all | solution.py:145
  63.4 2.3 %collective-permute-start.4 = (f32[1,96,256]{2,1,0:T(8,128)S(1)}, f32[1,96,256]{2,1,0:T(8,128)S(1)}, u32[]{:S(2)}, u32[]{:S(2)}) collective-permute-start(f32[1,96,256]{2,1,0:T(8,128)S(1)} %get-tuple-element.28), channel_id=1, source_target_pairs={{0,4},{4,8},{8,12},{12,16},{16,20},{20,24},{24,28},{1,5},{5,9},{9,... | collective-permute-start | bytes 294920 | tf_op jit(solution)/shard_map/ppermute | solution.py:24
  67.1 1.7 collective-permute-start.6
  71.5 2.1 collective-permute-done.6
  73.6 4.6 %collective-permute-done.7 = f32[2,96,256]{2,1,0:T(8,128)S(1)} collective-permute-done((f32[2,96,256]{2,1,0:T(8,128)S(1)}, f32[2,96,256]{2,1,0:T(8,128)S(1)}, u32[]{:S(2)}, u32[]{:S(2)}) %collective-permute-start.7) | collective-permute-done | bytes 196640 | tf_op jit(solution)/shard_map/ppermute | solution.py:29
  82.5 2.5 %multiply_reduce_fusion.3 = (f32[96]{0:T(128)S(1)}, f32[2,96,1024]{2,1,0:T(8,128)}) fusion(f32[2,96,1024]{2,1,0:T(8,128)} %copy-done.12, f32[2,96,1024]{2,1,0:T(8,128)} %copy-done.7, f32[2,96,1024]{2,1,0:T(8,128)S(1)} %bitcast.239), kind=kLoop, calls=%fused_computation.59 | loop fusion | flops 589728 | bytes 3146112 | tf_op jit(solution)/shard_map/reduce_sum | solution.py:177
  85.1 12.2 %all_to_all.52 = f32[32,1,1248]{2,1,0:T(1,128)S(1)} all-to-all(f32[32,1,1248]{2,1,0:T(1,128)S(1)} %broadcast_in_dim.45), channel_id=1, replica_groups=mesh['sub'=8,'grp'=4] {'grp','sub'}, dimensions={0} | all-to-all | bytes 319488 | tf_op jit(solution)/shard_map/all_to_all | solution.py:145
  103.0 2.3 %collective-permute-start.8 = (f32[1,96,256]{2,1,0:T(8,128)S(1)}, f32[1,96,256]{2,1,0:T(8,128)S(1)}, u32[]{:S(2)}, u32[]{:S(2)}) collective-permute-start(f32[1,96,256]{2,1,0:T(8,128)S(1)} %get-tuple-element.22), channel_id=1, source_target_pairs={{0,4},{4,8},{8,12},{12,16},{16,20},{20,24},{24,28},{1,5},{5,9},{9,... | collective-permute-start | bytes 294920 | tf_op jit(solution)/shard_map/ppermute | solution.py:24
  106.7 1.7 collective-permute-start.10
  110.9 2.3 %collective-permute-done.10 = f32[2,96,256]{2,1,0:T(8,128)S(1)} collective-permute-done((f32[2,96,256]{2,1,0:T(8,128)S(1)}, f32[2,96,256]{2,1,0:T(8,128)S(1)}, u32[]{:S(2)}, u32[]{:S(2)}) %collective-permute-start.10) | collective-permute-done | bytes 196640 | tf_op jit(solution)/shard_map/ppermute | solution.py:28
  113.2 4.6 %collective-permute-done.11 = f32[2,96,256]{2,1,0:T(8,128)S(1)} collective-permute-done((f32[2,96,256]{2,1,0:T(8,128)S(1)}, f32[2,96,256]{2,1,0:T(8,128)S(1)}, u32[]{:S(2)}, u32[]{:S(2)}) %collective-permute-start.11) | collective-permute-done | bytes 196640 | tf_op jit(solution)/shard_map/ppermute | solution.py:29
  122.1 2.5 %multiply_reduce_fusion.2 = (f32[96]{0:T(128)S(1)}, f32[2,96,1024]{2,1,0:T(8,128)}) fusion(f32[2,96,1024]{2,1,0:T(8,128)} %copy-done, f32[2,96,1024]{2,1,0:T(8,128)} %copy-done.8, f32[2,96,1024]{2,1,0:T(8,128)S(1)} %bitcast.241), kind=kLoop, calls=%fused_computation.58 | loop fusion | flops 589728 | bytes 3146112 | tf_op jit(solution)/shard_map/reduce_sum | solution.py:184
  125.4 3.8 %all-to-all-start.3 = ((f32[32,1,1248]{2,1,0:T(1,128)}), f32[32,1,1248]{2,1,0:T(1,128)S(1)}, u32[]{:S(2)}, u32[]{:S(2)}) async-start(f32[32,1,1248]{2,1,0:T(1,128)} %broadcast_in_dim.47), calls=%async_computation.3 | async-start | bytes 327680 | tf_op jit(solution)/shard_map/all_to_all | solution.py:145
  130.0 7.8 %all-to-all-done.3 = f32[32,1,1248]{2,1,0:T(1,128)S(1)} async-done(((f32[32,1,1248]{2,1,0:T(1,128)}), f32[32,1,1248]{2,1,0:T(1,128)S(1)}, u32[]{:S(2)}, u32[]{:S(2)}) %all-to-all-start.3) | async-done | bytes 159776 | tf_op jit(solution)/shard_map/all_to_all | solution.py:145
  143.9 2.3 %collective-permute-start.12 = (f32[1,96,256]{2,1,0:T(8,128)S(1)}, f32[1,96,256]{2,1,0:T(8,128)S(1)}, u32[]{:S(2)}, u32[]{:S(2)}) collective-permute-start(f32[1,96,256]{2,1,0:T(8,128)S(1)} %get-tuple-element.16), channel_id=1, source_target_pairs={{0,4},{4,8},{8,12},{12,16},{16,20},{20,24},{24,28},{1,5},{5,9},{9,... | collective-permute-start | bytes 294920 | tf_op jit(solution)/shard_map/ppermute | solution.py:24
  147.6 1.7 collective-permute-start.14
  152.1 2.1 collective-permute-done.14
  154.1 4.6 %collective-permute-done.15 = f32[2,96,256]{2,1,0:T(8,128)S(1)} collective-permute-done((f32[2,96,256]{2,1,0:T(8,128)S(1)}, f32[2,96,256]{2,1,0:T(8,128)S(1)}, u32[]{:S(2)}, u32[]{:S(2)}) %collective-permute-start.15) | collective-permute-done | bytes 196640 | tf_op jit(solution)/shard_map/ppermute | solution.py:29
  163.0 2.6 %multiply_reduce_fusion.1 = (f32[96]{0:T(128)S(1)}, f32[2,96,1024]{2,1,0:T(8,128)}) fusion(f32[2,96,1024]{2,1,0:T(8,128)} %copy-done.13, f32[2,96,1024]{2,1,0:T(8,128)} %copy-done.6, f32[2,96,1024]{2,1,0:T(8,128)S(1)} %bitcast.240), kind=kLoop, calls=%fused_computation.56 | loop fusion | flops 589728 | bytes 3146112 | tf_op jit(solution)/shard_map/reduce_sum | solution.py:177
  165.7 12.2 %all_to_all.53 = f32[32,1,1248]{2,1,0:T(1,128)S(1)} all-to-all(f32[32,1,1248]{2,1,0:T(1,128)S(1)} %broadcast_in_dim.49), channel_id=1, replica_groups=mesh['sub'=8,'grp'=4] {'grp','sub'}, dimensions={0} | all-to-all | bytes 319488 | tf_op jit(solution)/shard_map/all_to_all | solution.py:145
  183.2 2.3 %collective-permute-start.16 = (f32[1,96,256]{2,1,0:T(8,128)S(1)}, f32[1,96,256]{2,1,0:T(8,128)S(1)}, u32[]{:S(2)}, u32[]{:S(2)}) collective-permute-start(f32[1,96,256]{2,1,0:T(8,128)S(1)} %get-tuple-element.10), channel_id=1, source_target_pairs={{0,4},{4,8},{8,12},{12,16},{16,20},{20,24},{24,28},{1,5},{5,9},{9,... | collective-permute-start | bytes 294920 | tf_op jit(solution)/shard_map/ppermute | solution.py:24
  190.7 2.7 %collective-permute-done.18 = f32[2,96,256]{2,1,0:T(8,128)S(1)} collective-permute-done((f32[2,96,256]{2,1,0:T(8,128)S(1)}, f32[2,96,256]{2,1,0:T(8,128)S(1)}, u32[]{:S(2)}, u32[]{:S(2)}) %collective-permute-start.18) | collective-permute-done | bytes 196640 | tf_op jit(solution)/shard_map/ppermute | solution.py:28
  193.4 4.6 %collective-permute-done.19 = f32[2,96,256]{2,1,0:T(8,128)S(1)} collective-permute-done((f32[2,96,256]{2,1,0:T(8,128)S(1)}, f32[2,96,256]{2,1,0:T(8,128)S(1)}, u32[]{:S(2)}, u32[]{:S(2)}) %collective-permute-start.19) | collective-permute-done | bytes 196640 | tf_op jit(solution)/shard_map/ppermute | solution.py:29
  199.2 10.8 %all_to_all.54 = f32[32,1,96]{2,1,0:T(1,128)S(1)} all-to-all(f32[32,1,96]{2,1,0:T(1,128)S(1)} %broadcast_in_dim.97), channel_id=1, replica_groups=mesh['sub'=8,'grp'=4] {'grp','sub'}, dimensions={0} | all-to-all | bytes 24576 | tf_op jit(solution)/shard_map/all_to_all | solution.py:145
  210.0 3.2 %subtract_bitcast_fusion = (f32[1,2,96,1024]{3,2,1,0:T(8,128)}, f32[1,2,96,1024]{3,2,1,0:T(8,128)}) fusion(f32[2,96,1024]{2,1,0:T(8,128)S(1)} %get-tuple-element.3, f32[96]{0:T(128)S(1)} %div.27, f32[2,96,1024]{2,1,0:T(8,128)S(1)} %fusion.87, f32[2,96,1024]{2,1,0:T(8,128)} %get-tuple-element.7, f32[96]{0:T(128)S(1)} %div.25, f32[2,96,1024]{2,1,0:T(8,128)} %copy-done.9, ...), kind=kLoop, calls=%fused_computation.52 | loop fusion | flops 1376256 | bytes 5505792 | tf_op jit(solution)/shard_map/broadcast_in_dim | solution.py:195
  (228 shorter events, 73.9 us)
Async XLA Ops:
  0.6 14.1 %copy-start.22 = (s32[2]{0:T(128)S(1)}, s32[2]{0:T(128)}, u32[]{:S(2)}) copy-start(s32[2]{0:T(128)} %constant.42) | copy-start | bytes 28
  0.6 13.1 %copy-start.20 = (s32[1,2,1024]{2,1,0:T(2,128)S(1)}, s32[1,2,1024]{2,1,0:T(2,128)}, u32[]{:S(2)}) copy-start(s32[1,2,1024]{2,1,0:T(2,128)} %param.12) | copy-start | bytes 24580
  4.3 18.0 %copy-start.21 = (s32[2]{0:T(128)S(1)}, s32[2]{0:T(128)}, u32[]{:S(2)}) copy-start(s32[2]{0:T(128)} %constant.43) | copy-start | bytes 28
  4.4 10.2 %collective-permute-start = (f32[1,112,256]{2,1,0:T(8,128)S(1)}, f32[1,112,256]{2,1,0:T(8,128)S(1)}, u32[]{:S(2)}, u32[]{:S(2)}) collective-permute-start(f32[1,112,256]{2,1,0:T(8,128)S(1)} %get-tuple-element.38), channel_id=1, source_target_pairs={{0,4},{4,8},{8,12},{12,16},{16,20},{20,24},{24,28},{1,5},{5,9},{9,... | collective-permute-start | bytes 344072 | tf_op jit(solution)/shard_map/ppermute | solution.py:24
  6.8 7.9 %collective-permute-start.1 = (f32[1,112,256]{2,1,0:T(8,128)S(1)}, f32[1,112,256]{2,1,0:T(8,128)S(1)}, u32[]{:S(2)}, u32[]{:S(2)}) collective-permute-start(f32[1,112,256]{2,1,0:T(8,128)S(1)} %get-tuple-element.41), channel_id=1, source_target_pairs={{4,0},{8,4},{12,8},{16,12},{20,16},{24,20},{28,24},{5,1},{9,5},{13... | collective-permute-start | bytes 344072 | tf_op jit(solution)/shard_map/ppermute | solution.py:25
  8.1 8.8 %collective-permute-start.2 = (f32[2,112,256]{2,1,0:T(8,128)S(1)}, f32[2,112,256]{2,1,0:T(8,128)S(1)}, u32[]{:S(2)}, u32[]{:S(2)}) collective-permute-start(f32[2,112,256]{2,1,0:T(8,128)S(1)} %get-tuple-element.48), channel_id=1, source_target_pairs={{0,1},{1,2},{2,3},{4,5},{5,6},{6,7},{8,9},{9,10},{10,11},{12,13},{... | collective-permute-start | bytes 688136 | tf_op jit(solution)/shard_map/ppermute | solution.py:28
  12.5 9.2 %collective-permute-start.3 = (f32[2,112,256]{2,1,0:T(8,128)S(1)}, f32[2,112,256]{2,1,0:T(8,128)S(1)}, u32[]{:S(2)}, u32[]{:S(2)}) collective-permute-start(f32[2,112,256]{2,1,0:T(8,128)S(1)} %get-tuple-element.49), channel_id=1, source_target_pairs={{1,0},{2,1},{3,2},{5,4},{6,5},{7,6},{9,8},{10,9},{11,10},{13,12},{... | collective-permute-start | bytes 688136 | tf_op jit(solution)/shard_map/ppermute | solution.py:29
  15.2 10.4 %copy-start.10 = (f32[1,2,96,1024]{3,2,1,0:T(8,128)S(1)}, f32[1,2,96,1024]{3,2,1,0:T(8,128)}, u32[]{:S(2)}) copy-start(f32[1,2,96,1024]{3,2,1,0:T(8,128)} %param.7) | copy-start | bytes 2359300
  15.2 10.4 %copy-start.14 = (f32[1,2,6,1024]{3,1,2,0:T(2,128)S(1)}, f32[1,2,6,1024]{3,1,2,0:T(2,128)}, u32[]{:S(2)}) copy-start(f32[1,2,6,1024]{3,1,2,0:T(2,128)} %param.10) | copy-start | bytes 147460
  27.3 14.8 %all-to-all-start = ((f32[32,1,1153]{2,1,0:T(1,128)}), f32[32,1,1153]{2,1,0:T(1,128)S(1)}, u32[]{:S(2)}, u32[]{:S(2)}) async-start(f32[32,1,1153]{2,1,0:T(1,128)} %broadcast_in_dim.41), calls=%async_computation | async-start | bytes 327680 | tf_op jit(solution)/shard_map/all_to_all | solution.py:145
  63.4 17.1 %copy-start.7 = (f32[2,96,1024]{2,1,0:T(8,128)}, f32[2,96,1024]{2,1,0:T(8,128)S(1)}, u32[]{:S(2)}) copy-start(f32[2,96,1024]{2,1,0:T(8,128)S(1)} %fusion.6) | copy-start | bytes 2359300
  63.4 6.8 %collective-permute-start.4 = (f32[1,96,256]{2,1,0:T(8,128)S(1)}, f32[1,96,256]{2,1,0:T(8,128)S(1)}, u32[]{:S(2)}, u32[]{:S(2)}) collective-permute-start(f32[1,96,256]{2,1,0:T(8,128)S(1)} %get-tuple-element.28), channel_id=1, source_target_pairs={{0,4},{4,8},{8,12},{12,16},{16,20},{20,24},{24,28},{1,5},{5,9},{9,... | collective-permute-start | bytes 294920 | tf_op jit(solution)/shard_map/ppermute | solution.py:24
  65.8 4.5 %collective-permute-start.5 = (f32[1,96,256]{2,1,0:T(8,128)S(1)}, f32[1,96,256]{2,1,0:T(8,128)S(1)}, u32[]{:S(2)}, u32[]{:S(2)}) collective-permute-start(f32[1,96,256]{2,1,0:T(8,128)S(1)} %get-tuple-element.29), channel_id=1, source_target_pairs={{4,0},{8,4},{12,8},{16,12},{20,16},{24,20},{28,24},{5,1},{9,5},{13... | collective-permute-start | bytes 294920 | tf_op jit(solution)/shard_map/ppermute | solution.py:25
  67.1 6.6 %collective-permute-start.6 = (f32[2,96,256]{2,1,0:T(8,128)S(1)}, f32[2,96,256]{2,1,0:T(8,128)S(1)}, u32[]{:S(2)}, u32[]{:S(2)}) collective-permute-start(f32[2,96,256]{2,1,0:T(8,128)S(1)} %get-tuple-element.32), channel_id=1, source_target_pairs={{0,1},{1,2},{2,3},{4,5},{5,6},{6,7},{8,9},{9,10},{10,11},{12,13},{... | collective-permute-start | bytes 589832 | tf_op jit(solution)/shard_map/ppermute | solution.py:28
  68.7 9.5 %collective-permute-start.7 = (f32[2,96,256]{2,1,0:T(8,128)S(1)}, f32[2,96,256]{2,1,0:T(8,128)S(1)}, u32[]{:S(2)}, u32[]{:S(2)}) collective-permute-start(f32[2,96,256]{2,1,0:T(8,128)S(1)} %get-tuple-element.33), channel_id=1, source_target_pairs={{1,0},{2,1},{3,2},{5,4},{6,5},{7,6},{9,8},{10,9},{11,10},{13,12},{... | collective-permute-start | bytes 589832 | tf_op jit(solution)/shard_map/ppermute | solution.py:29
  103.0 17.1 %copy-start.8 = (f32[2,96,1024]{2,1,0:T(8,128)}, f32[2,96,1024]{2,1,0:T(8,128)S(1)}, u32[]{:S(2)}) copy-start(f32[2,96,1024]{2,1,0:T(8,128)S(1)} %fusion.2) | copy-start | bytes 2359300
  103.0 6.6 %collective-permute-start.8 = (f32[1,96,256]{2,1,0:T(8,128)S(1)}, f32[1,96,256]{2,1,0:T(8,128)S(1)}, u32[]{:S(2)}, u32[]{:S(2)}) collective-permute-start(f32[1,96,256]{2,1,0:T(8,128)S(1)} %get-tuple-element.22), channel_id=1, source_target_pairs={{0,4},{4,8},{8,12},{12,16},{16,20},{20,24},{24,28},{1,5},{5,9},{9,... | collective-permute-start | bytes 294920 | tf_op jit(solution)/shard_map/ppermute | solution.py:24
  105.4 4.3 %collective-permute-start.9 = (f32[1,96,256]{2,1,0:T(8,128)S(1)}, f32[1,96,256]{2,1,0:T(8,128)S(1)}, u32[]{:S(2)}, u32[]{:S(2)}) collective-permute-start(f32[1,96,256]{2,1,0:T(8,128)S(1)} %get-tuple-element.23), channel_id=1, source_target_pairs={{4,0},{8,4},{12,8},{16,12},{20,16},{24,20},{28,24},{5,1},{9,5},{13... | collective-permute-start | bytes 294920 | tf_op jit(solution)/shard_map/ppermute | solution.py:25
  106.7 6.6 %collective-permute-start.10 = (f32[2,96,256]{2,1,0:T(8,128)S(1)}, f32[2,96,256]{2,1,0:T(8,128)S(1)}, u32[]{:S(2)}, u32[]{:S(2)}) collective-permute-start(f32[2,96,256]{2,1,0:T(8,128)S(1)} %get-tuple-element.26), channel_id=1, source_target_pairs={{0,1},{1,2},{2,3},{4,5},{5,6},{6,7},{8,9},{9,10},{10,11},{12,13},{... | collective-permute-start | bytes 589832 | tf_op jit(solution)/shard_map/ppermute | solution.py:28
  108.3 9.5 %collective-permute-start.11 = (f32[2,96,256]{2,1,0:T(8,128)S(1)}, f32[2,96,256]{2,1,0:T(8,128)S(1)}, u32[]{:S(2)}, u32[]{:S(2)}) collective-permute-start(f32[2,96,256]{2,1,0:T(8,128)S(1)} %get-tuple-element.27), channel_id=1, source_target_pairs={{1,0},{2,1},{3,2},{5,4},{6,5},{7,6},{9,8},{10,9},{11,10},{13,12},{... | collective-permute-start | bytes 589832 | tf_op jit(solution)/shard_map/ppermute | solution.py:29
  125.4 12.4 %all-to-all-start.3 = ((f32[32,1,1248]{2,1,0:T(1,128)}), f32[32,1,1248]{2,1,0:T(1,128)S(1)}, u32[]{:S(2)}, u32[]{:S(2)}) async-start(f32[32,1,1248]{2,1,0:T(1,128)} %broadcast_in_dim.47), calls=%async_computation.3 | async-start | bytes 327680 | tf_op jit(solution)/shard_map/all_to_all | solution.py:145
  143.9 17.1 %copy-start.6 = (f32[2,96,1024]{2,1,0:T(8,128)}, f32[2,96,1024]{2,1,0:T(8,128)S(1)}, u32[]{:S(2)}) copy-start(f32[2,96,1024]{2,1,0:T(8,128)S(1)} %fusion.4) | copy-start | bytes 2359300
  143.9 6.8 %collective-permute-start.12 = (f32[1,96,256]{2,1,0:T(8,128)S(1)}, f32[1,96,256]{2,1,0:T(8,128)S(1)}, u32[]{:S(2)}, u32[]{:S(2)}) collective-permute-start(f32[1,96,256]{2,1,0:T(8,128)S(1)} %get-tuple-element.16), channel_id=1, source_target_pairs={{0,4},{4,8},{8,12},{12,16},{16,20},{20,24},{24,28},{1,5},{5,9},{9,... | collective-permute-start | bytes 294920 | tf_op jit(solution)/shard_map/ppermute | solution.py:24
  146.3 4.5 %collective-permute-start.13 = (f32[1,96,256]{2,1,0:T(8,128)S(1)}, f32[1,96,256]{2,1,0:T(8,128)S(1)}, u32[]{:S(2)}, u32[]{:S(2)}) collective-permute-start(f32[1,96,256]{2,1,0:T(8,128)S(1)} %get-tuple-element.17), channel_id=1, source_target_pairs={{4,0},{8,4},{12,8},{16,12},{20,16},{24,20},{28,24},{5,1},{9,5},{13... | collective-permute-start | bytes 294920 | tf_op jit(solution)/shard_map/ppermute | solution.py:25
  147.6 6.6 %collective-permute-start.14 = (f32[2,96,256]{2,1,0:T(8,128)S(1)}, f32[2,96,256]{2,1,0:T(8,128)S(1)}, u32[]{:S(2)}, u32[]{:S(2)}) collective-permute-start(f32[2,96,256]{2,1,0:T(8,128)S(1)} %get-tuple-element.20), channel_id=1, source_target_pairs={{0,1},{1,2},{2,3},{4,5},{5,6},{6,7},{8,9},{9,10},{10,11},{12,13},{... | collective-permute-start | bytes 589832 | tf_op jit(solution)/shard_map/ppermute | solution.py:28
  149.2 9.5 %collective-permute-start.15 = (f32[2,96,256]{2,1,0:T(8,128)S(1)}, f32[2,96,256]{2,1,0:T(8,128)S(1)}, u32[]{:S(2)}, u32[]{:S(2)}) collective-permute-start(f32[2,96,256]{2,1,0:T(8,128)S(1)} %get-tuple-element.21), channel_id=1, source_target_pairs={{1,0},{2,1},{3,2},{5,4},{6,5},{7,6},{9,8},{10,9},{11,10},{13,12},{... | collective-permute-start | bytes 589832 | tf_op jit(solution)/shard_map/ppermute | solution.py:29
  182.4 16.6 %copy-start.9 = (f32[2,96,1024]{2,1,0:T(8,128)}, f32[2,96,1024]{2,1,0:T(8,128)S(1)}, u32[]{:S(2)}) copy-start(f32[2,96,1024]{2,1,0:T(8,128)S(1)} %multiply_add_fusion) | copy-start | bytes 2359300
  183.2 6.6 %collective-permute-start.16 = (f32[1,96,256]{2,1,0:T(8,128)S(1)}, f32[1,96,256]{2,1,0:T(8,128)S(1)}, u32[]{:S(2)}, u32[]{:S(2)}) collective-permute-start(f32[1,96,256]{2,1,0:T(8,128)S(1)} %get-tuple-element.10), channel_id=1, source_target_pairs={{0,4},{4,8},{8,12},{12,16},{16,20},{20,24},{24,28},{1,5},{5,9},{9,... | collective-permute-start | bytes 294920 | tf_op jit(solution)/shard_map/ppermute | solution.py:24
  185.6 4.3 %collective-permute-start.17 = (f32[1,96,256]{2,1,0:T(8,128)S(1)}, f32[1,96,256]{2,1,0:T(8,128)S(1)}, u32[]{:S(2)}, u32[]{:S(2)}) collective-permute-start(f32[1,96,256]{2,1,0:T(8,128)S(1)} %get-tuple-element.11), channel_id=1, source_target_pairs={{4,0},{8,4},{12,8},{16,12},{20,16},{24,20},{28,24},{5,1},{9,5},{13... | collective-permute-start | bytes 294920 | tf_op jit(solution)/shard_map/ppermute | solution.py:25
  186.9 6.6 %collective-permute-start.18 = (f32[2,96,256]{2,1,0:T(8,128)S(1)}, f32[2,96,256]{2,1,0:T(8,128)S(1)}, u32[]{:S(2)}, u32[]{:S(2)}) collective-permute-start(f32[2,96,256]{2,1,0:T(8,128)S(1)} %get-tuple-element.14), channel_id=1, source_target_pairs={{0,1},{1,2},{2,3},{4,5},{5,6},{6,7},{8,9},{9,10},{10,11},{12,13},{... | collective-permute-start | bytes 589832 | tf_op jit(solution)/shard_map/ppermute | solution.py:28
  188.5 9.5 %collective-permute-start.19 = (f32[2,96,256]{2,1,0:T(8,128)S(1)}, f32[2,96,256]{2,1,0:T(8,128)S(1)}, u32[]{:S(2)}, u32[]{:S(2)}) collective-permute-start(f32[2,96,256]{2,1,0:T(8,128)S(1)} %get-tuple-element.15), channel_id=1, source_target_pairs={{1,0},{2,1},{3,2},{5,4},{6,5},{7,6},{9,8},{10,9},{11,10},{13,12},{... | collective-permute-start | bytes 589832 | tf_op jit(solution)/shard_map/ppermute | solution.py:29
  190.7 19.3 %copy-start.1 = (f32[2,96,1024]{2,1,0:T(8,128)S(1)}, f32[2,96,1024]{2,1,0:T(8,128)}, u32[]{:S(2)}) copy-start(f32[2,96,1024]{2,1,0:T(8,128)} %copy-done) | copy-start | bytes 2359300
  (13 other events, 57.0 us)

commit v16 on v13

--- a/solution.py
+++ b/solution.py
@@ -164,16 +164,17 @@
     rho_prev = jnp.ones((columns,), jnp.float32)
     for step_index in range(ITERS):
         projected = project_with(residual, flat_residual)
-        precond = jump(apply_blocks(projected, schur_blocks))
-        flat_precond, rho_now = gathered(
-            coefficients(precond), jnp.sum(projected * precond, axis=(0, 2))
-        )
+        product = apply_blocks(projected, schur_blocks)
+        rho_part = jnp.sum(slot_weight[:, None, :] * projected * product, axis=(0, 2))
+        precond = jump(product)
+        flat_precond, rho_now = gathered(coefficients(precond), rho_part)
         search = project_with(precond, flat_precond)
         if step_index > 0:
             search = search + (rho_now / rho_prev)[None, :, None] * direction
         direction = search
-        image = jump(apply_blocks(direction, stiffness))
-        partial_dot = jnp.sum(direction * image, axis=(0, 2))
+        product = apply_blocks(direction, stiffness)
+        partial_dot = jnp.sum(slot_weight[:, None, :] * direction * product, axis=(0, 2))
+        image = jump(product)
         if step_index + 1 < ITERS:
             flat_image, curvature = gathered(coefficients(image), partial_dot)
         else:

time: 204 us -> 204 us (level)
  blocking collectives: 46 us -> 35.2 us
  local copies, waits for them, and re-layouts: 16.5 us -> 22.9 us
  starting transfers between devices: 46 us -> 50.9 us
    all_to_all x4 -> x3, blocking collectives: 46 us -> 35.2 us  [gathered(): everything = lax.all_to_all(copies, ('grp', 'sub'), 0, 0, tiled=True)]
    dot_general x4, matrix products: 3.19 us -> 8.63 us  [apply_blocks(): jnp.einsum('snm,smk->snk', values.astype(jnp.bfloat16), matrices, preferr...]
    dot_general x5, matrix products: 4.97 us -> 1.39 us  [lift(): jnp.einsum('sfkc,cn->skfn', partner_rows, flat, precision=HIGHEST)]
    all_to_all x2 -> x3, starting transfers between devices: 10.2 us -> 12.6 us  [gathered(): everything = lax.all_to_all(copies, ('grp', 'sub'), 0, 0, tiled=True)]
    sub x0 -> x1, other arithmetic: none -> 2.16 us  [shards(): residual = residual - step_len[None, :, None] * image]
    unnamed x54 -> x52, local copies, waits for them, and re-layouts: 8.44 us -> 6.88 us
    sub x4 -> x2, other arithmetic: 4.36 us -> 2.84 us  [project_with(): return values - lift(flat)]
    all_to_all x2 -> x3, waiting for transfers between devices: 13.6 us -> 14.5 us  [gathered(): everything = lax.all_to_all(copies, ('grp', 'sub'), 0, 0, tiled=True)]
  transfers between devices with their start and end apart: 22 -> 23, of which waited for: 12 -> 12; matrix products, arithmetic and copies ran while one was open for 4% -> 7% of each run, Pallas kernels for 0% -> 0%
where the time goes in v16:
time: 204 us; the launch traced here: 203 us
  starting transfers between devices  50.9 us (25%)
  waiting for transfers between devices  47.4 us (23%)
  blocking collectives  35.2 us (17%)
  matrix products  24.5 us (12%)
  local copies, waits for them, and re-layouts  22.9 us (11%)
  other arithmetic  19.9 us (10%)
    all_to_all x3, blocking collectives, gathered(): everything = lax.all_to_all(copies, ('grp', 'sub'), 0, 0, tiled=True)  35.2 us
    ppermute x5, waiting for transfers between devices, neighbor_parts(): from_above = lax.ppermute(d2, 'grp', down_grp)  23.1 us
    all_to_all x3, waiting for transfers between devices, gathered(): everything = lax.all_to_all(copies, ('grp', 'sub'), 0, 0, tiled=True)  14.5 us
    ppermute x5, starting transfers between devices, neighbor_parts(): from_below = lax.ppermute(d3, 'grp', up_grp)  12.8 us
    all_to_all x3, starting transfers between devices, gathered(): everything = lax.all_to_all(copies, ('grp', 'sub'), 0, 0, tiled=True)  12.6 us
    ppermute x5, starting transfers between devices, neighbor_parts(): left_dev = lax.ppermute(d1[-1:], 'sub', up_sub)  12.2 us
    ppermute x5, waiting for transfers between devices, neighbor_parts(): from_below = lax.ppermute(d3, 'grp', up_grp)  9.81 us
    dot_general x4, matrix products, apply_blocks(): jnp.einsum('snm,smk->snk', values.astype(jnp.bfloat16), matrices, preferr...  8.63 us
  transfers between devices with their start and end apart: 23, of which 12 were waited for; matrix products, arithmetic and copies ran while one was open for 7% of the time, Pallas kernels for 0%

profile of v16, /device:TPU:0, one launch (start us, length us, event | category | flops | bytes accessed | tf_op | source)
XLA Modules:
  0.0 202.6 jit_solution(9129542362000797368)
XLA Ops:
  4.4 2.4 %collective-permute-start = (f32[1,112,256]{2,1,0:T(8,128)S(1)}, f32[1,112,256]{2,1,0:T(8,128)S(1)}, u32[]{:S(2)}, u32[]{:S(2)}) collective-permute-start(f32[1,112,256]{2,1,0:T(8,128)S(1)} %get-tuple-element.36), channel_id=1, source_target_pairs={{0,4},{4,8},{8,12},{12,16},{16,20},{20,24},{24,28},{1,5},{5,9},{9,... | collective-permute-start | bytes 344072 | tf_op jit(solution)/shard_map/ppermute | solution.py:24
  8.1 4.3 %collective-permute-start.2 = (f32[2,112,256]{2,1,0:T(8,128)S(1)}, f32[2,112,256]{2,1,0:T(8,128)S(1)}, u32[]{:S(2)}, u32[]{:S(2)}) collective-permute-start(f32[2,112,256]{2,1,0:T(8,128)S(1)} %get-tuple-element.46), channel_id=1, source_target_pairs={{0,1},{1,2},{2,3},{4,5},{5,6},{6,7},{8,9},{9,10},{10,11},{12,13},{... | collective-permute-start | bytes 688136 | tf_op jit(solution)/shard_map/ppermute | solution.py:28
  16.9 4.7 %collective-permute-done.3 = f32[2,112,256]{2,1,0:T(8,128)S(1)} collective-permute-done((f32[2,112,256]{2,1,0:T(8,128)S(1)}, f32[2,112,256]{2,1,0:T(8,128)S(1)}, u32[]{:S(2)}, u32[]{:S(2)}) %collective-permute-start.3) | collective-permute-done | bytes 229408 | tf_op jit(solution)/shard_map/ppermute | solution.py:29
  25.6 6.2 %all-to-all-start = ((f32[32,1,1153]{2,1,0:T(1,128)}), f32[32,1,1153]{2,1,0:T(1,128)S(1)}, u32[]{:S(2)}, u32[]{:S(2)}) async-start(f32[32,1,1153]{2,1,0:T(1,128)} %broadcast_in_dim.41), calls=%async_computation | async-start | bytes 327680 | tf_op jit(solution)/shard_map/all_to_all | solution.py:137
  33.7 6.7 %all-to-all-done = f32[32,1,1153]{2,1,0:T(1,128)S(1)} async-done(((f32[32,1,1153]{2,1,0:T(1,128)}), f32[32,1,1153]{2,1,0:T(1,128)S(1)}, u32[]{:S(2)}, u32[]{:S(2)}) %all-to-all-start) | async-done | bytes 147616 | tf_op jit(solution)/shard_map/all_to_all | solution.py:137
  44.8 10.7 %all_to_all.51 = f32[32,1,1153]{2,1,0:T(1,128)S(1)} all-to-all(f32[32,1,1153]{2,1,0:T(1,128)S(1)} %broadcast_in_dim.43), channel_id=1, replica_groups=mesh['sub'=8,'grp'=4] {'grp','sub'}, dimensions={0} | all-to-all | bytes 295168 | tf_op jit(solution)/shard_map/all_to_all | solution.py:137
  58.9 3.0 %fusion.6 = f32[2,96,1024]{2,1,0:T(8,128)S(1)} fusion(bf16[1,2,1024,1024]{3,2,1,0:T(8,128)(2,1)} %param.9, f32[2,96,1024]{2,1,0:T(8,128)S(1)} %fusion.82, f32[2,96,1024]{2,1,0:T(8,128)S(1)} %bitcast.198), kind=kOutput, calls=%fused_computation.11 | convolution fusion | flops 403046400 | bytes 6553600 | tf_op jit(solution)/shard_map/snm,smk->snk/dot_general | solution.py:39
  62.0 2.3 %collective-permute-start.4 = (f32[1,96,256]{2,1,0:T(8,128)S(1)}, f32[1,96,256]{2,1,0:T(8,128)S(1)}, u32[]{:S(2)}, u32[]{:S(2)}) collective-permute-start(f32[1,96,256]{2,1,0:T(8,128)S(1)} %get-tuple-element.26), channel_id=1, source_target_pairs={{0,4},{4,8},{8,12},{12,16},{16,20},{20,24},{24,28},{1,5},{5,9},{9,... | collective-permute-start | bytes 294920 | tf_op jit(solution)/shard_map/ppermute | solution.py:24
  65.6 1.7 collective-permute-start.6
  69.6 2.6 %collective-permute-done.6 = f32[2,96,256]{2,1,0:T(8,128)S(1)} collective-permute-done((f32[2,96,256]{2,1,0:T(8,128)S(1)}, f32[2,96,256]{2,1,0:T(8,128)S(1)}, u32[]{:S(2)}, u32[]{:S(2)}) %collective-permute-start.6) | collective-permute-done | bytes 196640 | tf_op jit(solution)/shard_map/ppermute | solution.py:28
  72.2 4.6 %collective-permute-done.7 = f32[2,96,256]{2,1,0:T(8,128)S(1)} collective-permute-done((f32[2,96,256]{2,1,0:T(8,128)S(1)}, f32[2,96,256]{2,1,0:T(8,128)S(1)}, u32[]{:S(2)}, u32[]{:S(2)}) %collective-permute-start.7) | collective-permute-done | bytes 196640 | tf_op jit(solution)/shard_map/ppermute | solution.py:29
  80.0 12.2 %all_to_all.52 = f32[32,1,1248]{2,1,0:T(1,128)S(1)} all-to-all(f32[32,1,1248]{2,1,0:T(1,128)S(1)} %broadcast_in_dim.45), channel_id=1, replica_groups=mesh['sub'=8,'grp'=4] {'grp','sub'}, dimensions={0} | all-to-all | bytes 319488 | tf_op jit(solution)/shard_map/all_to_all | solution.py:137
  98.5 2.3 %collective-permute-start.8 = (f32[1,96,256]{2,1,0:T(8,128)S(1)}, f32[1,96,256]{2,1,0:T(8,128)S(1)}, u32[]{:S(2)}, u32[]{:S(2)}) collective-permute-start(f32[1,96,256]{2,1,0:T(8,128)S(1)} %get-tuple-element.18), channel_id=1, source_target_pairs={{0,4},{4,8},{8,12},{12,16},{16,20},{20,24},{24,28},{1,5},{5,9},{9,... | collective-permute-start | bytes 294920 | tf_op jit(solution)/shard_map/ppermute | solution.py:24
  102.1 1.7 collective-permute-start.10
  105.9 2.8 %collective-permute-done.10 = f32[2,96,256]{2,1,0:T(8,128)S(1)} collective-permute-done((f32[2,96,256]{2,1,0:T(8,128)S(1)}, f32[2,96,256]{2,1,0:T(8,128)S(1)}, u32[]{:S(2)}, u32[]{:S(2)}) %collective-permute-start.10) | collective-permute-done | bytes 196640 | tf_op jit(solution)/shard_map/ppermute | solution.py:28
  108.7 4.6 %collective-permute-done.11 = f32[2,96,256]{2,1,0:T(8,128)S(1)} collective-permute-done((f32[2,96,256]{2,1,0:T(8,128)S(1)}, f32[2,96,256]{2,1,0:T(8,128)S(1)}, u32[]{:S(2)}, u32[]{:S(2)}) %collective-permute-start.11) | collective-permute-done | bytes 196640 | tf_op jit(solution)/shard_map/ppermute | solution.py:29
  116.9 4.0 %all-to-all-start.3 = ((f32[32,1,1248]{2,1,0:T(1,128)}), f32[32,1,1248]{2,1,0:T(1,128)}, u32[]{:S(2)}, u32[]{:S(2)}) async-start(f32[32,1,1248]{2,1,0:T(1,128)} %broadcast_in_dim.47), calls=%async_computation.3 | async-start | bytes 327680 | tf_op jit(solution)/shard_map/all_to_all | solution.py:137
  121.6 7.8 %all-to-all-done.3 = f32[32,1,1248]{2,1,0:T(1,128)} async-done(((f32[32,1,1248]{2,1,0:T(1,128)}), f32[32,1,1248]{2,1,0:T(1,128)}, u32[]{:S(2)}, u32[]{:S(2)}) %all-to-all-start.3) | async-done | bytes 159776 | tf_op jit(solution)/shard_map/all_to_all | solution.py:137
  130.4 2.2 %multiply_subtract_fusion = f32[2,96,1024]{2,1,0:T(8,128)} fusion(f32[2,96,1024]{2,1,0:T(8,128)S(1)} %fusion.82, f32[2,96,1024]{2,1,0:T(8,128)} %copy-done.9, f32[96]{0:T(128)S(1)} %div.25), kind=kLoop, calls=%fused_computation.45 | loop fusion | flops 393216 | bytes 2359680 | tf_op jit(solution)/shard_map/sub | solution.py:184
  136.1 3.0 %fusion.4 = f32[2,96,1024]{2,1,0:T(8,128)S(1)} fusion(bf16[1,2,1024,1024]{3,2,1,0:T(8,128)(2,1)} %param.9, f32[2,96,1024]{2,1,0:T(8,128)S(1)} %copy-done.4, f32[2,96,1024]{2,1,0:T(8,128)S(1)} %bitcast.200), kind=kOutput, calls=%fused_computation.9 | convolution fusion | flops 403046400 | bytes 6553600 | tf_op jit(solution)/shard_map/snm,smk->snk/dot_general | solution.py:39
  139.2 2.4 %collective-permute-start.12 = (f32[1,96,256]{2,1,0:T(8,128)S(1)}, f32[1,96,256]{2,1,0:T(8,128)S(1)}, u32[]{:S(2)}, u32[]{:S(2)}) collective-permute-start(f32[1,96,256]{2,1,0:T(8,128)S(1)} %get-tuple-element.10), channel_id=1, source_target_pairs={{0,4},{4,8},{8,12},{12,16},{16,20},{20,24},{24,28},{1,5},{5,9},{9,... | collective-permute-start | bytes 294920 | tf_op jit(solution)/shard_map/ppermute | solution.py:24
  143.0 1.7 collective-permute-start.14
  147.0 2.5 %collective-permute-done.14 = f32[2,96,256]{2,1,0:T(8,128)S(1)} collective-permute-done((f32[2,96,256]{2,1,0:T(8,128)S(1)}, f32[2,96,256]{2,1,0:T(8,128)S(1)}, u32[]{:S(2)}, u32[]{:S(2)}) %collective-permute-start.14) | collective-permute-done | bytes 196640 | tf_op jit(solution)/shard_map/ppermute | solution.py:28
  149.5 4.6 %collective-permute-done.15 = f32[2,96,256]{2,1,0:T(8,128)S(1)} collective-permute-done((f32[2,96,256]{2,1,0:T(8,128)S(1)}, f32[2,96,256]{2,1,0:T(8,128)S(1)}, u32[]{:S(2)}, u32[]{:S(2)}) %collective-permute-start.15) | collective-permute-done | bytes 196640 | tf_op jit(solution)/shard_map/ppermute | solution.py:29
  157.3 12.2 %all_to_all.53 = f32[32,1,1248]{2,1,0:T(1,128)S(1)} all-to-all(f32[32,1,1248]{2,1,0:T(1,128)S(1)} %broadcast_in_dim.49), channel_id=1, replica_groups=mesh['sub'=8,'grp'=4] {'grp','sub'}, dimensions={0} | all-to-all | bytes 319488 | tf_op jit(solution)/shard_map/all_to_all | solution.py:137
  174.5 1.8 multiply_reduce_fusion
  176.9 2.5 %all-to-all-start.5 = ((f32[32,1,96]{2,1,0:T(1,128)}), f32[32,1,96]{2,1,0:T(1,128)S(1)}, u32[]{:S(2)}, u32[]{:S(2)}) async-start(f32[32,1,96]{2,1,0:T(1,128)} %broadcast_in_dim.97), calls=%async_computation.5 | async-start | bytes 32768 | tf_op jit(solution)/shard_map/all_to_all | solution.py:137
  179.4 1.8 fusion.83
  181.1 2.8 %collective-permute-start.16 = (f32[1,96,256]{2,1,0:T(8,128)}, f32[1,96,256]{2,1,0:T(8,128)}, u32[]{:S(2)}, u32[]{:S(2)}) collective-permute-start(f32[1,96,256]{2,1,0:T(8,128)} %get-tuple-element.2), channel_id=1, source_target_pairs={{0,4},{4,8},{8,12},{12,16},{16,20},{20,24},{24,28},{1,5},{5,9},{9,... | collective-permute-start | bytes 294920 | tf_op jit(solution)/shard_map/ppermute | solution.py:24
  183.9 1.8 fusion.84
  187.0 3.5 %collective-permute-start.18 = (f32[2,96,256]{2,1,0:T(8,128)}, f32[2,96,256]{2,1,0:T(8,128)S(1)}, u32[]{:S(2)}, u32[]{:S(2)}) collective-permute-start(f32[2,96,256]{2,1,0:T(8,128)} %get-tuple-element.6), channel_id=1, source_target_pairs={{0,1},{1,2},{2,3},{4,5},{5,6},{6,7},{8,9},{9,10},{10,11},{12,13},{... | collective-permute-start | bytes 589832 | tf_op jit(solution)/shard_map/ppermute | solution.py:28
  195.7 4.5 %collective-permute-done.19 = f32[2,96,256]{2,1,0:T(8,128)S(1)} collective-permute-done((f32[2,96,256]{2,1,0:T(8,128)}, f32[2,96,256]{2,1,0:T(8,128)S(1)}, u32[]{:S(2)}, u32[]{:S(2)}) %collective-permute-start.19) | collective-permute-done | bytes 196640 | tf_op jit(solution)/shard_map/ppermute | solution.py:29
  (217 shorter events, 69.0 us)
Async XLA Ops:
  0.6 14.1 %copy-start.20 = (s32[2]{0:T(128)S(1)}, s32[2]{0:T(128)}, u32[]{:S(2)}) copy-start(s32[2]{0:T(128)} %constant.42) | copy-start | bytes 28
  0.6 13.1 %copy-start.18 = (s32[1,2,1024]{2,1,0:T(2,128)S(1)}, s32[1,2,1024]{2,1,0:T(2,128)}, u32[]{:S(2)}) copy-start(s32[1,2,1024]{2,1,0:T(2,128)} %param.12) | copy-start | bytes 24580
  4.3 17.4 %copy-start.19 = (s32[2]{0:T(128)S(1)}, s32[2]{0:T(128)}, u32[]{:S(2)}) copy-start(s32[2]{0:T(128)} %constant.43) | copy-start | bytes 28
  4.4 10.2 %collective-permute-start = (f32[1,112,256]{2,1,0:T(8,128)S(1)}, f32[1,112,256]{2,1,0:T(8,128)S(1)}, u32[]{:S(2)}, u32[]{:S(2)}) collective-permute-start(f32[1,112,256]{2,1,0:T(8,128)S(1)} %get-tuple-element.36), channel_id=1, source_target_pairs={{0,4},{4,8},{8,12},{12,16},{16,20},{20,24},{24,28},{1,5},{5,9},{9,... | collective-permute-start | bytes 344072 | tf_op jit(solution)/shard_map/ppermute | solution.py:24
  6.8 7.9 %collective-permute-start.1 = (f32[1,112,256]{2,1,0:T(8,128)S(1)}, f32[1,112,256]{2,1,0:T(8,128)S(1)}, u32[]{:S(2)}, u32[]{:S(2)}) collective-permute-start(f32[1,112,256]{2,1,0:T(8,128)S(1)} %get-tuple-element.39), channel_id=1, source_target_pairs={{4,0},{8,4},{12,8},{16,12},{20,16},{24,20},{28,24},{5,1},{9,5},{13... | collective-permute-start | bytes 344072 | tf_op jit(solution)/shard_map/ppermute | solution.py:25
  8.1 8.8 %collective-permute-start.2 = (f32[2,112,256]{2,1,0:T(8,128)S(1)}, f32[2,112,256]{2,1,0:T(8,128)S(1)}, u32[]{:S(2)}, u32[]{:S(2)}) collective-permute-start(f32[2,112,256]{2,1,0:T(8,128)S(1)} %get-tuple-element.46), channel_id=1, source_target_pairs={{0,1},{1,2},{2,3},{4,5},{5,6},{6,7},{8,9},{9,10},{10,11},{12,13},{... | collective-permute-start | bytes 688136 | tf_op jit(solution)/shard_map/ppermute | solution.py:28
  12.5 9.2 %collective-permute-start.3 = (f32[2,112,256]{2,1,0:T(8,128)S(1)}, f32[2,112,256]{2,1,0:T(8,128)S(1)}, u32[]{:S(2)}, u32[]{:S(2)}) collective-permute-start(f32[2,112,256]{2,1,0:T(8,128)S(1)} %get-tuple-element.47), channel_id=1, source_target_pairs={{1,0},{2,1},{3,2},{5,4},{6,5},{7,6},{9,8},{10,9},{11,10},{13,12},{... | collective-permute-start | bytes 688136 | tf_op jit(solution)/shard_map/ppermute | solution.py:29
  25.6 14.8 %all-to-all-start = ((f32[32,1,1153]{2,1,0:T(1,128)}), f32[32,1,1153]{2,1,0:T(1,128)S(1)}, u32[]{:S(2)}, u32[]{:S(2)}) async-start(f32[32,1,1153]{2,1,0:T(1,128)} %broadcast_in_dim.41), calls=%async_computation | async-start | bytes 327680 | tf_op jit(solution)/shard_map/all_to_all | solution.py:137
  62.0 6.8 %collective-permute-start.4 = (f32[1,96,256]{2,1,0:T(8,128)S(1)}, f32[1,96,256]{2,1,0:T(8,128)S(1)}, u32[]{:S(2)}, u32[]{:S(2)}) collective-permute-start(f32[1,96,256]{2,1,0:T(8,128)S(1)} %get-tuple-element.26), channel_id=1, source_target_pairs={{0,4},{4,8},{8,12},{12,16},{16,20},{20,24},{24,28},{1,5},{5,9},{9,... | collective-permute-start | bytes 294920 | tf_op jit(solution)/shard_map/ppermute | solution.py:24
  64.3 4.5 %collective-permute-start.5 = (f32[1,96,256]{2,1,0:T(8,128)S(1)}, f32[1,96,256]{2,1,0:T(8,128)S(1)}, u32[]{:S(2)}, u32[]{:S(2)}) collective-permute-start(f32[1,96,256]{2,1,0:T(8,128)S(1)} %get-tuple-element.27), channel_id=1, source_target_pairs={{4,0},{8,4},{12,8},{16,12},{20,16},{24,20},{28,24},{5,1},{9,5},{13... | collective-permute-start | bytes 294920 | tf_op jit(solution)/shard_map/ppermute | solution.py:25
  65.6 6.6 %collective-permute-start.6 = (f32[2,96,256]{2,1,0:T(8,128)S(1)}, f32[2,96,256]{2,1,0:T(8,128)S(1)}, u32[]{:S(2)}, u32[]{:S(2)}) collective-permute-start(f32[2,96,256]{2,1,0:T(8,128)S(1)} %get-tuple-element.30), channel_id=1, source_target_pairs={{0,1},{1,2},{2,3},{4,5},{5,6},{6,7},{8,9},{9,10},{10,11},{12,13},{... | collective-permute-start | bytes 589832 | tf_op jit(solution)/shard_map/ppermute | solution.py:28
  67.3 9.5 %collective-permute-start.7 = (f32[2,96,256]{2,1,0:T(8,128)S(1)}, f32[2,96,256]{2,1,0:T(8,128)S(1)}, u32[]{:S(2)}, u32[]{:S(2)}) collective-permute-start(f32[2,96,256]{2,1,0:T(8,128)S(1)} %get-tuple-element.31), channel_id=1, source_target_pairs={{1,0},{2,1},{3,2},{5,4},{6,5},{7,6},{9,8},{10,9},{11,10},{13,12},{... | collective-permute-start | bytes 589832 | tf_op jit(solution)/shard_map/ppermute | solution.py:29
  97.6 16.6 %copy-start = (f32[2,96,1024]{2,1,0:T(8,128)}, f32[2,96,1024]{2,1,0:T(8,128)S(1)}, u32[]{:S(2)}) copy-start(f32[2,96,1024]{2,1,0:T(8,128)S(1)} %sub.112) | copy-start | bytes 2359300
  98.5 6.6 %collective-permute-start.8 = (f32[1,96,256]{2,1,0:T(8,128)S(1)}, f32[1,96,256]{2,1,0:T(8,128)S(1)}, u32[]{:S(2)}, u32[]{:S(2)}) collective-permute-start(f32[1,96,256]{2,1,0:T(8,128)S(1)} %get-tuple-element.18), channel_id=1, source_target_pairs={{0,4},{4,8},{8,12},{12,16},{16,20},{20,24},{24,28},{1,5},{5,9},{9,... | collective-permute-start | bytes 294920 | tf_op jit(solution)/shard_map/ppermute | solution.py:24
  100.8 4.3 %collective-permute-start.9 = (f32[1,96,256]{2,1,0:T(8,128)S(1)}, f32[1,96,256]{2,1,0:T(8,128)S(1)}, u32[]{:S(2)}, u32[]{:S(2)}) collective-permute-start(f32[1,96,256]{2,1,0:T(8,128)S(1)} %get-tuple-element.19), channel_id=1, source_target_pairs={{4,0},{8,4},{12,8},{16,12},{20,16},{24,20},{28,24},{5,1},{9,5},{13... | collective-permute-start | bytes 294920 | tf_op jit(solution)/shard_map/ppermute | solution.py:25
  102.1 6.6 %collective-permute-start.10 = (f32[2,96,256]{2,1,0:T(8,128)S(1)}, f32[2,96,256]{2,1,0:T(8,128)S(1)}, u32[]{:S(2)}, u32[]{:S(2)}) collective-permute-start(f32[2,96,256]{2,1,0:T(8,128)S(1)} %get-tuple-element.22), channel_id=1, source_target_pairs={{0,1},{1,2},{2,3},{4,5},{5,6},{6,7},{8,9},{9,10},{10,11},{12,13},{... | collective-permute-start | bytes 589832 | tf_op jit(solution)/shard_map/ppermute | solution.py:28
  103.8 9.5 %collective-permute-start.11 = (f32[2,96,256]{2,1,0:T(8,128)S(1)}, f32[2,96,256]{2,1,0:T(8,128)S(1)}, u32[]{:S(2)}, u32[]{:S(2)}) collective-permute-start(f32[2,96,256]{2,1,0:T(8,128)S(1)} %get-tuple-element.23), channel_id=1, source_target_pairs={{1,0},{2,1},{3,2},{5,4},{6,5},{7,6},{9,8},{10,9},{11,10},{13,12},{... | collective-permute-start | bytes 589832 | tf_op jit(solution)/shard_map/ppermute | solution.py:29
  116.9 12.5 %all-to-all-start.3 = ((f32[32,1,1248]{2,1,0:T(1,128)}), f32[32,1,1248]{2,1,0:T(1,128)}, u32[]{:S(2)}, u32[]{:S(2)}) async-start(f32[32,1,1248]{2,1,0:T(1,128)} %broadcast_in_dim.47), calls=%async_computation.3 | async-start | bytes 327680 | tf_op jit(solution)/shard_map/all_to_all | solution.py:137
  139.2 15.9 %copy-start.5 = (f32[2,96,1024]{2,1,0:T(8,128)S(1)}, f32[2,96,1024]{2,1,0:T(8,128)}, u32[]{:S(2)}) copy-start(f32[2,96,1024]{2,1,0:T(8,128)} %multiply_subtract_fusion) | copy-start | bytes 2359300
  139.2 7.0 %collective-permute-start.12 = (f32[1,96,256]{2,1,0:T(8,128)S(1)}, f32[1,96,256]{2,1,0:T(8,128)S(1)}, u32[]{:S(2)}, u32[]{:S(2)}) collective-permute-start(f32[1,96,256]{2,1,0:T(8,128)S(1)} %get-tuple-element.10), channel_id=1, source_target_pairs={{0,4},{4,8},{8,12},{12,16},{16,20},{20,24},{24,28},{1,5},{5,9},{9,... | collective-permute-start | bytes 294920 | tf_op jit(solution)/shard_map/ppermute | solution.py:24
  141.7 4.5 %collective-permute-start.13 = (f32[1,96,256]{2,1,0:T(8,128)S(1)}, f32[1,96,256]{2,1,0:T(8,128)S(1)}, u32[]{:S(2)}, u32[]{:S(2)}) collective-permute-start(f32[1,96,256]{2,1,0:T(8,128)S(1)} %get-tuple-element.11), channel_id=1, source_target_pairs={{4,0},{8,4},{12,8},{16,12},{20,16},{24,20},{28,24},{5,1},{9,5},{13... | collective-permute-start | bytes 294920 | tf_op jit(solution)/shard_map/ppermute | solution.py:25
  143.0 6.6 %collective-permute-start.14 = (f32[2,96,256]{2,1,0:T(8,128)S(1)}, f32[2,96,256]{2,1,0:T(8,128)S(1)}, u32[]{:S(2)}, u32[]{:S(2)}) collective-permute-start(f32[2,96,256]{2,1,0:T(8,128)S(1)} %get-tuple-element.14), channel_id=1, source_target_pairs={{0,1},{1,2},{2,3},{4,5},{5,6},{6,7},{8,9},{9,10},{10,11},{12,13},{... | collective-permute-start | bytes 589832 | tf_op jit(solution)/shard_map/ppermute | solution.py:28
  144.6 9.5 %collective-permute-start.15 = (f32[2,96,256]{2,1,0:T(8,128)S(1)}, f32[2,96,256]{2,1,0:T(8,128)S(1)}, u32[]{:S(2)}, u32[]{:S(2)}) collective-permute-start(f32[2,96,256]{2,1,0:T(8,128)S(1)} %get-tuple-element.15), channel_id=1, source_target_pairs={{1,0},{2,1},{3,2},{5,4},{6,5},{7,6},{9,8},{10,9},{11,10},{13,12},{... | collective-permute-start | bytes 589832 | tf_op jit(solution)/shard_map/ppermute | solution.py:29
  155.1 18.0 %copy-start.1 = (f32[2,96,1024]{2,1,0:T(8,128)S(1)}, f32[2,96,1024]{2,1,0:T(8,128)}, u32[]{:S(2)}) copy-start(f32[2,96,1024]{2,1,0:T(8,128)} %copy-done) | copy-start | bytes 2359300
  176.9 14.9 %all-to-all-start.5 = ((f32[32,1,96]{2,1,0:T(1,128)}), f32[32,1,96]{2,1,0:T(1,128)S(1)}, u32[]{:S(2)}, u32[]{:S(2)}) async-start(f32[32,1,96]{2,1,0:T(1,128)} %broadcast_in_dim.97), calls=%async_computation.5 | async-start | bytes 32768 | tf_op jit(solution)/shard_map/all_to_all | solution.py:137
  181.1 10.8 %collective-permute-start.16 = (f32[1,96,256]{2,1,0:T(8,128)}, f32[1,96,256]{2,1,0:T(8,128)}, u32[]{:S(2)}, u32[]{:S(2)}) collective-permute-start(f32[1,96,256]{2,1,0:T(8,128)} %get-tuple-element.2), channel_id=1, source_target_pairs={{0,4},{4,8},{8,12},{12,16},{16,20},{20,24},{24,28},{1,5},{5,9},{9,... | collective-permute-start | bytes 294920 | tf_op jit(solution)/shard_map/ppermute | solution.py:24
  185.7 7.3 %collective-permute-start.17 = (f32[1,96,256]{2,1,0:T(8,128)}, f32[1,96,256]{2,1,0:T(8,128)}, u32[]{:S(2)}, u32[]{:S(2)}) collective-permute-start(f32[1,96,256]{2,1,0:T(8,128)} %get-tuple-element.3), channel_id=1, source_target_pairs={{4,0},{8,4},{12,8},{16,12},{20,16},{24,20},{28,24},{5,1},{9,5},{13... | collective-permute-start | bytes 294920 | tf_op jit(solution)/shard_map/ppermute | solution.py:25
  187.0 8.7 %collective-permute-start.18 = (f32[2,96,256]{2,1,0:T(8,128)}, f32[2,96,256]{2,1,0:T(8,128)S(1)}, u32[]{:S(2)}, u32[]{:S(2)}) collective-permute-start(f32[2,96,256]{2,1,0:T(8,128)} %get-tuple-element.6), channel_id=1, source_target_pairs={{0,1},{1,2},{2,3},{4,5},{5,6},{6,7},{8,9},{9,10},{10,11},{12,13},{... | collective-permute-start | bytes 589832 | tf_op jit(solution)/shard_map/ppermute | solution.py:28
  190.5 9.7 %collective-permute-start.19 = (f32[2,96,256]{2,1,0:T(8,128)}, f32[2,96,256]{2,1,0:T(8,128)S(1)}, u32[]{:S(2)}, u32[]{:S(2)}) collective-permute-start(f32[2,96,256]{2,1,0:T(8,128)} %get-tuple-element.7), channel_id=1, source_target_pairs={{1,0},{2,1},{3,2},{5,4},{6,5},{7,6},{9,8},{10,9},{11,10},{13,12},{... | collective-permute-start | bytes 589832 | tf_op jit(solution)/shard_map/ppermute | solution.py:29
  191.8 9.3 %copy-start.6 = (f32[2,96,1024]{2,1,0:T(8,128)S(1)}, f32[2,96,1024]{2,1,0:T(8,128)}, u32[]{:S(2)}) copy-start(f32[2,96,1024]{2,1,0:T(8,128)} %multiply_subtract_fusion) | copy-start | bytes 2359300
  191.8 9.3 %copy-start.11 = (f32[2,96,1024]{2,1,0:T(8,128)S(1)}, f32[2,96,1024]{2,1,0:T(8,128)}, u32[]{:S(2)}) copy-start(f32[2,96,1024]{2,1,0:T(8,128)} %get-tuple-element.55) | copy-start | bytes 2359300
  191.9 9.3 %copy-start.14 = (f32[2,96,1024]{2,1,0:T(8,128)S(1)}, f32[2,96,1024]{2,1,0:T(8,128)}, u32[]{:S(2)}) copy-start(f32[2,96,1024]{2,1,0:T(8,128)} %copy-done.13) | copy-start | bytes 2359300
  (12 other events, 40.3 us)
